TPU v7x, 32 devices: a whole 2x2x4 slice. The times are simulated.
32 devices in a mesh: vis: 16 (over z, y, x), chan: 2 (over core).
Axes of the slice: x: 2, y: 2, z: 4, core: 2. Of those that a mesh axis runs over, the one named last changes fastest.
Arguments:
- patch_intensity: float32 [512, 2, 2, 512], P('vis', 'chan'), may hold values from -6 to 6
- recorded_samples: float32 [2, 2, 16384], P('chan', None, 'vis'), may hold values from -6 to 6
- sample_importance: float32 [16384], P('vis'), may hold values from 0.3 to 3
- block_populations: int32 [64], P('vis'), may hold values from 64 to 256, as said below
- receiver_pairs: int32 [16384, 2], P('vis'), may hold values from 0 to 511
- sample_rotation_phase: float32 [16384], P('vis'), may hold values from -1 to 1
- spectral_scaling: float32 [2], P('chan'), may hold values from 0.7 to 1.4
- receiver_positions: float32 [2, 512], replicated, may hold values from -2500 to 2500
- patch_layout_position: int32 [2, 2], replicated, may hold values from 0 to 63
Outputs:
- new_sky: float32 [512, 2, 2, 512], P('vis', 'chan')
- residual: float32 [2, 2, 16384], P('chan', None, 'vis')
Inputs may be any that keep to these rules, and one draw needn't show every extreme that they name: `block_populations`: live visibility slots of each block; some block is full.
All inputs are finite; a program needn't handle non-finite values.
Results may differ from a plain program's by a relative error of at most 0.006.
Values may be sent and summed in bfloat16 or wider, within the bound.
No kernel may reach another device: no remote copies, remote signals or barrier semaphores. Data moves between devices by JAX's collectives and lax.ppermute only.
A program may use at most 128 MiB of HBM per device.

v0:
```python
import math

import jax
import jax.numpy as jnp
from jax import lax
from jax.sharding import PartitionSpec as P

GRID = 64
BLOCK = 256
LANE_BLOCK = 128
COORD_STEPS = 16


full_turn = 6.283185307179586
step_size = 0.5
smooth_weight = 0.5


def extended(cells, sides, width):
    for axis, dim in sides:
        count = lax.axis_size(axis)
        ends = count - 1
        head = lax.slice_in_dim(cells, 0, width, axis=dim)
        tail = lax.slice_in_dim(cells, cells.shape[dim] - width, cells.shape[dim], axis=dim)
        cells = jnp.concatenate(
            [
                lax.ppermute(tail, axis, [(i, (i + 1) % count) for i in range(ends)]),
                cells,
                lax.ppermute(head, axis, [((i + 1) % count, i) for i in range(ends)]),
            ],
            axis=dim,
        )
    return cells


def receiver_lookup_dict(table_row, antenna_ids):
    numbers = jnp.arange(table_row.shape[0], dtype=jnp.int32)
    return jnp.sum(
        jnp.where(antenna_ids[:, None] == numbers[None, :], table_row[None, :], 0.0), axis=1
    )


def turns(coord, pixel, image):
    whole = jnp.round(coord * COORD_STEPS).astype(jnp.int32)
    rest = coord - whole.astype(jnp.float32) / COORD_STEPS
    period = COORD_STEPS * image
    exact = jnp.bitwise_and(whole[None, :] * pixel, period - 1).astype(jnp.float32) / period
    return exact + rest[None, :] * pixel.astype(jnp.float32) / image


def phase_table(coord, first_pixel, facet, image):
    blocks = facet // LANE_BLOCK
    starts = first_pixel[:, None] + LANE_BLOCK * jnp.arange(blocks, dtype=jnp.int32)[None, :]
    coarse = full_turn * turns(coord, starts.reshape(-1, 1), image)
    fine = full_turn * turns(coord, jnp.arange(LANE_BLOCK, dtype=jnp.int32)[:, None], image)
    coarse_c, coarse_s, fine_c, fine_s = lax.optimization_barrier(
        (jnp.cos(coarse), jnp.sin(coarse), jnp.cos(fine), jnp.sin(fine))
    )
    count = coord.shape[0]
    faces = first_pixel.shape[0]

    def spread(a):
        return jnp.broadcast_to(
            a.reshape(faces, blocks, 1, count), (faces, blocks, LANE_BLOCK, count)
        ).reshape(faces, facet, count)

    def tile(a):
        return jnp.broadcast_to(a[None, None], (faces, blocks, LANE_BLOCK, count)).reshape(
            faces, facet, count
        )

    pc, ps, qc, qs = spread(coarse_c), spread(coarse_s), tile(fine_c), tile(fine_s)
    return (pc * qc - ps * qs, ps * qc + pc * qs)


def local(
    patch_intensity,
    recorded_samples,
    sample_importance,
    block_populations,
    receiver_pairs,
    sample_rotation_phase,
    spectral_scaling,
    receiver_positions,
    patch_layout_position,
):
    rows_dev = patch_intensity.shape[0]
    ch_local = patch_intensity.shape[1]
    facets_here = patch_intensity.shape[2]
    facet = patch_intensity.shape[3]
    nvis = sample_importance.shape[0]
    n_vis = lax.axis_size("vis")
    image = GRID * facet
    norm_pred = 1.0 / math.sqrt(facets_here * facet * facet)
    norm_grad = 1.0 / math.sqrt(nvis * n_vis)
    eastward_shift = receiver_lookup_dict(
        receiver_positions[0], receiver_pairs[:, 0]
    ) - receiver_lookup_dict(receiver_positions[0], receiver_pairs[:, 1])
    northward_shift = receiver_lookup_dict(
        receiver_positions[1], receiver_pairs[:, 0]
    ) - receiver_lookup_dict(receiver_positions[1], receiver_pairs[:, 1])
    base_u = eastward_shift * jnp.cos(sample_rotation_phase) - northward_shift * jnp.sin(
        sample_rotation_phase
    )
    base_v = eastward_shift * jnp.sin(sample_rotation_phase) + northward_shift * jnp.cos(
        sample_rotation_phase
    )
    slots = jnp.arange(nvis, dtype=jnp.int32)
    block_of = slots // BLOCK
    block_numbers = jnp.arange(block_populations.shape[0], dtype=jnp.int32)
    block_count = jnp.sum(
        jnp.where(block_of[:, None] == block_numbers[None, :], block_populations[None, :], 0),
        axis=1,
    )
    scale_vis = (slots % BLOCK < block_count).astype(jnp.float32) * sample_importance
    sky_half = patch_intensity.astype(jnp.bfloat16)
    first_row = patch_layout_position[:, 0] * facet - image // 2
    first_col = patch_layout_position[:, 1] * facet - image // 2

    piece = lax.all_to_all(
        jnp.broadcast_to(sky_half[None], (n_vis,) + sky_half.shape).reshape(
            (n_vis * rows_dev,) + sky_half.shape[1:]
        ),
        "vis",
        0,
        0,
        tiled=True,
    )

    new_rows = []
    residuals = []
    for c in range(ch_local):
        coord_u = spectral_scaling[c] * base_u
        coord_v = spectral_scaling[c] * base_v
        row_cos, row_sin = phase_table(coord_u, first_row, facet, image)
        col_cos, col_sin = phase_table(coord_v, first_col, facet, image)
        cols = lax.optimization_barrier(
            jnp.concatenate([col_cos, col_sin], axis=2).astype(jnp.bfloat16)
        )
        sky_rows = jnp.transpose(piece[:, c], (1, 0, 2))
        waves = jnp.einsum("fij,fjk->fik", sky_rows, cols, preferred_element_type=jnp.float32)
        wave_c = waves[:, :, :nvis]
        wave_s = waves[:, :, nvis:]
        sum_re = jnp.sum(row_cos * wave_c - row_sin * wave_s, axis=(0, 1))
        sum_im = -jnp.sum(row_cos * wave_s + row_sin * wave_c, axis=(0, 1))
        resid_real = scale_vis * (norm_pred * sum_re - recorded_samples[c, 0])
        resid_imag = scale_vis * (norm_pred * sum_im - recorded_samples[c, 1])
        z_one = (row_cos * resid_real[None, None, :] - row_sin * resid_imag[None, None, :]).astype(
            jnp.bfloat16
        )
        z_two = (row_sin * resid_real[None, None, :] + row_cos * resid_imag[None, None, :]).astype(
            jnp.bfloat16
        )
        zs = jnp.concatenate([z_one, -z_two], axis=2)
        grad = jnp.einsum("fik,fjk->ifj", zs, cols, preferred_element_type=jnp.float32)
        new_rows.append(grad)
        residuals.append(jnp.stack([resid_real, resid_imag], axis=0))
    partial = jnp.stack(new_rows, axis=1)
    parts = lax.all_to_all(partial, "vis", 0, 0, tiled=True)
    gradient = jnp.sum(parts.reshape((n_vis, rows_dev) + parts.shape[1:]), axis=0)
    padded = extended(patch_intensity.astype(jnp.bfloat16), (("chan", 1),), 1).astype(
        patch_intensity.dtype
    )
    left_side = padded[:, :-2]
    right_side = padded[:, 2:]
    chan_index = lax.axis_index("chan") * ch_local + jnp.arange(ch_local, dtype=jnp.int32)
    total_chan = ch_local * lax.axis_size("chan")
    has_left = (chan_index >= 1).astype(jnp.float32)[None, :, None, None]
    has_right = (chan_index <= total_chan - 2).astype(jnp.float32)[None, :, None, None]
    smooth = has_left * (patch_intensity - left_side) + has_right * (patch_intensity - right_side)
    new_sky = patch_intensity - step_size * (norm_grad * gradient + smooth_weight * smooth)
    residual = jnp.stack(residuals, axis=0)
    return (new_sky, residual)


def solution(mesh):
    return jax.shard_map(
        local,
        mesh=mesh,
        in_specs=(
            P("vis", "chan", None, None),
            P("chan", None, "vis"),
            P("vis"),
            P("vis"),
            P("vis", None),
            P("vis"),
            P("chan"),
            P(),
            P(),
        ),
        out_specs=(P("vis", "chan", None, None), P("chan", None, "vis")),
        check_vma=False,
    )
```

profile of v0, /device:TPU:12, one launch (start us, length us, event | category | flops | bytes accessed | tf_op | source)
XLA Modules:
  0.0 105.1 jit_solution(17170103534239344598)
XLA Ops:
  0.6 0.9 copy.42
  1.6 0.1 copy.24
  1.6 1.8 %broadcast_in_dim.175 = bf16[16,32,2,512]{3,2,1,0:T(2,128)(2,1)} broadcast(bf16[32,2,512]{2,1,0:T(2,128)(2,1)S(1)} %copy.24), dimensions={1,2,3} | broadcast | bytes 1114112 | tf_op jit(solution)/shard_map/broadcast_in_dim | solution.py:121
  3.4 7.2 %all-to-all-start = ((bf16[512,1,2,512]{3,2,1,0:T(2,128)(2,1)}), bf16[512,1,2,512]{3,2,1,0:T(2,128)(2,1)S(1)}, u32[]{:S(2)}, u32[]{:S(2)}) async-start(bf16[512,1,2,512]{3,2,1,0:T(2,128)(2,1)} %bitcast.14), calls=%async_computation | async-start | bytes 2097152 | tf_op jit(solution)/shard_map/all_to_all | solution.py:120
  10.6 0.8 fusion.55
  11.4 0.8 fusion.57
  12.2 0.7 fusion.56
  12.9 1.0 add_reduce_fusion
  13.9 0.1 broadcast_add_fusion
  13.9 1.6 %select_reduce_fusion.3 = (f32[1024]{0:T(1024)S(1)}, f32[1024]{0:T(1024)S(1)}, f32[1024]{0:T(1024)S(1)}, f32[1024]{0:T(1024)S(1)}) fusion(f32[512]{0:T(512)S(1)} %bitcast.174, s32[1024]{0:T(1024)S(1)} %bitcast.170, f32[512]{0:T(512)S(1)} %bitcast.173, s32[1024]{0:T(1024)S(1)} %bitcast.169), kind=kLoop, calls=%fused_computation.41 | loop fusion | flops 5238784 | bytes 28672 | tf_op jit(solution)/shard_map/reduce_sum | solution.py:38
  16.2 0.1 add.106
  16.3 0.1 add.113
  16.4 0.3 fusion.42
  16.8 4.0 %fusion.32 = (f32[128,1024]{1,0:T(8,128)S(1)}, f32[128,1024]{1,0:T(8,128)S(1)}, f32[128,1024]{1,0:T(8,128)S(1)}, f32[128,1024]{1,0:T(8,128)S(1)}) fusion(f32[1024]{0:T(1024)S(1)} %multiply_subtract_fusion, s32[1024]{0:T(1024)S(1)} %get-tuple-element.32, f32[128]{0:T(128)S(1)} %iota_convert_fusion, f32[1024]{0:T(1024)S(1)} %multiply_subtract_fusion.1, ...), kind=kLoop, calls=%fused_computation.47 | loop fusion | flops 2097152 | bytes 2114048 | tf_op jit(solution)/shard_map/sin | solution.py:57
  20.8 0.2 broadcast_in_dim.154
  21.0 0.2 broadcast_in_dim.159
  21.3 1.2 %fusion.1 = (bf16[2,512,1024]{2,1,0:T(8,128)(2,1)S(1)}, bf16[2,512,1024]{2,1,0:T(8,128)(2,1)S(1)}) fusion(f32[512,1024]{1,0:T(8,128)S(1)} %bitcast.165, f32[2,4,1024]{2,1,0:T(4,128)S(1)} %broadcast_in_dim.157, f32[512,1024]{1,0:T(8,128)S(1)} %bitcast.164, f32[2,4,1024]{2,1,0:T(4,128)S(1)} %broadcast_in_dim.152), kind=kLoop, calls=%fused_computation.10 | loop fusion | flops 8388608 | bytes 8454144 | tf_op jit(solution)/shard_map/convert
  22.5 0.0 copy-start.4
  22.5 0.0 copy-start.2
  22.5 2.3 %pad_maximum_fusion = bf16[2,512,2048]{2,1,0:T(8,128)(2,1)} fusion(bf16[2,512,1024]{2,1,0:T(8,128)(2,1)S(1)} %get-tuple-element.37, bf16[2,512,1024]{2,1,0:T(8,128)(2,1)S(1)} %get-tuple-element.36), kind=kLoop, calls=%fused_computation.31 | loop fusion | flops 8388608 | bytes 8388608 | tf_op jit(solution)/shard_map/concatenate | solution.py:138
  24.9 0.0 copy-done.4
  24.9 0.1 select_reduce_fusion.4
  25.0 0.0 copy-done.2
  25.0 10.9 %all-to-all-done = bf16[512,1,2,512]{3,2,1,0:T(2,128)(2,1)S(1)} async-done(((bf16[512,1,2,512]{3,2,1,0:T(2,128)(2,1)}), bf16[512,1,2,512]{3,2,1,0:T(2,128)(2,1)S(1)}, u32[]{:S(2)}, u32[]{:S(2)}) %all-to-all-start) | async-done | bytes 1048608 | tf_op jit(solution)/shard_map/all_to_all | solution.py:120
  35.9 4.5 %convolution_bitcast_fusion = f32[2,512,2048]{2,1,0:T(8,128)S(1)} fusion(bf16[2,512,2048]{2,1,0:T(8,128)(2,1)} %pad_maximum_fusion, bf16[512,1,2,512]{3,2,1,0:T(2,128)(2,1)S(1)} %all-to-all-done), kind=kOutput, calls=%fused_computation.8 | convolution fusion | flops 2147483648 | bytes 13631488 | tf_op jit(solution)/shard_map/fij,fjk->fik/dot_general | solution.py:141
  40.5 0.3 broadcast_in_dim.164
  40.7 0.3 broadcast_in_dim.169
  41.0 0.0 copy-start.3
  41.0 2.2 %fusion.11 = (f32[1024]{0:T(1024)S(1)}, f32[1024]{0:T(1024)S(1)}) fusion(f32[2,512,2048]{2,1,0:T(8,128)S(1)} %convolution_bitcast_fusion, f32[512,1024]{1,0:T(8,128)S(1)} %bitcast.160, f32[2,4,1024]{2,1,0:T(4,128)S(1)} %broadcast_in_dim.167, f32[512,1024]{1,0:T(8,128)S(1)} %bitcast.157, f32[2,4,1024]{2,1,0:T(4,128)S(1)} %broadcast_in_dim.162), kind=kLoop, calls=%fused_computation.20 | loop fusion | flops 14678016 | bytes 12656640 | tf_op jit(solution)/shard_map/reduce_sum | solution.py:144
  43.2 0.0 copy-done.3
  43.2 1.4 %fusion.13 = bf16[2,512,1024]{2,1,0:T(8,128)(2,1)S(1)} fusion(f32[1024]{0:T(1024)S(1)} %get-tuple-element.49, f32[1024]{0:T(1024)S(1)} %get-tuple-element.48, f32[512,1024]{1,0:T(8,128)S(1)} %bitcast.161, f32[2,4,1024]{2,1,0:T(4,128)S(1)} %broadcast_in_dim.167, f32[512,1024]{1,0:T(8,128)S(1)} %bitcast.158, f32[2,4,1024]{2,1,0:T(4,128)S(1)} %broadcast_in_dim.162), kind=kLoop, calls=%fused_computation.22 | loop fusion | flops 10485760 | bytes 6365184 | tf_op jit(solution)/shard_map/convert_element_type | solution.py:148
  44.6 0.0 copy-start
  44.6 1.5 %fusion.26 = bf16[2,512,1024]{2,1,0:T(8,128)(2,1)S(1)} fusion(f32[1024]{0:T(1024)S(1)} %get-tuple-element.49, f32[1024]{0:T(1024)S(1)} %get-tuple-element.48, f32[512,1024]{1,0:T(8,128)S(1)} %bitcast.162, f32[2,4,1024]{2,1,0:T(4,128)S(1)} %broadcast_in_dim.167, f32[512,1024]{1,0:T(8,128)S(1)} %bitcast.159, f32[2,4,1024]{2,1,0:T(4,128)S(1)} %broadcast_in_dim.162), kind=kLoop, calls=%fused_computation.36 | loop fusion | flops 11534336 | bytes 6365184 | tf_op jit(solution)/shard_map/neg | solution.py:154
  46.1 0.7 copy-done
  46.8 2.4 %fusion.27 = f32[512,1,2,512]{0,3,2,1:T(8,128)S(1)} fusion(bf16[2,512,2048]{2,1,0:T(8,128)(2,1)S(1)} %copy-done, bf16[2,512,1024]{2,1,0:T(8,128)(2,1)S(1)} %fusion.26, bf16[2,512,1024]{2,1,0:T(8,128)(2,1)S(1)} %fusion.13), kind=kOutput, calls=%fused_computation.43 | convolution fusion | flops 2155872256 | bytes 10485760 | tf_op jit(solution)/shard_map/fik,fjk->ifj/dot_general | solution.py:155
  49.1 0.0 copy-start.1
  49.1 2.5 %copy.26 = f32[512,1,2,512]{3,2,1,0:T(2,128)} copy(f32[512,1,2,512]{0,3,2,1:T(8,128)S(1)} %fusion.27) | data formatting | bytes 4194304 | tf_op jit(solution)/shard_map/stack | solution.py:158
  51.6 4.9 %all-to-all-start.1 = ((f32[512,1,2,512]{3,2,1,0:T(2,128)}), f32[512,1,2,512]{3,2,1,0:T(2,128)S(1)}, u32[]{:S(2)}, u32[]{:S(2)}) async-start(f32[512,1,2,512]{3,2,1,0:T(2,128)} %copy.26), calls=%async_computation.1 | async-start | bytes 4194304 | tf_op jit(solution)/shard_map/all_to_all | solution.py:159
  56.5 0.0 copy-done.1
  56.6 1.3 %collective-permute-start = (bf16[32,1,2,512]{3,0,2,1:T(8,128)(2,1)S(1)}, bf16[32,1,2,512]{3,0,2,1:T(8,128)(2,1)S(1)}, u32[]{:S(2)}, u32[]{:S(2)}) collective-permute-start(bf16[32,1,2,512]{3,0,2,1:T(8,128)(2,1)S(1)} %copy.40), channel_id=1, source_target_pairs={{0,1},{2,3},{4,5},{6,7},{8,9},{10,11},{12,13},{14,15},{16,17},{18,... | collective-permute-start | bytes 196616 | tf_op jit(solution)/shard_map/ppermute | solution.py:27
  57.9 1.3 %collective-permute-start.1 = (bf16[32,1,2,512]{3,0,2,1:T(8,128)(2,1)S(1)}, bf16[32,1,2,512]{3,0,2,1:T(8,128)(2,1)S(1)}, u32[]{:S(2)}, u32[]{:S(2)}) collective-permute-start(bf16[32,1,2,512]{3,0,2,1:T(8,128)(2,1)S(1)} %copy.40), channel_id=1, source_target_pairs={{1,0},{3,2},{5,4},{7,6},{9,8},{11,10},{13,12},{15,14},{17,16},{19,... | collective-permute-start | bytes 196616 | tf_op jit(solution)/shard_map/ppermute | solution.py:29
  59.2 0.6 maximum_bitcast_fusion
  59.8 43.6 %all-to-all-done.1 = f32[512,1,2,512]{3,2,1,0:T(2,128)S(1)} async-done(((f32[512,1,2,512]{3,2,1,0:T(2,128)}), f32[512,1,2,512]{3,2,1,0:T(2,128)S(1)}, u32[]{:S(2)}, u32[]{:S(2)}) %all-to-all-start.1) | async-done | bytes 2097184 | tf_op jit(solution)/shard_map/all_to_all | solution.py:159
  103.4 0.8 reduce.1
  104.2 0.0 collective-permute-done
  104.3 0.0 collective-permute-done.1
  104.3 0.1 fusion.41
  104.3 0.8 copy.31
  (15 shorter events, 0.2 us)
Async XLA Ops:
  3.4 32.5 %all-to-all-start = ((bf16[512,1,2,512]{3,2,1,0:T(2,128)(2,1)}), bf16[512,1,2,512]{3,2,1,0:T(2,128)(2,1)S(1)}, u32[]{:S(2)}, u32[]{:S(2)}) async-start(bf16[512,1,2,512]{3,2,1,0:T(2,128)(2,1)} %bitcast.14), calls=%async_computation | async-start | bytes 2097152 | tf_op jit(solution)/shard_map/all_to_all | solution.py:120
  22.5 2.4 %copy-start.4 = (s32[4]{0:T(128)S(1)}, s32[4]{0:T(128)}, u32[]{:S(2)}) copy-start(s32[4]{0:T(128)} %param.12) | copy-start | bytes 52
  22.5 2.5 %copy-start.2 = (f32[1,2,1024]{2,1,0:T(2,128)S(1)}, f32[1,2,1024]{2,1,0:T(2,128)}, u32[]{:S(2)}) copy-start(f32[1,2,1024]{2,1,0:T(2,128)} %param.10) | copy-start | bytes 24580
  41.0 2.2 %copy-start.3 = (f32[1024]{0:T(1024)S(1)}, f32[1024]{0:T(1024)}, u32[]{:S(2)}) copy-start(f32[1024]{0:T(1024)} %param.11) | copy-start | bytes 12292
  44.6 2.2 %copy-start = (bf16[2,512,2048]{2,1,0:T(8,128)(2,1)S(1)}, bf16[2,512,2048]{2,1,0:T(8,128)(2,1)}, u32[]{:S(2)}) copy-start(bf16[2,512,2048]{2,1,0:T(8,128)(2,1)} %pad_maximum_fusion) | copy-start | bytes 12582916
  49.1 7.4 %copy-start.1 = (f32[32,1,2,512]{3,2,1,0:T(2,128)S(1)}, f32[32,1,2,512]{3,2,1,0:T(2,128)}, u32[]{:S(2)}) copy-start(f32[32,1,2,512]{3,2,1,0:T(2,128)} %param.9) | copy-start | bytes 393220
  51.6 51.8 %all-to-all-start.1 = ((f32[512,1,2,512]{3,2,1,0:T(2,128)}), f32[512,1,2,512]{3,2,1,0:T(2,128)S(1)}, u32[]{:S(2)}, u32[]{:S(2)}) async-start(f32[512,1,2,512]{3,2,1,0:T(2,128)} %copy.26), calls=%async_computation.1 | async-start | bytes 4194304 | tf_op jit(solution)/shard_map/all_to_all | solution.py:159
  56.6 47.7 %collective-permute-start = (bf16[32,1,2,512]{3,0,2,1:T(8,128)(2,1)S(1)}, bf16[32,1,2,512]{3,0,2,1:T(8,128)(2,1)S(1)}, u32[]{:S(2)}, u32[]{:S(2)}) collective-permute-start(bf16[32,1,2,512]{3,0,2,1:T(8,128)(2,1)S(1)} %copy.40), channel_id=1, source_target_pairs={{0,1},{2,3},{4,5},{6,7},{8,9},{10,11},{12,13},{14,15},{16,17},{18,... | collective-permute-start | bytes 196616 | tf_op jit(solution)/shard_map/ppermute | solution.py:27
  57.9 46.4 %collective-permute-start.1 = (bf16[32,1,2,512]{3,0,2,1:T(8,128)(2,1)S(1)}, bf16[32,1,2,512]{3,0,2,1:T(8,128)(2,1)S(1)}, u32[]{:S(2)}, u32[]{:S(2)}) collective-permute-start(bf16[32,1,2,512]{3,0,2,1:T(8,128)(2,1)S(1)} %copy.40), channel_id=1, source_target_pairs={{1,0},{3,2},{5,4},{7,6},{9,8},{11,10},{13,12},{15,14},{17,16},{19,... | collective-permute-start | bytes 196616 | tf_op jit(solution)/shard_map/ppermute | solution.py:29
where the time goes:
time: 106 us; the launch traced here: 105 us
  waiting for transfers between devices  54.6 us (52%)
  other arithmetic  17.1 us (16%)
  starting transfers between devices  14.7 us (14%)
  local copies, waits for them, and re-layouts  10.3 us (10%)
  matrix products  6.89 us (6%)
  between operations  1.56 us (1%)
    all_to_all x1, waiting for transfers between devices, local(): parts = lax.all_to_all(partial, 'vis', 0, 0, tiled=True)  43.6 us
    all_to_all x1, waiting for transfers between devices, local(): lax.all_to_all(jnp.broadcast_to(sky_half[None], (n_vis,) + sky_half.shape...  10.9 us
    all_to_all x1, starting transfers between devices, local(): lax.all_to_all(jnp.broadcast_to(sky_half[None], (n_vis,) + sky_half.shape...  7.17 us
    all_to_all x1, starting transfers between devices, local(): parts = lax.all_to_all(partial, 'vis', 0, 0, tiled=True)  4.93 us
    dot_general x1, matrix products, local(): jnp.einsum('fij,fjk->fik', sky_rows, cols, preferred_element_type=jnp.flo...  4.53 us
    sin x1, other arithmetic, phase_table(): jnp.sin(fine)  3.95 us
    another operation x1, local copies, waits for them, and re-layouts, local(): partial = jnp.stack(new_rows, axis=1)  2.46 us
    unnamed x13, local copies, waits for them, and re-layouts  2.44 us
  transfers between devices with their start and end apart: 4, of which 2 were waited for; matrix products, arithmetic and copies ran while one was open for 14% of the time, Pallas kernels for 0%

commit v1 on v0

--- a/solution.py
+++ b/solution.py
@@ -156,8 +156,10 @@
         new_rows.append(grad)
         residuals.append(jnp.stack([resid_real, resid_imag], axis=0))
     partial = jnp.stack(new_rows, axis=1)
-    parts = lax.all_to_all(partial, "vis", 0, 0, tiled=True)
-    gradient = jnp.sum(parts.reshape((n_vis, rows_dev) + parts.shape[1:]), axis=0)
+    parts = lax.all_to_all(partial.astype(jnp.bfloat16), "vis", 0, 0, tiled=True)
+    gradient = jnp.sum(
+        parts.reshape((n_vis, rows_dev) + parts.shape[1:]).astype(jnp.float32), axis=0
+    )
     padded = extended(patch_intensity.astype(jnp.bfloat16), (("chan", 1),), 1).astype(
         patch_intensity.dtype
     )

time: 106 us -> 82 us (0.77)
  the two profiles are of different devices: /device:TPU:12 before, /device:TPU:0 now
where the time goes in v1:
time: 82 us; the launch traced here: 81.5 us
  waiting for transfers between devices  29.7 us (36%)
  starting transfers between devices  16.7 us (20%)
  other arithmetic  16.5 us (20%)
  local copies, waits for them, and re-layouts  10.1 us (12%)
  matrix products  6.89 us (8%)
  between operations  1.59 us (2%)
    all_to_all x1, waiting for transfers between devices, local(): lax.all_to_all(partial.astype(jnp.bfloat16), 'vis', 0, 0, tiled=True)  19.7 us
    all_to_all x1, waiting for transfers between devices, local(): lax.all_to_all(jnp.broadcast_to(sky_half[None], (n_vis,) + sky_half.shape...  10 us
    all_to_all x1, starting transfers between devices, local(): lax.all_to_all(jnp.broadcast_to(sky_half[None], (n_vis,) + sky_half.shape...  8.31 us
    all_to_all x1, starting transfers between devices, local(): lax.all_to_all(partial.astype(jnp.bfloat16), 'vis', 0, 0, tiled=True)  5.82 us
    dot_general x1, matrix products, local(): jnp.einsum('fij,fjk->fik', sky_rows, cols, preferred_element_type=jnp.flo...  4.53 us
    sin x1, other arithmetic, phase_table(): jnp.sin(fine)  3.95 us
    unnamed x13, local copies, waits for them, and re-layouts  2.44 us
    dot_general x1, matrix products, local(): jnp.einsum('fik,fjk->ifj', zs, cols, preferred_element_type=jnp.float32)  2.36 us
  transfers between devices with their start and end apart: 4, of which 2 were waited for; matrix products, arithmetic and copies ran while one was open for 18% of the time, Pallas kernels for 0%

profile of v1, /device:TPU:0, one launch (start us, length us, event | category | flops | bytes accessed | tf_op | source)
XLA Modules:
  0.0 81.5 jit_solution(12466118073585437597)
XLA Ops:
  0.6 0.9 %copy.40 = bf16[32,1,2,512]{3,0,2,1:T(8,128)(2,1)S(1)} copy(f32[32,1,2,512]{3,2,1,0:T(2,128)} %param.9) | data formatting | bytes 196608 | tf_op args[0]
  1.6 0.1 copy.24
  1.6 1.8 %broadcast_in_dim.175 = bf16[16,32,2,512]{3,2,1,0:T(2,128)(2,1)} broadcast(bf16[32,2,512]{2,1,0:T(2,128)(2,1)S(1)} %copy.24), dimensions={1,2,3} | broadcast | bytes 1114112 | tf_op jit(solution)/shard_map/broadcast_in_dim | solution.py:121
  3.4 8.3 %all-to-all-start = ((bf16[512,1,2,512]{3,2,1,0:T(2,128)(2,1)}), bf16[512,1,2,512]{3,2,1,0:T(2,128)(2,1)S(1)}, u32[]{:S(2)}, u32[]{:S(2)}) async-start(bf16[512,1,2,512]{3,2,1,0:T(2,128)(2,1)} %bitcast.14), calls=%async_computation | async-start | bytes 2097152 | tf_op jit(solution)/shard_map/all_to_all | solution.py:120
  11.8 0.8 fusion.58
  12.5 0.8 fusion.60
  13.3 0.7 fusion.59
  14.0 1.0 %add_reduce_fusion = (s32[2]{0:T(128)S(1)}, s32[2]{0:T(128)S(1)}) fusion(s32[2,2]{1,0:T(2,128)} %param.17), kind=kLoop, calls=%fused_computation.93 | loop fusion | flops 8 | bytes 32 | tf_op jit(solution)/shard_map/sub | solution.py:117
  15.0 0.1 broadcast_add_fusion
  15.1 1.6 %select_reduce_fusion.3 = (f32[1024]{0:T(1024)S(1)}, f32[1024]{0:T(1024)S(1)}, f32[1024]{0:T(1024)S(1)}, f32[1024]{0:T(1024)S(1)}) fusion(f32[512]{0:T(512)S(1)} %bitcast.170, s32[1024]{0:T(1024)S(1)} %bitcast.166, f32[512]{0:T(512)S(1)} %bitcast.169, s32[1024]{0:T(1024)S(1)} %bitcast.165), kind=kLoop, calls=%fused_computation.42 | loop fusion | flops 5238784 | bytes 28672 | tf_op jit(solution)/shard_map/reduce_sum | solution.py:38
  17.4 0.1 add.106
  17.5 0.1 add.113
  17.6 0.3 fusion.45
  17.9 4.0 %fusion.35 = (f32[128,1024]{1,0:T(8,128)S(1)}, f32[128,1024]{1,0:T(8,128)S(1)}, f32[128,1024]{1,0:T(8,128)S(1)}, f32[128,1024]{1,0:T(8,128)S(1)}) fusion(f32[1024]{0:T(1024)S(1)} %multiply_subtract_fusion, s32[1024]{0:T(1024)S(1)} %get-tuple-element.32, f32[128]{0:T(128)S(1)} %iota_convert_fusion, f32[1024]{0:T(1024)S(1)} %multiply_subtract_fusion.1, ...), kind=kLoop, calls=%fused_computation.49 | loop fusion | flops 2097152 | bytes 2114048 | tf_op jit(solution)/shard_map/sin | solution.py:57
  21.9 0.2 broadcast_in_dim.154
  22.2 0.2 broadcast_in_dim.159
  22.4 1.2 %fusion.1 = (bf16[2,512,1024]{2,1,0:T(8,128)(2,1)S(1)}, bf16[2,512,1024]{2,1,0:T(8,128)(2,1)S(1)}) fusion(f32[512,1024]{1,0:T(8,128)S(1)} %bitcast.160, f32[2,4,1024]{2,1,0:T(4,128)S(1)} %broadcast_in_dim.157, f32[512,1024]{1,0:T(8,128)S(1)} %bitcast.159, f32[2,4,1024]{2,1,0:T(4,128)S(1)} %broadcast_in_dim.152), kind=kLoop, calls=%fused_computation.10 | loop fusion | flops 8388608 | bytes 8454144 | tf_op jit(solution)/shard_map/convert.1
  23.7 0.0 copy-start.4
  23.7 0.0 copy-start.2
  23.7 2.3 %pad_maximum_fusion = bf16[2,512,2048]{2,1,0:T(8,128)(2,1)} fusion(bf16[2,512,1024]{2,1,0:T(8,128)(2,1)S(1)} %get-tuple-element.37, bf16[2,512,1024]{2,1,0:T(8,128)(2,1)S(1)} %get-tuple-element.36), kind=kLoop, calls=%fused_computation.31 | loop fusion | flops 8388608 | bytes 8388608 | tf_op jit(solution)/shard_map/concatenate | solution.py:138
  26.1 0.0 copy-done.4
  26.1 0.1 select_reduce_fusion.4
  26.2 0.0 copy-done.2
  26.2 10.0 %all-to-all-done = bf16[512,1,2,512]{3,2,1,0:T(2,128)(2,1)S(1)} async-done(((bf16[512,1,2,512]{3,2,1,0:T(2,128)(2,1)}), bf16[512,1,2,512]{3,2,1,0:T(2,128)(2,1)S(1)}, u32[]{:S(2)}, u32[]{:S(2)}) %all-to-all-start) | async-done | bytes 1048608 | tf_op jit(solution)/shard_map/all_to_all | solution.py:120
  36.2 4.5 %convolution_bitcast_fusion = f32[2,512,2048]{2,1,0:T(8,128)S(1)} fusion(bf16[2,512,2048]{2,1,0:T(8,128)(2,1)} %pad_maximum_fusion, bf16[512,1,2,512]{3,2,1,0:T(2,128)(2,1)S(1)} %all-to-all-done), kind=kOutput, calls=%fused_computation.8 | convolution fusion | flops 2147483648 | bytes 13631488 | tf_op jit(solution)/shard_map/fij,fjk->fik/dot_general | solution.py:141
  40.7 0.3 broadcast_in_dim.164
  41.0 0.3 broadcast_in_dim.169
  41.3 0.0 copy-start.3
  41.3 2.2 %fusion.11 = (f32[1024]{0:T(1024)S(1)}, f32[1024]{0:T(1024)S(1)}) fusion(f32[2,512,2048]{2,1,0:T(8,128)S(1)} %convolution_bitcast_fusion, f32[512,1024]{1,0:T(8,128)S(1)} %bitcast.156, f32[2,4,1024]{2,1,0:T(4,128)S(1)} %broadcast_in_dim.167, f32[512,1024]{1,0:T(8,128)S(1)} %bitcast.153, f32[2,4,1024]{2,1,0:T(4,128)S(1)} %broadcast_in_dim.162), kind=kLoop, calls=%fused_computation.20 | loop fusion | flops 14678016 | bytes 12656640 | tf_op jit(solution)/shard_map/reduce_sum | solution.py:144
  43.4 0.0 copy-done.3
  43.5 1.4 %fusion.13 = bf16[2,512,1024]{2,1,0:T(8,128)(2,1)S(1)} fusion(f32[1024]{0:T(1024)S(1)} %get-tuple-element.49, f32[1024]{0:T(1024)S(1)} %get-tuple-element.48, f32[512,1024]{1,0:T(8,128)S(1)} %bitcast.157, f32[2,4,1024]{2,1,0:T(4,128)S(1)} %broadcast_in_dim.167, f32[512,1024]{1,0:T(8,128)S(1)} %bitcast.154, f32[2,4,1024]{2,1,0:T(4,128)S(1)} %broadcast_in_dim.162), kind=kLoop, calls=%fused_computation.22 | loop fusion | flops 10485760 | bytes 6365184 | tf_op jit(solution)/shard_map/convert_element_type | solution.py:148
  44.8 0.0 copy-start
  44.8 1.5 %fusion.26 = bf16[2,512,1024]{2,1,0:T(8,128)(2,1)S(1)} fusion(f32[1024]{0:T(1024)S(1)} %get-tuple-element.49, f32[1024]{0:T(1024)S(1)} %get-tuple-element.48, f32[512,1024]{1,0:T(8,128)S(1)} %bitcast.158, f32[2,4,1024]{2,1,0:T(4,128)S(1)} %broadcast_in_dim.167, f32[512,1024]{1,0:T(8,128)S(1)} %bitcast.155, f32[2,4,1024]{2,1,0:T(4,128)S(1)} %broadcast_in_dim.162), kind=kLoop, calls=%fused_computation.36 | loop fusion | flops 11534336 | bytes 6365184 | tf_op jit(solution)/shard_map/neg | solution.py:154
  46.3 0.7 copy-done
  47.0 2.4 %fusion.30 = bf16[512,1,2,512]{0,3,2,1:T(8,128)(2,1)S(1)} fusion(bf16[2,512,2048]{2,1,0:T(8,128)(2,1)S(1)} %copy-done, bf16[2,512,1024]{2,1,0:T(8,128)(2,1)S(1)} %fusion.26, bf16[2,512,1024]{2,1,0:T(8,128)(2,1)S(1)} %fusion.13), kind=kOutput, calls=%fused_computation.45 | convolution fusion | flops 2156396544 | bytes 9437184 | tf_op jit(solution)/shard_map/fik,fjk->ifj/dot_general | solution.py:155
  49.4 0.0 copy-start.1
  49.4 2.1 %copy.26 = bf16[512,1,2,512]{3,2,1,0:T(2,128)(2,1)} copy(bf16[512,1,2,512]{0,3,2,1:T(8,128)(2,1)S(1)} %fusion.30) | data formatting | bytes 2097152 | tf_op jit(solution)/shard_map/convert_element_type | solution.py:159
  51.5 5.8 %all-to-all-start.1 = ((bf16[512,1,2,512]{3,2,1,0:T(2,128)(2,1)}), bf16[512,1,2,512]{3,2,1,0:T(2,128)(2,1)S(1)}, u32[]{:S(2)}, u32[]{:S(2)}) async-start(bf16[512,1,2,512]{3,2,1,0:T(2,128)(2,1)} %copy.26), calls=%async_computation.1 | async-start | bytes 2097152 | tf_op jit(solution)/shard_map/all_to_all | solution.py:159
  57.3 0.0 copy-done.1
  57.4 1.3 %collective-permute-start = (bf16[32,1,2,512]{3,0,2,1:T(8,128)(2,1)S(1)}, bf16[32,1,2,512]{3,0,2,1:T(8,128)(2,1)S(1)}, u32[]{:S(2)}, u32[]{:S(2)}) collective-permute-start(bf16[32,1,2,512]{3,0,2,1:T(8,128)(2,1)S(1)} %copy.38), channel_id=1, source_target_pairs={{0,1},{2,3},{4,5},{6,7},{8,9},{10,11},{12,13},{14,15},{16,17},{18,... | collective-permute-start | bytes 196616 | tf_op jit(solution)/shard_map/ppermute | solution.py:27
  58.7 1.3 %collective-permute-start.1 = (bf16[32,1,2,512]{3,0,2,1:T(8,128)(2,1)S(1)}, bf16[32,1,2,512]{3,0,2,1:T(8,128)(2,1)S(1)}, u32[]{:S(2)}, u32[]{:S(2)}) collective-permute-start(bf16[32,1,2,512]{3,0,2,1:T(8,128)(2,1)S(1)} %copy.38), channel_id=1, source_target_pairs={{1,0},{3,2},{5,4},{7,6},{9,8},{11,10},{13,12},{15,14},{17,16},{19,... | collective-permute-start | bytes 196616 | tf_op jit(solution)/shard_map/ppermute | solution.py:29
  60.0 0.6 maximum_bitcast_fusion
  60.6 19.7 %all-to-all-done.1 = bf16[512,1,2,512]{3,2,1,0:T(2,128)(2,1)S(1)} async-done(((bf16[512,1,2,512]{3,2,1,0:T(2,128)(2,1)}), bf16[512,1,2,512]{3,2,1,0:T(2,128)(2,1)S(1)}, u32[]{:S(2)}, u32[]{:S(2)}) %all-to-all-start.1) | async-done | bytes 1048608 | tf_op jit(solution)/shard_map/all_to_all | solution.py:159
  80.3 0.2 copy.27
  80.5 0.1 convert_reduce_fusion
  80.6 0.0 collective-permute-done
  80.6 0.0 collective-permute-done.1
  80.6 0.1 fusion.44
  80.7 0.8 copy.31
  (15 shorter events, 0.2 us)
Async XLA Ops:
  3.4 32.8 %all-to-all-start = ((bf16[512,1,2,512]{3,2,1,0:T(2,128)(2,1)}), bf16[512,1,2,512]{3,2,1,0:T(2,128)(2,1)S(1)}, u32[]{:S(2)}, u32[]{:S(2)}) async-start(bf16[512,1,2,512]{3,2,1,0:T(2,128)(2,1)} %bitcast.14), calls=%async_computation | async-start | bytes 2097152 | tf_op jit(solution)/shard_map/all_to_all | solution.py:120
  23.7 2.4 %copy-start.4 = (s32[4]{0:T(128)S(1)}, s32[4]{0:T(128)}, u32[]{:S(2)}) copy-start(s32[4]{0:T(128)} %param.12) | copy-start | bytes 52
  23.7 2.5 %copy-start.2 = (f32[1,2,1024]{2,1,0:T(2,128)S(1)}, f32[1,2,1024]{2,1,0:T(2,128)}, u32[]{:S(2)}) copy-start(f32[1,2,1024]{2,1,0:T(2,128)} %param.10) | copy-start | bytes 24580
  41.3 2.2 %copy-start.3 = (f32[1024]{0:T(1024)S(1)}, f32[1024]{0:T(1024)}, u32[]{:S(2)}) copy-start(f32[1024]{0:T(1024)} %param.11) | copy-start | bytes 12292
  44.8 2.2 %copy-start = (bf16[2,512,2048]{2,1,0:T(8,128)(2,1)S(1)}, bf16[2,512,2048]{2,1,0:T(8,128)(2,1)}, u32[]{:S(2)}) copy-start(bf16[2,512,2048]{2,1,0:T(8,128)(2,1)} %pad_maximum_fusion) | copy-start | bytes 12582916
  49.4 7.9 %copy-start.1 = (f32[32,1,2,512]{3,2,1,0:T(2,128)S(1)}, f32[32,1,2,512]{3,2,1,0:T(2,128)}, u32[]{:S(2)}) copy-start(f32[32,1,2,512]{3,2,1,0:T(2,128)} %param.9) | copy-start | bytes 393220
  51.5 28.8 %all-to-all-start.1 = ((bf16[512,1,2,512]{3,2,1,0:T(2,128)(2,1)}), bf16[512,1,2,512]{3,2,1,0:T(2,128)(2,1)S(1)}, u32[]{:S(2)}, u32[]{:S(2)}) async-start(bf16[512,1,2,512]{3,2,1,0:T(2,128)(2,1)} %copy.26), calls=%async_computation.1 | async-start | bytes 2097152 | tf_op jit(solution)/shard_map/all_to_all | solution.py:159
  57.4 23.2 %collective-permute-start = (bf16[32,1,2,512]{3,0,2,1:T(8,128)(2,1)S(1)}, bf16[32,1,2,512]{3,0,2,1:T(8,128)(2,1)S(1)}, u32[]{:S(2)}, u32[]{:S(2)}) collective-permute-start(bf16[32,1,2,512]{3,0,2,1:T(8,128)(2,1)S(1)} %copy.38), channel_id=1, source_target_pairs={{0,1},{2,3},{4,5},{6,7},{8,9},{10,11},{12,13},{14,15},{16,17},{18,... | collective-permute-start | bytes 196616 | tf_op jit(solution)/shard_map/ppermute | solution.py:27
  58.7 21.9 %collective-permute-start.1 = (bf16[32,1,2,512]{3,0,2,1:T(8,128)(2,1)S(1)}, bf16[32,1,2,512]{3,0,2,1:T(8,128)(2,1)S(1)}, u32[]{:S(2)}, u32[]{:S(2)}) collective-permute-start(bf16[32,1,2,512]{3,0,2,1:T(8,128)(2,1)S(1)} %copy.38), channel_id=1, source_target_pairs={{1,0},{3,2},{5,4},{7,6},{9,8},{11,10},{13,12},{15,14},{17,16},{19,... | collective-permute-start | bytes 196616 | tf_op jit(solution)/shard_map/ppermute | solution.py:29

commit v2 on v0

--- a/solution.py
+++ b/solution.py
@@ -71,6 +71,37 @@
 
     pc, ps, qc, qs = spread(coarse_c), spread(coarse_s), tile(fine_c), tile(fine_s)
     return (pc * qc - ps * qs, ps * qc + pc * qs)
+
+
+def exchange(x, n_vis, mask):
+    return lax.ppermute(x, "vis", [(i, i ^ mask) for i in range(n_vis)])
+
+
+def gather_rows(block, n_vis):
+    half = n_vis // 2
+    me = lax.axis_index("vis")
+    low = me % half
+    other = exchange(block, n_vis, half)
+    pair = jnp.where(me < half, jnp.stack([block, other]), jnp.stack([other, block]))
+    pairs = jnp.stack([pair] + [exchange(pair, n_vis, m) for m in range(1, half)])
+    order = jnp.bitwise_xor(jnp.arange(half, dtype=jnp.int32), low)
+    full = jnp.take(pairs, order, axis=0)
+    return jnp.swapaxes(full, 0, 1).reshape((n_vis * block.shape[0],) + block.shape[1:])
+
+
+def reduce_rows(partial, n_vis, rows):
+    half = n_vis // 2
+    me = lax.axis_index("vis")
+    low = me % half
+    slabs = partial.astype(jnp.bfloat16).reshape((2, half, rows) + partial.shape[1:])
+    order = jnp.bitwise_xor(jnp.arange(half, dtype=jnp.int32), low)
+    slabs = jnp.take(slabs, order, axis=1)
+    acc = slabs[:, 0].astype(jnp.float32)
+    for m in range(1, half):
+        acc = acc + exchange(slabs[:, m], n_vis, m).astype(jnp.float32)
+    mine = jnp.where(me < half, acc[0], acc[1])
+    send = jnp.where(me < half, acc[1], acc[0]).astype(jnp.bfloat16)
+    return mine + exchange(send, n_vis, half).astype(jnp.float32)
 
 
 def local(
@@ -117,15 +148,7 @@
     first_row = patch_layout_position[:, 0] * facet - image // 2
     first_col = patch_layout_position[:, 1] * facet - image // 2
 
-    piece = lax.all_to_all(
-        jnp.broadcast_to(sky_half[None], (n_vis,) + sky_half.shape).reshape(
-            (n_vis * rows_dev,) + sky_half.shape[1:]
-        ),
-        "vis",
-        0,
-        0,
-        tiled=True,
-    )
+    piece = gather_rows(sky_half, n_vis)
 
     new_rows = []
     residuals = []
@@ -156,8 +179,7 @@
         new_rows.append(grad)
         residuals.append(jnp.stack([resid_real, resid_imag], axis=0))
     partial = jnp.stack(new_rows, axis=1)
-    parts = lax.all_to_all(partial, "vis", 0, 0, tiled=True)
-    gradient = jnp.sum(parts.reshape((n_vis, rows_dev) + parts.shape[1:]), axis=0)
+    gradient = reduce_rows(partial, n_vis, rows_dev)
     padded = extended(patch_intensity.astype(jnp.bfloat16), (("chan", 1),), 1).astype(
         patch_intensity.dtype
     )

time: 106 us -> 77.7 us (0.73)
  the two profiles are of different devices: /device:TPU:12 before, /device:TPU:0 now
where the time goes in v2:
time: 77.7 us; the launch traced here: 77.3 us
  starting transfers between devices  27.8 us (36%)
  other arithmetic  17 us (22%)
  waiting for transfers between devices  15.4 us (20%)
  local copies, waits for them, and re-layouts  10.5 us (14%)
  matrix products  4.78 us (6%)
  between operations  1.75 us (2%)
    ppermute x16, starting transfers between devices, exchange(): return lax.ppermute(x, 'vis', [(i, i ^ mask) for i in range(n_vis)])  25.3 us
    ppermute x16, waiting for transfers between devices, exchange(): return lax.ppermute(x, 'vis', [(i, i ^ mask) for i in range(n_vis)])  15.4 us
    unnamed x20, local copies, waits for them, and re-layouts  5.53 us
    sin x1, other arithmetic, phase_table(): jnp.sin(fine)  3.96 us
    dot_general x1, matrix products, local(): jnp.einsum('fij,fjk->fik', sky_rows, cols, preferred_element_type=jnp.flo...  2.42 us
    dot_general x1, matrix products, local(): jnp.einsum('fik,fjk->ifj', zs, cols, preferred_element_type=jnp.float32)  2.36 us
    concatenate x1, other arithmetic, local(): jnp.concatenate([col_cos, col_sin], axis=2).astype(jnp.bfloat16)  2.35 us
    reduce_sum x1, other arithmetic, local(): sum_re = jnp.sum(row_cos * wave_c - row_sin * wave_s, axis=(0, 1))  2.14 us
  transfers between devices with their start and end apart: 18, of which 7 were waited for; matrix products, arithmetic and copies ran while one was open for 21% of the time, Pallas kernels for 0%

profile of v2, /device:TPU:0, one launch (start us, length us, event | category | flops | bytes accessed | tf_op | source)
XLA Modules:
  0.0 77.3 jit_solution(15345526465234388788)
XLA Ops:
  0.6 0.9 %copy.70 = bf16[32,1,2,512]{3,0,2,1:T(8,128)(2,1)S(1)} copy(f32[32,1,2,512]{3,2,1,0:T(2,128)} %param.9) | data formatting | bytes 196608 | tf_op args[0]
  1.6 4.1 %collective-permute-start = (bf16[32,1,2,512]{3,0,2,1:T(8,128)(2,1)S(1)}, bf16[32,1,2,512]{3,0,2,1:T(8,128)(2,1)S(1)}, u32[]{:S(2)}, u32[]{:S(2)}) collective-permute-start(bf16[32,1,2,512]{3,0,2,1:T(8,128)(2,1)S(1)} %copy.70), channel_id=1, source_target_pairs={{0,16},{2,18},{4,20},{6,22},{8,24},{10,26},{12,28},{14,30},{16,0},... | collective-permute-start | bytes 196616 | tf_op jit(solution)/shard_map/ppermute | solution.py:77
  5.7 0.9 %copy.73 = bf16[32,1,2,512]{3,0,2,1:T(8,128)(2,1)S(1)} copy(f32[32,1,2,512]{3,2,1,0:T(2,128)} %param.9) | data formatting | bytes 196608 | tf_op args[0]
  6.6 0.9 %copy.74 = bf16[32,1,2,512]{3,0,2,1:T(8,128)(2,1)S(1)} copy(f32[32,1,2,512]{3,2,1,0:T(2,128)} %param.9) | data formatting | bytes 196608 | tf_op args[0]
  7.6 0.8 %fusion.65 = (s32[1024,1]{0,1:T(1,128)S(1)}, s32[1024,1]{0,1:T(1,128)S(1)}) fusion(s32[1024,2]{0,1:T(2,128)} %param.13), kind=kLoop, calls=%fused_computation.137 | loop fusion | bytes 16384 | tf_op jit(solution)/shard_map/slice | solution.py:129
  8.4 0.8 fusion.67
  9.1 0.7 fusion.66
  10.5 1.7 %select_reduce_fusion.3 = (f32[1024]{0:T(1024)S(1)}, f32[1024]{0:T(1024)S(1)}, f32[1024]{0:T(1024)S(1)}, f32[1024]{0:T(1024)S(1)}) fusion(f32[512]{0:T(512)S(1)} %bitcast.258, s32[1024]{0:T(1024)S(1)} %bitcast.254, f32[512]{0:T(512)S(1)} %bitcast.257, s32[1024]{0:T(1024)S(1)} %bitcast.253), kind=kLoop, calls=%fused_computation.42 | loop fusion | flops 5238784 | bytes 28672 | tf_op jit(solution)/shard_map/reduce_sum | solution.py:38
  12.2 1.0 %add_reduce_fusion = (s32[2]{0:T(128)S(1)}, s32[2]{0:T(128)S(1)}) fusion(s32[2,2]{1,0:T(2,128)} %param.17), kind=kLoop, calls=%fused_computation.128 | loop fusion | flops 8 | bytes 32 | tf_op jit(solution)/shard_map/sub | solution.py:148
  13.2 0.1 broadcast_add_fusion
  13.3 0.1 add.154
  13.4 0.1 add.161
  13.5 4.0 %fusion.31 = (f32[128,1024]{1,0:T(8,128)S(1)}, f32[128,1024]{1,0:T(8,128)S(1)}, f32[128,1024]{1,0:T(8,128)S(1)}, f32[128,1024]{1,0:T(8,128)S(1)}) fusion(f32[1024]{0:T(1024)S(1)} %multiply_subtract_fusion, s32[1024]{0:T(1024)S(1)} %get-tuple-element.32, f32[128]{0:T(128)S(1)} %iota_convert_fusion, f32[1024]{0:T(1024)S(1)} %multiply_subtract_fusion.1, ...), kind=kLoop, calls=%fused_computation.49 | loop fusion | flops 2097152 | bytes 2114048 | tf_op jit(solution)/shard_map/sin | solution.py:57
  17.4 0.3 fusion.51
  17.8 0.2 broadcast_in_dim.165
  18.0 0.2 broadcast_in_dim.170
  18.3 1.2 %fusion.1 = (bf16[2,512,1024]{2,1,0:T(8,128)(2,1)S(1)}, bf16[2,512,1024]{2,1,0:T(8,128)(2,1)S(1)}) fusion(f32[512,1024]{1,0:T(8,128)S(1)} %bitcast.239, f32[2,4,1024]{2,1,0:T(4,128)S(1)} %broadcast_in_dim.168, f32[512,1024]{1,0:T(8,128)S(1)} %bitcast.238, f32[2,4,1024]{2,1,0:T(4,128)S(1)} %broadcast_in_dim.163), kind=kLoop, calls=%fused_computation.11 | loop fusion | flops 8388608 | bytes 8454144 | tf_op jit(solution)/shard_map/convert.1
  19.5 0.0 copy-start.2
  19.6 2.3 %pad_maximum_fusion = bf16[2,512,2048]{2,1,0:T(8,128)(2,1)} fusion(bf16[2,512,1024]{2,1,0:T(8,128)(2,1)S(1)} %get-tuple-element.37, bf16[2,512,1024]{2,1,0:T(8,128)(2,1)S(1)} %get-tuple-element.36), kind=kLoop, calls=%fused_computation.32 | loop fusion | flops 8388608 | bytes 8388608 | tf_op jit(solution)/shard_map/concatenate | solution.py:161
  22.0 0.1 select_reduce_fusion.4
  22.1 1.6 %collective-permute-start.1 = (bf16[2,32,1,2,512]{4,1,3,0,2:T(8,128)(2,1)S(1)}, bf16[2,32,1,2,512]{4,1,3,0,2:T(8,128)(2,1)S(1)}, u32[]{:S(2)}, u32[]{:S(2)}) collective-permute-start(bf16[2,32,1,2,512]{4,1,3,0,2:T(8,128)(2,1)S(1)} %fusion.73), channel_id=1, source_target_pairs={{0,2},{2,0},{4,6},{6,4},{8,10},{10,8},{12,14},{14,12},{16,18},{18,... | collective-permute-start | bytes 393224 | tf_op jit(solution)/shard_map/ppermute | solution.py:77
  23.7 1.5 %collective-permute-start.2 = (bf16[2,32,1,2,512]{4,1,3,0,2:T(8,128)(2,1)S(1)}, bf16[2,32,1,2,512]{4,1,3,0,2:T(8,128)(2,1)S(1)}, u32[]{:S(2)}, u32[]{:S(2)}) collective-permute-start(bf16[2,32,1,2,512]{4,1,3,0,2:T(8,128)(2,1)S(1)} %fusion.73), channel_id=1, source_target_pairs={{0,4},{2,6},{4,0},{6,2},{8,12},{10,14},{12,8},{14,10},{16,20},{18,... | collective-permute-start | bytes 393224 | tf_op jit(solution)/shard_map/ppermute | solution.py:77
  25.2 0.5 collective-permute-start.3
  25.7 1.6 %collective-permute-start.4 = (bf16[2,32,1,2,512]{4,1,3,0,2:T(8,128)(2,1)S(1)}, bf16[2,32,1,2,512]{4,1,3,0,2:T(8,128)(2,1)S(1)}, u32[]{:S(2)}, u32[]{:S(2)}) collective-permute-start(bf16[2,32,1,2,512]{4,1,3,0,2:T(8,128)(2,1)S(1)} %fusion.73), channel_id=1, source_target_pairs={{0,8},{2,10},{4,12},{6,14},{8,0},{10,2},{12,4},{14,6},{16,24},{18,... | collective-permute-start | bytes 393224 | tf_op jit(solution)/shard_map/ppermute | solution.py:77
  27.2 1.4 %collective-permute-start.5 = (bf16[2,32,1,2,512]{4,1,3,0,2:T(8,128)(2,1)S(1)}, bf16[2,32,1,2,512]{4,1,3,0,2:T(8,128)(2,1)S(1)}, u32[]{:S(2)}, u32[]{:S(2)}) collective-permute-start(bf16[2,32,1,2,512]{4,1,3,0,2:T(8,128)(2,1)S(1)} %fusion.73), channel_id=1, source_target_pairs={{0,10},{2,8},{4,14},{6,12},{8,2},{10,0},{12,6},{14,4},{16,26},{18,... | collective-permute-start | bytes 393224 | tf_op jit(solution)/shard_map/ppermute | solution.py:77
  28.7 2.6 %collective-permute-start.6 = (bf16[2,32,1,2,512]{4,1,3,0,2:T(8,128)(2,1)S(1)}, bf16[2,32,1,2,512]{4,1,3,0,2:T(8,128)(2,1)S(1)}, u32[]{:S(2)}, u32[]{:S(2)}) collective-permute-start(bf16[2,32,1,2,512]{4,1,3,0,2:T(8,128)(2,1)S(1)} %fusion.73), channel_id=1, source_target_pairs={{0,12},{2,14},{4,8},{6,10},{8,4},{10,6},{12,0},{14,2},{16,28},{18,... | collective-permute-start | bytes 393224 | tf_op jit(solution)/shard_map/ppermute | solution.py:77
  31.3 1.9 %collective-permute-start.7 = (bf16[2,32,1,2,512]{4,1,3,2,0:T(8,128)(2,1)S(1)}, bf16[2,32,1,2,512]{4,1,3,2,0:T(8,128)(2,1)S(1)}, u32[]{:S(2)}, u32[]{:S(2)}) collective-permute-start(bf16[2,32,1,2,512]{4,1,3,2,0:T(8,128)(2,1)S(1)} %maximum_select_fusion.1), channel_id=1, source_target_pairs={{0,14},{2,12},{4,10},{6,8},{8,6},{10,4},{12,2},{14,0},{16,30},{18,... | collective-permute-start | bytes 393224 | tf_op jit(solution)/shard_map/ppermute | solution.py:77
  33.2 2.6 %collective-permute-done.5 = bf16[2,32,1,2,512]{4,1,3,0,2:T(8,128)(2,1)S(1)} collective-permute-done((bf16[2,32,1,2,512]{4,1,3,0,2:T(8,128)(2,1)S(1)}, bf16[2,32,1,2,512]{4,1,3,0,2:T(8,128)(2,1)S(1)}, u32[]{:S(2)}, u32[]{:S(2)}) %collective-permute-start.5) | collective-permute-done | bytes 131104 | tf_op jit(solution)/shard_map/ppermute | solution.py:77
  35.8 2.7 %collective-permute-done.6 = bf16[2,32,1,2,512]{4,1,3,0,2:T(8,128)(2,1)S(1)} collective-permute-done((bf16[2,32,1,2,512]{4,1,3,0,2:T(8,128)(2,1)S(1)}, bf16[2,32,1,2,512]{4,1,3,0,2:T(8,128)(2,1)S(1)}, u32[]{:S(2)}, u32[]{:S(2)}) %collective-permute-start.6) | collective-permute-done | bytes 131104 | tf_op jit(solution)/shard_map/ppermute | solution.py:77
  38.6 1.5 %collective-permute-done.7 = bf16[2,32,1,2,512]{4,1,3,2,0:T(8,128)(2,1)S(1)} collective-permute-done((bf16[2,32,1,2,512]{4,1,3,2,0:T(8,128)(2,1)S(1)}, bf16[2,32,1,2,512]{4,1,3,2,0:T(8,128)(2,1)S(1)}, u32[]{:S(2)}, u32[]{:S(2)}) %collective-permute-start.7) | collective-permute-done | bytes 131104 | tf_op jit(solution)/shard_map/ppermute | solution.py:77
  40.1 0.6 gather_fusion
  40.7 0.2 fusion.30
  40.9 0.1 copy.51
  41.0 1.9 %copy-done = bf16[2,512,2048]{2,1,0:T(8,128)(2,1)S(1)} copy-done((bf16[2,512,2048]{2,1,0:T(8,128)(2,1)S(1)}, bf16[2,512,2048]{2,1,0:T(8,128)(2,1)}, u32[]{:S(2)}) %copy-start) | copy-done | bytes 4194328
  42.9 2.4 %fusion.68 = f32[2,512,2048]{2,1,0:T(8,128)S(1)} fusion(bf16[2,512,512]{2,1,0:T(8,128)(2,1)S(1)} %bitcast.240, bf16[2,512,2048]{2,1,0:T(8,128)(2,1)S(1)} %copy-done), kind=kOutput, calls=%fused_computation.140 | convolution fusion | flops 2147483648 | bytes 13631488 | tf_op jit(solution)/shard_map/fij,fjk->fik/dot_general | solution.py:164
  45.3 0.2 broadcast_in_dim.175
  45.6 0.3 broadcast_in_dim.180
  45.9 2.1 %fusion.11 = (f32[1024]{0:T(1024)S(1)}, f32[1024]{0:T(1024)S(1)}) fusion(f32[2,512,2048]{2,1,0:T(8,128)S(1)} %fusion.68, f32[512,1024]{1,0:T(8,128)S(1)} %bitcast.235, f32[2,4,1024]{2,1,0:T(4,128)S(1)} %broadcast_in_dim.178, f32[512,1024]{1,0:T(8,128)S(1)} %bitcast.232, f32[2,4,1024]{2,1,0:T(4,128)S(1)} %broadcast_in_dim.173), kind=kLoop, calls=%fused_computation.21 | loop fusion | flops 14678016 | bytes 12656640 | tf_op jit(solution)/shard_map/reduce_sum | solution.py:167
  48.0 1.3 %fusion.13 = bf16[2,512,1024]{2,1,0:T(8,128)(2,1)S(1)} fusion(f32[1024]{0:T(1024)S(1)} %get-tuple-element.55, f32[1024]{0:T(1024)S(1)} %get-tuple-element.54, f32[512,1024]{1,0:T(8,128)S(1)} %bitcast.236, f32[2,4,1024]{2,1,0:T(4,128)S(1)} %broadcast_in_dim.178, f32[512,1024]{1,0:T(8,128)S(1)} %bitcast.233, f32[2,4,1024]{2,1,0:T(4,128)S(1)} %broadcast_in_dim.173), kind=kLoop, calls=%fused_computation.23 | loop fusion | flops 10485760 | bytes 6365184 | tf_op jit(solution)/shard_map/convert_element_type | solution.py:171
  49.4 1.5 %fusion.26 = bf16[2,512,1024]{2,1,0:T(8,128)(2,1)S(1)} fusion(f32[1024]{0:T(1024)S(1)} %get-tuple-element.55, f32[1024]{0:T(1024)S(1)} %get-tuple-element.54, f32[512,1024]{1,0:T(8,128)S(1)} %bitcast.237, f32[2,4,1024]{2,1,0:T(4,128)S(1)} %broadcast_in_dim.178, f32[512,1024]{1,0:T(8,128)S(1)} %bitcast.234, f32[2,4,1024]{2,1,0:T(4,128)S(1)} %broadcast_in_dim.173), kind=kLoop, calls=%fused_computation.37 | loop fusion | flops 11534336 | bytes 6365184 | tf_op jit(solution)/shard_map/neg | solution.py:177
  50.8 2.4 %fusion.27 = bf16[2,512,512]{1,2,0:T(8,128)(2,1)S(1)} fusion(bf16[2,512,2048]{2,1,0:T(8,128)(2,1)S(1)} %copy-done, bf16[2,512,1024]{2,1,0:T(8,128)(2,1)S(1)} %fusion.26, bf16[2,512,1024]{2,1,0:T(8,128)(2,1)S(1)} %fusion.13), kind=kOutput, calls=%fused_computation.44 | convolution fusion | flops 2156396544 | bytes 9437184 | tf_op jit(solution)/shard_map/fik,fjk->ifj/dot_general | solution.py:178
  53.2 0.1 copy.52
  53.3 0.6 gather_fusion.1
  53.9 0.2 fusion.72
  54.1 0.2 bitcast_select_fusion
  54.2 0.1 slice_bitcast_fusion.6
  54.3 1.4 %collective-permute-start.10 = (bf16[2,32,1,2,512]{4,1,3,0,2:T(8,128)(2,1)S(1)}, bf16[2,32,1,2,512]{4,1,3,0,2:T(8,128)(2,1)S(1)}, u32[]{:S(2)}, u32[]{:S(2)}) collective-permute-start(bf16[2,32,1,2,512]{4,1,3,0,2:T(8,128)(2,1)S(1)} %get-tuple-element.42), channel_id=1, source_target_pairs={{0,6},{2,4},{4,2},{6,0},{8,14},{10,12},{12,10},{14,8},{16,22},{18,... | collective-permute-start | bytes 393224 | tf_op jit(solution)/shard_map/ppermute | solution.py:77
  55.7 0.8 %collective-permute-start.11 = (bf16[2,32,1,2,512]{4,1,3,0,2:T(8,128)(2,1)S(1)}, bf16[2,32,1,2,512]{4,1,3,0,2:T(8,128)(2,1)S(1)}, u32[]{:S(2)}, u32[]{:S(2)}) collective-permute-start(bf16[2,32,1,2,512]{4,1,3,0,2:T(8,128)(2,1)S(1)} %get-tuple-element.41), channel_id=1, source_target_pairs={{0,8},{2,10},{4,12},{6,14},{8,0},{10,2},{12,4},{14,6},{16,24},{18,... | collective-permute-start | bytes 393224 | tf_op jit(solution)/shard_map/ppermute | solution.py:77
  56.6 1.3 %collective-permute-start.12 = (bf16[2,32,1,2,512]{4,1,3,0,2:T(8,128)(2,1)S(1)}, bf16[2,32,1,2,512]{4,1,3,0,2:T(8,128)(2,1)S(1)}, u32[]{:S(2)}, u32[]{:S(2)}) collective-permute-start(bf16[2,32,1,2,512]{4,1,3,0,2:T(8,128)(2,1)S(1)} %get-tuple-element.40), channel_id=1, source_target_pairs={{0,10},{2,8},{4,14},{6,12},{8,2},{10,0},{12,6},{14,4},{16,26},{18,... | collective-permute-start | bytes 393224 | tf_op jit(solution)/shard_map/ppermute | solution.py:77
  57.8 2.5 %collective-permute-start.13 = (bf16[2,32,1,2,512]{4,1,3,0,2:T(8,128)(2,1)S(1)}, bf16[2,32,1,2,512]{4,1,3,0,2:T(8,128)(2,1)S(1)}, u32[]{:S(2)}, u32[]{:S(2)}) collective-permute-start(bf16[2,32,1,2,512]{4,1,3,0,2:T(8,128)(2,1)S(1)} %get-tuple-element.39), channel_id=1, source_target_pairs={{0,12},{2,14},{4,8},{6,10},{8,4},{10,6},{12,0},{14,2},{16,28},{18,... | collective-permute-start | bytes 393224 | tf_op jit(solution)/shard_map/ppermute | solution.py:77
  60.3 0.6 collective-permute-start.8
  60.9 1.9 %collective-permute-done.10 = bf16[2,32,1,2,512]{4,1,3,0,2:T(8,128)(2,1)S(1)} collective-permute-done((bf16[2,32,1,2,512]{4,1,3,0,2:T(8,128)(2,1)S(1)}, bf16[2,32,1,2,512]{4,1,3,0,2:T(8,128)(2,1)S(1)}, u32[]{:S(2)}, u32[]{:S(2)}) %collective-permute-start.10) | collective-permute-done | bytes 131104 | tf_op jit(solution)/shard_map/ppermute | solution.py:77
  62.8 0.2 collective-permute-start.9
  63.1 3.0 %collective-permute-start.14 = (bf16[2,32,1,2,512]{4,1,3,0,2:T(8,128)(2,1)S(1)}, bf16[2,32,1,2,512]{4,1,3,0,2:T(8,128)(2,1)S(1)}, u32[]{:S(2)}, u32[]{:S(2)}) collective-permute-start(bf16[2,32,1,2,512]{4,1,3,0,2:T(8,128)(2,1)S(1)} %slice_bitcast_fusion), channel_id=1, source_target_pairs={{0,14},{2,12},{4,10},{6,8},{8,6},{10,4},{12,2},{14,0},{16,30},{18,... | collective-permute-start | bytes 393224 | tf_op jit(solution)/shard_map/ppermute | solution.py:77
  66.0 1.3 %collective-permute-start.16 = (bf16[32,1,2,512]{3,0,2,1:T(8,128)(2,1)S(1)}, bf16[32,1,2,512]{3,0,2,1:T(8,128)(2,1)S(1)}, u32[]{:S(2)}, u32[]{:S(2)}) collective-permute-start(bf16[32,1,2,512]{3,0,2,1:T(8,128)(2,1)S(1)} %copy.70), channel_id=1, source_target_pairs={{0,1},{2,3},{4,5},{6,7},{8,9},{10,11},{12,13},{14,15},{16,17},{18,... | collective-permute-start | bytes 196616 | tf_op jit(solution)/shard_map/ppermute | solution.py:27
  67.3 0.1 collective-permute-done.13
  67.4 1.3 %collective-permute-start.17 = (bf16[32,1,2,512]{3,0,2,1:T(8,128)(2,1)S(1)}, bf16[32,1,2,512]{3,0,2,1:T(8,128)(2,1)S(1)}, u32[]{:S(2)}, u32[]{:S(2)}) collective-permute-start(bf16[32,1,2,512]{3,0,2,1:T(8,128)(2,1)S(1)} %copy.70), channel_id=1, source_target_pairs={{1,0},{3,2},{5,4},{7,6},{9,8},{11,10},{13,12},{15,14},{17,16},{19,... | collective-permute-start | bytes 196616 | tf_op jit(solution)/shard_map/ppermute | solution.py:29
  68.7 1.4 %collective-permute-done.9 = bf16[2,32,1,2,512]{4,1,3,0,2:T(8,128)(2,1)S(1)} collective-permute-done((bf16[2,32,1,2,512]{4,1,3,0,2:T(8,128)(2,1)S(1)}, bf16[2,32,1,2,512]{4,1,3,0,2:T(8,128)(2,1)S(1)}, u32[]{:S(2)}, u32[]{:S(2)}) %collective-permute-start.9) | collective-permute-done | bytes 131104 | tf_op jit(solution)/shard_map/ppermute | solution.py:77
  70.2 0.1 fusion.40
  70.3 0.4 collective-permute-start.15
  70.7 0.6 maximum_bitcast_fusion
  71.3 5.1 %collective-permute-done.15 = bf16[32,1,2,512]{3,0,2,1:T(8,128)(2,1)S(1)} collective-permute-done((bf16[32,1,2,512]{3,0,2,1:T(8,128)(2,1)S(1)}, bf16[32,1,2,512]{3,0,2,1:T(8,128)(2,1)S(1)}, u32[]{:S(2)}, u32[]{:S(2)}) %collective-permute-start.15) | collective-permute-done | bytes 65568 | tf_op jit(solution)/shard_map/ppermute | solution.py:77
  76.4 0.1 fusion.46
  76.5 0.8 copy.67
  (48 shorter events, 0.4 us)
Async XLA Ops:
  1.6 20.5 %collective-permute-start = (bf16[32,1,2,512]{3,0,2,1:T(8,128)(2,1)S(1)}, bf16[32,1,2,512]{3,0,2,1:T(8,128)(2,1)S(1)}, u32[]{:S(2)}, u32[]{:S(2)}) collective-permute-start(bf16[32,1,2,512]{3,0,2,1:T(8,128)(2,1)S(1)} %copy.70), channel_id=1, source_target_pairs={{0,16},{2,18},{4,20},{6,22},{8,24},{10,26},{12,28},{14,30},{16,0},... | collective-permute-start | bytes 196616 | tf_op jit(solution)/shard_map/ppermute | solution.py:77
  19.5 2.4 %copy-start.2 = (f32[1,2,1024]{2,1,0:T(2,128)S(1)}, f32[1,2,1024]{2,1,0:T(2,128)}, u32[]{:S(2)}) copy-start(f32[1,2,1024]{2,1,0:T(2,128)} %param.10) | copy-start | bytes 24580
  19.5 2.4 %copy-start.4 = (s32[4]{0:T(128)S(1)}, s32[4]{0:T(128)}, u32[]{:S(2)}) copy-start(s32[4]{0:T(128)} %param.12) | copy-start | bytes 52
  22.1 6.6 %collective-permute-start.1 = (bf16[2,32,1,2,512]{4,1,3,0,2:T(8,128)(2,1)S(1)}, bf16[2,32,1,2,512]{4,1,3,0,2:T(8,128)(2,1)S(1)}, u32[]{:S(2)}, u32[]{:S(2)}) collective-permute-start(bf16[2,32,1,2,512]{4,1,3,0,2:T(8,128)(2,1)S(1)} %fusion.73), channel_id=1, source_target_pairs={{0,2},{2,0},{4,6},{6,4},{8,10},{10,8},{12,14},{14,12},{16,18},{18,... | collective-permute-start | bytes 393224 | tf_op jit(solution)/shard_map/ppermute | solution.py:77
  23.7 7.6 %collective-permute-start.2 = (bf16[2,32,1,2,512]{4,1,3,0,2:T(8,128)(2,1)S(1)}, bf16[2,32,1,2,512]{4,1,3,0,2:T(8,128)(2,1)S(1)}, u32[]{:S(2)}, u32[]{:S(2)}) collective-permute-start(bf16[2,32,1,2,512]{4,1,3,0,2:T(8,128)(2,1)S(1)} %fusion.73), channel_id=1, source_target_pairs={{0,4},{2,6},{4,0},{6,2},{8,12},{10,14},{12,8},{14,10},{16,20},{18,... | collective-permute-start | bytes 393224 | tf_op jit(solution)/shard_map/ppermute | solution.py:77
  25.2 8.0 %collective-permute-start.3 = (bf16[2,32,1,2,512]{4,1,3,0,2:T(8,128)(2,1)S(1)}, bf16[2,32,1,2,512]{4,1,3,0,2:T(8,128)(2,1)S(1)}, u32[]{:S(2)}, u32[]{:S(2)}) collective-permute-start(bf16[2,32,1,2,512]{4,1,3,0,2:T(8,128)(2,1)S(1)} %fusion.73), channel_id=1, source_target_pairs={{0,6},{2,4},{4,2},{6,0},{8,14},{10,12},{12,10},{14,8},{16,22},{18,... | collective-permute-start | bytes 393224 | tf_op jit(solution)/shard_map/ppermute | solution.py:77
  25.7 7.5 %collective-permute-start.4 = (bf16[2,32,1,2,512]{4,1,3,0,2:T(8,128)(2,1)S(1)}, bf16[2,32,1,2,512]{4,1,3,0,2:T(8,128)(2,1)S(1)}, u32[]{:S(2)}, u32[]{:S(2)}) collective-permute-start(bf16[2,32,1,2,512]{4,1,3,0,2:T(8,128)(2,1)S(1)} %fusion.73), channel_id=1, source_target_pairs={{0,8},{2,10},{4,12},{6,14},{8,0},{10,2},{12,4},{14,6},{16,24},{18,... | collective-permute-start | bytes 393224 | tf_op jit(solution)/shard_map/ppermute | solution.py:77
  27.2 8.6 %collective-permute-start.5 = (bf16[2,32,1,2,512]{4,1,3,0,2:T(8,128)(2,1)S(1)}, bf16[2,32,1,2,512]{4,1,3,0,2:T(8,128)(2,1)S(1)}, u32[]{:S(2)}, u32[]{:S(2)}) collective-permute-start(bf16[2,32,1,2,512]{4,1,3,0,2:T(8,128)(2,1)S(1)} %fusion.73), channel_id=1, source_target_pairs={{0,10},{2,8},{4,14},{6,12},{8,2},{10,0},{12,6},{14,4},{16,26},{18,... | collective-permute-start | bytes 393224 | tf_op jit(solution)/shard_map/ppermute | solution.py:77
  28.7 9.9 %collective-permute-start.6 = (bf16[2,32,1,2,512]{4,1,3,0,2:T(8,128)(2,1)S(1)}, bf16[2,32,1,2,512]{4,1,3,0,2:T(8,128)(2,1)S(1)}, u32[]{:S(2)}, u32[]{:S(2)}) collective-permute-start(bf16[2,32,1,2,512]{4,1,3,0,2:T(8,128)(2,1)S(1)} %fusion.73), channel_id=1, source_target_pairs={{0,12},{2,14},{4,8},{6,10},{8,4},{10,6},{12,0},{14,2},{16,28},{18,... | collective-permute-start | bytes 393224 | tf_op jit(solution)/shard_map/ppermute | solution.py:77
  31.3 8.8 %collective-permute-start.7 = (bf16[2,32,1,2,512]{4,1,3,2,0:T(8,128)(2,1)S(1)}, bf16[2,32,1,2,512]{4,1,3,2,0:T(8,128)(2,1)S(1)}, u32[]{:S(2)}, u32[]{:S(2)}) collective-permute-start(bf16[2,32,1,2,512]{4,1,3,2,0:T(8,128)(2,1)S(1)} %maximum_select_fusion.1), channel_id=1, source_target_pairs={{0,14},{2,12},{4,10},{6,8},{8,6},{10,4},{12,2},{14,0},{16,30},{18,... | collective-permute-start | bytes 393224 | tf_op jit(solution)/shard_map/ppermute | solution.py:77
  40.7 2.2 %copy-start = (bf16[2,512,2048]{2,1,0:T(8,128)(2,1)S(1)}, bf16[2,512,2048]{2,1,0:T(8,128)(2,1)}, u32[]{:S(2)}) copy-start(bf16[2,512,2048]{2,1,0:T(8,128)(2,1)} %pad_maximum_fusion) | copy-start | bytes 12582916
  45.8 2.2 %copy-start.3 = (f32[1024]{0:T(1024)S(1)}, f32[1024]{0:T(1024)}, u32[]{:S(2)}) copy-start(f32[1024]{0:T(1024)} %param.11) | copy-start | bytes 12292
  53.9 22.5 %copy-start.1 = (f32[32,1,2,512]{3,2,1,0:T(2,128)S(1)}, f32[32,1,2,512]{3,2,1,0:T(2,128)}, u32[]{:S(2)}) copy-start(f32[32,1,2,512]{3,2,1,0:T(2,128)} %param.9) | copy-start | bytes 393220
  54.3 8.5 %collective-permute-start.10 = (bf16[2,32,1,2,512]{4,1,3,0,2:T(8,128)(2,1)S(1)}, bf16[2,32,1,2,512]{4,1,3,0,2:T(8,128)(2,1)S(1)}, u32[]{:S(2)}, u32[]{:S(2)}) collective-permute-start(bf16[2,32,1,2,512]{4,1,3,0,2:T(8,128)(2,1)S(1)} %get-tuple-element.42), channel_id=1, source_target_pairs={{0,6},{2,4},{4,2},{6,0},{8,14},{10,12},{12,10},{14,8},{16,22},{18,... | collective-permute-start | bytes 393224 | tf_op jit(solution)/shard_map/ppermute | solution.py:77
  55.7 7.3 %collective-permute-start.11 = (bf16[2,32,1,2,512]{4,1,3,0,2:T(8,128)(2,1)S(1)}, bf16[2,32,1,2,512]{4,1,3,0,2:T(8,128)(2,1)S(1)}, u32[]{:S(2)}, u32[]{:S(2)}) collective-permute-start(bf16[2,32,1,2,512]{4,1,3,0,2:T(8,128)(2,1)S(1)} %get-tuple-element.41), channel_id=1, source_target_pairs={{0,8},{2,10},{4,12},{6,14},{8,0},{10,2},{12,4},{14,6},{16,24},{18,... | collective-permute-start | bytes 393224 | tf_op jit(solution)/shard_map/ppermute | solution.py:77
  56.6 9.5 %collective-permute-start.12 = (bf16[2,32,1,2,512]{4,1,3,0,2:T(8,128)(2,1)S(1)}, bf16[2,32,1,2,512]{4,1,3,0,2:T(8,128)(2,1)S(1)}, u32[]{:S(2)}, u32[]{:S(2)}) collective-permute-start(bf16[2,32,1,2,512]{4,1,3,0,2:T(8,128)(2,1)S(1)} %get-tuple-element.40), channel_id=1, source_target_pairs={{0,10},{2,8},{4,14},{6,12},{8,2},{10,0},{12,6},{14,4},{16,26},{18,... | collective-permute-start | bytes 393224 | tf_op jit(solution)/shard_map/ppermute | solution.py:77
  57.8 9.6 %collective-permute-start.13 = (bf16[2,32,1,2,512]{4,1,3,0,2:T(8,128)(2,1)S(1)}, bf16[2,32,1,2,512]{4,1,3,0,2:T(8,128)(2,1)S(1)}, u32[]{:S(2)}, u32[]{:S(2)}) collective-permute-start(bf16[2,32,1,2,512]{4,1,3,0,2:T(8,128)(2,1)S(1)} %get-tuple-element.39), channel_id=1, source_target_pairs={{0,12},{2,14},{4,8},{6,10},{8,4},{10,6},{12,0},{14,2},{16,28},{18,... | collective-permute-start | bytes 393224 | tf_op jit(solution)/shard_map/ppermute | solution.py:77
  60.3 8.4 %collective-permute-start.8 = (bf16[2,32,1,2,512]{4,1,3,0,2:T(8,128)(2,1)S(1)}, bf16[2,32,1,2,512]{4,1,3,0,2:T(8,128)(2,1)S(1)}, u32[]{:S(2)}, u32[]{:S(2)}) collective-permute-start(bf16[2,32,1,2,512]{4,1,3,0,2:T(8,128)(2,1)S(1)} %get-tuple-element.38), channel_id=1, source_target_pairs={{0,2},{2,0},{4,6},{6,4},{8,10},{10,8},{12,14},{14,12},{16,18},{18,... | collective-permute-start | bytes 393224 | tf_op jit(solution)/shard_map/ppermute | solution.py:77
  62.8 7.3 %collective-permute-start.9 = (bf16[2,32,1,2,512]{4,1,3,0,2:T(8,128)(2,1)S(1)}, bf16[2,32,1,2,512]{4,1,3,0,2:T(8,128)(2,1)S(1)}, u32[]{:S(2)}, u32[]{:S(2)}) collective-permute-start(bf16[2,32,1,2,512]{4,1,3,0,2:T(8,128)(2,1)S(1)} %get-tuple-element.43), channel_id=1, source_target_pairs={{0,4},{2,6},{4,0},{6,2},{8,12},{10,14},{12,8},{14,10},{16,20},{18,... | collective-permute-start | bytes 393224 | tf_op jit(solution)/shard_map/ppermute | solution.py:77
  63.1 7.1 %collective-permute-start.14 = (bf16[2,32,1,2,512]{4,1,3,0,2:T(8,128)(2,1)S(1)}, bf16[2,32,1,2,512]{4,1,3,0,2:T(8,128)(2,1)S(1)}, u32[]{:S(2)}, u32[]{:S(2)}) collective-permute-start(bf16[2,32,1,2,512]{4,1,3,0,2:T(8,128)(2,1)S(1)} %slice_bitcast_fusion), channel_id=1, source_target_pairs={{0,14},{2,12},{4,10},{6,8},{8,6},{10,4},{12,2},{14,0},{16,30},{18,... | collective-permute-start | bytes 393224 | tf_op jit(solution)/shard_map/ppermute | solution.py:77
  66.0 5.3 %collective-permute-start.16 = (bf16[32,1,2,512]{3,0,2,1:T(8,128)(2,1)S(1)}, bf16[32,1,2,512]{3,0,2,1:T(8,128)(2,1)S(1)}, u32[]{:S(2)}, u32[]{:S(2)}) collective-permute-start(bf16[32,1,2,512]{3,0,2,1:T(8,128)(2,1)S(1)} %copy.70), channel_id=1, source_target_pairs={{0,1},{2,3},{4,5},{6,7},{8,9},{10,11},{12,13},{14,15},{16,17},{18,... | collective-permute-start | bytes 196616 | tf_op jit(solution)/shard_map/ppermute | solution.py:27
  67.4 3.9 %collective-permute-start.17 = (bf16[32,1,2,512]{3,0,2,1:T(8,128)(2,1)S(1)}, bf16[32,1,2,512]{3,0,2,1:T(8,128)(2,1)S(1)}, u32[]{:S(2)}, u32[]{:S(2)}) collective-permute-start(bf16[32,1,2,512]{3,0,2,1:T(8,128)(2,1)S(1)} %copy.70), channel_id=1, source_target_pairs={{1,0},{3,2},{5,4},{7,6},{9,8},{11,10},{13,12},{15,14},{17,16},{19,... | collective-permute-start | bytes 196616 | tf_op jit(solution)/shard_map/ppermute | solution.py:29
  70.3 6.1 %collective-permute-start.15 = (bf16[32,1,2,512]{3,0,2,1:T(8,128)(2,1)S(1)}, bf16[32,1,2,512]{3,0,2,1:T(8,128)(2,1)S(1)}, u32[]{:S(2)}, u32[]{:S(2)}) collective-permute-start(bf16[32,1,2,512]{3,0,2,1:T(8,128)(2,1)S(1)} %fusion.50), channel_id=1, source_target_pairs={{0,16},{2,18},{4,20},{6,22},{8,24},{10,26},{12,28},{14,30},{16,0},... | collective-permute-start | bytes 196616 | tf_op jit(solution)/shard_map/ppermute | solution.py:77

commit v3 on v2

--- a/solution.py
+++ b/solution.py
@@ -83,9 +83,10 @@
     low = me % half
     other = exchange(block, n_vis, half)
     pair = jnp.where(me < half, jnp.stack([block, other]), jnp.stack([other, block]))
-    pairs = jnp.stack([pair] + [exchange(pair, n_vis, m) for m in range(1, half)])
-    order = jnp.bitwise_xor(jnp.arange(half, dtype=jnp.int32), low)
-    full = jnp.take(pairs, order, axis=0)
+    groups = [list(range(half)), list(range(half, n_vis))]
+    full = lax.all_to_all(
+        jnp.broadcast_to(pair[None], (half,) + pair.shape), "vis", 0, 0, axis_index_groups=groups
+    )
     return jnp.swapaxes(full, 0, 1).reshape((n_vis * block.shape[0],) + block.shape[1:])
 
 
@@ -94,11 +95,9 @@
     me = lax.axis_index("vis")
     low = me % half
     slabs = partial.astype(jnp.bfloat16).reshape((2, half, rows) + partial.shape[1:])
-    order = jnp.bitwise_xor(jnp.arange(half, dtype=jnp.int32), low)
-    slabs = jnp.take(slabs, order, axis=1)
-    acc = slabs[:, 0].astype(jnp.float32)
-    for m in range(1, half):
-        acc = acc + exchange(slabs[:, m], n_vis, m).astype(jnp.float32)
+    groups = [list(range(half)), list(range(half, n_vis))]
+    got = lax.all_to_all(jnp.swapaxes(slabs, 0, 1), "vis", 0, 0, axis_index_groups=groups)
+    acc = jnp.sum(got.astype(jnp.float32), axis=0)
     mine = jnp.where(me < half, acc[0], acc[1])
     send = jnp.where(me < half, acc[1], acc[0]).astype(jnp.bfloat16)
     return mine + exchange(send, n_vis, half).astype(jnp.float32)

time: 77.7 us -> 72.9 us (0.938)
  starting transfers between devices: 27.8 us -> 15.4 us
  waiting for transfers between devices: 15.4 us -> 22.9 us
  matrix products: 4.78 us -> 6.89 us
  local copies, waits for them, and re-layouts: 10.5 us -> 9.12 us
    ppermute x16 -> x2, starting transfers between devices: 25.3 us -> 4.5 us  [exchange(): return lax.ppermute(x, 'vis', [(i, i ^ mask) for i in range(n_vis)])]
    all_to_all x0 -> x2, waiting for transfers between devices: none -> 17.6 us  [the longest x1 11.8 us: reduce_rows(): lax.all_to_all(jnp.swapaxes(slabs, 0, 1), 'vis', 0, 0, axis_index_groups=...]
    ppermute x16 -> x2, waiting for transfers between devices: 15.4 us -> 5.27 us  [exchange(): return lax.ppermute(x, 'vis', [(i, i ^ mask) for i in range(n_vis)])]
    all_to_all x0 -> x2, starting transfers between devices: none -> 8.29 us  [the longest x1 4.74 us: gather_rows(): lax.all_to_all(jnp.broadcast_to(pair[None], (half,) + pair.shape), 'vis',...]
    unnamed x20 -> x13, local copies, waits for them, and re-layouts: 5.53 us -> 3.35 us
    dot_general x1, matrix products: 2.42 us -> 4.54 us  [local(): jnp.einsum('fij,fjk->fik', sky_rows, cols, preferred_element_type=jnp.flo...]
    gather x2 -> x0, local copies, waits for them, and re-layouts: 1.23 us -> none  [the longest x1 0.61 us: gather_rows(): full = jnp.take(pairs, order, axis=0)]
    broadcast_in_dim x0 -> x1, local copies, waits for them, and re-layouts: none -> 1.09 us  [gather_rows(): jnp.broadcast_to(pair[None], (half,) + pair.shape)]
  transfers between devices with their start and end apart: 18 -> 6, of which waited for: 7 -> 3; matrix products, arithmetic and copies ran while one was open for 21% -> 21% of each run, Pallas kernels for 0% -> 0%
where the time goes in v3:
time: 72.9 us; the launch traced here: 72.4 us
  waiting for transfers between devices  22.9 us (31%)
  other arithmetic  16.5 us (23%)
  starting transfers between devices  15.4 us (21%)
  local copies, waits for them, and re-layouts  9.12 us (13%)
  matrix products  6.89 us (9%)
  between operations  1.57 us (2%)
    all_to_all x1, waiting for transfers between devices, reduce_rows(): lax.all_to_all(jnp.swapaxes(slabs, 0, 1), 'vis', 0, 0, axis_index_groups=...  11.8 us
    all_to_all x1, waiting for transfers between devices, gather_rows(): lax.all_to_all(jnp.broadcast_to(pair[None], (half,) + pair.shape), 'vis',...  5.79 us
    ppermute x2, waiting for transfers between devices, exchange(): return lax.ppermute(x, 'vis', [(i, i ^ mask) for i in range(n_vis)])  5.27 us
    all_to_all x1, starting transfers between devices, gather_rows(): lax.all_to_all(jnp.broadcast_to(pair[None], (half,) + pair.shape), 'vis',...  4.74 us
    dot_general x1, matrix products, local(): jnp.einsum('fij,fjk->fik', sky_rows, cols, preferred_element_type=jnp.flo...  4.54 us
    ppermute x2, starting transfers between devices, exchange(): return lax.ppermute(x, 'vis', [(i, i ^ mask) for i in range(n_vis)])  4.5 us
    sin x1, other arithmetic, phase_table(): jnp.sin(fine)  3.95 us
    all_to_all x1, starting transfers between devices, reduce_rows(): lax.all_to_all(jnp.swapaxes(slabs, 0, 1), 'vis', 0, 0, axis_index_groups=...  3.56 us
  transfers between devices with their start and end apart: 6, of which 3 were waited for; matrix products, arithmetic and copies ran while one was open for 21% of the time, Pallas kernels for 0%

profile of v3, /device:TPU:0, one launch (start us, length us, event | category | flops | bytes accessed | tf_op | source)
XLA Modules:
  0.0 72.4 jit_solution(9979360988341065004)
XLA Ops:
  0.6 0.9 %copy.44 = bf16[32,1,2,512]{3,0,2,1:T(8,128)(2,1)S(1)} copy(f32[32,1,2,512]{3,2,1,0:T(2,128)} %param.9) | data formatting | bytes 196608 | tf_op args[0]
  1.6 4.1 %collective-permute-start = (bf16[32,1,2,512]{3,0,2,1:T(8,128)(2,1)S(1)}, bf16[32,1,2,512]{3,0,2,1:T(8,128)(2,1)S(1)}, u32[]{:S(2)}, u32[]{:S(2)}) collective-permute-start(bf16[32,1,2,512]{3,0,2,1:T(8,128)(2,1)S(1)} %copy.44), channel_id=1, source_target_pairs={{0,16},{2,18},{4,20},{6,22},{8,24},{10,26},{12,28},{14,30},{16,0},... | collective-permute-start | bytes 196616 | tf_op jit(solution)/shard_map/ppermute | solution.py:77
  5.7 0.8 %fusion.57 = (s32[1024,1]{0,1:T(1,128)S(1)}, s32[1024,1]{0,1:T(1,128)S(1)}) fusion(s32[1024,2]{0,1:T(2,128)} %param.13), kind=kLoop, calls=%fused_computation.105 | loop fusion | bytes 16384 | tf_op jit(solution)/shard_map/slice | solution.py:128
  6.4 0.8 %fusion.59 = (f32[1,512]{1,0:T(1,128)S(1)}, f32[1,512]{1,0:T(1,128)S(1)}) fusion(f32[2,512]{1,0:T(2,128)} %param.16), kind=kLoop, calls=%fused_computation.107 | loop fusion | bytes 8192 | tf_op jit(solution)/shard_map/slice | solution.py:130
  7.2 0.7 %fusion.58 = (f32[1024]{0:T(1024)S(1)}, f32[1024]{0:T(1024)S(1)}) fusion(f32[1024]{0:T(1024)} %param.14), kind=kLoop, calls=%fused_computation.106 | loop fusion | bytes 12288 | tf_op jit(solution)/shard_map/sin | solution.py:135
  8.6 1.0 %add_reduce_fusion = (s32[2]{0:T(128)S(1)}, s32[2]{0:T(128)S(1)}) fusion(s32[2,2]{1,0:T(2,128)} %param.17), kind=kLoop, calls=%fused_computation.97 | loop fusion | flops 8 | bytes 32 | tf_op jit(solution)/shard_map/sub | solution.py:147
  9.6 1.7 %select_reduce_fusion.3 = (f32[1024]{0:T(1024)S(1)}, f32[1024]{0:T(1024)S(1)}, f32[1024]{0:T(1024)S(1)}, f32[1024]{0:T(1024)S(1)}) fusion(f32[512]{0:T(512)S(1)} %bitcast.197, s32[1024]{0:T(1024)S(1)} %bitcast.193, f32[512]{0:T(512)S(1)} %bitcast.196, s32[1024]{0:T(1024)S(1)} %bitcast.192), kind=kLoop, calls=%fused_computation.41 | loop fusion | flops 5238784 | bytes 28672 | tf_op jit(solution)/shard_map/reduce_sum | solution.py:38
  11.3 0.1 broadcast_add_fusion
  11.3 0.9 %copy.47 = bf16[32,1,2,512]{3,0,2,1:T(8,128)(2,1)S(1)} copy(f32[32,1,2,512]{3,2,1,0:T(2,128)} %param.9) | data formatting | bytes 196608 | tf_op args[0]
  12.3 0.1 add.109
  12.3 0.1 add.116
  12.4 0.0 collective-permute-done
  12.5 1.1 %broadcast_in_dim.170 = bf16[8,2,32,1,2,512]{5,2,1,4,3,0:T(8,128)(2,1)} broadcast(bf16[2,32,2,512]{3,1,0,2:T(8,128)(2,1)S(1)} %copy.27), dimensions={1,2,4,5} | broadcast | bytes 1179648 | tf_op jit(solution)/shard_map/broadcast_in_dim | solution.py:88
  13.6 4.7 %all-to-all-start = ((bf16[8,2,32,1,2,512]{5,2,1,4,3,0:T(8,128)(2,1)}), bf16[8,2,32,1,2,512]{5,2,1,4,3,0:T(8,128)(2,1)S(1)}, u32[]{:S(2)}, u32[]{:S(2)}) async-start(bf16[8,2,32,1,2,512]{5,2,1,4,3,0:T(8,128)(2,1)} %broadcast_in_dim.170), calls=%async_computation | async-start | bytes 2097152 | tf_op jit(solution)/shard_map/all_to_all | solution.py:87
  18.3 0.3 fusion.44
  18.7 4.0 %fusion.30 = (f32[128,1024]{1,0:T(8,128)S(1)}, f32[128,1024]{1,0:T(8,128)S(1)}, f32[128,1024]{1,0:T(8,128)S(1)}, f32[128,1024]{1,0:T(8,128)S(1)}) fusion(f32[1024]{0:T(1024)S(1)} %multiply_subtract_fusion, s32[1024]{0:T(1024)S(1)} %get-tuple-element.32, f32[128]{0:T(128)S(1)} %iota_convert_fusion, f32[1024]{0:T(1024)S(1)} %multiply_subtract_fusion.1, ...), kind=kLoop, calls=%fused_computation.46 | loop fusion | flops 2097152 | bytes 2114048 | tf_op jit(solution)/shard_map/sin | solution.py:57
  22.7 0.2 broadcast_in_dim.150
  22.9 0.2 broadcast_in_dim.155
  23.2 1.2 %fusion.1 = (bf16[2,512,1024]{2,1,0:T(8,128)(2,1)S(1)}, bf16[2,512,1024]{2,1,0:T(8,128)(2,1)S(1)}) fusion(f32[512,1024]{1,0:T(8,128)S(1)} %bitcast.184, f32[2,4,1024]{2,1,0:T(4,128)S(1)} %broadcast_in_dim.153, f32[512,1024]{1,0:T(8,128)S(1)} %bitcast.183, f32[2,4,1024]{2,1,0:T(4,128)S(1)} %broadcast_in_dim.148), kind=kLoop, calls=%fused_computation.9 | loop fusion | flops 8388608 | bytes 8454144 | tf_op jit(solution)/shard_map/convert
  24.4 0.0 copy-start.4
  24.4 0.0 copy-start.2
  24.4 2.3 %pad_maximum_fusion = bf16[2,512,2048]{2,1,0:T(8,128)(2,1)} fusion(bf16[2,512,1024]{2,1,0:T(8,128)(2,1)S(1)} %get-tuple-element.37, bf16[2,512,1024]{2,1,0:T(8,128)(2,1)S(1)} %get-tuple-element.36), kind=kLoop, calls=%fused_computation.30 | loop fusion | flops 8388608 | bytes 8388608 | tf_op jit(solution)/shard_map/concatenate | solution.py:160
  26.8 0.0 copy-done.4
  26.8 0.1 select_reduce_fusion.4
  26.9 0.0 copy-done.2
  26.9 5.8 %all-to-all-done = bf16[8,2,32,1,2,512]{5,2,1,4,3,0:T(8,128)(2,1)S(1)} async-done(((bf16[8,2,32,1,2,512]{5,2,1,4,3,0:T(8,128)(2,1)}), bf16[8,2,32,1,2,512]{5,2,1,4,3,0:T(8,128)(2,1)S(1)}, u32[]{:S(2)}, u32[]{:S(2)}) %all-to-all-start) | async-done | bytes 1048608 | tf_op jit(solution)/shard_map/all_to_all | solution.py:87
  32.7 0.1 copy.28
  32.8 4.5 %fusion.60 = f32[2,512,2048]{2,1,0:T(8,128)S(1)} fusion(bf16[2,512,512]{2,1,0:T(8,128)(2,1)S(1)} %bitcast.185, bf16[2,512,2048]{2,1,0:T(8,128)(2,1)} %pad_maximum_fusion), kind=kOutput, calls=%fused_computation.108 | convolution fusion | flops 2147483648 | bytes 13631488 | tf_op jit(solution)/shard_map/fij,fjk->fik/dot_general | solution.py:163
  37.4 0.3 broadcast_in_dim.160
  37.6 0.3 broadcast_in_dim.165
  37.9 0.0 copy-start.3
  37.9 2.2 %fusion.11 = (f32[1024]{0:T(1024)S(1)}, f32[1024]{0:T(1024)S(1)}) fusion(f32[2,512,2048]{2,1,0:T(8,128)S(1)} %fusion.60, f32[512,1024]{1,0:T(8,128)S(1)} %bitcast.180, f32[2,4,1024]{2,1,0:T(4,128)S(1)} %broadcast_in_dim.163, f32[512,1024]{1,0:T(8,128)S(1)} %bitcast.177, f32[2,4,1024]{2,1,0:T(4,128)S(1)} %broadcast_in_dim.158), kind=kLoop, calls=%fused_computation.19 | loop fusion | flops 14678016 | bytes 12656640 | tf_op jit(solution)/shard_map/reduce_sum | solution.py:166
  40.1 0.0 copy-done.3
  40.1 1.4 %fusion.13 = bf16[2,512,1024]{2,1,0:T(8,128)(2,1)S(1)} fusion(f32[1024]{0:T(1024)S(1)} %get-tuple-element.49, f32[1024]{0:T(1024)S(1)} %get-tuple-element.48, f32[512,1024]{1,0:T(8,128)S(1)} %bitcast.181, f32[2,4,1024]{2,1,0:T(4,128)S(1)} %broadcast_in_dim.163, f32[512,1024]{1,0:T(8,128)S(1)} %bitcast.178, f32[2,4,1024]{2,1,0:T(4,128)S(1)} %broadcast_in_dim.158), kind=kLoop, calls=%fused_computation.21 | loop fusion | flops 10485760 | bytes 6365184 | tf_op jit(solution)/shard_map/convert_element_type | solution.py:170
  41.5 0.0 copy-start
  41.5 1.5 %fusion.26 = bf16[2,512,1024]{2,1,0:T(8,128)(2,1)S(1)} fusion(f32[1024]{0:T(1024)S(1)} %get-tuple-element.49, f32[1024]{0:T(1024)S(1)} %get-tuple-element.48, f32[512,1024]{1,0:T(8,128)S(1)} %bitcast.182, f32[2,4,1024]{2,1,0:T(4,128)S(1)} %broadcast_in_dim.163, f32[512,1024]{1,0:T(8,128)S(1)} %bitcast.179, f32[2,4,1024]{2,1,0:T(4,128)S(1)} %broadcast_in_dim.158), kind=kLoop, calls=%fused_computation.35 | loop fusion | flops 11534336 | bytes 6365184 | tf_op jit(solution)/shard_map/neg | solution.py:176
  42.9 0.7 copy-done
  43.6 2.4 %fusion.27 = bf16[2,512,512]{1,2,0:T(8,128)(2,1)S(1)} fusion(bf16[2,512,2048]{2,1,0:T(8,128)(2,1)S(1)} %copy-done, bf16[2,512,1024]{2,1,0:T(8,128)(2,1)S(1)} %fusion.26, bf16[2,512,1024]{2,1,0:T(8,128)(2,1)S(1)} %fusion.13), kind=kOutput, calls=%fused_computation.43 | convolution fusion | flops 2156396544 | bytes 9437184 | tf_op jit(solution)/shard_map/fik,fjk->ifj/dot_general | solution.py:177
  46.0 0.0 copy-start.1
  46.0 1.1 %copy.46 = bf16[2,8,32,1,2,512]{5,2,0,4,3,1:T(8,128)(2,1)} copy(bf16[2,8,32,1,2,512]{5,2,1,0,4,3:T(8,128)(2,1)S(1)} %bitcast.187) | data formatting | bytes 2097152 | tf_op jit(solution)/shard_map/reshape | solution.py:97
  47.1 3.6 %all-to-all-start.1 = ((bf16[8,2,32,1,2,512]{5,2,1,4,3,0:T(8,128)(2,1)}), bf16[8,2,32,1,2,512]{5,2,1,4,3,0:T(8,128)(2,1)S(1)}, u32[]{:S(2)}, u32[]{:S(2)}) async-start(bf16[8,2,32,1,2,512]{5,2,1,4,3,0:T(8,128)(2,1)} %bitcast.174), calls=%async_computation.1 | async-start | bytes 2097152 | tf_op jit(solution)/shard_map/all_to_all | solution.py:99
  50.6 1.3 %collective-permute-start.2 = (bf16[32,1,2,512]{3,0,2,1:T(8,128)(2,1)S(1)}, bf16[32,1,2,512]{3,0,2,1:T(8,128)(2,1)S(1)}, u32[]{:S(2)}, u32[]{:S(2)}) collective-permute-start(bf16[32,1,2,512]{3,0,2,1:T(8,128)(2,1)S(1)} %copy.44), channel_id=1, source_target_pairs={{0,1},{2,3},{4,5},{6,7},{8,9},{10,11},{12,13},{14,15},{16,17},{18,... | collective-permute-start | bytes 196616 | tf_op jit(solution)/shard_map/ppermute | solution.py:27
  51.9 1.3 %collective-permute-start.3 = (bf16[32,1,2,512]{3,0,2,1:T(8,128)(2,1)S(1)}, bf16[32,1,2,512]{3,0,2,1:T(8,128)(2,1)S(1)}, u32[]{:S(2)}, u32[]{:S(2)}) collective-permute-start(bf16[32,1,2,512]{3,0,2,1:T(8,128)(2,1)S(1)} %copy.44), channel_id=1, source_target_pairs={{1,0},{3,2},{5,4},{7,6},{9,8},{11,10},{13,12},{15,14},{17,16},{19,... | collective-permute-start | bytes 196616 | tf_op jit(solution)/shard_map/ppermute | solution.py:29
  53.3 11.8 %all-to-all-done.1 = bf16[8,2,32,1,2,512]{5,2,1,4,3,0:T(8,128)(2,1)S(1)} async-done(((bf16[8,2,32,1,2,512]{5,2,1,4,3,0:T(8,128)(2,1)}), bf16[8,2,32,1,2,512]{5,2,1,4,3,0:T(8,128)(2,1)S(1)}, u32[]{:S(2)}, u32[]{:S(2)}) %all-to-all-start.1) | async-done | bytes 1048608 | tf_op jit(solution)/shard_map/all_to_all | solution.py:99
  65.1 0.1 convert_reduce_fusion
  65.2 0.4 collective-permute-start.1
  65.6 0.6 maximum_bitcast_fusion
  66.3 0.0 collective-permute-done.2
  66.3 0.0 collective-permute-done.3
  66.3 5.3 %collective-permute-done.1 = bf16[32,1,2,512]{3,0,2,1:T(8,128)(2,1)S(1)} collective-permute-done((bf16[32,1,2,512]{3,0,2,1:T(8,128)(2,1)S(1)}, bf16[32,1,2,512]{3,0,2,1:T(8,128)(2,1)S(1)}, u32[]{:S(2)}, u32[]{:S(2)}) %collective-permute-start.1) | collective-permute-done | bytes 65568 | tf_op jit(solution)/shard_map/ppermute | solution.py:77
  71.5 0.0 copy-done.1
  71.5 0.1 fusion.39
  71.6 0.8 %copy.38 = f32[32,1,2,512]{3,2,1,0:T(2,128)} copy(f32[32,1,2,512]{3,0,2,1:T(8,128)S(1)} %fusion.39) | data formatting | bytes 262144
  (17 shorter events, 0.2 us)
Async XLA Ops:
  1.6 10.9 %collective-permute-start = (bf16[32,1,2,512]{3,0,2,1:T(8,128)(2,1)S(1)}, bf16[32,1,2,512]{3,0,2,1:T(8,128)(2,1)S(1)}, u32[]{:S(2)}, u32[]{:S(2)}) collective-permute-start(bf16[32,1,2,512]{3,0,2,1:T(8,128)(2,1)S(1)} %copy.44), channel_id=1, source_target_pairs={{0,16},{2,18},{4,20},{6,22},{8,24},{10,26},{12,28},{14,30},{16,0},... | collective-permute-start | bytes 196616 | tf_op jit(solution)/shard_map/ppermute | solution.py:77
  13.6 19.1 %all-to-all-start = ((bf16[8,2,32,1,2,512]{5,2,1,4,3,0:T(8,128)(2,1)}), bf16[8,2,32,1,2,512]{5,2,1,4,3,0:T(8,128)(2,1)S(1)}, u32[]{:S(2)}, u32[]{:S(2)}) async-start(bf16[8,2,32,1,2,512]{5,2,1,4,3,0:T(8,128)(2,1)} %broadcast_in_dim.170), calls=%async_computation | async-start | bytes 2097152 | tf_op jit(solution)/shard_map/all_to_all | solution.py:87
  24.4 2.4 %copy-start.4 = (s32[4]{0:T(128)S(1)}, s32[4]{0:T(128)}, u32[]{:S(2)}) copy-start(s32[4]{0:T(128)} %param.12) | copy-start | bytes 52
  24.4 2.5 %copy-start.2 = (f32[1,2,1024]{2,1,0:T(2,128)S(1)}, f32[1,2,1024]{2,1,0:T(2,128)}, u32[]{:S(2)}) copy-start(f32[1,2,1024]{2,1,0:T(2,128)} %param.10) | copy-start | bytes 24580
  37.9 2.2 %copy-start.3 = (f32[1024]{0:T(1024)S(1)}, f32[1024]{0:T(1024)}, u32[]{:S(2)}) copy-start(f32[1024]{0:T(1024)} %param.11) | copy-start | bytes 12292
  41.5 2.2 %copy-start = (bf16[2,512,2048]{2,1,0:T(8,128)(2,1)S(1)}, bf16[2,512,2048]{2,1,0:T(8,128)(2,1)}, u32[]{:S(2)}) copy-start(bf16[2,512,2048]{2,1,0:T(8,128)(2,1)} %pad_maximum_fusion) | copy-start | bytes 12582916
  46.0 25.5 %copy-start.1 = (f32[32,1,2,512]{3,2,1,0:T(2,128)S(1)}, f32[32,1,2,512]{3,2,1,0:T(2,128)}, u32[]{:S(2)}) copy-start(f32[32,1,2,512]{3,2,1,0:T(2,128)} %param.9) | copy-start | bytes 393220
  47.1 18.0 %all-to-all-start.1 = ((bf16[8,2,32,1,2,512]{5,2,1,4,3,0:T(8,128)(2,1)}), bf16[8,2,32,1,2,512]{5,2,1,4,3,0:T(8,128)(2,1)S(1)}, u32[]{:S(2)}, u32[]{:S(2)}) async-start(bf16[8,2,32,1,2,512]{5,2,1,4,3,0:T(8,128)(2,1)} %bitcast.174), calls=%async_computation.1 | async-start | bytes 2097152 | tf_op jit(solution)/shard_map/all_to_all | solution.py:99
  50.6 15.6 %collective-permute-start.2 = (bf16[32,1,2,512]{3,0,2,1:T(8,128)(2,1)S(1)}, bf16[32,1,2,512]{3,0,2,1:T(8,128)(2,1)S(1)}, u32[]{:S(2)}, u32[]{:S(2)}) collective-permute-start(bf16[32,1,2,512]{3,0,2,1:T(8,128)(2,1)S(1)} %copy.44), channel_id=1, source_target_pairs={{0,1},{2,3},{4,5},{6,7},{8,9},{10,11},{12,13},{14,15},{16,17},{18,... | collective-permute-start | bytes 196616 | tf_op jit(solution)/shard_map/ppermute | solution.py:27
  51.9 14.3 %collective-permute-start.3 = (bf16[32,1,2,512]{3,0,2,1:T(8,128)(2,1)S(1)}, bf16[32,1,2,512]{3,0,2,1:T(8,128)(2,1)S(1)}, u32[]{:S(2)}, u32[]{:S(2)}) collective-permute-start(bf16[32,1,2,512]{3,0,2,1:T(8,128)(2,1)S(1)} %copy.44), channel_id=1, source_target_pairs={{1,0},{3,2},{5,4},{7,6},{9,8},{11,10},{13,12},{15,14},{17,16},{19,... | collective-permute-start | bytes 196616 | tf_op jit(solution)/shard_map/ppermute | solution.py:29
  65.2 6.3 %collective-permute-start.1 = (bf16[32,1,2,512]{3,0,2,1:T(8,128)(2,1)S(1)}, bf16[32,1,2,512]{3,0,2,1:T(8,128)(2,1)S(1)}, u32[]{:S(2)}, u32[]{:S(2)}) collective-permute-start(bf16[32,1,2,512]{3,0,2,1:T(8,128)(2,1)S(1)} %fusion.43), channel_id=1, source_target_pairs={{0,16},{2,18},{4,20},{6,22},{8,24},{10,26},{12,28},{14,30},{16,0},... | collective-permute-start | bytes 196616 | tf_op jit(solution)/shard_map/ppermute | solution.py:77

commit v4 on v3

--- a/solution.py
+++ b/solution.py
@@ -48,25 +48,23 @@
     return exact + rest[None, :] * pixel.astype(jnp.float32) / image
 
 
-def phase_table(coord, first_pixel, facet, image):
-    blocks = facet // LANE_BLOCK
-    starts = first_pixel[:, None] + LANE_BLOCK * jnp.arange(blocks, dtype=jnp.int32)[None, :]
+def phase_table(coord, starts, span, image):
+    faces, chunks = starts.shape
     coarse = full_turn * turns(coord, starts.reshape(-1, 1), image)
-    fine = full_turn * turns(coord, jnp.arange(LANE_BLOCK, dtype=jnp.int32)[:, None], image)
+    fine = full_turn * turns(coord, jnp.arange(span, dtype=jnp.int32)[:, None], image)
     coarse_c, coarse_s, fine_c, fine_s = lax.optimization_barrier(
         (jnp.cos(coarse), jnp.sin(coarse), jnp.cos(fine), jnp.sin(fine))
     )
     count = coord.shape[0]
-    faces = first_pixel.shape[0]
 
     def spread(a):
         return jnp.broadcast_to(
-            a.reshape(faces, blocks, 1, count), (faces, blocks, LANE_BLOCK, count)
-        ).reshape(faces, facet, count)
+            a.reshape(faces, chunks, 1, count), (faces, chunks, span, count)
+        ).reshape(faces, chunks * span, count)
 
     def tile(a):
-        return jnp.broadcast_to(a[None, None], (faces, blocks, LANE_BLOCK, count)).reshape(
-            faces, facet, count
+        return jnp.broadcast_to(a[None, None], (faces, chunks, span, count)).reshape(
+            faces, chunks * span, count
         )
 
     pc, ps, qc, qs = spread(coarse_c), spread(coarse_s), tile(fine_c), tile(fine_s)
@@ -80,23 +78,21 @@
 def gather_rows(block, n_vis):
     half = n_vis // 2
     me = lax.axis_index("vis")
-    low = me % half
     other = exchange(block, n_vis, half)
     pair = jnp.where(me < half, jnp.stack([block, other]), jnp.stack([other, block]))
     groups = [list(range(half)), list(range(half, n_vis))]
     full = lax.all_to_all(
         jnp.broadcast_to(pair[None], (half,) + pair.shape), "vis", 0, 0, axis_index_groups=groups
     )
-    return jnp.swapaxes(full, 0, 1).reshape((n_vis * block.shape[0],) + block.shape[1:])
+    return full.reshape((n_vis * block.shape[0],) + block.shape[1:])
 
 
 def reduce_rows(partial, n_vis, rows):
     half = n_vis // 2
     me = lax.axis_index("vis")
-    low = me % half
-    slabs = partial.astype(jnp.bfloat16).reshape((2, half, rows) + partial.shape[1:])
+    slabs = partial.astype(jnp.bfloat16).reshape((half, 2, rows) + partial.shape[1:])
     groups = [list(range(half)), list(range(half, n_vis))]
-    got = lax.all_to_all(jnp.swapaxes(slabs, 0, 1), "vis", 0, 0, axis_index_groups=groups)
+    got = lax.all_to_all(slabs, "vis", 0, 0, axis_index_groups=groups)
     acc = jnp.sum(got.astype(jnp.float32), axis=0)
     mine = jnp.where(me < half, acc[0], acc[1])
     send = jnp.where(me < half, acc[1], acc[0]).astype(jnp.bfloat16)
@@ -146,6 +142,10 @@
     sky_half = patch_intensity.astype(jnp.bfloat16)
     first_row = patch_layout_position[:, 0] * facet - image // 2
     first_col = patch_layout_position[:, 1] * facet - image // 2
+    chunk = jnp.arange(n_vis, dtype=jnp.int32)
+    owner = (chunk % 2) * (n_vis // 2) + chunk // 2
+    row_starts = first_row[:, None] + rows_dev * owner[None, :]
+    col_starts = first_col[:, None] + LANE_BLOCK * jnp.arange(facet // LANE_BLOCK, dtype=jnp.int32)
 
     piece = gather_rows(sky_half, n_vis)
 
@@ -154,8 +154,8 @@
     for c in range(ch_local):
         coord_u = spectral_scaling[c] * base_u
         coord_v = spectral_scaling[c] * base_v
-        row_cos, row_sin = phase_table(coord_u, first_row, facet, image)
-        col_cos, col_sin = phase_table(coord_v, first_col, facet, image)
+        row_cos, row_sin = phase_table(coord_u, row_starts, rows_dev, image)
+        col_cos, col_sin = phase_table(coord_v, col_starts, LANE_BLOCK, image)
         cols = lax.optimization_barrier(
             jnp.concatenate([col_cos, col_sin], axis=2).astype(jnp.bfloat16)
         )

time: 72.9 us -> 72.7 us (level)
  waiting for transfers between devices: 22.9 us -> 23.8 us
  other arithmetic: 16.5 us -> 15.6 us
    sin x1 -> x2, other arithmetic: 3.95 us -> 3.07 us  [phase_table(): jnp.sin(fine)]
    all_to_all x1, waiting for transfers between devices: 5.79 us -> 6.67 us  [gather_rows(): lax.all_to_all(jnp.broadcast_to(pair[None], (half,) + pair.shape), 'vis',...]
  transfers between devices with their start and end apart: 6 -> 6, of which waited for: 3 -> 3; matrix products, arithmetic and copies ran while one was open for 21% -> 20% of each run, Pallas kernels for 0% -> 0%
where the time goes in v4:
time: 72.7 us; the launch traced here: 72.2 us
  waiting for transfers between devices  23.8 us (33%)
  other arithmetic  15.6 us (21%)
  starting transfers between devices  15.4 us (21%)
  local copies, waits for them, and re-layouts  9.05 us (12%)
  matrix products  6.89 us (9%)
  between operations  1.58 us (2%)
    all_to_all x1, waiting for transfers between devices, reduce_rows(): got = lax.all_to_all(slabs, 'vis', 0, 0, axis_index_groups=groups)  11.8 us
    all_to_all x1, waiting for transfers between devices, gather_rows(): lax.all_to_all(jnp.broadcast_to(pair[None], (half,) + pair.shape), 'vis',...  6.67 us
    ppermute x2, waiting for transfers between devices, exchange(): return lax.ppermute(x, 'vis', [(i, i ^ mask) for i in range(n_vis)])  5.27 us
    all_to_all x1, starting transfers between devices, gather_rows(): lax.all_to_all(jnp.broadcast_to(pair[None], (half,) + pair.shape), 'vis',...  4.74 us
    dot_general x1, matrix products, local(): jnp.einsum('fij,fjk->fik', sky_rows, cols, preferred_element_type=jnp.flo...  4.54 us
    ppermute x2, starting transfers between devices, exchange(): return lax.ppermute(x, 'vis', [(i, i ^ mask) for i in range(n_vis)])  4.5 us
    all_to_all x1, starting transfers between devices, reduce_rows(): got = lax.all_to_all(slabs, 'vis', 0, 0, axis_index_groups=groups)  3.56 us
    unnamed x13, local copies, waits for them, and re-layouts  3.33 us
  transfers between devices with their start and end apart: 6, of which 3 were waited for; matrix products, arithmetic and copies ran while one was open for 20% of the time, Pallas kernels for 0%

profile of v4, /device:TPU:0, one launch (start us, length us, event | category | flops | bytes accessed | tf_op | source)
XLA Modules:
  0.0 72.2 jit_solution(6000840356658315632)
XLA Ops:
  0.6 0.9 %copy.43 = bf16[32,1,2,512]{3,0,2,1:T(8,128)(2,1)S(1)} copy(f32[32,1,2,512]{3,2,1,0:T(2,128)} %param.9) | data formatting | bytes 196608 | tf_op args[0]
  1.6 4.1 %collective-permute-start = (bf16[32,1,2,512]{3,0,2,1:T(8,128)(2,1)S(1)}, bf16[32,1,2,512]{3,0,2,1:T(8,128)(2,1)S(1)}, u32[]{:S(2)}, u32[]{:S(2)}) collective-permute-start(bf16[32,1,2,512]{3,0,2,1:T(8,128)(2,1)S(1)} %copy.43), channel_id=1, source_target_pairs={{0,16},{2,18},{4,20},{6,22},{8,24},{10,26},{12,28},{14,30},{16,0},... | collective-permute-start | bytes 196616 | tf_op jit(solution)/shard_map/ppermute | solution.py:75
  5.7 0.8 %fusion.60 = (s32[1024,1]{0,1:T(1,128)S(1)}, s32[1024,1]{0,1:T(1,128)S(1)}) fusion(s32[1024,2]{0,1:T(2,128)} %param.13), kind=kLoop, calls=%fused_computation.113 | loop fusion | bytes 16384 | tf_op jit(solution)/shard_map/slice | solution.py:124
  6.4 0.8 %fusion.62 = (f32[1,512]{1,0:T(1,128)S(1)}, f32[1,512]{1,0:T(1,128)S(1)}) fusion(f32[2,512]{1,0:T(2,128)} %param.16), kind=kLoop, calls=%fused_computation.115 | loop fusion | bytes 8192 | tf_op jit(solution)/shard_map/slice | solution.py:126
  7.2 0.7 %fusion.61 = (f32[1024]{0:T(1024)S(1)}, f32[1024]{0:T(1024)S(1)}) fusion(f32[1024]{0:T(1024)} %param.14), kind=kLoop, calls=%fused_computation.114 | loop fusion | bytes 12288 | tf_op jit(solution)/shard_map/sin | solution.py:131
  8.6 1.0 %add_reduce_fusion = (s32[2]{0:T(128)S(1)}, s32[2]{0:T(128)S(1)}) fusion(s32[2,2]{1,0:T(2,128)} %param.17), kind=kLoop, calls=%fused_computation.101 | loop fusion | flops 8 | bytes 32 | tf_op jit(solution)/shard_map/sub | solution.py:143
  9.6 1.7 %select_reduce_fusion.3 = (f32[1024]{0:T(1024)S(1)}, f32[1024]{0:T(1024)S(1)}, f32[1024]{0:T(1024)S(1)}, f32[1024]{0:T(1024)S(1)}) fusion(f32[512]{0:T(512)S(1)} %bitcast.200, s32[1024]{0:T(1024)S(1)} %bitcast.196, f32[512]{0:T(512)S(1)} %bitcast.199, s32[1024]{0:T(1024)S(1)} %bitcast.195), kind=kLoop, calls=%fused_computation.41 | loop fusion | flops 5238784 | bytes 28672 | tf_op jit(solution)/shard_map/reduce_sum | solution.py:38
  11.3 0.1 broadcast_add_fusion.1
  11.3 0.9 %copy.45 = bf16[32,1,2,512]{3,0,2,1:T(8,128)(2,1)S(1)} copy(f32[32,1,2,512]{3,2,1,0:T(2,128)} %param.9) | data formatting | bytes 196608 | tf_op args[0]
  12.3 0.1 add.131
  12.4 0.0 collective-permute-done
  12.4 1.1 %broadcast_in_dim.170 = bf16[8,2,32,1,2,512]{5,2,1,4,3,0:T(8,128)(2,1)} broadcast(bf16[2,32,2,512]{3,1,0,2:T(8,128)(2,1)S(1)} %copy.27), dimensions={1,2,4,5} | broadcast | bytes 1179648 | tf_op jit(solution)/shard_map/broadcast_in_dim | solution.py:85
  13.5 4.7 %all-to-all-start = ((bf16[8,2,32,1,2,512]{5,2,1,4,3,0:T(8,128)(2,1)}), bf16[8,2,32,1,2,512]{5,2,1,4,3,0:T(8,128)(2,1)S(1)}, u32[]{:S(2)}, u32[]{:S(2)}) async-start(bf16[8,2,32,1,2,512]{5,2,1,4,3,0:T(8,128)(2,1)} %broadcast_in_dim.170), calls=%async_computation | async-start | bytes 2097152 | tf_op jit(solution)/shard_map/all_to_all | solution.py:84
  18.2 0.2 fusion.46
  18.4 2.0 %fusion.30 = (f32[128,1024]{1,0:T(8,128)S(1)}, f32[128,1024]{1,0:T(8,128)S(1)}) fusion(f32[128]{0:T(128)S(1)} %iota_convert_fusion.1, f32[1024]{0:T(1024)S(1)} %get-tuple-element.61, s32[1024]{0:T(1024)S(1)} %get-tuple-element.38), kind=kLoop, calls=%fused_computation.45 | loop fusion | flops 1048576 | bytes 1057280 | tf_op jit(solution)/shard_map/sin | solution.py:56
  20.5 0.2 broadcast_in_dim.150
  20.8 0.2 broadcast_in_dim.155
  21.0 1.2 %fusion.1 = (bf16[2,512,1024]{2,1,0:T(8,128)(2,1)S(1)}, bf16[2,512,1024]{2,1,0:T(8,128)(2,1)S(1)}) fusion(f32[512,1024]{1,0:T(8,128)S(1)} %bitcast.182, f32[2,4,1024]{2,1,0:T(4,128)S(1)} %broadcast_in_dim.153, f32[512,1024]{1,0:T(8,128)S(1)} %bitcast.181, f32[2,4,1024]{2,1,0:T(4,128)S(1)} %broadcast_in_dim.148), kind=kLoop, calls=%fused_computation.9 | loop fusion | flops 8388608 | bytes 8454144 | tf_op jit(solution)/shard_map/convert
  22.2 0.0 copy-start.4
  22.3 0.0 copy-start.2
  22.3 2.3 %pad_maximum_fusion = bf16[2,512,2048]{2,1,0:T(8,128)(2,1)} fusion(bf16[2,512,1024]{2,1,0:T(8,128)(2,1)S(1)} %get-tuple-element.37, bf16[2,512,1024]{2,1,0:T(8,128)(2,1)S(1)} %get-tuple-element.36), kind=kLoop, calls=%fused_computation.30 | loop fusion | flops 8388608 | bytes 8388608 | tf_op jit(solution)/shard_map/concatenate | solution.py:160
  24.6 0.1 broadcast_add_fusion
  24.7 0.1 add.141
  24.8 1.0 %fusion.41 = (f32[32,1024]{1,0:T(8,128)S(1)}, f32[32,1024]{1,0:T(8,128)S(1)}, f32[32,1024]{1,0:T(8,128)S(1)}, f32[32,1024]{1,0:T(8,128)S(1)}) fusion(f32[32]{0:T(128)S(1)} %iota_convert_fusion, f32[1024]{0:T(1024)S(1)} %get-tuple-element.60, s32[1024]{0:T(1024)S(1)} %get-tuple-element.32, f32[32]{0:T(128)S(1)} %convert_element_type.119, s32[32]{0:T(128)S(1)} %add.141), kind=kLoop, calls=%fused_computation.61 | loop fusion | flops 524288 | bytes 532864 | tf_op jit(solution)/shard_map/sin | solution.py:56
  25.8 0.0 copy-done.4
  25.8 0.1 select_reduce_fusion.4
  25.9 0.0 copy-done.2
  26.0 6.7 %all-to-all-done = bf16[8,2,32,1,2,512]{5,2,1,4,3,0:T(8,128)(2,1)S(1)} async-done(((bf16[8,2,32,1,2,512]{5,2,1,4,3,0:T(8,128)(2,1)}), bf16[8,2,32,1,2,512]{5,2,1,4,3,0:T(8,128)(2,1)S(1)}, u32[]{:S(2)}, u32[]{:S(2)}) %all-to-all-start) | async-done | bytes 1048608 | tf_op jit(solution)/shard_map/all_to_all | solution.py:84
  32.6 0.1 copy.28
  32.7 4.5 %fusion.63 = f32[2,512,2048]{2,1,0:T(8,128)S(1)} fusion(bf16[2,512,512]{2,1,0:T(8,128)(2,1)S(1)} %bitcast.183, bf16[2,512,2048]{2,1,0:T(8,128)(2,1)} %pad_maximum_fusion), kind=kOutput, calls=%fused_computation.116 | convolution fusion | flops 2147483648 | bytes 13631488 | tf_op jit(solution)/shard_map/fij,fjk->fik/dot_general | solution.py:163
  37.3 0.2 broadcast_in_dim.160
  37.5 0.2 broadcast_in_dim.165
  37.8 0.0 copy-start.3
  37.8 2.1 %fusion.11 = (f32[1024]{0:T(1024)S(1)}, f32[1024]{0:T(1024)S(1)}) fusion(f32[2,512,2048]{2,1,0:T(8,128)S(1)} %fusion.63, f32[512,1024]{1,0:T(8,128)S(1)} %bitcast.178, f32[2,16,1024]{2,1,0:T(8,128)S(1)} %bitcast.187, f32[512,1024]{1,0:T(8,128)S(1)} %bitcast.175, f32[2,16,1024]{2,1,0:T(8,128)S(1)} %bitcast.184), kind=kLoop, calls=%fused_computation.19 | loop fusion | flops 14678016 | bytes 12853248 | tf_op jit(solution)/shard_map/reduce_sum | solution.py:166
  39.9 0.0 copy-done.3
  40.0 1.3 %fusion.13 = bf16[2,512,1024]{2,1,0:T(8,128)(2,1)S(1)} fusion(f32[1024]{0:T(1024)S(1)} %get-tuple-element.49, f32[1024]{0:T(1024)S(1)} %get-tuple-element.48, f32[512,1024]{1,0:T(8,128)S(1)} %bitcast.179, f32[2,16,1024]{2,1,0:T(8,128)S(1)} %bitcast.188, f32[512,1024]{1,0:T(8,128)S(1)} %bitcast.176, f32[2,16,1024]{2,1,0:T(8,128)S(1)} %bitcast.185), kind=kLoop, calls=%fused_computation.21 | loop fusion | flops 10485760 | bytes 6561792 | tf_op jit(solution)/shard_map/convert_element_type | solution.py:170
  41.3 0.0 copy-start
  41.3 1.5 %fusion.26 = bf16[2,512,1024]{2,1,0:T(8,128)(2,1)S(1)} fusion(f32[1024]{0:T(1024)S(1)} %get-tuple-element.49, f32[1024]{0:T(1024)S(1)} %get-tuple-element.48, f32[512,1024]{1,0:T(8,128)S(1)} %bitcast.180, f32[2,16,1024]{2,1,0:T(8,128)S(1)} %bitcast.189, f32[512,1024]{1,0:T(8,128)S(1)} %bitcast.177, f32[2,16,1024]{2,1,0:T(8,128)S(1)} %bitcast.186), kind=kLoop, calls=%fused_computation.35 | loop fusion | flops 11534336 | bytes 6561792 | tf_op jit(solution)/shard_map/neg | solution.py:176
  42.8 0.7 copy-done
  43.5 2.4 %fusion.27 = bf16[2,512,512]{1,2,0:T(8,128)(2,1)S(1)} fusion(bf16[2,512,2048]{2,1,0:T(8,128)(2,1)S(1)} %copy-done, bf16[2,512,1024]{2,1,0:T(8,128)(2,1)S(1)} %fusion.26, bf16[2,512,1024]{2,1,0:T(8,128)(2,1)S(1)} %fusion.13), kind=kOutput, calls=%fused_computation.43 | convolution fusion | flops 2156396544 | bytes 9437184 | tf_op jit(solution)/shard_map/fik,fjk->ifj/dot_general | solution.py:177
  45.9 0.0 copy-start.1
  45.9 1.1 %copy.29 = bf16[8,2,32,1,2,512]{5,2,1,4,3,0:T(8,128)(2,1)} copy(bf16[8,2,32,1,2,512]{5,2,1,0,4,3:T(8,128)(2,1)S(1)} %bitcast.190) | data formatting | bytes 2097152 | tf_op jit(solution)/shard_map/reshape | solution.py:93
  46.9 3.6 %all-to-all-start.1 = ((bf16[8,2,32,1,2,512]{5,2,1,4,3,0:T(8,128)(2,1)}), bf16[8,2,32,1,2,512]{5,2,1,4,3,0:T(8,128)(2,1)S(1)}, u32[]{:S(2)}, u32[]{:S(2)}) async-start(bf16[8,2,32,1,2,512]{5,2,1,4,3,0:T(8,128)(2,1)} %copy.29), calls=%async_computation.1 | async-start | bytes 2097152 | tf_op jit(solution)/shard_map/all_to_all | solution.py:95
  50.5 1.3 %collective-permute-start.2 = (bf16[32,1,2,512]{3,0,2,1:T(8,128)(2,1)S(1)}, bf16[32,1,2,512]{3,0,2,1:T(8,128)(2,1)S(1)}, u32[]{:S(2)}, u32[]{:S(2)}) collective-permute-start(bf16[32,1,2,512]{3,0,2,1:T(8,128)(2,1)S(1)} %copy.43), channel_id=1, source_target_pairs={{0,1},{2,3},{4,5},{6,7},{8,9},{10,11},{12,13},{14,15},{16,17},{18,... | collective-permute-start | bytes 196616 | tf_op jit(solution)/shard_map/ppermute | solution.py:27
  51.8 1.3 %collective-permute-start.3 = (bf16[32,1,2,512]{3,0,2,1:T(8,128)(2,1)S(1)}, bf16[32,1,2,512]{3,0,2,1:T(8,128)(2,1)S(1)}, u32[]{:S(2)}, u32[]{:S(2)}) collective-permute-start(bf16[32,1,2,512]{3,0,2,1:T(8,128)(2,1)S(1)} %copy.43), channel_id=1, source_target_pairs={{1,0},{3,2},{5,4},{7,6},{9,8},{11,10},{13,12},{15,14},{17,16},{19,... | collective-permute-start | bytes 196616 | tf_op jit(solution)/shard_map/ppermute | solution.py:29
  53.1 11.8 %all-to-all-done.1 = bf16[8,2,32,1,2,512]{5,2,1,4,3,0:T(8,128)(2,1)S(1)} async-done(((bf16[8,2,32,1,2,512]{5,2,1,4,3,0:T(8,128)(2,1)}), bf16[8,2,32,1,2,512]{5,2,1,4,3,0:T(8,128)(2,1)S(1)}, u32[]{:S(2)}, u32[]{:S(2)}) %all-to-all-start.1) | async-done | bytes 1048608 | tf_op jit(solution)/shard_map/all_to_all | solution.py:95
  64.9 0.1 convert_reduce_fusion
  65.1 0.4 collective-permute-start.1
  65.5 0.6 maximum_bitcast_fusion
  66.1 0.0 collective-permute-done.2
  66.1 0.0 collective-permute-done.3
  66.1 5.3 %collective-permute-done.1 = bf16[32,1,2,512]{3,0,2,1:T(8,128)(2,1)S(1)} collective-permute-done((bf16[32,1,2,512]{3,0,2,1:T(8,128)(2,1)S(1)}, bf16[32,1,2,512]{3,0,2,1:T(8,128)(2,1)S(1)}, u32[]{:S(2)}, u32[]{:S(2)}) %collective-permute-start.1) | collective-permute-done | bytes 65568 | tf_op jit(solution)/shard_map/ppermute | solution.py:75
  71.4 0.0 copy-done.1
  71.4 0.1 fusion.37
  71.5 0.8 %copy.38 = f32[32,1,2,512]{3,2,1,0:T(2,128)} copy(f32[32,1,2,512]{3,0,2,1:T(8,128)S(1)} %fusion.37) | data formatting | bytes 262144
  (16 shorter events, 0.1 us)
Async XLA Ops:
  1.6 10.8 %collective-permute-start = (bf16[32,1,2,512]{3,0,2,1:T(8,128)(2,1)S(1)}, bf16[32,1,2,512]{3,0,2,1:T(8,128)(2,1)S(1)}, u32[]{:S(2)}, u32[]{:S(2)}) collective-permute-start(bf16[32,1,2,512]{3,0,2,1:T(8,128)(2,1)S(1)} %copy.43), channel_id=1, source_target_pairs={{0,16},{2,18},{4,20},{6,22},{8,24},{10,26},{12,28},{14,30},{16,0},... | collective-permute-start | bytes 196616 | tf_op jit(solution)/shard_map/ppermute | solution.py:75
  13.5 19.1 %all-to-all-start = ((bf16[8,2,32,1,2,512]{5,2,1,4,3,0:T(8,128)(2,1)}), bf16[8,2,32,1,2,512]{5,2,1,4,3,0:T(8,128)(2,1)S(1)}, u32[]{:S(2)}, u32[]{:S(2)}) async-start(bf16[8,2,32,1,2,512]{5,2,1,4,3,0:T(8,128)(2,1)} %broadcast_in_dim.170), calls=%async_computation | async-start | bytes 2097152 | tf_op jit(solution)/shard_map/all_to_all | solution.py:84
  22.2 3.6 %copy-start.4 = (s32[4]{0:T(128)S(1)}, s32[4]{0:T(128)}, u32[]{:S(2)}) copy-start(s32[4]{0:T(128)} %param.12) | copy-start | bytes 52
  22.3 3.7 %copy-start.2 = (f32[1,2,1024]{2,1,0:T(2,128)S(1)}, f32[1,2,1024]{2,1,0:T(2,128)}, u32[]{:S(2)}) copy-start(f32[1,2,1024]{2,1,0:T(2,128)} %param.10) | copy-start | bytes 24580
  37.8 2.2 %copy-start.3 = (f32[1024]{0:T(1024)S(1)}, f32[1024]{0:T(1024)}, u32[]{:S(2)}) copy-start(f32[1024]{0:T(1024)} %param.11) | copy-start | bytes 12292
  41.3 2.2 %copy-start = (bf16[2,512,2048]{2,1,0:T(8,128)(2,1)S(1)}, bf16[2,512,2048]{2,1,0:T(8,128)(2,1)}, u32[]{:S(2)}) copy-start(bf16[2,512,2048]{2,1,0:T(8,128)(2,1)} %pad_maximum_fusion) | copy-start | bytes 12582916
  45.9 25.5 %copy-start.1 = (f32[32,1,2,512]{3,2,1,0:T(2,128)S(1)}, f32[32,1,2,512]{3,2,1,0:T(2,128)}, u32[]{:S(2)}) copy-start(f32[32,1,2,512]{3,2,1,0:T(2,128)} %param.9) | copy-start | bytes 393220
  46.9 18.0 %all-to-all-start.1 = ((bf16[8,2,32,1,2,512]{5,2,1,4,3,0:T(8,128)(2,1)}), bf16[8,2,32,1,2,512]{5,2,1,4,3,0:T(8,128)(2,1)S(1)}, u32[]{:S(2)}, u32[]{:S(2)}) async-start(bf16[8,2,32,1,2,512]{5,2,1,4,3,0:T(8,128)(2,1)} %copy.29), calls=%async_computation.1 | async-start | bytes 2097152 | tf_op jit(solution)/shard_map/all_to_all | solution.py:95
  50.5 15.6 %collective-permute-start.2 = (bf16[32,1,2,512]{3,0,2,1:T(8,128)(2,1)S(1)}, bf16[32,1,2,512]{3,0,2,1:T(8,128)(2,1)S(1)}, u32[]{:S(2)}, u32[]{:S(2)}) collective-permute-start(bf16[32,1,2,512]{3,0,2,1:T(8,128)(2,1)S(1)} %copy.43), channel_id=1, source_target_pairs={{0,1},{2,3},{4,5},{6,7},{8,9},{10,11},{12,13},{14,15},{16,17},{18,... | collective-permute-start | bytes 196616 | tf_op jit(solution)/shard_map/ppermute | solution.py:27
  51.8 14.3 %collective-permute-start.3 = (bf16[32,1,2,512]{3,0,2,1:T(8,128)(2,1)S(1)}, bf16[32,1,2,512]{3,0,2,1:T(8,128)(2,1)S(1)}, u32[]{:S(2)}, u32[]{:S(2)}) collective-permute-start(bf16[32,1,2,512]{3,0,2,1:T(8,128)(2,1)S(1)} %copy.43), channel_id=1, source_target_pairs={{1,0},{3,2},{5,4},{7,6},{9,8},{11,10},{13,12},{15,14},{17,16},{19,... | collective-permute-start | bytes 196616 | tf_op jit(solution)/shard_map/ppermute | solution.py:29
  65.1 6.3 %collective-permute-start.1 = (bf16[32,1,2,512]{3,0,2,1:T(8,128)(2,1)S(1)}, bf16[32,1,2,512]{3,0,2,1:T(8,128)(2,1)S(1)}, u32[]{:S(2)}, u32[]{:S(2)}) collective-permute-start(bf16[32,1,2,512]{3,0,2,1:T(8,128)(2,1)S(1)} %fusion.45), channel_id=1, source_target_pairs={{0,16},{2,18},{4,20},{6,22},{8,24},{10,26},{12,28},{14,30},{16,0},... | collective-permute-start | bytes 196616 | tf_op jit(solution)/shard_map/ppermute | solution.py:75

commit v5 on v4

--- a/solution.py
+++ b/solution.py
@@ -160,7 +160,7 @@
             jnp.concatenate([col_cos, col_sin], axis=2).astype(jnp.bfloat16)
         )
         sky_rows = jnp.transpose(piece[:, c], (1, 0, 2))
-        waves = jnp.einsum("fij,fjk->fik", sky_rows, cols, preferred_element_type=jnp.float32)
+        waves = lax.optimization_barrier(jnp.einsum("fij,fjk->fik", sky_rows, cols, preferred_element_type=jnp.bfloat16)).astype(jnp.float32)
         wave_c = waves[:, :, :nvis]
         wave_s = waves[:, :, nvis:]
         sum_re = jnp.sum(row_cos * wave_c - row_sin * wave_s, axis=(0, 1))

time: 72.7 us -> 73.8 us (1.015)
  other arithmetic: 15.6 us -> 16.6 us
    convert_element_type x0 -> x1, other arithmetic: none -> 1.07 us  [local(): lax.optimization_barrier(jnp.einsum('fij,fjk->fik', sky_rows, cols, prefe...]
where the time goes in v5:
time: 73.8 us; the launch traced here: 73.3 us
  waiting for transfers between devices  23.7 us (32%)
  other arithmetic  16.6 us (22%)
  starting transfers between devices  15.4 us (21%)
  local copies, waits for them, and re-layouts  9.09 us (12%)
  matrix products  6.9 us (9%)
  between operations  1.59 us (2%)
    all_to_all x1, waiting for transfers between devices, reduce_rows(): got = lax.all_to_all(slabs, 'vis', 0, 0, axis_index_groups=groups)  11.8 us
    all_to_all x1, waiting for transfers between devices, gather_rows(): lax.all_to_all(jnp.broadcast_to(pair[None], (half,) + pair.shape), 'vis',...  6.62 us
    ppermute x2, waiting for transfers between devices, exchange(): return lax.ppermute(x, 'vis', [(i, i ^ mask) for i in range(n_vis)])  5.25 us
    all_to_all x1, starting transfers between devices, gather_rows(): lax.all_to_all(jnp.broadcast_to(pair[None], (half,) + pair.shape), 'vis',...  4.74 us
    dot_general x1, matrix products, local(): jnp.einsum('fij,fjk->fik', sky_rows, cols, preferred_element_type=jnp.bfl...  4.54 us
    ppermute x2, starting transfers between devices, exchange(): return lax.ppermute(x, 'vis', [(i, i ^ mask) for i in range(n_vis)])  4.51 us
    all_to_all x1, starting transfers between devices, reduce_rows(): got = lax.all_to_all(slabs, 'vis', 0, 0, axis_index_groups=groups)  3.56 us
    unnamed x13, local copies, waits for them, and re-layouts  3.33 us
  transfers between devices with their start and end apart: 6, of which 3 were waited for; matrix products, arithmetic and copies ran while one was open for 20% of the time, Pallas kernels for 0%

profile of v5, /device:TPU:0, one launch (start us, length us, event | category | flops | bytes accessed | tf_op | source)
XLA Modules:
  0.0 73.3 jit_solution(18105728457439360106)
XLA Ops:
  0.6 0.9 %copy.43 = bf16[32,1,2,512]{3,0,2,1:T(8,128)(2,1)S(1)} copy(f32[32,1,2,512]{3,2,1,0:T(2,128)} %param.9) | data formatting | bytes 196608 | tf_op args[0]
  1.6 4.1 %collective-permute-start = (bf16[32,1,2,512]{3,0,2,1:T(8,128)(2,1)S(1)}, bf16[32,1,2,512]{3,0,2,1:T(8,128)(2,1)S(1)}, u32[]{:S(2)}, u32[]{:S(2)}) collective-permute-start(bf16[32,1,2,512]{3,0,2,1:T(8,128)(2,1)S(1)} %copy.43), channel_id=1, source_target_pairs={{0,16},{2,18},{4,20},{6,22},{8,24},{10,26},{12,28},{14,30},{16,0},... | collective-permute-start | bytes 196616 | tf_op jit(solution)/shard_map/ppermute | solution.py:75
  5.7 0.8 %fusion.60 = (s32[1024,1]{0,1:T(1,128)S(1)}, s32[1024,1]{0,1:T(1,128)S(1)}) fusion(s32[1024,2]{0,1:T(2,128)} %param.13), kind=kLoop, calls=%fused_computation.113 | loop fusion | bytes 16384 | tf_op jit(solution)/shard_map/slice | solution.py:124
  6.4 0.8 %fusion.62 = (f32[1,512]{1,0:T(1,128)S(1)}, f32[1,512]{1,0:T(1,128)S(1)}) fusion(f32[2,512]{1,0:T(2,128)} %param.16), kind=kLoop, calls=%fused_computation.115 | loop fusion | bytes 8192 | tf_op jit(solution)/shard_map/slice | solution.py:126
  7.2 0.7 fusion.61
  8.6 1.0 %add_reduce_fusion = (s32[2]{0:T(128)S(1)}, s32[2]{0:T(128)S(1)}) fusion(s32[2,2]{1,0:T(2,128)} %param.17), kind=kLoop, calls=%fused_computation.101 | loop fusion | flops 8 | bytes 32 | tf_op jit(solution)/shard_map/sub | solution.py:143
  9.6 1.7 %select_reduce_fusion.3 = (f32[1024]{0:T(1024)S(1)}, f32[1024]{0:T(1024)S(1)}, f32[1024]{0:T(1024)S(1)}, f32[1024]{0:T(1024)S(1)}) fusion(f32[512]{0:T(512)S(1)} %bitcast.200, s32[1024]{0:T(1024)S(1)} %bitcast.196, f32[512]{0:T(512)S(1)} %bitcast.199, s32[1024]{0:T(1024)S(1)} %bitcast.195), kind=kLoop, calls=%fused_computation.41 | loop fusion | flops 5238784 | bytes 28672 | tf_op jit(solution)/shard_map/reduce_sum | solution.py:38
  11.3 0.1 broadcast_add_fusion.1
  11.3 0.9 %copy.45 = bf16[32,1,2,512]{3,0,2,1:T(8,128)(2,1)S(1)} copy(f32[32,1,2,512]{3,2,1,0:T(2,128)} %param.9) | data formatting | bytes 196608 | tf_op args[0]
  12.3 0.1 add.131
  12.4 0.0 collective-permute-done
  12.4 1.1 %broadcast_in_dim.170 = bf16[8,2,32,1,2,512]{5,2,1,4,3,0:T(8,128)(2,1)} broadcast(bf16[2,32,2,512]{3,1,0,2:T(8,128)(2,1)S(1)} %copy.27), dimensions={1,2,4,5} | broadcast | bytes 1179648 | tf_op jit(solution)/shard_map/broadcast_in_dim | solution.py:85
  13.5 4.7 %all-to-all-start = ((bf16[8,2,32,1,2,512]{5,2,1,4,3,0:T(8,128)(2,1)}), bf16[8,2,32,1,2,512]{5,2,1,4,3,0:T(8,128)(2,1)S(1)}, u32[]{:S(2)}, u32[]{:S(2)}) async-start(bf16[8,2,32,1,2,512]{5,2,1,4,3,0:T(8,128)(2,1)} %broadcast_in_dim.170), calls=%async_computation | async-start | bytes 2097152 | tf_op jit(solution)/shard_map/all_to_all | solution.py:84
  18.2 0.2 fusion.46
  18.4 2.0 %fusion.30 = (f32[128,1024]{1,0:T(8,128)S(1)}, f32[128,1024]{1,0:T(8,128)S(1)}) fusion(f32[128]{0:T(128)S(1)} %iota_convert_fusion.1, f32[1024]{0:T(1024)S(1)} %get-tuple-element.61, s32[1024]{0:T(1024)S(1)} %get-tuple-element.38), kind=kLoop, calls=%fused_computation.45 | loop fusion | flops 1048576 | bytes 1057280 | tf_op jit(solution)/shard_map/sin | solution.py:56
  20.5 0.2 broadcast_in_dim.150
  20.8 0.3 broadcast_in_dim.155
  21.0 1.2 %fusion.1 = (bf16[2,512,1024]{2,1,0:T(8,128)(2,1)S(1)}, bf16[2,512,1024]{2,1,0:T(8,128)(2,1)S(1)}) fusion(f32[512,1024]{1,0:T(8,128)S(1)} %bitcast.182, f32[2,4,1024]{2,1,0:T(4,128)S(1)} %broadcast_in_dim.153, f32[512,1024]{1,0:T(8,128)S(1)} %bitcast.181, f32[2,4,1024]{2,1,0:T(4,128)S(1)} %broadcast_in_dim.148), kind=kLoop, calls=%fused_computation.9 | loop fusion | flops 8388608 | bytes 8454144 | tf_op jit(solution)/shard_map/convert
  22.3 0.0 copy-start.4
  22.3 0.0 copy-start.2
  22.3 2.4 %pad_maximum_fusion = bf16[2,512,2048]{2,1,0:T(8,128)(2,1)} fusion(bf16[2,512,1024]{2,1,0:T(8,128)(2,1)S(1)} %get-tuple-element.37, bf16[2,512,1024]{2,1,0:T(8,128)(2,1)S(1)} %get-tuple-element.36), kind=kLoop, calls=%fused_computation.30 | loop fusion | flops 8388608 | bytes 8388608 | tf_op jit(solution)/shard_map/concatenate | solution.py:160
  24.6 0.1 broadcast_add_fusion
  24.7 0.1 add.141
  24.8 1.0 %fusion.41 = (f32[32,1024]{1,0:T(8,128)S(1)}, f32[32,1024]{1,0:T(8,128)S(1)}, f32[32,1024]{1,0:T(8,128)S(1)}, f32[32,1024]{1,0:T(8,128)S(1)}) fusion(f32[32]{0:T(128)S(1)} %iota_convert_fusion, f32[1024]{0:T(1024)S(1)} %get-tuple-element.60, s32[1024]{0:T(1024)S(1)} %get-tuple-element.32, f32[32]{0:T(128)S(1)} %convert_element_type.122, s32[32]{0:T(128)S(1)} %add.141), kind=kLoop, calls=%fused_computation.61 | loop fusion | flops 524288 | bytes 532864 | tf_op jit(solution)/shard_map/sin | solution.py:56
  25.9 0.0 copy-done.4
  25.9 0.1 select_reduce_fusion.4
  26.0 0.0 copy-done.2
  26.0 6.6 %all-to-all-done = bf16[8,2,32,1,2,512]{5,2,1,4,3,0:T(8,128)(2,1)S(1)} async-done(((bf16[8,2,32,1,2,512]{5,2,1,4,3,0:T(8,128)(2,1)}), bf16[8,2,32,1,2,512]{5,2,1,4,3,0:T(8,128)(2,1)S(1)}, u32[]{:S(2)}, u32[]{:S(2)}) %all-to-all-start) | async-done | bytes 1048608 | tf_op jit(solution)/shard_map/all_to_all | solution.py:84
  32.6 0.1 copy.28
  32.7 4.5 %fusion.63 = bf16[2,512,2048]{2,1,0:T(8,128)(2,1)S(1)} fusion(bf16[2,512,512]{2,1,0:T(8,128)(2,1)S(1)} %bitcast.190, bf16[2,512,2048]{2,1,0:T(8,128)(2,1)} %pad_maximum_fusion), kind=kOutput, calls=%fused_computation.116 | convolution fusion | flops 2147483648 | bytes 9437184 | tf_op jit(solution)/shard_map/fij,fjk->fik/dot_general | solution.py:163
  37.3 1.1 %convert_element_type.126 = f32[2,512,2048]{2,1,0:T(8,128)S(1)} convert(bf16[2,512,2048]{2,1,0:T(8,128)(2,1)S(1)} %fusion.63) | non-fusion elementwise | flops 2097152 | bytes 12582912 | tf_op jit(solution)/shard_map/convert_element_type | solution.py:163
  38.4 0.3 broadcast_in_dim.160
  38.6 0.2 broadcast_in_dim.165
  38.9 0.0 copy-start.3
  38.9 2.1 %fusion.11 = (f32[1024]{0:T(1024)S(1)}, f32[1024]{0:T(1024)S(1)}) fusion(f32[2,512,2048]{2,1,0:T(8,128)S(1)} %convert_element_type.126, f32[512,1024]{1,0:T(8,128)S(1)} %bitcast.178, f32[2,16,1024]{2,1,0:T(8,128)S(1)} %bitcast.186, f32[512,1024]{1,0:T(8,128)S(1)} %bitcast.175, f32[2,16,1024]{2,1,0:T(8,128)S(1)} %bitcast.183), kind=kLoop, calls=%fused_computation.19 | loop fusion | flops 14678016 | bytes 12853248 | tf_op jit(solution)/shard_map/reduce_sum | solution.py:166
  41.0 0.0 copy-done.3
  41.1 1.3 %fusion.13 = bf16[2,512,1024]{2,1,0:T(8,128)(2,1)S(1)} fusion(f32[1024]{0:T(1024)S(1)} %get-tuple-element.49, f32[1024]{0:T(1024)S(1)} %get-tuple-element.48, f32[512,1024]{1,0:T(8,128)S(1)} %bitcast.179, f32[2,16,1024]{2,1,0:T(8,128)S(1)} %bitcast.187, f32[512,1024]{1,0:T(8,128)S(1)} %bitcast.176, f32[2,16,1024]{2,1,0:T(8,128)S(1)} %bitcast.184), kind=kLoop, calls=%fused_computation.21 | loop fusion | flops 10485760 | bytes 6561792 | tf_op jit(solution)/shard_map/convert_element_type | solution.py:170
  42.4 0.0 copy-start
  42.4 1.5 %fusion.26 = bf16[2,512,1024]{2,1,0:T(8,128)(2,1)S(1)} fusion(f32[1024]{0:T(1024)S(1)} %get-tuple-element.49, f32[1024]{0:T(1024)S(1)} %get-tuple-element.48, f32[512,1024]{1,0:T(8,128)S(1)} %bitcast.180, f32[2,16,1024]{2,1,0:T(8,128)S(1)} %bitcast.188, f32[512,1024]{1,0:T(8,128)S(1)} %bitcast.177, f32[2,16,1024]{2,1,0:T(8,128)S(1)} %bitcast.185), kind=kLoop, calls=%fused_computation.35 | loop fusion | flops 11534336 | bytes 6561792 | tf_op jit(solution)/shard_map/neg | solution.py:176
  43.9 0.7 copy-done
  44.6 2.4 %fusion.27 = bf16[2,512,512]{1,2,0:T(8,128)(2,1)S(1)} fusion(bf16[2,512,2048]{2,1,0:T(8,128)(2,1)S(1)} %copy-done, bf16[2,512,1024]{2,1,0:T(8,128)(2,1)S(1)} %fusion.26, bf16[2,512,1024]{2,1,0:T(8,128)(2,1)S(1)} %fusion.13), kind=kOutput, calls=%fused_computation.43 | convolution fusion | flops 2156396544 | bytes 9437184 | tf_op jit(solution)/shard_map/fik,fjk->ifj/dot_general | solution.py:177
  47.0 0.0 copy-start.1
  47.0 1.1 %copy.29 = bf16[8,2,32,1,2,512]{5,2,1,4,3,0:T(8,128)(2,1)} copy(bf16[8,2,32,1,2,512]{5,2,1,0,4,3:T(8,128)(2,1)S(1)} %bitcast.189) | data formatting | bytes 2097152 | tf_op jit(solution)/shard_map/reshape | solution.py:93
  48.0 3.6 %all-to-all-start.1 = ((bf16[8,2,32,1,2,512]{5,2,1,4,3,0:T(8,128)(2,1)}), bf16[8,2,32,1,2,512]{5,2,1,4,3,0:T(8,128)(2,1)S(1)}, u32[]{:S(2)}, u32[]{:S(2)}) async-start(bf16[8,2,32,1,2,512]{5,2,1,4,3,0:T(8,128)(2,1)} %copy.29), calls=%async_computation.1 | async-start | bytes 2097152 | tf_op jit(solution)/shard_map/all_to_all | solution.py:95
  51.6 1.3 %collective-permute-start.2 = (bf16[32,1,2,512]{3,0,2,1:T(8,128)(2,1)S(1)}, bf16[32,1,2,512]{3,0,2,1:T(8,128)(2,1)S(1)}, u32[]{:S(2)}, u32[]{:S(2)}) collective-permute-start(bf16[32,1,2,512]{3,0,2,1:T(8,128)(2,1)S(1)} %copy.43), channel_id=1, source_target_pairs={{0,1},{2,3},{4,5},{6,7},{8,9},{10,11},{12,13},{14,15},{16,17},{18,... | collective-permute-start | bytes 196616 | tf_op jit(solution)/shard_map/ppermute | solution.py:27
  52.9 1.3 %collective-permute-start.3 = (bf16[32,1,2,512]{3,0,2,1:T(8,128)(2,1)S(1)}, bf16[32,1,2,512]{3,0,2,1:T(8,128)(2,1)S(1)}, u32[]{:S(2)}, u32[]{:S(2)}) collective-permute-start(bf16[32,1,2,512]{3,0,2,1:T(8,128)(2,1)S(1)} %copy.43), channel_id=1, source_target_pairs={{1,0},{3,2},{5,4},{7,6},{9,8},{11,10},{13,12},{15,14},{17,16},{19,... | collective-permute-start | bytes 196616 | tf_op jit(solution)/shard_map/ppermute | solution.py:29
  54.2 11.8 %all-to-all-done.1 = bf16[8,2,32,1,2,512]{5,2,1,4,3,0:T(8,128)(2,1)S(1)} async-done(((bf16[8,2,32,1,2,512]{5,2,1,4,3,0:T(8,128)(2,1)}), bf16[8,2,32,1,2,512]{5,2,1,4,3,0:T(8,128)(2,1)S(1)}, u32[]{:S(2)}, u32[]{:S(2)}) %all-to-all-start.1) | async-done | bytes 1048608 | tf_op jit(solution)/shard_map/all_to_all | solution.py:95
  66.0 0.1 convert_reduce_fusion
  66.2 0.4 collective-permute-start.1
  66.6 0.6 maximum_bitcast_fusion
  67.2 0.0 collective-permute-done.2
  67.2 0.0 collective-permute-done.3
  67.2 5.3 %collective-permute-done.1 = bf16[32,1,2,512]{3,0,2,1:T(8,128)(2,1)S(1)} collective-permute-done((bf16[32,1,2,512]{3,0,2,1:T(8,128)(2,1)S(1)}, bf16[32,1,2,512]{3,0,2,1:T(8,128)(2,1)S(1)}, u32[]{:S(2)}, u32[]{:S(2)}) %collective-permute-start.1) | collective-permute-done | bytes 65568 | tf_op jit(solution)/shard_map/ppermute | solution.py:75
  72.5 0.0 copy-done.1
  72.5 0.1 fusion.37
  72.5 0.8 %copy.38 = f32[32,1,2,512]{3,2,1,0:T(2,128)} copy(f32[32,1,2,512]{3,0,2,1:T(8,128)S(1)} %fusion.37) | data formatting | bytes 262144
  (16 shorter events, 0.1 us)
Async XLA Ops:
  1.6 10.8 %collective-permute-start = (bf16[32,1,2,512]{3,0,2,1:T(8,128)(2,1)S(1)}, bf16[32,1,2,512]{3,0,2,1:T(8,128)(2,1)S(1)}, u32[]{:S(2)}, u32[]{:S(2)}) collective-permute-start(bf16[32,1,2,512]{3,0,2,1:T(8,128)(2,1)S(1)} %copy.43), channel_id=1, source_target_pairs={{0,16},{2,18},{4,20},{6,22},{8,24},{10,26},{12,28},{14,30},{16,0},... | collective-permute-start | bytes 196616 | tf_op jit(solution)/shard_map/ppermute | solution.py:75
  13.5 19.1 %all-to-all-start = ((bf16[8,2,32,1,2,512]{5,2,1,4,3,0:T(8,128)(2,1)}), bf16[8,2,32,1,2,512]{5,2,1,4,3,0:T(8,128)(2,1)S(1)}, u32[]{:S(2)}, u32[]{:S(2)}) async-start(bf16[8,2,32,1,2,512]{5,2,1,4,3,0:T(8,128)(2,1)} %broadcast_in_dim.170), calls=%async_computation | async-start | bytes 2097152 | tf_op jit(solution)/shard_map/all_to_all | solution.py:84
  22.3 3.6 %copy-start.4 = (s32[4]{0:T(128)S(1)}, s32[4]{0:T(128)}, u32[]{:S(2)}) copy-start(s32[4]{0:T(128)} %param.12) | copy-start | bytes 52
  22.3 3.7 %copy-start.2 = (f32[1,2,1024]{2,1,0:T(2,128)S(1)}, f32[1,2,1024]{2,1,0:T(2,128)}, u32[]{:S(2)}) copy-start(f32[1,2,1024]{2,1,0:T(2,128)} %param.10) | copy-start | bytes 24580
  38.9 2.2 %copy-start.3 = (f32[1024]{0:T(1024)S(1)}, f32[1024]{0:T(1024)}, u32[]{:S(2)}) copy-start(f32[1024]{0:T(1024)} %param.11) | copy-start | bytes 12292
  42.4 2.2 %copy-start = (bf16[2,512,2048]{2,1,0:T(8,128)(2,1)S(1)}, bf16[2,512,2048]{2,1,0:T(8,128)(2,1)}, u32[]{:S(2)}) copy-start(bf16[2,512,2048]{2,1,0:T(8,128)(2,1)} %pad_maximum_fusion) | copy-start | bytes 12582916
  47.0 25.5 %copy-start.1 = (f32[32,1,2,512]{3,2,1,0:T(2,128)S(1)}, f32[32,1,2,512]{3,2,1,0:T(2,128)}, u32[]{:S(2)}) copy-start(f32[32,1,2,512]{3,2,1,0:T(2,128)} %param.9) | copy-start | bytes 393220
  48.0 18.0 %all-to-all-start.1 = ((bf16[8,2,32,1,2,512]{5,2,1,4,3,0:T(8,128)(2,1)}), bf16[8,2,32,1,2,512]{5,2,1,4,3,0:T(8,128)(2,1)S(1)}, u32[]{:S(2)}, u32[]{:S(2)}) async-start(bf16[8,2,32,1,2,512]{5,2,1,4,3,0:T(8,128)(2,1)} %copy.29), calls=%async_computation.1 | async-start | bytes 2097152 | tf_op jit(solution)/shard_map/all_to_all | solution.py:95
  51.6 15.6 %collective-permute-start.2 = (bf16[32,1,2,512]{3,0,2,1:T(8,128)(2,1)S(1)}, bf16[32,1,2,512]{3,0,2,1:T(8,128)(2,1)S(1)}, u32[]{:S(2)}, u32[]{:S(2)}) collective-permute-start(bf16[32,1,2,512]{3,0,2,1:T(8,128)(2,1)S(1)} %copy.43), channel_id=1, source_target_pairs={{0,1},{2,3},{4,5},{6,7},{8,9},{10,11},{12,13},{14,15},{16,17},{18,... | collective-permute-start | bytes 196616 | tf_op jit(solution)/shard_map/ppermute | solution.py:27
  52.9 14.3 %collective-permute-start.3 = (bf16[32,1,2,512]{3,0,2,1:T(8,128)(2,1)S(1)}, bf16[32,1,2,512]{3,0,2,1:T(8,128)(2,1)S(1)}, u32[]{:S(2)}, u32[]{:S(2)}) collective-permute-start(bf16[32,1,2,512]{3,0,2,1:T(8,128)(2,1)S(1)} %copy.43), channel_id=1, source_target_pairs={{1,0},{3,2},{5,4},{7,6},{9,8},{11,10},{13,12},{15,14},{17,16},{19,... | collective-permute-start | bytes 196616 | tf_op jit(solution)/shard_map/ppermute | solution.py:29
  66.2 6.3 %collective-permute-start.1 = (bf16[32,1,2,512]{3,0,2,1:T(8,128)(2,1)S(1)}, bf16[32,1,2,512]{3,0,2,1:T(8,128)(2,1)S(1)}, u32[]{:S(2)}, u32[]{:S(2)}) collective-permute-start(bf16[32,1,2,512]{3,0,2,1:T(8,128)(2,1)S(1)} %fusion.45), channel_id=1, source_target_pairs={{0,16},{2,18},{4,20},{6,22},{8,24},{10,26},{12,28},{14,30},{16,0},... | collective-permute-start | bytes 196616 | tf_op jit(solution)/shard_map/ppermute | solution.py:75

commit v6 on v5

--- a/solution.py
+++ b/solution.py
@@ -157,10 +157,10 @@
         row_cos, row_sin = phase_table(coord_u, row_starts, rows_dev, image)
         col_cos, col_sin = phase_table(coord_v, col_starts, LANE_BLOCK, image)
         cols = lax.optimization_barrier(
-            jnp.concatenate([col_cos, col_sin], axis=2).astype(jnp.bfloat16)
+            jnp.swapaxes(jnp.concatenate([col_cos, col_sin], axis=2), 1, 2).astype(jnp.bfloat16)
         )
         sky_rows = jnp.transpose(piece[:, c], (1, 0, 2))
-        waves = lax.optimization_barrier(jnp.einsum("fij,fjk->fik", sky_rows, cols, preferred_element_type=jnp.bfloat16)).astype(jnp.float32)
+        waves = jnp.einsum("fij,fkj->fik", sky_rows, cols, preferred_element_type=jnp.float32)
         wave_c = waves[:, :, :nvis]
         wave_s = waves[:, :, nvis:]
         sum_re = jnp.sum(row_cos * wave_c - row_sin * wave_s, axis=(0, 1))
@@ -174,7 +174,7 @@
             jnp.bfloat16
         )
         zs = jnp.concatenate([z_one, -z_two], axis=2)
-        grad = jnp.einsum("fik,fjk->ifj", zs, cols, preferred_element_type=jnp.float32)
+        grad = jnp.einsum("fik,fkj->ifj", zs, cols, preferred_element_type=jnp.float32)
         new_rows.append(grad)
         residuals.append(jnp.stack([resid_real, resid_imag], axis=0))
     partial = jnp.stack(new_rows, axis=1)

time: 73.8 us -> 96.9 us (1.31)
  local copies, waits for them, and re-layouts: 9.09 us -> 30.4 us
  other arithmetic: 16.6 us -> 19 us
    reshape x0 -> x2, local copies, waits for them, and re-layouts: none -> 10.9 us  [spread(): return jnp.broadcast_to(a.reshape(faces, chunks, 1, count), (faces, chunk...]
    broadcast_in_dim x2 -> x6, local copies, waits for them, and re-layouts: 0.03 us -> 8.46 us  [spread(): jnp.broadcast_to(a.reshape(faces, chunks, 1, count), (faces, chunks, span...]
    another operation x1, other arithmetic: 1.2 us -> 4.92 us
    concatenate x1 -> x0, other arithmetic: 2.37 us -> none  [local(): jnp.concatenate([col_cos, col_sin], axis=2).astype(jnp.bfloat16)]
    unnamed x13 -> x15, local copies, waits for them, and re-layouts: 3.33 us -> 5.07 us
    convert_element_type x1, other arithmetic: 1.07 us -> 2.2 us  [local(): jnp.swapaxes(jnp.concatenate([col_cos, col_sin], axis=2), 1, 2)]
  transfers between devices with their start and end apart: 6 -> 6, of which waited for: 3 -> 3; matrix products, arithmetic and copies ran while one was open for 20% -> 41% of each run, Pallas kernels for 0% -> 0%
where the time goes in v6:
time: 96.9 us; the launch traced here: 96.2 us
  local copies, waits for them, and re-layouts  30.4 us (31%)
  waiting for transfers between devices  23 us (24%)
  other arithmetic  19 us (20%)
  starting transfers between devices  15.4 us (16%)
  matrix products  6.89 us (7%)
  between operations  1.59 us (2%)
    all_to_all x1, waiting for transfers between devices, reduce_rows(): got = lax.all_to_all(slabs, 'vis', 0, 0, axis_index_groups=groups)  11.8 us
    reshape x2, local copies, waits for them, and re-layouts, spread(): return jnp.broadcast_to(a.reshape(faces, chunks, 1, count), (faces, chunk...  10.9 us
    broadcast_in_dim x6, local copies, waits for them, and re-layouts, spread(): jnp.broadcast_to(a.reshape(faces, chunks, 1, count), (faces, chunks, span...  8.46 us
    all_to_all x1, waiting for transfers between devices, gather_rows(): lax.all_to_all(jnp.broadcast_to(pair[None], (half,) + pair.shape), 'vis',...  5.89 us
    ppermute x2, waiting for transfers between devices, exchange(): return lax.ppermute(x, 'vis', [(i, i ^ mask) for i in range(n_vis)])  5.27 us
    unnamed x15, local copies, waits for them, and re-layouts  5.07 us
    another operation x1, other arithmetic  4.92 us
    all_to_all x1, starting transfers between devices, gather_rows(): lax.all_to_all(jnp.broadcast_to(pair[None], (half,) + pair.shape), 'vis',...  4.74 us
  transfers between devices with their start and end apart: 6, of which 3 were waited for; matrix products, arithmetic and copies ran while one was open for 41% of the time, Pallas kernels for 0%

profile of v6, /device:TPU:0, one launch (start us, length us, event | category | flops | bytes accessed | tf_op | source)
XLA Modules:
  0.0 96.2 jit_solution(7587417362379851943)
XLA Ops:
  0.6 0.9 copy.55
  1.6 4.1 %collective-permute-start = (bf16[32,1,2,512]{3,0,2,1:T(8,128)(2,1)S(1)}, bf16[32,1,2,512]{3,0,2,1:T(8,128)(2,1)S(1)}, u32[]{:S(2)}, u32[]{:S(2)}) collective-permute-start(bf16[32,1,2,512]{3,0,2,1:T(8,128)(2,1)S(1)} %copy.55), channel_id=1, source_target_pairs={{0,16},{2,18},{4,20},{6,22},{8,24},{10,26},{12,28},{14,30},{16,0},... | collective-permute-start | bytes 196616 | tf_op jit(solution)/shard_map/ppermute | solution.py:75
  5.7 0.8 fusion.56
  6.5 0.8 fusion.58
  7.2 0.7 fusion.57
  8.6 1.0 %add_reduce_fusion = (s32[2]{0:T(128)S(1)}, s32[2]{0:T(128)S(1)}) fusion(s32[2,2]{1,0:T(2,128)} %param.17), kind=kLoop, calls=%fused_computation.97 | loop fusion | flops 8 | bytes 32 | tf_op jit(solution)/shard_map/sub | solution.py:143
  9.6 0.1 broadcast_add_fusion.1
  9.6 0.1 add.131
  9.7 1.6 %select_reduce_fusion.3 = (f32[1024]{0:T(1024)S(1)}, f32[1024]{0:T(1024)S(1)}, f32[1024]{0:T(1024)S(1)}, f32[1024]{0:T(1024)S(1)}) fusion(f32[512]{0:T(512)S(1)} %bitcast.200, s32[1024]{0:T(1024)S(1)} %bitcast.196, f32[512]{0:T(512)S(1)} %bitcast.199, s32[1024]{0:T(1024)S(1)} %bitcast.195), kind=kLoop, calls=%fused_computation.37 | loop fusion | flops 5238784 | bytes 28672 | tf_op jit(solution)/shard_map/reduce_sum | solution.py:38
  11.4 2.1 %fusion.26 = (f32[128,1024]{0,1:T(8,128)S(1)}, f32[128,1024]{0,1:T(8,128)S(1)}) fusion(f32[128]{0:T(128)S(1)} %iota_convert_fusion.1, f32[1024]{0:T(1024)S(1)} %get-tuple-element.61, s32[1024]{0:T(1024)S(1)} %get-tuple-element.38), kind=kLoop, calls=%fused_computation.41 | loop fusion | flops 1048576 | bytes 1057280 | tf_op jit(solution)/shard_map/sin | solution.py:56
  13.5 0.2 fusion.42
  13.7 0.9 copy.59
  14.6 0.4 copy.32
  15.0 3.8 %broadcast_in_dim.149 = f32[2,4,128,1024]{2,1,3,0:T(4,128)} broadcast(f32[2,4,1024]{1,2,0:T(8,128)S(1)} %copy.32), dimensions={0,1,3} | broadcast | bytes 4227072 | tf_op jit(solution)/shard_map/broadcast_in_dim | solution.py:61
  18.8 5.5 %reshape.273 = f32[2,512,1024]{1,2,0:T(8,128)} reshape(f32[2,4,128,1024]{2,1,3,0:T(4,128)} %broadcast_in_dim.149) | data formatting | bytes 8388608 | tf_op jit(solution)/shard_map/reshape | solution.py:63
  24.3 0.4 copy.33
  24.7 3.9 %broadcast_in_dim.154 = f32[2,4,128,1024]{2,1,3,0:T(4,128)} broadcast(f32[2,4,1024]{1,2,0:T(8,128)S(1)} %copy.33), dimensions={0,1,3} | broadcast | bytes 4227072 | tf_op jit(solution)/shard_map/broadcast_in_dim | solution.py:61
  28.6 5.5 %reshape.274 = f32[2,512,1024]{1,2,0:T(8,128)} reshape(f32[2,4,128,1024]{2,1,3,0:T(4,128)} %broadcast_in_dim.154) | data formatting | bytes 8388608 | tf_op jit(solution)/shard_map/reshape | solution.py:63
  34.0 0.4 broadcast_in_dim.155
  34.4 0.2 copy.57
  34.6 0.4 broadcast_in_dim.150
  34.9 1.6 %copy.58 = f32[128,8,4,128]{3,1,2,0:T(8,128)} copy(f32[128,8,4,128]{3,2,1,0:T(4,128)S(1)} %bitcast.180) | data formatting | bytes 4194304
  36.5 0.0 collective-permute-done
  36.5 1.1 %broadcast_in_dim.170 = bf16[8,2,32,1,2,512]{5,2,1,4,3,0:T(8,128)(2,1)} broadcast(bf16[2,32,2,512]{3,1,0,2:T(8,128)(2,1)S(1)} %copy.35), dimensions={1,2,4,5} | broadcast | bytes 1179648 | tf_op jit(solution)/shard_map/broadcast_in_dim | solution.py:85
  37.6 4.7 %all-to-all-start = ((bf16[8,2,32,1,2,512]{5,2,1,4,3,0:T(8,128)(2,1)}), bf16[8,2,32,1,2,512]{5,2,1,4,3,0:T(8,128)(2,1)S(1)}, u32[]{:S(2)}, u32[]{:S(2)}) async-start(bf16[8,2,32,1,2,512]{5,2,1,4,3,0:T(8,128)(2,1)} %broadcast_in_dim.170), calls=%async_computation | async-start | bytes 2097152 | tf_op jit(solution)/shard_map/all_to_all | solution.py:84
  42.4 4.9 %subtract_convert_fusion = (bf16[2,512,1024]{1,2,0:T(8,128)(2,1)S(1)}, bf16[2,512,1024]{1,2,0:T(8,128)(2,1)S(1)}) fusion(f32[2,512,1024]{1,2,0:T(8,128)} %reshape.274, f32[2,512,1024]{1,2,0:T(8,128)} %reshape.273, f32[512,1024]{0,1:T(8,128)S(1)} %bitcast.181, f32[512,1024]{0,1:T(8,128)} %bitcast.182), kind=kLoop, calls=%fused_computation.28 | loop fusion | flops 8388608 | bytes 16777216 | tf_op jit(solution)/shard_map/convert
  47.3 0.0 copy-start.4
  47.3 0.0 copy-start.2
  47.3 2.2 %maximum_bitcast_fusion = bf16[2,2048,512]{2,1,0:T(8,128)(2,1)} fusion(bf16[2,512,1024]{1,2,0:T(8,128)(2,1)S(1)} %get-tuple-element.37, bf16[2,512,1024]{1,2,0:T(8,128)(2,1)S(1)} %get-tuple-element.36), kind=kLoop, calls=%fused_computation.22 | loop fusion | flops 8388608 | bytes 8388608 | tf_op jit(solution)/shard_map/convert_element_type | solution.py:160
  49.5 0.1 broadcast_add_fusion
  49.6 0.1 add.141
  49.7 1.0 %fusion.37 = (f32[32,1024]{1,0:T(8,128)S(1)}, f32[32,1024]{1,0:T(8,128)S(1)}, f32[32,1024]{1,0:T(8,128)S(1)}, f32[32,1024]{1,0:T(8,128)S(1)}) fusion(f32[32]{0:T(128)S(1)} %iota_convert_fusion, f32[1024]{0:T(1024)S(1)} %get-tuple-element.60, s32[1024]{0:T(1024)S(1)} %get-tuple-element.32, f32[32]{0:T(128)S(1)} %convert_element_type.123, s32[32]{0:T(128)S(1)} %add.141), kind=kLoop, calls=%fused_computation.57 | loop fusion | flops 524288 | bytes 532864 | tf_op jit(solution)/shard_map/sin | solution.py:56
  50.8 0.0 copy-done.4
  50.8 0.1 select_reduce_fusion.4
  50.9 0.0 copy-done.2
  50.9 5.9 %all-to-all-done = bf16[8,2,32,1,2,512]{5,2,1,4,3,0:T(8,128)(2,1)S(1)} async-done(((bf16[8,2,32,1,2,512]{5,2,1,4,3,0:T(8,128)(2,1)}), bf16[8,2,32,1,2,512]{5,2,1,4,3,0:T(8,128)(2,1)S(1)}, u32[]{:S(2)}, u32[]{:S(2)}) %all-to-all-start) | async-done | bytes 1048608 | tf_op jit(solution)/shard_map/all_to_all | solution.py:84
  56.8 0.1 copy.36
  56.9 4.6 %fusion.59 = f32[2,512,2048]{2,1,0:T(8,128)S(1)} fusion(bf16[2,512,512]{2,1,0:T(8,128)(2,1)S(1)} %bitcast.183, bf16[2,2048,512]{2,1,0:T(8,128)(2,1)} %maximum_bitcast_fusion), kind=kOutput, calls=%fused_computation.112 | convolution fusion | flops 2147483648 | bytes 13631488 | tf_op jit(solution)/shard_map/fij,fkj->fik/dot_general | solution.py:163
  61.5 0.2 broadcast_in_dim.165
  61.7 0.2 broadcast_in_dim.160
  62.0 0.0 copy-start.3
  62.0 2.0 %fusion.7 = (f32[1024]{0:T(1024)S(1)}, f32[1024]{0:T(1024)S(1)}) fusion(f32[2,512,2048]{2,1,0:T(8,128)S(1)} %fusion.59, f32[512,1024]{1,0:T(8,128)S(1)} %bitcast.173, f32[2,16,1024]{2,1,0:T(8,128)S(1)} %bitcast.187, f32[512,1024]{1,0:T(8,128)S(1)} %bitcast.176, f32[2,16,1024]{2,1,0:T(8,128)S(1)} %bitcast.184), kind=kLoop, calls=%fused_computation.11 | loop fusion | flops 14678016 | bytes 12853248 | tf_op jit(solution)/shard_map/reduce_sum | solution.py:166
  63.9 0.0 copy-done.3
  64.0 1.3 %fusion.9 = bf16[2,512,1024]{2,1,0:T(8,128)(2,1)S(1)} fusion(f32[1024]{0:T(1024)S(1)} %get-tuple-element.49, f32[1024]{0:T(1024)S(1)} %get-tuple-element.48, f32[512,1024]{1,0:T(8,128)S(1)} %bitcast.174, f32[2,16,1024]{2,1,0:T(8,128)S(1)} %bitcast.188, f32[512,1024]{1,0:T(8,128)S(1)} %bitcast.177, f32[2,16,1024]{2,1,0:T(8,128)S(1)} %bitcast.185), kind=kLoop, calls=%fused_computation.13 | loop fusion | flops 10485760 | bytes 6561792 | tf_op jit(solution)/shard_map/convert_element_type | solution.py:170
  65.3 0.0 copy-start
  65.3 1.5 %fusion.22 = bf16[2,512,1024]{2,1,0:T(8,128)(2,1)S(1)} fusion(f32[1024]{0:T(1024)S(1)} %get-tuple-element.49, f32[1024]{0:T(1024)S(1)} %get-tuple-element.48, f32[512,1024]{1,0:T(8,128)S(1)} %bitcast.175, f32[2,16,1024]{2,1,0:T(8,128)S(1)} %bitcast.189, f32[512,1024]{1,0:T(8,128)S(1)} %bitcast.178, f32[2,16,1024]{2,1,0:T(8,128)S(1)} %bitcast.186), kind=kLoop, calls=%fused_computation.29 | loop fusion | flops 11534336 | bytes 6561792 | tf_op jit(solution)/shard_map/neg | solution.py:176
  66.8 0.7 copy-done
  67.5 2.3 %fusion.23 = bf16[2,512,512]{1,2,0:T(8,128)(2,1)S(1)} fusion(bf16[2,2048,512]{2,1,0:T(8,128)(2,1)S(1)} %copy-done, bf16[2,512,1024]{2,1,0:T(8,128)(2,1)S(1)} %fusion.22, bf16[2,512,1024]{2,1,0:T(8,128)(2,1)S(1)} %fusion.9), kind=kOutput, calls=%fused_computation.39 | convolution fusion | flops 2156396544 | bytes 9437184 | tf_op jit(solution)/shard_map/fik,fkj->ifj/dot_general | solution.py:177
  69.8 0.0 copy-start.1
  69.8 1.1 %copy.37 = bf16[8,2,32,1,2,512]{5,2,1,4,3,0:T(8,128)(2,1)} copy(bf16[8,2,32,1,2,512]{5,2,1,0,4,3:T(8,128)(2,1)S(1)} %bitcast.190) | data formatting | bytes 2097152 | tf_op jit(solution)/shard_map/reshape | solution.py:93
  70.9 3.6 %all-to-all-start.1 = ((bf16[8,2,32,1,2,512]{5,2,1,4,3,0:T(8,128)(2,1)}), bf16[8,2,32,1,2,512]{5,2,1,4,3,0:T(8,128)(2,1)S(1)}, u32[]{:S(2)}, u32[]{:S(2)}) async-start(bf16[8,2,32,1,2,512]{5,2,1,4,3,0:T(8,128)(2,1)} %copy.37), calls=%async_computation.1 | async-start | bytes 2097152 | tf_op jit(solution)/shard_map/all_to_all | solution.py:95
  74.5 1.3 %collective-permute-start.2 = (bf16[32,1,2,512]{3,0,2,1:T(8,128)(2,1)S(1)}, bf16[32,1,2,512]{3,0,2,1:T(8,128)(2,1)S(1)}, u32[]{:S(2)}, u32[]{:S(2)}) collective-permute-start(bf16[32,1,2,512]{3,0,2,1:T(8,128)(2,1)S(1)} %copy.55), channel_id=1, source_target_pairs={{0,1},{2,3},{4,5},{6,7},{8,9},{10,11},{12,13},{14,15},{16,17},{18,... | collective-permute-start | bytes 196616 | tf_op jit(solution)/shard_map/ppermute | solution.py:27
  75.8 1.3 %collective-permute-start.3 = (bf16[32,1,2,512]{3,0,2,1:T(8,128)(2,1)S(1)}, bf16[32,1,2,512]{3,0,2,1:T(8,128)(2,1)S(1)}, u32[]{:S(2)}, u32[]{:S(2)}) collective-permute-start(bf16[32,1,2,512]{3,0,2,1:T(8,128)(2,1)S(1)} %copy.55), channel_id=1, source_target_pairs={{1,0},{3,2},{5,4},{7,6},{9,8},{11,10},{13,12},{15,14},{17,16},{19,... | collective-permute-start | bytes 196616 | tf_op jit(solution)/shard_map/ppermute | solution.py:29
  77.1 11.8 %all-to-all-done.1 = bf16[8,2,32,1,2,512]{5,2,1,4,3,0:T(8,128)(2,1)S(1)} async-done(((bf16[8,2,32,1,2,512]{5,2,1,4,3,0:T(8,128)(2,1)}), bf16[8,2,32,1,2,512]{5,2,1,4,3,0:T(8,128)(2,1)S(1)}, u32[]{:S(2)}, u32[]{:S(2)}) %all-to-all-start.1) | async-done | bytes 1048608 | tf_op jit(solution)/shard_map/all_to_all | solution.py:95
  88.9 0.1 convert_reduce_fusion
  89.1 0.4 collective-permute-start.1
  89.5 0.6 maximum_bitcast_fusion.1
  90.1 0.0 collective-permute-done.2
  90.1 0.0 collective-permute-done.3
  90.1 5.3 %collective-permute-done.1 = bf16[32,1,2,512]{3,0,2,1:T(8,128)(2,1)S(1)} collective-permute-done((bf16[32,1,2,512]{3,0,2,1:T(8,128)(2,1)S(1)}, bf16[32,1,2,512]{3,0,2,1:T(8,128)(2,1)S(1)}, u32[]{:S(2)}, u32[]{:S(2)}) %collective-permute-start.1) | collective-permute-done | bytes 65568 | tf_op jit(solution)/shard_map/ppermute | solution.py:75
  95.4 0.0 copy-done.1
  95.4 0.1 fusion.33
  95.5 0.8 copy.46
  (16 shorter events, 0.1 us)
Async XLA Ops:
  1.6 34.9 %collective-permute-start = (bf16[32,1,2,512]{3,0,2,1:T(8,128)(2,1)S(1)}, bf16[32,1,2,512]{3,0,2,1:T(8,128)(2,1)S(1)}, u32[]{:S(2)}, u32[]{:S(2)}) collective-permute-start(bf16[32,1,2,512]{3,0,2,1:T(8,128)(2,1)S(1)} %copy.55), channel_id=1, source_target_pairs={{0,16},{2,18},{4,20},{6,22},{8,24},{10,26},{12,28},{14,30},{16,0},... | collective-permute-start | bytes 196616 | tf_op jit(solution)/shard_map/ppermute | solution.py:75
  37.6 19.1 %all-to-all-start = ((bf16[8,2,32,1,2,512]{5,2,1,4,3,0:T(8,128)(2,1)}), bf16[8,2,32,1,2,512]{5,2,1,4,3,0:T(8,128)(2,1)S(1)}, u32[]{:S(2)}, u32[]{:S(2)}) async-start(bf16[8,2,32,1,2,512]{5,2,1,4,3,0:T(8,128)(2,1)} %broadcast_in_dim.170), calls=%async_computation | async-start | bytes 2097152 | tf_op jit(solution)/shard_map/all_to_all | solution.py:84
  47.3 3.5 %copy-start.4 = (s32[4]{0:T(128)S(1)}, s32[4]{0:T(128)}, u32[]{:S(2)}) copy-start(s32[4]{0:T(128)} %param.12) | copy-start | bytes 52
  47.3 3.5 %copy-start.2 = (f32[1,2,1024]{2,1,0:T(2,128)S(1)}, f32[1,2,1024]{2,1,0:T(2,128)}, u32[]{:S(2)}) copy-start(f32[1,2,1024]{2,1,0:T(2,128)} %param.10) | copy-start | bytes 24580
  62.0 2.0 %copy-start.3 = (f32[1024]{0:T(1024)S(1)}, f32[1024]{0:T(1024)}, u32[]{:S(2)}) copy-start(f32[1024]{0:T(1024)} %param.11) | copy-start | bytes 12292
  65.3 2.2 %copy-start = (bf16[2,2048,512]{2,1,0:T(8,128)(2,1)S(1)}, bf16[2,2048,512]{2,1,0:T(8,128)(2,1)}, u32[]{:S(2)}) copy-start(bf16[2,2048,512]{2,1,0:T(8,128)(2,1)} %maximum_bitcast_fusion) | copy-start | bytes 12582916
  69.8 25.6 %copy-start.1 = (f32[32,1,2,512]{3,2,1,0:T(2,128)S(1)}, f32[32,1,2,512]{3,2,1,0:T(2,128)}, u32[]{:S(2)}) copy-start(f32[32,1,2,512]{3,2,1,0:T(2,128)} %param.9) | copy-start | bytes 393220
  70.9 18.0 %all-to-all-start.1 = ((bf16[8,2,32,1,2,512]{5,2,1,4,3,0:T(8,128)(2,1)}), bf16[8,2,32,1,2,512]{5,2,1,4,3,0:T(8,128)(2,1)S(1)}, u32[]{:S(2)}, u32[]{:S(2)}) async-start(bf16[8,2,32,1,2,512]{5,2,1,4,3,0:T(8,128)(2,1)} %copy.37), calls=%async_computation.1 | async-start | bytes 2097152 | tf_op jit(solution)/shard_map/all_to_all | solution.py:95
  74.5 15.6 %collective-permute-start.2 = (bf16[32,1,2,512]{3,0,2,1:T(8,128)(2,1)S(1)}, bf16[32,1,2,512]{3,0,2,1:T(8,128)(2,1)S(1)}, u32[]{:S(2)}, u32[]{:S(2)}) collective-permute-start(bf16[32,1,2,512]{3,0,2,1:T(8,128)(2,1)S(1)} %copy.55), channel_id=1, source_target_pairs={{0,1},{2,3},{4,5},{6,7},{8,9},{10,11},{12,13},{14,15},{16,17},{18,... | collective-permute-start | bytes 196616 | tf_op jit(solution)/shard_map/ppermute | solution.py:27
  75.8 14.3 %collective-permute-start.3 = (bf16[32,1,2,512]{3,0,2,1:T(8,128)(2,1)S(1)}, bf16[32,1,2,512]{3,0,2,1:T(8,128)(2,1)S(1)}, u32[]{:S(2)}, u32[]{:S(2)}) collective-permute-start(bf16[32,1,2,512]{3,0,2,1:T(8,128)(2,1)S(1)} %copy.55), channel_id=1, source_target_pairs={{1,0},{3,2},{5,4},{7,6},{9,8},{11,10},{13,12},{15,14},{17,16},{19,... | collective-permute-start | bytes 196616 | tf_op jit(solution)/shard_map/ppermute | solution.py:29
  89.1 6.3 %collective-permute-start.1 = (bf16[32,1,2,512]{3,0,2,1:T(8,128)(2,1)S(1)}, bf16[32,1,2,512]{3,0,2,1:T(8,128)(2,1)S(1)}, u32[]{:S(2)}, u32[]{:S(2)}) collective-permute-start(bf16[32,1,2,512]{3,0,2,1:T(8,128)(2,1)S(1)} %fusion.41), channel_id=1, source_target_pairs={{0,16},{2,18},{4,20},{6,22},{8,24},{10,26},{12,28},{14,30},{16,0},... | collective-permute-start | bytes 196616 | tf_op jit(solution)/shard_map/ppermute | solution.py:75

commit v7 on v4

--- a/solution.py
+++ b/solution.py
@@ -75,16 +75,17 @@
     return lax.ppermute(x, "vis", [(i, i ^ mask) for i in range(n_vis)])
 
 
-def gather_rows(block, n_vis):
+def gather_rows(block, n_vis, tied):
     half = n_vis // 2
     me = lax.axis_index("vis")
     other = exchange(block, n_vis, half)
+    other, tied = lax.optimization_barrier((other, tied))
     pair = jnp.where(me < half, jnp.stack([block, other]), jnp.stack([other, block]))
     groups = [list(range(half)), list(range(half, n_vis))]
     full = lax.all_to_all(
         jnp.broadcast_to(pair[None], (half,) + pair.shape), "vis", 0, 0, axis_index_groups=groups
     )
-    return full.reshape((n_vis * block.shape[0],) + block.shape[1:])
+    return full.reshape((n_vis * block.shape[0],) + block.shape[1:]), tied
 
 
 def reduce_rows(partial, n_vis, rows):
@@ -119,6 +120,10 @@
     image = GRID * facet
     norm_pred = 1.0 / math.sqrt(facets_here * facet * facet)
     norm_grad = 1.0 / math.sqrt(nvis * n_vis)
+    sky_half = patch_intensity.astype(jnp.bfloat16)
+    piece, (receiver_pairs, sample_rotation_phase) = gather_rows(
+        sky_half, n_vis, (receiver_pairs, sample_rotation_phase)
+    )
     eastward_shift = receiver_lookup_dict(
         receiver_positions[0], receiver_pairs[:, 0]
     ) - receiver_lookup_dict(receiver_positions[0], receiver_pairs[:, 1])
@@ -139,7 +144,6 @@
         axis=1,
     )
     scale_vis = (slots % BLOCK < block_count).astype(jnp.float32) * sample_importance
-    sky_half = patch_intensity.astype(jnp.bfloat16)
     first_row = patch_layout_position[:, 0] * facet - image // 2
     first_col = patch_layout_position[:, 1] * facet - image // 2
     chunk = jnp.arange(n_vis, dtype=jnp.int32)
@@ -147,7 +151,6 @@
     row_starts = first_row[:, None] + rows_dev * owner[None, :]
     col_starts = first_col[:, None] + LANE_BLOCK * jnp.arange(facet // LANE_BLOCK, dtype=jnp.int32)
 
-    piece = gather_rows(sky_half, n_vis)
 
     new_rows = []
     residuals = []

time: 72.7 us -> 72.2 us (level)
  waiting for transfers between devices: 23.8 us -> 21.8 us
    all_to_all x1, waiting for transfers between devices: 6.67 us -> 5.27 us  [gather_rows(): lax.all_to_all(jnp.broadcast_to(pair[None], (half,) + pair.shape), 'vis',...]
    slice x1, local copies, waits for them, and re-layouts: 0.01 us -> 0.79 us  [local(): resid_real = scale_vis * (norm_pred * sum_re - recorded_samples[c, 0])]
    unnamed x13 -> x11, local copies, waits for them, and re-layouts: 3.33 us -> 3.33 us
where the time goes in v7:
time: 72.2 us; the launch traced here: 71.6 us
  waiting for transfers between devices  21.8 us (30%)
  other arithmetic  16.2 us (22%)
  starting transfers between devices  16 us (22%)
  local copies, waits for them, and re-layouts  9.15 us (13%)
  matrix products  6.89 us (10%)
  between operations  1.57 us (2%)
    all_to_all x1, waiting for transfers between devices, reduce_rows(): got = lax.all_to_all(slabs, 'vis', 0, 0, axis_index_groups=groups)  11.8 us
    all_to_all x1, waiting for transfers between devices, gather_rows(): lax.all_to_all(jnp.broadcast_to(pair[None], (half,) + pair.shape), 'vis',...  5.27 us
    ppermute x2, starting transfers between devices, exchange(): return lax.ppermute(x, 'vis', [(i, i ^ mask) for i in range(n_vis)])  5.1 us
    all_to_all x1, starting transfers between devices, gather_rows(): lax.all_to_all(jnp.broadcast_to(pair[None], (half,) + pair.shape), 'vis',...  4.74 us
    ppermute x2, waiting for transfers between devices, exchange(): return lax.ppermute(x, 'vis', [(i, i ^ mask) for i in range(n_vis)])  4.67 us
    dot_general x1, matrix products, local(): jnp.einsum('fij,fjk->fik', sky_rows, cols, preferred_element_type=jnp.flo...  4.54 us
    all_to_all x1, starting transfers between devices, reduce_rows(): got = lax.all_to_all(slabs, 'vis', 0, 0, axis_index_groups=groups)  3.56 us
    unnamed x11, local copies, waits for them, and re-layouts  3.33 us
  transfers between devices with their start and end apart: 6, of which 3 were waited for; matrix products, arithmetic and copies ran while one was open for 20% of the time, Pallas kernels for 0%

profile of v7, /device:TPU:0, one launch (start us, length us, event | category | flops | bytes accessed | tf_op | source)
XLA Modules:
  0.0 71.6 jit_solution(11538110379561218938)
XLA Ops:
  0.6 0.0 copy-start.2
  0.6 0.9 %copy.44 = bf16[32,1,2,512]{3,0,2,1:T(8,128)(2,1)S(1)} copy(f32[32,1,2,512]{3,2,1,0:T(2,128)} %param.9) | data formatting | bytes 196608 | tf_op args[0]
  1.6 4.1 %collective-permute-start = (bf16[32,1,2,512]{3,0,2,1:T(8,128)(2,1)S(1)}, bf16[32,1,2,512]{3,0,2,1:T(8,128)(2,1)S(1)}, u32[]{:S(2)}, u32[]{:S(2)}) collective-permute-start(bf16[32,1,2,512]{3,0,2,1:T(8,128)(2,1)S(1)} %copy.44), channel_id=1, source_target_pairs={{0,16},{2,18},{4,20},{6,22},{8,24},{10,26},{12,28},{14,30},{16,0},... | collective-permute-start | bytes 196616 | tf_op jit(solution)/shard_map/ppermute | solution.py:75
  5.7 0.9 %copy.46 = bf16[32,1,2,512]{3,0,2,1:T(8,128)(2,1)S(1)} copy(f32[32,1,2,512]{3,2,1,0:T(2,128)} %param.9) | data formatting | bytes 196608 | tf_op args[0]
  6.6 0.8 %fusion.62 = (f32[1,512]{1,0:T(1,128)S(1)}, f32[1,512]{1,0:T(1,128)S(1)}) fusion(f32[2,512]{1,0:T(2,128)} %param.16), kind=kLoop, calls=%fused_computation.115 | loop fusion | bytes 8192 | tf_op jit(solution)/shard_map/slice | solution.py:131
  8.1 1.0 %add_reduce_fusion = (s32[2]{0:T(128)S(1)}, s32[2]{0:T(128)S(1)}) fusion(s32[2,2]{1,0:T(2,128)} %param.17), kind=kLoop, calls=%fused_computation.101 | loop fusion | flops 8 | bytes 32 | tf_op jit(solution)/shard_map/sub | solution.py:147
  9.0 0.1 broadcast_add_fusion.1
  9.1 0.1 add.131
  9.2 0.1 broadcast_add_fusion
  9.3 0.1 add.141
  9.4 0.8 %fusion.59 = (f32[1,1,1024]{2,1,0:T(1,128)S(1)}, f32[1,1,1024]{2,1,0:T(1,128)S(1)}) fusion(f32[1,2,1024]{2,1,0:T(2,128)} %param.10), kind=kLoop, calls=%fused_computation.112 | loop fusion | bytes 16384 | tf_op jit(solution)/shard_map/slice | solution.py:171
  10.2 0.7 %select_reduce_fusion.4 = s32[1024]{0:T(1024)S(1)} fusion(s32[4]{0:T(128)} %param.12, s32[1024]{0:T(1024)S(1)} %add_select_fusion), kind=kLoop, calls=%fused_computation.73 | loop fusion | flops 11264 | bytes 8208 | tf_op jit(solution)/shard_map/reduce_sum | solution.py:142
  10.9 0.0 collective-permute-done
  10.9 0.8 %fusion.60 = (s32[1024,1]{0,1:T(1,128)S(1)}, s32[1024,1]{0,1:T(1,128)S(1)}) fusion(s32[1024,2]{0,1:T(2,128)} %param.13), kind=kLoop, calls=%fused_computation.113 | loop fusion | bytes 16384 | tf_op jit(solution)/shard_map/slice | solution.py:129
  11.7 1.1 %broadcast_in_dim.170 = bf16[8,2,32,1,2,512]{5,2,1,4,3,0:T(8,128)(2,1)} broadcast(bf16[2,32,2,512]{3,1,0,2:T(8,128)(2,1)S(1)} %copy.28), dimensions={1,2,4,5} | broadcast | bytes 1179648 | tf_op jit(solution)/shard_map/broadcast_in_dim | solution.py:86
  12.8 4.7 %all-to-all-start = ((bf16[8,2,32,1,2,512]{5,2,1,4,3,0:T(8,128)(2,1)}), bf16[8,2,32,1,2,512]{5,2,1,4,3,0:T(8,128)(2,1)S(1)}, u32[]{:S(2)}, u32[]{:S(2)}) async-start(bf16[8,2,32,1,2,512]{5,2,1,4,3,0:T(8,128)(2,1)} %broadcast_in_dim.170), calls=%async_computation | async-start | bytes 2097152 | tf_op jit(solution)/shard_map/all_to_all | solution.py:85
  17.6 0.0 copy-done.2
  17.6 1.7 %select_reduce_fusion.3 = (f32[1024]{0:T(1024)S(1)}, f32[1024]{0:T(1024)S(1)}, f32[1024]{0:T(1024)S(1)}, f32[1024]{0:T(1024)S(1)}) fusion(f32[512]{0:T(512)S(1)} %bitcast.200, s32[1024]{0:T(1024)S(1)} %bitcast.196, f32[512]{0:T(512)S(1)} %bitcast.199, s32[1024]{0:T(1024)S(1)} %bitcast.195), kind=kLoop, calls=%fused_computation.41 | loop fusion | flops 5238784 | bytes 28672 | tf_op jit(solution)/shard_map/reduce_sum | solution.py:38
  19.3 0.2 fusion.46
  19.5 2.0 %fusion.30 = (f32[128,1024]{1,0:T(8,128)S(1)}, f32[128,1024]{1,0:T(8,128)S(1)}) fusion(f32[128]{0:T(128)S(1)} %iota_convert_fusion.1, f32[1024]{0:T(1024)S(1)} %get-tuple-element.67, s32[1024]{0:T(1024)S(1)} %get-tuple-element.44), kind=kLoop, calls=%fused_computation.45 | loop fusion | flops 1048576 | bytes 1057280 | tf_op jit(solution)/shard_map/sin | solution.py:56
  21.6 0.2 broadcast_in_dim.150
  21.8 0.2 broadcast_in_dim.155
  22.1 1.2 %fusion.1 = (bf16[2,512,1024]{2,1,0:T(8,128)(2,1)S(1)}, bf16[2,512,1024]{2,1,0:T(8,128)(2,1)S(1)}) fusion(f32[512,1024]{1,0:T(8,128)S(1)} %bitcast.182, f32[2,4,1024]{2,1,0:T(4,128)S(1)} %broadcast_in_dim.153, f32[512,1024]{1,0:T(8,128)S(1)} %bitcast.181, f32[2,4,1024]{2,1,0:T(4,128)S(1)} %broadcast_in_dim.148), kind=kLoop, calls=%fused_computation.9 | loop fusion | flops 8388608 | bytes 8454144 | tf_op jit(solution)/shard_map/convert
  23.3 2.3 %pad_maximum_fusion = bf16[2,512,2048]{2,1,0:T(8,128)(2,1)} fusion(bf16[2,512,1024]{2,1,0:T(8,128)(2,1)S(1)} %get-tuple-element.43, bf16[2,512,1024]{2,1,0:T(8,128)(2,1)S(1)} %get-tuple-element.42), kind=kLoop, calls=%fused_computation.30 | loop fusion | flops 8388608 | bytes 8388608 | tf_op jit(solution)/shard_map/concatenate | solution.py:163
  25.6 1.0 %fusion.41 = (f32[32,1024]{1,0:T(8,128)S(1)}, f32[32,1024]{1,0:T(8,128)S(1)}, f32[32,1024]{1,0:T(8,128)S(1)}, f32[32,1024]{1,0:T(8,128)S(1)}) fusion(f32[32]{0:T(128)S(1)} %iota_convert_fusion, f32[1024]{0:T(1024)S(1)} %get-tuple-element.66, s32[1024]{0:T(1024)S(1)} %get-tuple-element.38, f32[32]{0:T(128)S(1)} %convert_element_type.120, s32[32]{0:T(128)S(1)} %add.141), kind=kLoop, calls=%fused_computation.61 | loop fusion | flops 524288 | bytes 532864 | tf_op jit(solution)/shard_map/sin | solution.py:56
  26.7 5.3 %all-to-all-done = bf16[8,2,32,1,2,512]{5,2,1,4,3,0:T(8,128)(2,1)S(1)} async-done(((bf16[8,2,32,1,2,512]{5,2,1,4,3,0:T(8,128)(2,1)}), bf16[8,2,32,1,2,512]{5,2,1,4,3,0:T(8,128)(2,1)S(1)}, u32[]{:S(2)}, u32[]{:S(2)}) %all-to-all-start) | async-done | bytes 1048608 | tf_op jit(solution)/shard_map/all_to_all | solution.py:85
  32.0 0.1 copy.29
  32.1 4.5 %fusion.63 = f32[2,512,2048]{2,1,0:T(8,128)S(1)} fusion(bf16[2,512,512]{2,1,0:T(8,128)(2,1)S(1)} %bitcast.183, bf16[2,512,2048]{2,1,0:T(8,128)(2,1)} %pad_maximum_fusion), kind=kOutput, calls=%fused_computation.116 | convolution fusion | flops 2147483648 | bytes 13631488 | tf_op jit(solution)/shard_map/fij,fjk->fik/dot_general | solution.py:166
  36.6 0.2 broadcast_in_dim.160
  36.9 0.2 broadcast_in_dim.165
  37.1 0.0 copy-start.3
  37.1 2.1 %fusion.11 = (f32[1024]{0:T(1024)S(1)}, f32[1024]{0:T(1024)S(1)}) fusion(f32[2,512,2048]{2,1,0:T(8,128)S(1)} %fusion.63, f32[512,1024]{1,0:T(8,128)S(1)} %bitcast.178, f32[2,16,1024]{2,1,0:T(8,128)S(1)} %bitcast.187, f32[512,1024]{1,0:T(8,128)S(1)} %bitcast.175, f32[2,16,1024]{2,1,0:T(8,128)S(1)} %bitcast.184), kind=kLoop, calls=%fused_computation.19 | loop fusion | flops 14678016 | bytes 12853248 | tf_op jit(solution)/shard_map/reduce_sum | solution.py:169
  39.3 0.0 copy-done.3
  39.3 1.3 %fusion.13 = bf16[2,512,1024]{2,1,0:T(8,128)(2,1)S(1)} fusion(f32[1024]{0:T(1024)S(1)} %get-tuple-element.55, f32[1024]{0:T(1024)S(1)} %get-tuple-element.54, f32[512,1024]{1,0:T(8,128)S(1)} %bitcast.179, f32[2,16,1024]{2,1,0:T(8,128)S(1)} %bitcast.188, f32[512,1024]{1,0:T(8,128)S(1)} %bitcast.176, f32[2,16,1024]{2,1,0:T(8,128)S(1)} %bitcast.185), kind=kLoop, calls=%fused_computation.21 | loop fusion | flops 10485760 | bytes 6561792 | tf_op jit(solution)/shard_map/convert_element_type | solution.py:173
  40.7 0.0 copy-start
  40.7 1.5 %fusion.26 = bf16[2,512,1024]{2,1,0:T(8,128)(2,1)S(1)} fusion(f32[1024]{0:T(1024)S(1)} %get-tuple-element.55, f32[1024]{0:T(1024)S(1)} %get-tuple-element.54, f32[512,1024]{1,0:T(8,128)S(1)} %bitcast.180, f32[2,16,1024]{2,1,0:T(8,128)S(1)} %bitcast.189, f32[512,1024]{1,0:T(8,128)S(1)} %bitcast.177, f32[2,16,1024]{2,1,0:T(8,128)S(1)} %bitcast.186), kind=kLoop, calls=%fused_computation.35 | loop fusion | flops 11534336 | bytes 6561792 | tf_op jit(solution)/shard_map/neg | solution.py:179
  42.2 0.7 copy-done
  42.8 2.4 %fusion.27 = bf16[2,512,512]{1,2,0:T(8,128)(2,1)S(1)} fusion(bf16[2,512,2048]{2,1,0:T(8,128)(2,1)S(1)} %copy-done, bf16[2,512,1024]{2,1,0:T(8,128)(2,1)S(1)} %fusion.26, bf16[2,512,1024]{2,1,0:T(8,128)(2,1)S(1)} %fusion.13), kind=kOutput, calls=%fused_computation.43 | convolution fusion | flops 2156396544 | bytes 9437184 | tf_op jit(solution)/shard_map/fik,fjk->ifj/dot_general | solution.py:180
  45.2 0.0 copy-start.1
  45.2 1.1 %copy.30 = bf16[8,2,32,1,2,512]{5,2,1,4,3,0:T(8,128)(2,1)} copy(bf16[8,2,32,1,2,512]{5,2,1,0,4,3:T(8,128)(2,1)S(1)} %bitcast.190) | data formatting | bytes 2097152 | tf_op jit(solution)/shard_map/reshape | solution.py:94
  46.3 3.6 %all-to-all-start.1 = ((bf16[8,2,32,1,2,512]{5,2,1,4,3,0:T(8,128)(2,1)}), bf16[8,2,32,1,2,512]{5,2,1,4,3,0:T(8,128)(2,1)S(1)}, u32[]{:S(2)}, u32[]{:S(2)}) async-start(bf16[8,2,32,1,2,512]{5,2,1,4,3,0:T(8,128)(2,1)} %copy.30), calls=%async_computation.1 | async-start | bytes 2097152 | tf_op jit(solution)/shard_map/all_to_all | solution.py:96
  49.8 1.3 %collective-permute-start.2 = (bf16[32,1,2,512]{3,0,2,1:T(8,128)(2,1)S(1)}, bf16[32,1,2,512]{3,0,2,1:T(8,128)(2,1)S(1)}, u32[]{:S(2)}, u32[]{:S(2)}) collective-permute-start(bf16[32,1,2,512]{3,0,2,1:T(8,128)(2,1)S(1)} %copy.44), channel_id=1, source_target_pairs={{0,1},{2,3},{4,5},{6,7},{8,9},{10,11},{12,13},{14,15},{16,17},{18,... | collective-permute-start | bytes 196616 | tf_op jit(solution)/shard_map/ppermute | solution.py:27
  51.1 1.3 %collective-permute-start.3 = (bf16[32,1,2,512]{3,0,2,1:T(8,128)(2,1)S(1)}, bf16[32,1,2,512]{3,0,2,1:T(8,128)(2,1)S(1)}, u32[]{:S(2)}, u32[]{:S(2)}) collective-permute-start(bf16[32,1,2,512]{3,0,2,1:T(8,128)(2,1)S(1)} %copy.44), channel_id=1, source_target_pairs={{1,0},{3,2},{5,4},{7,6},{9,8},{11,10},{13,12},{15,14},{17,16},{19,... | collective-permute-start | bytes 196616 | tf_op jit(solution)/shard_map/ppermute | solution.py:29
  52.5 11.8 %all-to-all-done.1 = bf16[8,2,32,1,2,512]{5,2,1,4,3,0:T(8,128)(2,1)S(1)} async-done(((bf16[8,2,32,1,2,512]{5,2,1,4,3,0:T(8,128)(2,1)}), bf16[8,2,32,1,2,512]{5,2,1,4,3,0:T(8,128)(2,1)S(1)}, u32[]{:S(2)}, u32[]{:S(2)}) %all-to-all-start.1) | async-done | bytes 1048608 | tf_op jit(solution)/shard_map/all_to_all | solution.py:96
  64.3 0.1 convert_reduce_fusion
  64.4 1.0 %collective-permute-start.1 = (bf16[32,1,2,512]{3,0,2,1:T(8,128)(2,1)S(1)}, bf16[32,1,2,512]{3,0,2,1:T(8,128)(2,1)S(1)}, u32[]{:S(2)}, u32[]{:S(2)}) collective-permute-start(bf16[32,1,2,512]{3,0,2,1:T(8,128)(2,1)S(1)} %fusion.45), channel_id=1, source_target_pairs={{0,16},{2,18},{4,20},{6,22},{8,24},{10,26},{12,28},{14,30},{16,0},... | collective-permute-start | bytes 196616 | tf_op jit(solution)/shard_map/ppermute | solution.py:75
  65.4 0.6 maximum_bitcast_fusion
  66.0 0.0 collective-permute-done.2
  66.0 0.0 collective-permute-done.3
  66.1 4.7 %collective-permute-done.1 = bf16[32,1,2,512]{3,0,2,1:T(8,128)(2,1)S(1)} collective-permute-done((bf16[32,1,2,512]{3,0,2,1:T(8,128)(2,1)S(1)}, bf16[32,1,2,512]{3,0,2,1:T(8,128)(2,1)S(1)}, u32[]{:S(2)}, u32[]{:S(2)}) %collective-permute-start.1) | collective-permute-done | bytes 65568 | tf_op jit(solution)/shard_map/ppermute | solution.py:75
  70.7 0.0 copy-done.1
  70.7 0.1 fusion.37
  70.8 0.8 %copy.39 = f32[32,1,2,512]{3,2,1,0:T(2,128)} copy(f32[32,1,2,512]{3,0,2,1:T(8,128)S(1)} %fusion.37) | data formatting | bytes 262144
  (16 shorter events, 0.2 us)
Async XLA Ops:
  0.6 16.9 %copy-start.2 = (f32[1024]{0:T(1024)S(1)}, f32[1024]{0:T(1024)}, u32[]{:S(2)}) copy-start(f32[1024]{0:T(1024)} %param.14) | copy-start | bytes 12292
  1.6 9.3 %collective-permute-start = (bf16[32,1,2,512]{3,0,2,1:T(8,128)(2,1)S(1)}, bf16[32,1,2,512]{3,0,2,1:T(8,128)(2,1)S(1)}, u32[]{:S(2)}, u32[]{:S(2)}) collective-permute-start(bf16[32,1,2,512]{3,0,2,1:T(8,128)(2,1)S(1)} %copy.44), channel_id=1, source_target_pairs={{0,16},{2,18},{4,20},{6,22},{8,24},{10,26},{12,28},{14,30},{16,0},... | collective-permute-start | bytes 196616 | tf_op jit(solution)/shard_map/ppermute | solution.py:75
  12.8 19.1 %all-to-all-start = ((bf16[8,2,32,1,2,512]{5,2,1,4,3,0:T(8,128)(2,1)}), bf16[8,2,32,1,2,512]{5,2,1,4,3,0:T(8,128)(2,1)S(1)}, u32[]{:S(2)}, u32[]{:S(2)}) async-start(bf16[8,2,32,1,2,512]{5,2,1,4,3,0:T(8,128)(2,1)} %broadcast_in_dim.170), calls=%async_computation | async-start | bytes 2097152 | tf_op jit(solution)/shard_map/all_to_all | solution.py:85
  37.1 2.2 %copy-start.3 = (f32[1024]{0:T(1024)S(1)}, f32[1024]{0:T(1024)}, u32[]{:S(2)}) copy-start(f32[1024]{0:T(1024)} %param.11) | copy-start | bytes 12292
  40.7 2.2 %copy-start = (bf16[2,512,2048]{2,1,0:T(8,128)(2,1)S(1)}, bf16[2,512,2048]{2,1,0:T(8,128)(2,1)}, u32[]{:S(2)}) copy-start(bf16[2,512,2048]{2,1,0:T(8,128)(2,1)} %pad_maximum_fusion) | copy-start | bytes 12582916
  45.2 25.5 %copy-start.1 = (f32[32,1,2,512]{3,2,1,0:T(2,128)S(1)}, f32[32,1,2,512]{3,2,1,0:T(2,128)}, u32[]{:S(2)}) copy-start(f32[32,1,2,512]{3,2,1,0:T(2,128)} %param.9) | copy-start | bytes 393220
  46.3 18.0 %all-to-all-start.1 = ((bf16[8,2,32,1,2,512]{5,2,1,4,3,0:T(8,128)(2,1)}), bf16[8,2,32,1,2,512]{5,2,1,4,3,0:T(8,128)(2,1)S(1)}, u32[]{:S(2)}, u32[]{:S(2)}) async-start(bf16[8,2,32,1,2,512]{5,2,1,4,3,0:T(8,128)(2,1)} %copy.30), calls=%async_computation.1 | async-start | bytes 2097152 | tf_op jit(solution)/shard_map/all_to_all | solution.py:96
  49.8 16.2 %collective-permute-start.2 = (bf16[32,1,2,512]{3,0,2,1:T(8,128)(2,1)S(1)}, bf16[32,1,2,512]{3,0,2,1:T(8,128)(2,1)S(1)}, u32[]{:S(2)}, u32[]{:S(2)}) collective-permute-start(bf16[32,1,2,512]{3,0,2,1:T(8,128)(2,1)S(1)} %copy.44), channel_id=1, source_target_pairs={{0,1},{2,3},{4,5},{6,7},{8,9},{10,11},{12,13},{14,15},{16,17},{18,... | collective-permute-start | bytes 196616 | tf_op jit(solution)/shard_map/ppermute | solution.py:27
  51.1 14.9 %collective-permute-start.3 = (bf16[32,1,2,512]{3,0,2,1:T(8,128)(2,1)S(1)}, bf16[32,1,2,512]{3,0,2,1:T(8,128)(2,1)S(1)}, u32[]{:S(2)}, u32[]{:S(2)}) collective-permute-start(bf16[32,1,2,512]{3,0,2,1:T(8,128)(2,1)S(1)} %copy.44), channel_id=1, source_target_pairs={{1,0},{3,2},{5,4},{7,6},{9,8},{11,10},{13,12},{15,14},{17,16},{19,... | collective-permute-start | bytes 196616 | tf_op jit(solution)/shard_map/ppermute | solution.py:29
  64.4 6.3 %collective-permute-start.1 = (bf16[32,1,2,512]{3,0,2,1:T(8,128)(2,1)S(1)}, bf16[32,1,2,512]{3,0,2,1:T(8,128)(2,1)S(1)}, u32[]{:S(2)}, u32[]{:S(2)}) collective-permute-start(bf16[32,1,2,512]{3,0,2,1:T(8,128)(2,1)S(1)} %fusion.45), channel_id=1, source_target_pairs={{0,16},{2,18},{4,20},{6,22},{8,24},{10,26},{12,28},{14,30},{16,0},... | collective-permute-start | bytes 196616 | tf_op jit(solution)/shard_map/ppermute | solution.py:75

commit v8 on v7

--- a/solution.py
+++ b/solution.py
@@ -3,6 +3,7 @@
 import jax
 import jax.numpy as jnp
 from jax import lax
+from jax.experimental import pallas as pl
 from jax.sharding import PartitionSpec as P
 
 GRID = 64
@@ -48,7 +49,7 @@
     return exact + rest[None, :] * pixel.astype(jnp.float32) / image
 
 
-def phase_table(coord, starts, span, image):
+def phase_factors(coord, starts, span, image):
     faces, chunks = starts.shape
     coarse = full_turn * turns(coord, starts.reshape(-1, 1), image)
     fine = full_turn * turns(coord, jnp.arange(span, dtype=jnp.int32)[:, None], image)
@@ -56,11 +57,23 @@
         (jnp.cos(coarse), jnp.sin(coarse), jnp.cos(fine), jnp.sin(fine))
     )
     count = coord.shape[0]
+    return (
+        coarse_c.reshape(faces, chunks, count),
+        coarse_s.reshape(faces, chunks, count),
+        fine_c,
+        fine_s,
+    )
+
+
+def phase_table(factors):
+    coarse_c, coarse_s, fine_c, fine_s = factors
+    faces, chunks, count = coarse_c.shape
+    span = fine_c.shape[0]
 
     def spread(a):
-        return jnp.broadcast_to(
-            a.reshape(faces, chunks, 1, count), (faces, chunks, span, count)
-        ).reshape(faces, chunks * span, count)
+        return jnp.broadcast_to(a[:, :, None, :], (faces, chunks, span, count)).reshape(
+            faces, chunks * span, count
+        )
 
     def tile(a):
         return jnp.broadcast_to(a[None, None], (faces, chunks, span, count)).reshape(
@@ -69,6 +82,54 @@
 
     pc, ps, qc, qs = spread(coarse_c), spread(coarse_s), tile(fine_c), tile(fine_s)
     return (pc * qc - ps * qs, ps * qc + pc * qs)
+
+
+def predict_kernel(sky_ref, ccos_ref, csin_ref, pc_ref, ps_ref, qc_ref, qs_ref, re_ref, im_ref):
+    sky = sky_ref[...]
+    wave_c = jnp.dot(sky, ccos_ref[...], preferred_element_type=jnp.float32)
+    wave_s = jnp.dot(sky, csin_ref[...], preferred_element_type=jnp.float32)
+    chunks = pc_ref.shape[0]
+    span = qc_ref.shape[0]
+    tk = wave_c.shape[1]
+    wave_c = wave_c.reshape(chunks, span, tk)
+    wave_s = wave_s.reshape(chunks, span, tk)
+    qc = qc_ref[...][None]
+    qs = qs_ref[...][None]
+    a = jnp.sum(qc * wave_c - qs * wave_s, axis=1)
+    b = jnp.sum(qs * wave_c + qc * wave_s, axis=1)
+    pc = pc_ref[...]
+    ps = ps_ref[...]
+    re_ref[...] = jnp.sum(pc * a - ps * b, axis=0, keepdims=True)
+    im_ref[...] = -jnp.sum(pc * b + ps * a, axis=0, keepdims=True)
+
+
+def predict_sums(sky_rows, cols, factors, tk):
+    coarse_c, coarse_s, fine_c, fine_s = factors
+    faces, rows, width = sky_rows.shape
+    chunks = coarse_c.shape[1]
+    span = fine_c.shape[0]
+    count = fine_c.shape[1]
+    tiles = count // tk
+    out = jax.ShapeDtypeStruct((faces, 1, count), jnp.float32)
+    re, im = pl.pallas_call(
+        predict_kernel,
+        grid=(faces, tiles),
+        in_specs=[
+            pl.BlockSpec((None, rows, width), lambda f, t: (f, 0, 0)),
+            pl.BlockSpec((None, width, tk), lambda f, t: (f, 0, t)),
+            pl.BlockSpec((None, width, tk), lambda f, t: (f, 0, t + tiles)),
+            pl.BlockSpec((None, chunks, tk), lambda f, t: (f, 0, t)),
+            pl.BlockSpec((None, chunks, tk), lambda f, t: (f, 0, t)),
+            pl.BlockSpec((span, tk), lambda f, t: (0, t)),
+            pl.BlockSpec((span, tk), lambda f, t: (0, t)),
+        ],
+        out_specs=[
+            pl.BlockSpec((None, 1, tk), lambda f, t: (f, 0, t)),
+            pl.BlockSpec((None, 1, tk), lambda f, t: (f, 0, t)),
+        ],
+        out_shape=[out, out],
+    )(sky_rows, cols, cols, coarse_c, coarse_s, fine_c, fine_s)
+    return jnp.sum(re, axis=(0, 1)), jnp.sum(im, axis=(0, 1))
 
 
 def exchange(x, n_vis, mask):
@@ -157,17 +218,14 @@
     for c in range(ch_local):
         coord_u = spectral_scaling[c] * base_u
         coord_v = spectral_scaling[c] * base_v
-        row_cos, row_sin = phase_table(coord_u, row_starts, rows_dev, image)
-        col_cos, col_sin = phase_table(coord_v, col_starts, LANE_BLOCK, image)
+        row_factors = phase_factors(coord_u, row_starts, rows_dev, image)
+        row_cos, row_sin = phase_table(row_factors)
+        col_cos, col_sin = phase_table(phase_factors(coord_v, col_starts, LANE_BLOCK, image))
         cols = lax.optimization_barrier(
             jnp.concatenate([col_cos, col_sin], axis=2).astype(jnp.bfloat16)
         )
         sky_rows = jnp.transpose(piece[:, c], (1, 0, 2))
-        waves = jnp.einsum("fij,fjk->fik", sky_rows, cols, preferred_element_type=jnp.float32)
-        wave_c = waves[:, :, :nvis]
-        wave_s = waves[:, :, nvis:]
-        sum_re = jnp.sum(row_cos * wave_c - row_sin * wave_s, axis=(0, 1))
-        sum_im = -jnp.sum(row_cos * wave_s + row_sin * wave_c, axis=(0, 1))
+        sum_re, sum_im = predict_sums(sky_rows, cols, row_factors, min(nvis, 512))
         resid_real = scale_vis * (norm_pred * sum_re - recorded_samples[c, 0])
         resid_imag = scale_vis * (norm_pred * sum_im - recorded_samples[c, 1])
         z_one = (row_cos * resid_real[None, None, :] - row_sin * resid_imag[None, None, :]).astype(

time: 72.2 us -> 74.8 us (1.036)
  Pallas kernels: 0 us -> 6.57 us
  matrix products: 6.89 us -> 2.36 us
  waiting for transfers between devices: 21.8 us -> 19.2 us
  starting transfers between devices: 16 us -> 17.7 us
  local copies, waits for them, and re-layouts: 9.15 us -> 10.2 us
    pallas_call x0 -> x1, Pallas kernels: none -> 6.57 us  [predict_sums(): pl.pallas_call(predict_kernel, grid=(faces, tiles), in_specs=[pl.BlockSpe...]
    dot_general x1 -> x0, matrix products: 4.54 us -> none  [local(): jnp.einsum('fij,fjk->fik', sky_rows, cols, preferred_element_type=jnp.flo...]
    all_to_all x1, waiting for transfers between devices: 11.8 us -> 10.1 us  [reduce_rows(): got = lax.all_to_all(slabs, 'vis', 0, 0, axis_index_groups=groups)]
    ppermute x1, starting transfers between devices: 1.29 us -> 3.03 us  [extended(): lax.ppermute(tail, axis, [(i, (i + 1) % count) for i in range(ends)])]
    all_to_all x1, local copies, waits for them, and re-layouts: 0.1 us -> 1.05 us  [gather_rows(): lax.all_to_all(jnp.broadcast_to(pair[None], (half,) + pair.shape), 'vis',...]
    all_to_all x1, waiting for transfers between devices: 5.27 us -> 4.46 us  [gather_rows(): lax.all_to_all(jnp.broadcast_to(pair[None], (half,) + pair.shape), 'vis',...]
    sin x3, other arithmetic: 3.27 us -> 4.07 us  [the longest x2 3.87 us: phase_factors(): jnp.sin(fine)]
    reduce_sum x1 -> x2, other arithmetic: 2.14 us -> 1.47 us  [predict_sums(): return (jnp.sum(re, axis=(0, 1)), jnp.sum(im, axis=(0, 1)))]
  transfers between devices with their start and end apart: 6 -> 6, of which waited for: 3 -> 3; matrix products, arithmetic and copies ran while one was open for 20% -> 21% of each run, Pallas kernels for 0% -> 0%
where the time goes in v8:
time: 74.8 us; the launch traced here: 74 us
  waiting for transfers between devices  19.2 us (26%)
  starting transfers between devices  17.7 us (24%)
  other arithmetic  16.4 us (22%)
  local copies, waits for them, and re-layouts  10.2 us (14%)
  Pallas kernels  6.57 us (9%)
  matrix products  2.36 us (3%)
  between operations  1.59 us (2%)
    all_to_all x1, waiting for transfers between devices, reduce_rows(): got = lax.all_to_all(slabs, 'vis', 0, 0, axis_index_groups=groups)  10.1 us
    pallas_call x1, Pallas kernels, predict_sums(): pl.pallas_call(predict_kernel, grid=(faces, tiles), in_specs=[pl.BlockSpe...  6.57 us
    ppermute x2, starting transfers between devices, exchange(): return lax.ppermute(x, 'vis', [(i, i ^ mask) for i in range(n_vis)])  5.09 us
    all_to_all x1, starting transfers between devices, gather_rows(): lax.all_to_all(jnp.broadcast_to(pair[None], (half,) + pair.shape), 'vis',...  4.74 us
    ppermute x2, waiting for transfers between devices, exchange(): return lax.ppermute(x, 'vis', [(i, i ^ mask) for i in range(n_vis)])  4.67 us
    all_to_all x1, waiting for transfers between devices, gather_rows(): lax.all_to_all(jnp.broadcast_to(pair[None], (half,) + pair.shape), 'vis',...  4.46 us
    sin x2, other arithmetic, phase_factors(): jnp.sin(fine)  3.87 us
    all_to_all x1, starting transfers between devices, reduce_rows(): got = lax.all_to_all(slabs, 'vis', 0, 0, axis_index_groups=groups)  3.56 us
  transfers between devices with their start and end apart: 6, of which 3 were waited for; matrix products, arithmetic and copies ran while one was open for 21% of the time, Pallas kernels for 0%

profile of v8, /device:TPU:0, one launch (start us, length us, event | category | flops | bytes accessed | tf_op | source)
XLA Modules:
  0.0 74.0 jit_solution(15615479810650632620)
XLA Ops:
  0.6 0.0 copy-start.6
  0.6 0.9 %copy.44 = bf16[32,1,2,512]{3,0,2,1:T(8,128)(2,1)S(1)} copy(f32[32,1,2,512]{3,2,1,0:T(2,128)} %param.9) | data formatting | bytes 196608 | tf_op args[0]
  1.6 4.1 %collective-permute-start = (bf16[32,1,2,512]{3,0,2,1:T(8,128)(2,1)S(1)}, bf16[32,1,2,512]{3,0,2,1:T(8,128)(2,1)S(1)}, u32[]{:S(2)}, u32[]{:S(2)}) collective-permute-start(bf16[32,1,2,512]{3,0,2,1:T(8,128)(2,1)S(1)} %copy.44), channel_id=1, source_target_pairs={{0,16},{2,18},{4,20},{6,22},{8,24},{10,26},{12,28},{14,30},{16,0},... | collective-permute-start | bytes 196616 | tf_op jit(solution)/shard_map/ppermute | solution.py:136
  5.7 0.9 %copy.46 = bf16[32,1,2,512]{3,0,2,1:T(8,128)(2,1)S(1)} copy(f32[32,1,2,512]{3,2,1,0:T(2,128)} %param.9) | data formatting | bytes 196608 | tf_op args[0]
  6.6 1.0 %add_reduce_fusion = (s32[2]{0:T(128)S(1)}, s32[2]{0:T(128)S(1)}) fusion(s32[2,2]{1,0:T(2,128)} %param.17), kind=kLoop, calls=%fused_computation.93 | loop fusion | flops 8 | bytes 32 | tf_op jit(solution)/shard_map/sub | solution.py:208
  7.6 0.1 broadcast_add_fusion.1
  7.7 0.1 add.128
  7.8 0.8 %fusion.54 = (f32[1,512]{1,0:T(1,128)S(1)}, f32[1,512]{1,0:T(1,128)S(1)}) fusion(f32[2,512]{1,0:T(2,128)} %param.16), kind=kLoop, calls=%fused_computation.107 | loop fusion | bytes 8192 | tf_op jit(solution)/shard_map/slice | solution.py:192
  9.2 0.8 %fusion.51 = (f32[1,1,1024]{2,1,0:T(1,128)S(1)}, f32[1,1,1024]{2,1,0:T(1,128)S(1)}) fusion(f32[1,2,1024]{2,1,0:T(2,128)} %param.10), kind=kLoop, calls=%fused_computation.104 | loop fusion | bytes 16384 | tf_op jit(solution)/shard_map/slice | solution.py:229
  10.0 0.1 broadcast_add_fusion
  10.1 0.1 add.138
  10.2 0.7 select_reduce_fusion.4
  10.9 0.0 collective-permute-done
  10.9 0.8 %fusion.52 = (s32[1024,1]{0,1:T(1,128)S(1)}, s32[1024,1]{0,1:T(1,128)S(1)}) fusion(s32[1024,2]{0,1:T(2,128)} %param.13), kind=kLoop, calls=%fused_computation.105 | loop fusion | bytes 16384 | tf_op jit(solution)/shard_map/slice | solution.py:190
  11.7 1.1 %broadcast_in_dim.170 = bf16[8,2,32,1,2,512]{5,2,1,4,3,0:T(8,128)(2,1)} broadcast(bf16[2,32,2,512]{3,1,0,2:T(8,128)(2,1)S(1)} %copy.28), dimensions={1,2,4,5} | broadcast | bytes 1179648 | tf_op jit(solution)/shard_map/broadcast_in_dim | solution.py:147
  12.8 4.7 %all-to-all-start = ((bf16[8,2,32,1,2,512]{5,2,1,4,3,0:T(8,128)(2,1)}), bf16[8,2,32,1,2,512]{5,2,1,4,3,0:T(8,128)(2,1)S(1)}, u32[]{:S(2)}, u32[]{:S(2)}) async-start(bf16[8,2,32,1,2,512]{5,2,1,4,3,0:T(8,128)(2,1)} %broadcast_in_dim.170), calls=%async_computation | async-start | bytes 2097152 | tf_op jit(solution)/shard_map/all_to_all | solution.py:146
  17.6 0.0 copy-done.6
  17.6 1.7 %select_reduce_fusion.3 = (f32[1024]{0:T(1024)S(1)}, f32[1024]{0:T(1024)S(1)}, f32[1024]{0:T(1024)S(1)}, f32[1024]{0:T(1024)S(1)}) fusion(f32[512]{0:T(512)S(1)} %bitcast.156, s32[1024]{0:T(1024)S(1)} %bitcast.152, f32[512]{0:T(512)S(1)} %bitcast.155, s32[1024]{0:T(1024)S(1)} %bitcast.151), kind=kLoop, calls=%fused_computation.33 | loop fusion | flops 5238784 | bytes 28672 | tf_op jit(solution)/shard_map/reduce_sum | solution.py:39
  19.3 0.2 fusion.38
  19.5 2.0 %fusion.22 = (f32[128,1024]{1,0:T(8,128)S(1)}, f32[128,1024]{1,0:T(8,128)S(1)}) fusion(f32[128]{0:T(128)S(1)} %iota_convert_fusion.1, f32[1024]{0:T(1024)S(1)} %get-tuple-element.69, s32[1024]{0:T(1024)S(1)} %get-tuple-element.46), kind=kLoop, calls=%fused_computation.37 | loop fusion | flops 1048576 | bytes 1057280 | tf_op jit(solution)/shard_map/sin | solution.py:57
  21.6 0.2 broadcast_in_dim.155
  21.8 0.2 broadcast_in_dim.150
  22.1 1.2 %fusion.1 = (bf16[2,512,1024]{2,1,0:T(8,128)(2,1)S(1)}, bf16[2,512,1024]{2,1,0:T(8,128)(2,1)S(1)}) fusion(f32[512,1024]{1,0:T(8,128)S(1)} %bitcast.137, f32[2,4,1024]{2,1,0:T(4,128)S(1)} %broadcast_in_dim.153, f32[512,1024]{1,0:T(8,128)S(1)} %bitcast.138, f32[2,4,1024]{2,1,0:T(4,128)S(1)} %broadcast_in_dim.148), kind=kLoop, calls=%fused_computation.9 | loop fusion | flops 8388608 | bytes 8454144 | tf_op jit(solution)/shard_map/convert
  23.3 2.3 %pad_maximum_fusion.ccos_ref.csin_ref = bf16[2,512,2048]{2,1,0:T(8,128)(2,1)} fusion(bf16[2,512,1024]{2,1,0:T(8,128)(2,1)S(1)} %get-tuple-element.45, bf16[2,512,1024]{2,1,0:T(8,128)(2,1)S(1)} %get-tuple-element.44), kind=kLoop, calls=%fused_computation.22 | loop fusion | flops 8388608 | bytes 8388608 | tf_op jit(solution)/shard_map/concatenate | solution.py:225
  25.7 1.8 %fusion.33 = (f32[32,1024]{1,0:T(8,128)}, f32[32,1024]{1,0:T(8,128)}, f32[32,1024]{1,0:T(8,128)}, f32[32,1024]{1,0:T(8,128)}) fusion(f32[32]{0:T(128)S(1)} %iota_convert_fusion, f32[1024]{0:T(1024)S(1)} %get-tuple-element.68, s32[1024]{0:T(1024)S(1)} %get-tuple-element.40, f32[32]{0:T(128)S(1)} %convert_element_type.120, s32[32]{0:T(128)S(1)} %add.138), kind=kLoop, calls=%fused_computation.53 | loop fusion | flops 524288 | bytes 532864 | tf_op jit(solution)/shard_map/sin | solution.py:57
  27.5 4.5 %all-to-all-done = bf16[8,2,32,1,2,512]{5,2,1,4,3,0:T(8,128)(2,1)S(1)} async-done(((bf16[8,2,32,1,2,512]{5,2,1,4,3,0:T(8,128)(2,1)}), bf16[8,2,32,1,2,512]{5,2,1,4,3,0:T(8,128)(2,1)S(1)}, u32[]{:S(2)}, u32[]{:S(2)}) %all-to-all-start) | async-done | bytes 1048608 | tf_op jit(solution)/shard_map/all_to_all | solution.py:146
  32.0 1.0 %copy.29 = bf16[8,2,32,1,2,512]{5,2,1,0,4,3:T(8,128)(2,1)} copy(bf16[8,2,32,1,2,512]{5,2,1,4,3,0:T(8,128)(2,1)S(1)} %all-to-all-done) | data formatting | bytes 2097152 | tf_op jit(solution)/shard_map/all_to_all | solution.py:146
  33.0 0.0 copy-start.7
  33.0 0.0 copy-start.4
  33.0 0.0 copy-start.3
  33.0 6.6 %shard_map.104 = (f32[2,1,1024]{2,1,0:T(1,128)}, f32[2,1,1024]{2,1,0:T(1,128)}) custom-call(bf16[2,512,512]{2,1,0:T(8,128)(2,1)} %bitcast.139, bf16[2,512,2048]{2,1,0:T(8,128)(2,1)} %pad_maximum_fusion.ccos_ref.csin_ref, bf16[2,512,2048]{2,1,0:T(8,128)(2,1)} %pad_maximum_fusion.ccos_ref.csin_ref, f32[2,16,1024]{2,1,0:T(8,128)} %bitcast.140, ...), custom_call_target="tpu_custom_call" | custom-call | tf_op jit(solution)/shard_map/pallas_call | solution.py:114
  39.6 0.0 copy-start.1
  39.6 0.0 copy-start.2
  39.6 0.8 %reduce_sum.77 = f32[1024]{0:T(1024)S(1)} reduce(f32[2,1,1024]{2,1,0:T(1,128)} %get-tuple-element.26, f32[]{:T(128)} %constant.100.clone.1), dimensions={0,1}, to_apply=%region_5.6 | reduce | flops 1024 | bytes 12292 | tf_op jit(solution)/shard_map/reduce_sum | solution.py:132
  40.4 0.7 reduce_sum.78
  41.1 0.0 copy-done.7
  41.1 0.0 copy-done.4
  41.1 0.2 broadcast_in_dim.165
  41.4 0.0 copy-done.3
  41.4 0.2 broadcast_in_dim.160
  41.6 0.0 copy-done.1
  41.6 0.0 copy-done.2
  41.7 1.5 %fusion.18 = bf16[2,512,1024]{2,1,0:T(8,128)(2,1)S(1)} fusion(f32[1024]{0:T(1024)S(1)} %get-tuple-element.57, f32[1024]{0:T(1024)S(1)} %get-tuple-element.56, f32[512,1024]{1,0:T(8,128)S(1)} %bitcast.133, f32[2,16,1024]{2,1,0:T(8,128)S(1)} %bitcast.144, f32[512,1024]{1,0:T(8,128)S(1)} %bitcast.135, f32[2,16,1024]{2,1,0:T(8,128)S(1)} %bitcast.141), kind=kLoop, calls=%fused_computation.27 | loop fusion | flops 11534336 | bytes 6561792 | tf_op jit(solution)/shard_map/neg | solution.py:237
  43.1 0.0 copy-start
  43.2 1.3 %fusion.9 = bf16[2,512,1024]{2,1,0:T(8,128)(2,1)S(1)} fusion(f32[1024]{0:T(1024)S(1)} %get-tuple-element.57, f32[1024]{0:T(1024)S(1)} %get-tuple-element.56, f32[512,1024]{1,0:T(8,128)S(1)} %bitcast.134, f32[2,16,1024]{2,1,0:T(8,128)S(1)} %bitcast.145, f32[512,1024]{1,0:T(8,128)S(1)} %bitcast.136, f32[2,16,1024]{2,1,0:T(8,128)S(1)} %bitcast.142), kind=kLoop, calls=%fused_computation.17 | loop fusion | flops 10485760 | bytes 6561792 | tf_op jit(solution)/shard_map/convert_element_type | solution.py:231
  44.5 0.8 %copy-done = bf16[2,512,2048]{2,1,0:T(8,128)(2,1)S(1)} copy-done((bf16[2,512,2048]{2,1,0:T(8,128)(2,1)S(1)}, bf16[2,512,2048]{2,1,0:T(8,128)(2,1)}, u32[]{:S(2)}) %copy-start) | copy-done | bytes 4194328
  45.3 2.4 %fusion.19 = bf16[2,512,512]{1,2,0:T(8,128)(2,1)S(1)} fusion(bf16[2,512,2048]{2,1,0:T(8,128)(2,1)S(1)} %copy-done, bf16[2,512,1024]{2,1,0:T(8,128)(2,1)S(1)} %fusion.18, bf16[2,512,1024]{2,1,0:T(8,128)(2,1)S(1)} %fusion.9), kind=kOutput, calls=%fused_computation.35 | convolution fusion | flops 2156396544 | bytes 9437184 | tf_op jit(solution)/shard_map/fik,fjk->ifj/dot_general | solution.py:238
  47.7 0.0 copy-start.5
  47.7 1.1 %copy.30 = bf16[8,2,32,1,2,512]{5,2,1,4,3,0:T(8,128)(2,1)} copy(bf16[8,2,32,1,2,512]{5,2,1,0,4,3:T(8,128)(2,1)S(1)} %bitcast.146) | data formatting | bytes 2097152 | tf_op jit(solution)/shard_map/reshape | solution.py:155
  48.8 3.6 %all-to-all-start.1 = ((bf16[8,2,32,1,2,512]{5,2,1,4,3,0:T(8,128)(2,1)}), bf16[8,2,32,1,2,512]{5,2,1,4,3,0:T(8,128)(2,1)S(1)}, u32[]{:S(2)}, u32[]{:S(2)}) async-start(bf16[8,2,32,1,2,512]{5,2,1,4,3,0:T(8,128)(2,1)} %copy.30), calls=%async_computation.1 | async-start | bytes 2097152 | tf_op jit(solution)/shard_map/all_to_all | solution.py:157
  52.3 1.3 %collective-permute-start.3 = (bf16[32,1,2,512]{3,0,2,1:T(8,128)(2,1)S(1)}, bf16[32,1,2,512]{3,0,2,1:T(8,128)(2,1)S(1)}, u32[]{:S(2)}, u32[]{:S(2)}) collective-permute-start(bf16[32,1,2,512]{3,0,2,1:T(8,128)(2,1)S(1)} %copy.44), channel_id=1, source_target_pairs={{1,0},{3,2},{5,4},{7,6},{9,8},{11,10},{13,12},{15,14},{17,16},{19,... | collective-permute-start | bytes 196616 | tf_op jit(solution)/shard_map/ppermute | solution.py:30
  53.6 3.0 %collective-permute-start.2 = (bf16[32,1,2,512]{3,0,2,1:T(8,128)(2,1)S(1)}, bf16[32,1,2,512]{3,0,2,1:T(8,128)(2,1)S(1)}, u32[]{:S(2)}, u32[]{:S(2)}) collective-permute-start(bf16[32,1,2,512]{3,0,2,1:T(8,128)(2,1)S(1)} %copy.44), channel_id=1, source_target_pairs={{0,1},{2,3},{4,5},{6,7},{8,9},{10,11},{12,13},{14,15},{16,17},{18,... | collective-permute-start | bytes 196616 | tf_op jit(solution)/shard_map/ppermute | solution.py:28
  56.7 10.1 %all-to-all-done.1 = bf16[8,2,32,1,2,512]{5,2,1,4,3,0:T(8,128)(2,1)S(1)} async-done(((bf16[8,2,32,1,2,512]{5,2,1,4,3,0:T(8,128)(2,1)}), bf16[8,2,32,1,2,512]{5,2,1,4,3,0:T(8,128)(2,1)S(1)}, u32[]{:S(2)}, u32[]{:S(2)}) %all-to-all-start.1) | async-done | bytes 1048608 | tf_op jit(solution)/shard_map/all_to_all | solution.py:157
  66.8 0.1 convert_reduce_fusion
  66.9 1.0 %collective-permute-start.1 = (bf16[32,1,2,512]{3,0,2,1:T(8,128)(2,1)S(1)}, bf16[32,1,2,512]{3,0,2,1:T(8,128)(2,1)S(1)}, u32[]{:S(2)}, u32[]{:S(2)}) collective-permute-start(bf16[32,1,2,512]{3,0,2,1:T(8,128)(2,1)S(1)} %fusion.37), channel_id=1, source_target_pairs={{0,16},{2,18},{4,20},{6,22},{8,24},{10,26},{12,28},{14,30},{16,0},... | collective-permute-start | bytes 196616 | tf_op jit(solution)/shard_map/ppermute | solution.py:136
  67.9 0.6 maximum_bitcast_fusion
  68.5 0.0 collective-permute-done.3
  68.5 0.0 collective-permute-done.2
  68.5 4.7 %collective-permute-done.1 = bf16[32,1,2,512]{3,0,2,1:T(8,128)(2,1)S(1)} collective-permute-done((bf16[32,1,2,512]{3,0,2,1:T(8,128)(2,1)S(1)}, bf16[32,1,2,512]{3,0,2,1:T(8,128)(2,1)S(1)}, u32[]{:S(2)}, u32[]{:S(2)}) %collective-permute-start.1) | collective-permute-done | bytes 65568 | tf_op jit(solution)/shard_map/ppermute | solution.py:136
  73.2 0.0 copy-done.5
  73.2 0.1 fusion.29
  73.3 0.8 %copy.39 = f32[32,1,2,512]{3,2,1,0:T(2,128)} copy(f32[32,1,2,512]{3,0,2,1:T(8,128)S(1)} %fusion.29) | data formatting | bytes 262144
  (16 shorter events, 0.2 us)
Async XLA Ops:
  0.6 16.9 %copy-start.6 = (f32[1024]{0:T(1024)S(1)}, f32[1024]{0:T(1024)}, u32[]{:S(2)}) copy-start(f32[1024]{0:T(1024)} %param.14) | copy-start | bytes 12292
  1.6 9.3 %collective-permute-start = (bf16[32,1,2,512]{3,0,2,1:T(8,128)(2,1)S(1)}, bf16[32,1,2,512]{3,0,2,1:T(8,128)(2,1)S(1)}, u32[]{:S(2)}, u32[]{:S(2)}) collective-permute-start(bf16[32,1,2,512]{3,0,2,1:T(8,128)(2,1)S(1)} %copy.44), channel_id=1, source_target_pairs={{0,16},{2,18},{4,20},{6,22},{8,24},{10,26},{12,28},{14,30},{16,0},... | collective-permute-start | bytes 196616 | tf_op jit(solution)/shard_map/ppermute | solution.py:136
  12.8 19.1 %all-to-all-start = ((bf16[8,2,32,1,2,512]{5,2,1,4,3,0:T(8,128)(2,1)}), bf16[8,2,32,1,2,512]{5,2,1,4,3,0:T(8,128)(2,1)S(1)}, u32[]{:S(2)}, u32[]{:S(2)}) async-start(bf16[8,2,32,1,2,512]{5,2,1,4,3,0:T(8,128)(2,1)} %broadcast_in_dim.170), calls=%async_computation | async-start | bytes 2097152 | tf_op jit(solution)/shard_map/all_to_all | solution.py:146
  33.0 8.1 %copy-start.7 = (f32[1024]{0:T(1024)S(1)}, f32[1024]{0:T(1024)}, u32[]{:S(2)}) copy-start(f32[1024]{0:T(1024)} %param.11) | copy-start | bytes 12292
  33.0 8.1 %copy-start.4 = (f32[32,1024]{1,0:T(8,128)S(1)}, f32[32,1024]{1,0:T(8,128)}, u32[]{:S(2)}) copy-start(f32[32,1024]{1,0:T(8,128)} %get-tuple-element.24.qs_ref) | copy-start | bytes 393220
  33.0 8.4 %copy-start.3 = (f32[32,1024]{1,0:T(8,128)S(1)}, f32[32,1024]{1,0:T(8,128)}, u32[]{:S(2)}) copy-start(f32[32,1024]{1,0:T(8,128)} %get-tuple-element.22.qc_ref) | copy-start | bytes 393220
  39.6 2.0 %copy-start.1 = (f32[32,1024]{1,0:T(8,128)S(1)}, f32[32,1024]{1,0:T(8,128)}, u32[]{:S(2)}) copy-start(f32[32,1024]{1,0:T(8,128)} %get-tuple-element.21) | copy-start | bytes 393220
  39.6 2.0 %copy-start.2 = (f32[32,1024]{1,0:T(8,128)S(1)}, f32[32,1024]{1,0:T(8,128)}, u32[]{:S(2)}) copy-start(f32[32,1024]{1,0:T(8,128)} %get-tuple-element.23) | copy-start | bytes 393220
  43.1 2.2 %copy-start = (bf16[2,512,2048]{2,1,0:T(8,128)(2,1)S(1)}, bf16[2,512,2048]{2,1,0:T(8,128)(2,1)}, u32[]{:S(2)}) copy-start(bf16[2,512,2048]{2,1,0:T(8,128)(2,1)} %pad_maximum_fusion.ccos_ref.csin_ref) | copy-start | bytes 12582916
  47.7 25.5 %copy-start.5 = (f32[32,1,2,512]{3,2,1,0:T(2,128)S(1)}, f32[32,1,2,512]{3,2,1,0:T(2,128)}, u32[]{:S(2)}) copy-start(f32[32,1,2,512]{3,2,1,0:T(2,128)} %param.9) | copy-start | bytes 393220
  48.8 18.0 %all-to-all-start.1 = ((bf16[8,2,32,1,2,512]{5,2,1,4,3,0:T(8,128)(2,1)}), bf16[8,2,32,1,2,512]{5,2,1,4,3,0:T(8,128)(2,1)S(1)}, u32[]{:S(2)}, u32[]{:S(2)}) async-start(bf16[8,2,32,1,2,512]{5,2,1,4,3,0:T(8,128)(2,1)} %copy.30), calls=%async_computation.1 | async-start | bytes 2097152 | tf_op jit(solution)/shard_map/all_to_all | solution.py:157
  52.3 16.2 %collective-permute-start.3 = (bf16[32,1,2,512]{3,0,2,1:T(8,128)(2,1)S(1)}, bf16[32,1,2,512]{3,0,2,1:T(8,128)(2,1)S(1)}, u32[]{:S(2)}, u32[]{:S(2)}) collective-permute-start(bf16[32,1,2,512]{3,0,2,1:T(8,128)(2,1)S(1)} %copy.44), channel_id=1, source_target_pairs={{1,0},{3,2},{5,4},{7,6},{9,8},{11,10},{13,12},{15,14},{17,16},{19,... | collective-permute-start | bytes 196616 | tf_op jit(solution)/shard_map/ppermute | solution.py:30
  53.6 14.9 %collective-permute-start.2 = (bf16[32,1,2,512]{3,0,2,1:T(8,128)(2,1)S(1)}, bf16[32,1,2,512]{3,0,2,1:T(8,128)(2,1)S(1)}, u32[]{:S(2)}, u32[]{:S(2)}) collective-permute-start(bf16[32,1,2,512]{3,0,2,1:T(8,128)(2,1)S(1)} %copy.44), channel_id=1, source_target_pairs={{0,1},{2,3},{4,5},{6,7},{8,9},{10,11},{12,13},{14,15},{16,17},{18,... | collective-permute-start | bytes 196616 | tf_op jit(solution)/shard_map/ppermute | solution.py:28
  66.9 6.3 %collective-permute-start.1 = (bf16[32,1,2,512]{3,0,2,1:T(8,128)(2,1)S(1)}, bf16[32,1,2,512]{3,0,2,1:T(8,128)(2,1)S(1)}, u32[]{:S(2)}, u32[]{:S(2)}) collective-permute-start(bf16[32,1,2,512]{3,0,2,1:T(8,128)(2,1)S(1)} %fusion.37), channel_id=1, source_target_pairs={{0,16},{2,18},{4,20},{6,22},{8,24},{10,26},{12,28},{14,30},{16,0},... | collective-permute-start | bytes 196616 | tf_op jit(solution)/shard_map/ppermute | solution.py:136

commit v9 on v7

--- a/solution.py
+++ b/solution.py
@@ -48,7 +48,7 @@
     return exact + rest[None, :] * pixel.astype(jnp.float32) / image
 
 
-def phase_table(coord, starts, span, image):
+def phase_factors(coord, starts, span, image):
     faces, chunks = starts.shape
     coarse = full_turn * turns(coord, starts.reshape(-1, 1), image)
     fine = full_turn * turns(coord, jnp.arange(span, dtype=jnp.int32)[:, None], image)
@@ -56,19 +56,39 @@
         (jnp.cos(coarse), jnp.sin(coarse), jnp.cos(fine), jnp.sin(fine))
     )
     count = coord.shape[0]
-
-    def spread(a):
-        return jnp.broadcast_to(
-            a.reshape(faces, chunks, 1, count), (faces, chunks, span, count)
-        ).reshape(faces, chunks * span, count)
-
-    def tile(a):
-        return jnp.broadcast_to(a[None, None], (faces, chunks, span, count)).reshape(
-            faces, chunks * span, count
-        )
-
-    pc, ps, qc, qs = spread(coarse_c), spread(coarse_s), tile(fine_c), tile(fine_s)
+    return (
+        coarse_c.reshape(faces, chunks, count),
+        coarse_s.reshape(faces, chunks, count),
+        fine_c,
+        fine_s,
+    )
+
+
+def spread(a, span):
+    faces, chunks, count = a.shape
+    return jnp.broadcast_to(a[:, :, None, :], (faces, chunks, span, count)).reshape(
+        faces, chunks * span, count
+    )
+
+
+def tile(a, faces, chunks):
+    span, count = a.shape
+    return jnp.broadcast_to(a[None, None], (faces, chunks, span, count)).reshape(
+        faces, chunks * span, count
+    )
+
+
+def rotate(factors, fine_c, fine_s):
+    coarse_c, coarse_s = factors[0], factors[1]
+    faces, chunks, _ = coarse_c.shape
+    span = fine_c.shape[0]
+    pc, ps = spread(coarse_c, span), spread(coarse_s, span)
+    qc, qs = tile(fine_c, faces, chunks), tile(fine_s, faces, chunks)
     return (pc * qc - ps * qs, ps * qc + pc * qs)
+
+
+def phase_table(factors):
+    return rotate(factors, factors[2], factors[3])
 
 
 def exchange(x, n_vis, mask):
@@ -157,8 +177,9 @@
     for c in range(ch_local):
         coord_u = spectral_scaling[c] * base_u
         coord_v = spectral_scaling[c] * base_v
-        row_cos, row_sin = phase_table(coord_u, row_starts, rows_dev, image)
-        col_cos, col_sin = phase_table(coord_v, col_starts, LANE_BLOCK, image)
+        row_factors = phase_factors(coord_u, row_starts, rows_dev, image)
+        row_cos, row_sin = phase_table(row_factors)
+        col_cos, col_sin = phase_table(phase_factors(coord_v, col_starts, LANE_BLOCK, image))
         cols = lax.optimization_barrier(
             jnp.concatenate([col_cos, col_sin], axis=2).astype(jnp.bfloat16)
         )
@@ -170,12 +191,12 @@
         sum_im = -jnp.sum(row_cos * wave_s + row_sin * wave_c, axis=(0, 1))
         resid_real = scale_vis * (norm_pred * sum_re - recorded_samples[c, 0])
         resid_imag = scale_vis * (norm_pred * sum_im - recorded_samples[c, 1])
-        z_one = (row_cos * resid_real[None, None, :] - row_sin * resid_imag[None, None, :]).astype(
-            jnp.bfloat16
-        )
-        z_two = (row_sin * resid_real[None, None, :] + row_cos * resid_imag[None, None, :]).astype(
-            jnp.bfloat16
-        )
+        fine_c, fine_s = row_factors[2], row_factors[3]
+        turned_c = fine_c * resid_real[None, :] - fine_s * resid_imag[None, :]
+        turned_s = fine_s * resid_real[None, :] + fine_c * resid_imag[None, :]
+        z_one, z_two = rotate(row_factors, turned_c, turned_s)
+        z_one = z_one.astype(jnp.bfloat16)
+        z_two = z_two.astype(jnp.bfloat16)
         zs = jnp.concatenate([z_one, -z_two], axis=2)
         grad = jnp.einsum("fik,fjk->ifj", zs, cols, preferred_element_type=jnp.float32)
         new_rows.append(grad)

time: 72.2 us -> 72.2 us (level)
  local copies, waits for them, and re-layouts: 9.15 us -> 10.3 us
  other arithmetic: 16.2 us -> 15.1 us
    broadcast_in_dim x4 -> x6, local copies, waits for them, and re-layouts: 0.98 us -> 1.47 us  [tile(): jnp.broadcast_to(a[None, None], (faces, chunks, span, count))]
where the time goes in v9:
time: 72.2 us; the launch traced here: 71.6 us
  waiting for transfers between devices  21.8 us (30%)
  starting transfers between devices  16 us (22%)
  other arithmetic  15.1 us (21%)
  local copies, waits for them, and re-layouts  10.3 us (14%)
  matrix products  6.89 us (10%)
  between operations  1.6 us (2%)
    all_to_all x1, waiting for transfers between devices, reduce_rows(): got = lax.all_to_all(slabs, 'vis', 0, 0, axis_index_groups=groups)  11.8 us
    all_to_all x1, waiting for transfers between devices, gather_rows(): lax.all_to_all(jnp.broadcast_to(pair[None], (half,) + pair.shape), 'vis',...  5.27 us
    ppermute x2, starting transfers between devices, exchange(): return lax.ppermute(x, 'vis', [(i, i ^ mask) for i in range(n_vis)])  5.1 us
    all_to_all x1, starting transfers between devices, gather_rows(): lax.all_to_all(jnp.broadcast_to(pair[None], (half,) + pair.shape), 'vis',...  4.74 us
    ppermute x2, waiting for transfers between devices, exchange(): return lax.ppermute(x, 'vis', [(i, i ^ mask) for i in range(n_vis)])  4.67 us
    dot_general x1, matrix products, local(): jnp.einsum('fij,fjk->fik', sky_rows, cols, preferred_element_type=jnp.flo...  4.54 us
    unnamed x11, local copies, waits for them, and re-layouts  4.02 us
    all_to_all x1, starting transfers between devices, reduce_rows(): got = lax.all_to_all(slabs, 'vis', 0, 0, axis_index_groups=groups)  3.56 us
  transfers between devices with their start and end apart: 6, of which 3 were waited for; matrix products, arithmetic and copies ran while one was open for 20% of the time, Pallas kernels for 0%

profile of v9, /device:TPU:0, one launch (start us, length us, event | category | flops | bytes accessed | tf_op | source)
XLA Modules:
  0.0 71.6 jit_solution(7535896432619090908)
XLA Ops:
  0.6 0.0 copy-start.2
  0.6 0.9 %copy.44 = bf16[32,1,2,512]{3,0,2,1:T(8,128)(2,1)S(1)} copy(f32[32,1,2,512]{3,2,1,0:T(2,128)} %param.9) | data formatting | bytes 196608 | tf_op args[0]
  1.6 4.1 %collective-permute-start = (bf16[32,1,2,512]{3,0,2,1:T(8,128)(2,1)S(1)}, bf16[32,1,2,512]{3,0,2,1:T(8,128)(2,1)S(1)}, u32[]{:S(2)}, u32[]{:S(2)}) collective-permute-start(bf16[32,1,2,512]{3,0,2,1:T(8,128)(2,1)S(1)} %copy.44), channel_id=1, source_target_pairs={{0,16},{2,18},{4,20},{6,22},{8,24},{10,26},{12,28},{14,30},{16,0},... | collective-permute-start | bytes 196616 | tf_op jit(solution)/shard_map/ppermute | solution.py:95
  5.7 0.9 %copy.46 = bf16[32,1,2,512]{3,0,2,1:T(8,128)(2,1)S(1)} copy(f32[32,1,2,512]{3,2,1,0:T(2,128)} %param.9) | data formatting | bytes 196608 | tf_op args[0]
  6.6 0.8 %fusion.58 = (f32[1,512]{1,0:T(1,128)S(1)}, f32[1,512]{1,0:T(1,128)S(1)}) fusion(f32[2,512]{1,0:T(2,128)} %param.16), kind=kLoop, calls=%fused_computation.117 | loop fusion | bytes 8192 | tf_op jit(solution)/shard_map/slice | solution.py:151
  8.1 1.0 %add_reduce_fusion = (s32[2]{0:T(128)S(1)}, s32[2]{0:T(128)S(1)}) fusion(s32[2,2]{1,0:T(2,128)} %param.17), kind=kLoop, calls=%fused_computation.103 | loop fusion | flops 8 | bytes 32 | tf_op jit(solution)/shard_map/sub | solution.py:167
  9.0 0.1 broadcast_add_fusion.1
  9.1 0.1 add.134
  9.2 0.1 broadcast_add_fusion
  9.3 0.1 add.144
  9.4 0.8 %fusion.55 = (f32[1,1,1024]{2,1,0:T(1,128)S(1)}, f32[1,1,1024]{2,1,0:T(1,128)S(1)}) fusion(f32[1,2,1024]{2,1,0:T(2,128)} %param.10), kind=kLoop, calls=%fused_computation.114 | loop fusion | bytes 16384 | tf_op jit(solution)/shard_map/slice | solution.py:192
  10.2 0.7 %select_reduce_fusion.4 = s32[1024]{0:T(1024)S(1)} fusion(s32[4]{0:T(128)} %param.12, s32[1024]{0:T(1024)S(1)} %add_select_fusion), kind=kLoop, calls=%fused_computation.75 | loop fusion | flops 11264 | bytes 8208 | tf_op jit(solution)/shard_map/reduce_sum | solution.py:162
  10.9 0.0 collective-permute-done
  10.9 0.8 %fusion.56 = (s32[1024,1]{0,1:T(1,128)S(1)}, s32[1024,1]{0,1:T(1,128)S(1)}) fusion(s32[1024,2]{0,1:T(2,128)} %param.13), kind=kLoop, calls=%fused_computation.115 | loop fusion | bytes 16384 | tf_op jit(solution)/shard_map/slice | solution.py:149
  11.7 1.1 %broadcast_in_dim.200 = bf16[8,2,32,1,2,512]{5,2,1,4,3,0:T(8,128)(2,1)} broadcast(bf16[2,32,2,512]{3,1,0,2:T(8,128)(2,1)S(1)} %copy.28), dimensions={1,2,4,5} | broadcast | bytes 1179648 | tf_op jit(solution)/shard_map/broadcast_in_dim | solution.py:106
  12.8 4.7 %all-to-all-start = ((bf16[8,2,32,1,2,512]{5,2,1,4,3,0:T(8,128)(2,1)}), bf16[8,2,32,1,2,512]{5,2,1,4,3,0:T(8,128)(2,1)S(1)}, u32[]{:S(2)}, u32[]{:S(2)}) async-start(bf16[8,2,32,1,2,512]{5,2,1,4,3,0:T(8,128)(2,1)} %broadcast_in_dim.200), calls=%async_computation | async-start | bytes 2097152 | tf_op jit(solution)/shard_map/all_to_all | solution.py:105
  17.6 0.0 copy-done.2
  17.6 1.7 %select_reduce_fusion.3 = (f32[1024]{0:T(1024)S(1)}, f32[1024]{0:T(1024)S(1)}, f32[1024]{0:T(1024)S(1)}, f32[1024]{0:T(1024)S(1)}) fusion(f32[512]{0:T(512)S(1)} %bitcast.178, s32[1024]{0:T(1024)S(1)} %bitcast.174, f32[512]{0:T(512)S(1)} %bitcast.177, s32[1024]{0:T(1024)S(1)} %bitcast.173), kind=kLoop, calls=%fused_computation.41 | loop fusion | flops 5238784 | bytes 28672 | tf_op jit(solution)/shard_map/reduce_sum | solution.py:38
  19.3 0.2 fusion.42
  19.5 2.0 %fusion.26 = (f32[128,1024]{1,0:T(8,128)S(1)}, f32[128,1024]{1,0:T(8,128)S(1)}) fusion(f32[128]{0:T(128)S(1)} %iota_convert_fusion.1, f32[1024]{0:T(1024)S(1)} %get-tuple-element.69, s32[1024]{0:T(1024)S(1)} %get-tuple-element.46), kind=kLoop, calls=%fused_computation.45 | loop fusion | flops 1048576 | bytes 1057280 | tf_op jit(solution)/shard_map/sin | solution.py:56
  21.6 0.2 broadcast_in_dim.180
  21.8 0.2 broadcast_in_dim.185
  22.1 1.2 %fusion.1 = (bf16[2,512,1024]{2,1,0:T(8,128)(2,1)S(1)}, bf16[2,512,1024]{2,1,0:T(8,128)(2,1)S(1)}) fusion(f32[512,1024]{1,0:T(8,128)S(1)} %bitcast.158, f32[2,4,1024]{2,1,0:T(4,128)S(1)} %broadcast_in_dim.183, f32[512,1024]{1,0:T(8,128)S(1)} %bitcast.157, f32[2,4,1024]{2,1,0:T(4,128)S(1)} %broadcast_in_dim.178), kind=kLoop, calls=%fused_computation.13 | loop fusion | flops 8388608 | bytes 8454144 | tf_op jit(solution)/shard_map/convert
  23.3 2.3 %pad_maximum_fusion = bf16[2,512,2048]{2,1,0:T(8,128)(2,1)} fusion(bf16[2,512,1024]{2,1,0:T(8,128)(2,1)S(1)} %get-tuple-element.43, bf16[2,512,1024]{2,1,0:T(8,128)(2,1)S(1)} %get-tuple-element.42), kind=kLoop, calls=%fused_computation.30 | loop fusion | flops 8388608 | bytes 8388608 | tf_op jit(solution)/shard_map/concatenate | solution.py:184
  25.6 1.0 %fusion.37 = (f32[32,1024]{1,0:T(8,128)S(1)}, f32[32,1024]{1,0:T(8,128)S(1)}, f32[32,1024]{1,0:T(8,128)S(1)}, f32[32,1024]{1,0:T(8,128)S(1)}) fusion(f32[32]{0:T(128)S(1)} %iota_convert_fusion, f32[1024]{0:T(1024)S(1)} %get-tuple-element.68, s32[1024]{0:T(1024)S(1)} %get-tuple-element.38, f32[32]{0:T(128)S(1)} %convert_element_type.120, s32[32]{0:T(128)S(1)} %add.144), kind=kLoop, calls=%fused_computation.63 | loop fusion | flops 524288 | bytes 532864 | tf_op jit(solution)/shard_map/sin | solution.py:56
  26.7 5.3 %all-to-all-done = bf16[8,2,32,1,2,512]{5,2,1,4,3,0:T(8,128)(2,1)S(1)} async-done(((bf16[8,2,32,1,2,512]{5,2,1,4,3,0:T(8,128)(2,1)}), bf16[8,2,32,1,2,512]{5,2,1,4,3,0:T(8,128)(2,1)S(1)}, u32[]{:S(2)}, u32[]{:S(2)}) %all-to-all-start) | async-done | bytes 1048608 | tf_op jit(solution)/shard_map/all_to_all | solution.py:105
  32.0 0.1 copy.29
  32.1 4.5 %fusion.59 = f32[2,512,2048]{2,1,0:T(8,128)S(1)} fusion(bf16[2,512,512]{2,1,0:T(8,128)(2,1)S(1)} %bitcast.161, bf16[2,512,2048]{2,1,0:T(8,128)(2,1)} %pad_maximum_fusion), kind=kOutput, calls=%fused_computation.118 | convolution fusion | flops 2147483648 | bytes 13631488 | tf_op jit(solution)/shard_map/fij,fjk->fik/dot_general | solution.py:187
  36.6 0.2 broadcast_in_dim.192
  36.9 0.2 broadcast_in_dim.197
  37.1 0.0 copy-start.3
  37.1 2.1 %fusion.13 = (f32[1024]{0:T(1024)S(1)}, f32[1024]{0:T(1024)S(1)}) fusion(f32[2,512,2048]{2,1,0:T(8,128)S(1)} %fusion.59, f32[512,1024]{1,0:T(8,128)S(1)} %bitcast.160, f32[2,16,1024]{2,1,0:T(8,128)S(1)} %bitcast.165, f32[512,1024]{1,0:T(8,128)S(1)} %bitcast.159, f32[2,16,1024]{2,1,0:T(8,128)S(1)} %bitcast.162), kind=kLoop, calls=%fused_computation.25 | loop fusion | flops 14678016 | bytes 12853248 | tf_op jit(solution)/shard_map/reduce_sum | solution.py:190
  39.3 0.0 copy-done.3
  39.4 0.2 broadcast_in_dim.201
  39.6 0.2 broadcast_in_dim.204
  39.9 0.9 %fusion.7 = bf16[2,512,1024]{2,1,0:T(8,128)(2,1)S(1)} fusion(f32[512,1024]{1,0:T(8,128)S(1)} %bitcast.155, f32[512,1024]{1,0:T(8,128)S(1)} %bitcast.153, f32[2,16,1024]{2,1,0:T(8,128)S(1)} %bitcast.166, f32[2,16,1024]{2,1,0:T(8,128)S(1)} %bitcast.163), kind=kLoop, calls=%fused_computation.19 | loop fusion | flops 4194304 | bytes 6553600 | tf_op jit(solution)/shard_map/convert_element_type | solution.py:198
  40.7 0.0 copy-start
  40.7 0.8 %fusion.22 = bf16[2,512,1024]{2,1,0:T(8,128)(2,1)S(1)} fusion(f32[512,1024]{1,0:T(8,128)S(1)} %bitcast.156, f32[512,1024]{1,0:T(8,128)S(1)} %bitcast.154, f32[2,16,1024]{2,1,0:T(8,128)S(1)} %bitcast.167, f32[2,16,1024]{2,1,0:T(8,128)S(1)} %bitcast.164), kind=kLoop, calls=%fused_computation.35 | loop fusion | flops 5242880 | bytes 6553600 | tf_op jit(solution)/shard_map/neg | solution.py:200
  41.5 1.4 %copy-done = bf16[2,512,2048]{2,1,0:T(8,128)(2,1)S(1)} copy-done((bf16[2,512,2048]{2,1,0:T(8,128)(2,1)S(1)}, bf16[2,512,2048]{2,1,0:T(8,128)(2,1)}, u32[]{:S(2)}) %copy-start) | copy-done | bytes 4194328
  42.9 2.4 %fusion.23 = bf16[2,512,512]{1,2,0:T(8,128)(2,1)S(1)} fusion(bf16[2,512,2048]{2,1,0:T(8,128)(2,1)S(1)} %copy-done, bf16[2,512,1024]{2,1,0:T(8,128)(2,1)S(1)} %fusion.22, bf16[2,512,1024]{2,1,0:T(8,128)(2,1)S(1)} %fusion.7), kind=kOutput, calls=%fused_computation.43 | convolution fusion | flops 2156396544 | bytes 9437184 | tf_op jit(solution)/shard_map/fik,fjk->ifj/dot_general | solution.py:201
  45.3 0.0 copy-start.1
  45.3 1.1 %copy.30 = bf16[8,2,32,1,2,512]{5,2,1,4,3,0:T(8,128)(2,1)} copy(bf16[8,2,32,1,2,512]{5,2,1,0,4,3:T(8,128)(2,1)S(1)} %bitcast.168) | data formatting | bytes 2097152 | tf_op jit(solution)/shard_map/reshape | solution.py:114
  46.3 3.6 %all-to-all-start.1 = ((bf16[8,2,32,1,2,512]{5,2,1,4,3,0:T(8,128)(2,1)}), bf16[8,2,32,1,2,512]{5,2,1,4,3,0:T(8,128)(2,1)S(1)}, u32[]{:S(2)}, u32[]{:S(2)}) async-start(bf16[8,2,32,1,2,512]{5,2,1,4,3,0:T(8,128)(2,1)} %copy.30), calls=%async_computation.1 | async-start | bytes 2097152 | tf_op jit(solution)/shard_map/all_to_all | solution.py:116
  49.9 1.3 %collective-permute-start.2 = (bf16[32,1,2,512]{3,0,2,1:T(8,128)(2,1)S(1)}, bf16[32,1,2,512]{3,0,2,1:T(8,128)(2,1)S(1)}, u32[]{:S(2)}, u32[]{:S(2)}) collective-permute-start(bf16[32,1,2,512]{3,0,2,1:T(8,128)(2,1)S(1)} %copy.44), channel_id=1, source_target_pairs={{0,1},{2,3},{4,5},{6,7},{8,9},{10,11},{12,13},{14,15},{16,17},{18,... | collective-permute-start | bytes 196616 | tf_op jit(solution)/shard_map/ppermute | solution.py:27
  51.2 1.3 %collective-permute-start.3 = (bf16[32,1,2,512]{3,0,2,1:T(8,128)(2,1)S(1)}, bf16[32,1,2,512]{3,0,2,1:T(8,128)(2,1)S(1)}, u32[]{:S(2)}, u32[]{:S(2)}) collective-permute-start(bf16[32,1,2,512]{3,0,2,1:T(8,128)(2,1)S(1)} %copy.44), channel_id=1, source_target_pairs={{1,0},{3,2},{5,4},{7,6},{9,8},{11,10},{13,12},{15,14},{17,16},{19,... | collective-permute-start | bytes 196616 | tf_op jit(solution)/shard_map/ppermute | solution.py:29
  52.5 11.8 %all-to-all-done.1 = bf16[8,2,32,1,2,512]{5,2,1,4,3,0:T(8,128)(2,1)S(1)} async-done(((bf16[8,2,32,1,2,512]{5,2,1,4,3,0:T(8,128)(2,1)}), bf16[8,2,32,1,2,512]{5,2,1,4,3,0:T(8,128)(2,1)S(1)}, u32[]{:S(2)}, u32[]{:S(2)}) %all-to-all-start.1) | async-done | bytes 1048608 | tf_op jit(solution)/shard_map/all_to_all | solution.py:116
  64.3 0.1 convert_reduce_fusion
  64.5 1.0 %collective-permute-start.1 = (bf16[32,1,2,512]{3,0,2,1:T(8,128)(2,1)S(1)}, bf16[32,1,2,512]{3,0,2,1:T(8,128)(2,1)S(1)}, u32[]{:S(2)}, u32[]{:S(2)}) collective-permute-start(bf16[32,1,2,512]{3,0,2,1:T(8,128)(2,1)S(1)} %fusion.41), channel_id=1, source_target_pairs={{0,16},{2,18},{4,20},{6,22},{8,24},{10,26},{12,28},{14,30},{16,0},... | collective-permute-start | bytes 196616 | tf_op jit(solution)/shard_map/ppermute | solution.py:95
  65.5 0.6 maximum_bitcast_fusion
  66.1 0.0 collective-permute-done.2
  66.1 0.0 collective-permute-done.3
  66.1 4.7 %collective-permute-done.1 = bf16[32,1,2,512]{3,0,2,1:T(8,128)(2,1)S(1)} collective-permute-done((bf16[32,1,2,512]{3,0,2,1:T(8,128)(2,1)S(1)}, bf16[32,1,2,512]{3,0,2,1:T(8,128)(2,1)S(1)}, u32[]{:S(2)}, u32[]{:S(2)}) %collective-permute-start.1) | collective-permute-done | bytes 65568 | tf_op jit(solution)/shard_map/ppermute | solution.py:95
  70.8 0.0 copy-done.1
  70.8 0.1 fusion.33
  70.9 0.8 %copy.39 = f32[32,1,2,512]{3,2,1,0:T(2,128)} copy(f32[32,1,2,512]{3,0,2,1:T(8,128)S(1)} %fusion.33) | data formatting | bytes 262144
  (17 shorter events, 0.2 us)
Async XLA Ops:
  0.6 16.9 %copy-start.2 = (f32[1024]{0:T(1024)S(1)}, f32[1024]{0:T(1024)}, u32[]{:S(2)}) copy-start(f32[1024]{0:T(1024)} %param.14) | copy-start | bytes 12292
  1.6 9.3 %collective-permute-start = (bf16[32,1,2,512]{3,0,2,1:T(8,128)(2,1)S(1)}, bf16[32,1,2,512]{3,0,2,1:T(8,128)(2,1)S(1)}, u32[]{:S(2)}, u32[]{:S(2)}) collective-permute-start(bf16[32,1,2,512]{3,0,2,1:T(8,128)(2,1)S(1)} %copy.44), channel_id=1, source_target_pairs={{0,16},{2,18},{4,20},{6,22},{8,24},{10,26},{12,28},{14,30},{16,0},... | collective-permute-start | bytes 196616 | tf_op jit(solution)/shard_map/ppermute | solution.py:95
  12.8 19.1 %all-to-all-start = ((bf16[8,2,32,1,2,512]{5,2,1,4,3,0:T(8,128)(2,1)}), bf16[8,2,32,1,2,512]{5,2,1,4,3,0:T(8,128)(2,1)S(1)}, u32[]{:S(2)}, u32[]{:S(2)}) async-start(bf16[8,2,32,1,2,512]{5,2,1,4,3,0:T(8,128)(2,1)} %broadcast_in_dim.200), calls=%async_computation | async-start | bytes 2097152 | tf_op jit(solution)/shard_map/all_to_all | solution.py:105
  37.1 2.2 %copy-start.3 = (f32[1024]{0:T(1024)S(1)}, f32[1024]{0:T(1024)}, u32[]{:S(2)}) copy-start(f32[1024]{0:T(1024)} %param.11) | copy-start | bytes 12292
  40.7 2.2 %copy-start = (bf16[2,512,2048]{2,1,0:T(8,128)(2,1)S(1)}, bf16[2,512,2048]{2,1,0:T(8,128)(2,1)}, u32[]{:S(2)}) copy-start(bf16[2,512,2048]{2,1,0:T(8,128)(2,1)} %pad_maximum_fusion) | copy-start | bytes 12582916
  45.3 25.5 %copy-start.1 = (f32[32,1,2,512]{3,2,1,0:T(2,128)S(1)}, f32[32,1,2,512]{3,2,1,0:T(2,128)}, u32[]{:S(2)}) copy-start(f32[32,1,2,512]{3,2,1,0:T(2,128)} %param.9) | copy-start | bytes 393220
  46.3 18.0 %all-to-all-start.1 = ((bf16[8,2,32,1,2,512]{5,2,1,4,3,0:T(8,128)(2,1)}), bf16[8,2,32,1,2,512]{5,2,1,4,3,0:T(8,128)(2,1)S(1)}, u32[]{:S(2)}, u32[]{:S(2)}) async-start(bf16[8,2,32,1,2,512]{5,2,1,4,3,0:T(8,128)(2,1)} %copy.30), calls=%async_computation.1 | async-start | bytes 2097152 | tf_op jit(solution)/shard_map/all_to_all | solution.py:116
  49.9 16.2 %collective-permute-start.2 = (bf16[32,1,2,512]{3,0,2,1:T(8,128)(2,1)S(1)}, bf16[32,1,2,512]{3,0,2,1:T(8,128)(2,1)S(1)}, u32[]{:S(2)}, u32[]{:S(2)}) collective-permute-start(bf16[32,1,2,512]{3,0,2,1:T(8,128)(2,1)S(1)} %copy.44), channel_id=1, source_target_pairs={{0,1},{2,3},{4,5},{6,7},{8,9},{10,11},{12,13},{14,15},{16,17},{18,... | collective-permute-start | bytes 196616 | tf_op jit(solution)/shard_map/ppermute | solution.py:27
  51.2 14.9 %collective-permute-start.3 = (bf16[32,1,2,512]{3,0,2,1:T(8,128)(2,1)S(1)}, bf16[32,1,2,512]{3,0,2,1:T(8,128)(2,1)S(1)}, u32[]{:S(2)}, u32[]{:S(2)}) collective-permute-start(bf16[32,1,2,512]{3,0,2,1:T(8,128)(2,1)S(1)} %copy.44), channel_id=1, source_target_pairs={{1,0},{3,2},{5,4},{7,6},{9,8},{11,10},{13,12},{15,14},{17,16},{19,... | collective-permute-start | bytes 196616 | tf_op jit(solution)/shard_map/ppermute | solution.py:29
  64.5 6.3 %collective-permute-start.1 = (bf16[32,1,2,512]{3,0,2,1:T(8,128)(2,1)S(1)}, bf16[32,1,2,512]{3,0,2,1:T(8,128)(2,1)S(1)}, u32[]{:S(2)}, u32[]{:S(2)}) collective-permute-start(bf16[32,1,2,512]{3,0,2,1:T(8,128)(2,1)S(1)} %fusion.41), channel_id=1, source_target_pairs={{0,16},{2,18},{4,20},{6,22},{8,24},{10,26},{12,28},{14,30},{16,0},... | collective-permute-start | bytes 196616 | tf_op jit(solution)/shard_map/ppermute | solution.py:95

commit v10 on v9

--- a/solution.py
+++ b/solution.py
@@ -180,9 +180,7 @@
         row_factors = phase_factors(coord_u, row_starts, rows_dev, image)
         row_cos, row_sin = phase_table(row_factors)
         col_cos, col_sin = phase_table(phase_factors(coord_v, col_starts, LANE_BLOCK, image))
-        cols = lax.optimization_barrier(
-            jnp.concatenate([col_cos, col_sin], axis=2).astype(jnp.bfloat16)
-        )
+        cols = jnp.concatenate([col_cos, col_sin], axis=2).astype(jnp.bfloat16)
         sky_rows = jnp.transpose(piece[:, c], (1, 0, 2))
         waves = jnp.einsum("fij,fjk->fik", sky_rows, cols, preferred_element_type=jnp.float32)
         wave_c = waves[:, :, :nvis]

time: 72.2 us -> 70.4 us (0.975)
  waiting for transfers between devices: 21.8 us -> 20.7 us
    concatenate x1 -> x0, other arithmetic: 2.32 us -> none  [local(): jnp.concatenate([col_cos, col_sin], axis=2).astype(jnp.bfloat16)]
    another operation x1, other arithmetic: 1.22 us -> 2.67 us
    broadcast_in_dim x2, local copies, waits for them, and re-layouts: 0.03 us -> 1.23 us  [spread(): jnp.broadcast_to(a[:, :, None, :], (faces, chunks, span, count))]
    all_to_all x1, waiting for transfers between devices: 5.27 us -> 4.19 us  [gather_rows(): lax.all_to_all(jnp.broadcast_to(pair[None], (half,) + pair.shape), 'vis',...]
    slice x1, local copies, waits for them, and re-layouts: 0.78 us -> 0.01 us  [local(): receiver_pairs[:, 1]]
    unnamed x11 -> x23, local copies, waits for them, and re-layouts: 4.02 us -> 3.45 us
  transfers between devices with their start and end apart: 6 -> 6, of which waited for: 3 -> 3; matrix products, arithmetic and copies ran while one was open for 20% -> 22% of each run, Pallas kernels for 0% -> 0%
where the time goes in v10:
time: 70.4 us; the launch traced here: 69.9 us
  waiting for transfers between devices  20.7 us (29%)
  starting transfers between devices  16 us (23%)
  other arithmetic  14.7 us (21%)
  local copies, waits for them, and re-layouts  10.2 us (14%)
  matrix products  6.72 us (10%)
  between operations  1.66 us (2%)
    all_to_all x1, waiting for transfers between devices, reduce_rows(): got = lax.all_to_all(slabs, 'vis', 0, 0, axis_index_groups=groups)  11.8 us
    ppermute x2, starting transfers between devices, exchange(): return lax.ppermute(x, 'vis', [(i, i ^ mask) for i in range(n_vis)])  5.1 us
    all_to_all x1, starting transfers between devices, gather_rows(): lax.all_to_all(jnp.broadcast_to(pair[None], (half,) + pair.shape), 'vis',...  4.74 us
    ppermute x2, waiting for transfers between devices, exchange(): return lax.ppermute(x, 'vis', [(i, i ^ mask) for i in range(n_vis)])  4.66 us
    all_to_all x1, waiting for transfers between devices, gather_rows(): lax.all_to_all(jnp.broadcast_to(pair[None], (half,) + pair.shape), 'vis',...  4.19 us
    dot_general x1, matrix products, local(): jnp.einsum('fij,fjk->fik', sky_rows, cols, preferred_element_type=jnp.flo...  4.05 us
    sin x2, other arithmetic, phase_factors(): jnp.sin(fine)  3.79 us
    all_to_all x1, starting transfers between devices, reduce_rows(): got = lax.all_to_all(slabs, 'vis', 0, 0, axis_index_groups=groups)  3.56 us
  transfers between devices with their start and end apart: 6, of which 3 were waited for; matrix products, arithmetic and copies ran while one was open for 22% of the time, Pallas kernels for 0%

profile of v10, /device:TPU:0, one launch (start us, length us, event | category | flops | bytes accessed | tf_op | source)
XLA Modules:
  0.0 69.9 jit_solution(3338773896750662189)
XLA Ops:
  0.6 0.0 copy-start.7
  0.6 0.0 copy-start.8
  0.6 0.9 %copy.44 = bf16[32,1,2,512]{3,0,2,1:T(8,128)(2,1)S(1)} copy(f32[32,1,2,512]{3,2,1,0:T(2,128)} %param.9) | data formatting | bytes 196608 | tf_op args[0]
  1.6 0.0 copy-start.3
  1.6 4.1 %collective-permute-start = (bf16[32,1,2,512]{3,0,2,1:T(8,128)(2,1)S(1)}, bf16[32,1,2,512]{3,0,2,1:T(8,128)(2,1)S(1)}, u32[]{:S(2)}, u32[]{:S(2)}) collective-permute-start(bf16[32,1,2,512]{3,0,2,1:T(8,128)(2,1)S(1)} %copy.44), channel_id=1, source_target_pairs={{0,16},{2,18},{4,20},{6,22},{8,24},{10,26},{12,28},{14,30},{16,0},... | collective-permute-start | bytes 196616 | tf_op jit(solution)/shard_map/ppermute | solution.py:95
  5.7 0.9 %copy.46 = bf16[32,1,2,512]{3,0,2,1:T(8,128)(2,1)S(1)} copy(f32[32,1,2,512]{3,2,1,0:T(2,128)} %param.9) | data formatting | bytes 196608 | tf_op args[0]
  6.7 0.8 %fusion.60 = (f32[1,512]{1,0:T(1,128)S(1)}, f32[1,512]{1,0:T(1,128)S(1)}) fusion(f32[2,512]{1,0:T(2,128)} %param.16), kind=kLoop, calls=%fused_computation.119 | loop fusion | bytes 8192 | tf_op jit(solution)/shard_map/slice | solution.py:151
  8.1 1.0 %add_reduce_fusion.1 = (s32[2]{0:T(128)S(1)}, s32[2]{0:T(128)S(1)}) fusion(s32[2,2]{1,0:T(2,128)} %param.17), kind=kLoop, calls=%fused_computation.105 | loop fusion | flops 8 | bytes 32 | tf_op jit(solution)/shard_map/sub | solution.py:168
  9.1 0.1 broadcast_add_fusion.1
  9.1 0.1 add.134
  9.2 0.1 broadcast_add_fusion
  9.3 0.1 add.144
  9.4 0.8 %fusion.57 = (f32[1,1,1024]{2,1,0:T(1,128)S(1)}, f32[1,1,1024]{2,1,0:T(1,128)S(1)}) fusion(f32[1,2,1024]{2,1,0:T(2,128)} %param.10), kind=kLoop, calls=%fused_computation.116 | loop fusion | bytes 16384 | tf_op jit(solution)/shard_map/slice | solution.py:190
  10.2 0.7 %select_reduce_fusion.4 = s32[1024]{0:T(1024)S(1)} fusion(s32[4]{0:T(128)} %param.12, s32[1024]{0:T(1024)S(1)} %add_select_fusion), kind=kLoop, calls=%fused_computation.76 | loop fusion | flops 11264 | bytes 8208 | tf_op jit(solution)/shard_map/reduce_sum | solution.py:162
  10.9 0.0 collective-permute-done
  11.0 1.1 %broadcast_in_dim.200 = bf16[8,2,32,1,2,512]{5,2,1,4,3,0:T(8,128)(2,1)} broadcast(bf16[2,32,2,512]{3,1,0,2:T(8,128)(2,1)S(1)} %copy.28), dimensions={1,2,4,5} | broadcast | bytes 1179648 | tf_op jit(solution)/shard_map/broadcast_in_dim | solution.py:106
  12.1 4.7 %all-to-all-start = ((bf16[8,2,32,1,2,512]{5,2,1,4,3,0:T(8,128)(2,1)}), bf16[8,2,32,1,2,512]{5,2,1,4,3,0:T(8,128)(2,1)S(1)}, u32[]{:S(2)}, u32[]{:S(2)}) async-start(bf16[8,2,32,1,2,512]{5,2,1,4,3,0:T(8,128)(2,1)} %broadcast_in_dim.200), calls=%async_computation | async-start | bytes 2097152 | tf_op jit(solution)/shard_map/all_to_all | solution.py:105
  16.8 0.0 copy-done.8
  16.9 0.0 copy-done.7
  16.9 1.7 %select_reduce_fusion.3 = (f32[1024]{0:T(1024)S(1)}, f32[1024]{0:T(1024)S(1)}, f32[1024]{0:T(1024)S(1)}, f32[1024]{0:T(1024)S(1)}) fusion(f32[512]{0:T(512)S(1)} %bitcast.176, s32[1024]{0:T(1024)S(1)} %bitcast.172, f32[512]{0:T(512)S(1)} %bitcast.175, s32[1024]{0:T(1024)S(1)} %bitcast.171), kind=kLoop, calls=%fused_computation.42 | loop fusion | flops 5238784 | bytes 28672 | tf_op jit(solution)/shard_map/reduce_sum | solution.py:38
  18.6 0.0 copy-done.3
  18.6 0.2 fusion.43
  18.8 2.0 %fusion.27 = (f32[128,1024]{1,0:T(8,128)S(1)}, f32[128,1024]{1,0:T(8,128)S(1)}) fusion(f32[128]{0:T(128)S(1)} %iota_convert_fusion.1, f32[1024]{0:T(1024)S(1)} %get-tuple-element.69, s32[1024]{0:T(1024)S(1)} %get-tuple-element.38), kind=kLoop, calls=%fused_computation.46 | loop fusion | flops 1048576 | bytes 1057280 | tf_op jit(solution)/shard_map/sin | solution.py:56
  20.8 0.6 broadcast_in_dim.178
  21.5 0.6 broadcast_in_dim.183
  22.1 1.8 %fusion.38 = (f32[32,1024]{1,0:T(8,128)S(1)}, f32[32,1024]{1,0:T(8,128)}, f32[32,1024]{1,0:T(8,128)S(1)}, f32[32,1024]{1,0:T(8,128)S(1)}) fusion(f32[32]{0:T(128)S(1)} %iota_convert_fusion, f32[1024]{0:T(1024)S(1)} %get-tuple-element.68, s32[1024]{0:T(1024)S(1)} %get-tuple-element.46, f32[32]{0:T(128)S(1)} %convert_element_type.120, s32[32]{0:T(128)S(1)} %add.144), kind=kLoop, calls=%fused_computation.64 | loop fusion | flops 524288 | bytes 532864 | tf_op jit(solution)/shard_map/sin | solution.py:56
  23.9 0.2 broadcast_in_dim.180
  24.1 0.2 broadcast_in_dim.185
  24.4 0.0 copy-done.5
  24.4 0.0 copy-done.6
  24.4 2.7 %fusion.1 = (bf16[2,512,1024]{2,1,0:T(8,128)(2,1)S(1)}, bf16[2,512,1024]{2,1,0:T(8,128)(2,1)}) fusion(f32[512,1024]{1,0:T(8,128)S(1)} %bitcast.156, f32[2,4,1024]{2,1,0:T(4,128)S(1)} %copy-done.6, f32[512,1024]{1,0:T(8,128)S(1)} %bitcast.155, f32[2,4,1024]{2,1,0:T(4,128)S(1)} %copy-done.5), kind=kLoop, calls=%fused_computation.13 | loop fusion | flops 8388608 | bytes 8454144 | tf_op jit(solution)/shard_map/convert
  27.0 4.2 %all-to-all-done = bf16[8,2,32,1,2,512]{5,2,1,4,3,0:T(8,128)(2,1)S(1)} async-done(((bf16[8,2,32,1,2,512]{5,2,1,4,3,0:T(8,128)(2,1)}), bf16[8,2,32,1,2,512]{5,2,1,4,3,0:T(8,128)(2,1)S(1)}, u32[]{:S(2)}, u32[]{:S(2)}) %all-to-all-start) | async-done | bytes 1048608 | tf_op jit(solution)/shard_map/all_to_all | solution.py:105
  31.2 0.1 copy.29
  31.3 0.0 copy-start.1
  31.3 4.0 %fusion.22 = f32[2,512,2048]{2,1,0:T(8,128)S(1)} fusion(bf16[2,512,512]{2,1,0:T(8,128)(2,1)S(1)} %bitcast.159, bf16[2,512,1024]{2,1,0:T(8,128)(2,1)} %get-tuple-element.43, bf16[2,512,1024]{2,1,0:T(8,128)(2,1)S(1)} %get-tuple-element.42), kind=kOutput, calls=%fused_computation.35 | convolution fusion | flops 2155872256 | bytes 13631488 | tf_op jit(solution)/shard_map/fij,fjk->fik/dot_general | solution.py:185
  35.4 0.0 copy-done.1
  35.4 0.2 broadcast_in_dim.192
  35.6 0.2 broadcast_in_dim.197
  35.9 0.0 copy-start.9
  35.9 2.0 %fusion.13 = (f32[1024]{0:T(1024)S(1)}, f32[1024]{0:T(1024)S(1)}) fusion(f32[2,512,2048]{2,1,0:T(8,128)S(1)} %fusion.22, f32[512,1024]{1,0:T(8,128)S(1)} %bitcast.158, f32[2,16,1024]{2,1,0:T(8,128)S(1)} %bitcast.163, f32[512,1024]{1,0:T(8,128)S(1)} %bitcast.157, f32[2,16,1024]{2,1,0:T(8,128)S(1)} %bitcast.160), kind=kLoop, calls=%fused_computation.25 | loop fusion | flops 14678016 | bytes 12853248 | tf_op jit(solution)/shard_map/reduce_sum | solution.py:188
  37.9 0.0 copy-done.9
  37.9 0.2 broadcast_in_dim.201
  38.2 0.2 broadcast_in_dim.204
  38.4 0.9 %fusion.7 = bf16[2,512,1024]{2,1,0:T(8,128)(2,1)S(1)} fusion(f32[512,1024]{1,0:T(8,128)S(1)} %bitcast.153, f32[512,1024]{1,0:T(8,128)S(1)} %bitcast.151, f32[2,16,1024]{2,1,0:T(8,128)S(1)} %bitcast.164, f32[2,16,1024]{2,1,0:T(8,128)S(1)} %bitcast.161), kind=kLoop, calls=%fused_computation.19 | loop fusion | flops 4194304 | bytes 6553600 | tf_op jit(solution)/shard_map/convert_element_type | solution.py:196
  39.3 0.0 copy-start
  39.3 0.8 %fusion.23 = bf16[2,512,1024]{2,1,0:T(8,128)(2,1)S(1)} fusion(f32[512,1024]{1,0:T(8,128)S(1)} %bitcast.154, f32[512,1024]{1,0:T(8,128)S(1)} %bitcast.152, f32[2,16,1024]{2,1,0:T(8,128)S(1)} %bitcast.165, f32[2,16,1024]{2,1,0:T(8,128)S(1)} %bitcast.162), kind=kLoop, calls=%fused_computation.36 | loop fusion | flops 5242880 | bytes 6553600 | tf_op jit(solution)/shard_map/neg | solution.py:198
  40.1 0.8 %copy-done = bf16[2,512,1024]{2,1,0:T(8,128)(2,1)S(1)} copy-done((bf16[2,512,1024]{2,1,0:T(8,128)(2,1)S(1)}, bf16[2,512,1024]{2,1,0:T(8,128)(2,1)}, u32[]{:S(2)}) %copy-start) | copy-done | bytes 2097176
  40.9 2.7 %fusion.24 = bf16[2,512,512]{1,2,0:T(8,128)(2,1)S(1)} fusion(bf16[2,512,1024]{2,1,0:T(8,128)(2,1)S(1)} %fusion.23, bf16[2,512,1024]{2,1,0:T(8,128)(2,1)S(1)} %fusion.7, bf16[2,512,1024]{2,1,0:T(8,128)(2,1)S(1)} %copy-done, bf16[2,512,1024]{2,1,0:T(8,128)(2,1)S(1)} %get-tuple-element.42), kind=kOutput, calls=%fused_computation.44 | convolution fusion | flops 2164785152 | bytes 9437184 | tf_op jit(solution)/shard_map/fik,fjk->ifj/dot_general | solution.py:199
  43.6 0.0 copy-start.4
  43.6 0.0 copy-start.2
  43.6 1.0 %copy.30 = bf16[8,2,32,1,2,512]{5,2,1,4,3,0:T(8,128)(2,1)} copy(bf16[8,2,32,1,2,512]{5,2,1,0,4,3:T(8,128)(2,1)S(1)} %bitcast.166) | data formatting | bytes 2097152 | tf_op jit(solution)/shard_map/reshape | solution.py:114
  44.6 3.6 %all-to-all-start.1 = ((bf16[8,2,32,1,2,512]{5,2,1,4,3,0:T(8,128)(2,1)}), bf16[8,2,32,1,2,512]{5,2,1,4,3,0:T(8,128)(2,1)S(1)}, u32[]{:S(2)}, u32[]{:S(2)}) async-start(bf16[8,2,32,1,2,512]{5,2,1,4,3,0:T(8,128)(2,1)} %copy.30), calls=%async_computation.1 | async-start | bytes 2097152 | tf_op jit(solution)/shard_map/all_to_all | solution.py:116
  48.2 0.0 copy-done.4
  48.2 1.3 %collective-permute-start.2 = (bf16[32,1,2,512]{3,0,2,1:T(8,128)(2,1)S(1)}, bf16[32,1,2,512]{3,0,2,1:T(8,128)(2,1)S(1)}, u32[]{:S(2)}, u32[]{:S(2)}) collective-permute-start(bf16[32,1,2,512]{3,0,2,1:T(8,128)(2,1)S(1)} %copy-done.4), channel_id=1, source_target_pairs={{0,1},{2,3},{4,5},{6,7},{8,9},{10,11},{12,13},{14,15},{16,17},{18,... | collective-permute-start | bytes 196616 | tf_op jit(solution)/shard_map/ppermute | solution.py:27
  49.5 1.3 %collective-permute-start.3 = (bf16[32,1,2,512]{3,0,2,1:T(8,128)(2,1)S(1)}, bf16[32,1,2,512]{3,0,2,1:T(8,128)(2,1)S(1)}, u32[]{:S(2)}, u32[]{:S(2)}) collective-permute-start(bf16[32,1,2,512]{3,0,2,1:T(8,128)(2,1)S(1)} %copy-done.4), channel_id=1, source_target_pairs={{1,0},{3,2},{5,4},{7,6},{9,8},{11,10},{13,12},{15,14},{17,16},{19,... | collective-permute-start | bytes 196616 | tf_op jit(solution)/shard_map/ppermute | solution.py:29
  50.8 11.8 %all-to-all-done.1 = bf16[8,2,32,1,2,512]{5,2,1,4,3,0:T(8,128)(2,1)S(1)} async-done(((bf16[8,2,32,1,2,512]{5,2,1,4,3,0:T(8,128)(2,1)}), bf16[8,2,32,1,2,512]{5,2,1,4,3,0:T(8,128)(2,1)S(1)}, u32[]{:S(2)}, u32[]{:S(2)}) %all-to-all-start.1) | async-done | bytes 1048608 | tf_op jit(solution)/shard_map/all_to_all | solution.py:116
  62.6 0.1 convert_reduce_fusion
  62.8 1.0 %collective-permute-start.1 = (bf16[32,1,2,512]{3,0,2,1:T(8,128)(2,1)S(1)}, bf16[32,1,2,512]{3,0,2,1:T(8,128)(2,1)S(1)}, u32[]{:S(2)}, u32[]{:S(2)}) collective-permute-start(bf16[32,1,2,512]{3,0,2,1:T(8,128)(2,1)S(1)} %fusion.42), channel_id=1, source_target_pairs={{0,16},{2,18},{4,20},{6,22},{8,24},{10,26},{12,28},{14,30},{16,0},... | collective-permute-start | bytes 196616 | tf_op jit(solution)/shard_map/ppermute | solution.py:95
  63.8 0.6 maximum_bitcast_fusion
  64.4 0.0 collective-permute-done.2
  64.4 0.0 collective-permute-done.3
  64.4 4.7 %collective-permute-done.1 = bf16[32,1,2,512]{3,0,2,1:T(8,128)(2,1)S(1)} collective-permute-done((bf16[32,1,2,512]{3,0,2,1:T(8,128)(2,1)S(1)}, bf16[32,1,2,512]{3,0,2,1:T(8,128)(2,1)S(1)}, u32[]{:S(2)}, u32[]{:S(2)}) %collective-permute-start.1) | collective-permute-done | bytes 65568 | tf_op jit(solution)/shard_map/ppermute | solution.py:95
  69.1 0.1 fusion.34
  69.2 0.8 %copy.39 = f32[32,1,2,512]{3,2,1,0:T(2,128)} copy(f32[32,1,2,512]{3,0,2,1:T(8,128)S(1)} %fusion.34) | data formatting | bytes 262144
  (19 shorter events, 0.2 us)
Async XLA Ops:
  0.6 16.3 %copy-start.7 = (s32[1024,2]{0,1:T(2,128)S(1)}, s32[1024,2]{0,1:T(2,128)}, u32[]{:S(2)}) copy-start(s32[1024,2]{0,1:T(2,128)} %param.13) | copy-start | bytes 24580
  0.6 16.2 %copy-start.8 = (f32[1024]{0:T(1024)S(1)}, f32[1024]{0:T(1024)}, u32[]{:S(2)}) copy-start(f32[1024]{0:T(1024)} %param.14) | copy-start | bytes 12292
  1.6 17.0 %copy-start.3 = (bf16[32,1,2,512]{3,0,2,1:T(8,128)(2,1)}, bf16[32,1,2,512]{3,0,2,1:T(8,128)(2,1)S(1)}, u32[]{:S(2)}) copy-start(bf16[32,1,2,512]{3,0,2,1:T(8,128)(2,1)S(1)} %copy.44) | copy-start | bytes 196612
  1.6 9.3 %collective-permute-start = (bf16[32,1,2,512]{3,0,2,1:T(8,128)(2,1)S(1)}, bf16[32,1,2,512]{3,0,2,1:T(8,128)(2,1)S(1)}, u32[]{:S(2)}, u32[]{:S(2)}) collective-permute-start(bf16[32,1,2,512]{3,0,2,1:T(8,128)(2,1)S(1)} %copy.44), channel_id=1, source_target_pairs={{0,16},{2,18},{4,20},{6,22},{8,24},{10,26},{12,28},{14,30},{16,0},... | collective-permute-start | bytes 196616 | tf_op jit(solution)/shard_map/ppermute | solution.py:95
  12.1 19.1 %all-to-all-start = ((bf16[8,2,32,1,2,512]{5,2,1,4,3,0:T(8,128)(2,1)}), bf16[8,2,32,1,2,512]{5,2,1,4,3,0:T(8,128)(2,1)S(1)}, u32[]{:S(2)}, u32[]{:S(2)}) async-start(bf16[8,2,32,1,2,512]{5,2,1,4,3,0:T(8,128)(2,1)} %broadcast_in_dim.200), calls=%async_computation | async-start | bytes 2097152 | tf_op jit(solution)/shard_map/all_to_all | solution.py:105
  22.1 2.3 %copy-start.5 = (f32[2,4,1024]{2,1,0:T(4,128)S(1)}, f32[2,4,1024]{2,1,0:T(4,128)}, u32[]{:S(2)}) copy-start(f32[2,4,1024]{2,1,0:T(4,128)} %broadcast_in_dim.178) | copy-start | bytes 98308
  22.1 2.3 %copy-start.6 = (f32[2,4,1024]{2,1,0:T(4,128)S(1)}, f32[2,4,1024]{2,1,0:T(4,128)}, u32[]{:S(2)}) copy-start(f32[2,4,1024]{2,1,0:T(4,128)} %broadcast_in_dim.183) | copy-start | bytes 98308
  31.3 4.1 %copy-start.1 = (f32[32,1024]{1,0:T(8,128)S(1)}, f32[32,1024]{1,0:T(8,128)}, u32[]{:S(2)}) copy-start(f32[32,1024]{1,0:T(8,128)} %get-tuple-element.20) | copy-start | bytes 393220
  35.9 2.0 %copy-start.9 = (f32[1024]{0:T(1024)S(1)}, f32[1024]{0:T(1024)}, u32[]{:S(2)}) copy-start(f32[1024]{0:T(1024)} %param.11) | copy-start | bytes 12292
  39.3 1.6 %copy-start = (bf16[2,512,1024]{2,1,0:T(8,128)(2,1)S(1)}, bf16[2,512,1024]{2,1,0:T(8,128)(2,1)}, u32[]{:S(2)}) copy-start(bf16[2,512,1024]{2,1,0:T(8,128)(2,1)} %get-tuple-element.43) | copy-start | bytes 6291460
  43.6 4.6 %copy-start.4 = (bf16[32,1,2,512]{3,0,2,1:T(8,128)(2,1)S(1)}, bf16[32,1,2,512]{3,0,2,1:T(8,128)(2,1)}, u32[]{:S(2)}) copy-start(bf16[32,1,2,512]{3,0,2,1:T(8,128)(2,1)} %copy-done.3) | copy-start | bytes 196612
  43.6 25.5 %copy-start.2 = (f32[32,1,2,512]{3,2,1,0:T(2,128)S(1)}, f32[32,1,2,512]{3,2,1,0:T(2,128)}, u32[]{:S(2)}) copy-start(f32[32,1,2,512]{3,2,1,0:T(2,128)} %param.9) | copy-start | bytes 393220
  44.6 18.0 %all-to-all-start.1 = ((bf16[8,2,32,1,2,512]{5,2,1,4,3,0:T(8,128)(2,1)}), bf16[8,2,32,1,2,512]{5,2,1,4,3,0:T(8,128)(2,1)S(1)}, u32[]{:S(2)}, u32[]{:S(2)}) async-start(bf16[8,2,32,1,2,512]{5,2,1,4,3,0:T(8,128)(2,1)} %copy.30), calls=%async_computation.1 | async-start | bytes 2097152 | tf_op jit(solution)/shard_map/all_to_all | solution.py:116
  48.2 16.2 %collective-permute-start.2 = (bf16[32,1,2,512]{3,0,2,1:T(8,128)(2,1)S(1)}, bf16[32,1,2,512]{3,0,2,1:T(8,128)(2,1)S(1)}, u32[]{:S(2)}, u32[]{:S(2)}) collective-permute-start(bf16[32,1,2,512]{3,0,2,1:T(8,128)(2,1)S(1)} %copy-done.4), channel_id=1, source_target_pairs={{0,1},{2,3},{4,5},{6,7},{8,9},{10,11},{12,13},{14,15},{16,17},{18,... | collective-permute-start | bytes 196616 | tf_op jit(solution)/shard_map/ppermute | solution.py:27
  49.5 14.9 %collective-permute-start.3 = (bf16[32,1,2,512]{3,0,2,1:T(8,128)(2,1)S(1)}, bf16[32,1,2,512]{3,0,2,1:T(8,128)(2,1)S(1)}, u32[]{:S(2)}, u32[]{:S(2)}) collective-permute-start(bf16[32,1,2,512]{3,0,2,1:T(8,128)(2,1)S(1)} %copy-done.4), channel_id=1, source_target_pairs={{1,0},{3,2},{5,4},{7,6},{9,8},{11,10},{13,12},{15,14},{17,16},{19,... | collective-permute-start | bytes 196616 | tf_op jit(solution)/shard_map/ppermute | solution.py:29
  62.8 6.3 %collective-permute-start.1 = (bf16[32,1,2,512]{3,0,2,1:T(8,128)(2,1)S(1)}, bf16[32,1,2,512]{3,0,2,1:T(8,128)(2,1)S(1)}, u32[]{:S(2)}, u32[]{:S(2)}) collective-permute-start(bf16[32,1,2,512]{3,0,2,1:T(8,128)(2,1)S(1)} %fusion.42), channel_id=1, source_target_pairs={{0,16},{2,18},{4,20},{6,22},{8,24},{10,26},{12,28},{14,30},{16,0},... | collective-permute-start | bytes 196616 | tf_op jit(solution)/shard_map/ppermute | solution.py:95

commit v11 on v10

--- a/solution.py
+++ b/solution.py
@@ -100,10 +100,13 @@
     me = lax.axis_index("vis")
     other = exchange(block, n_vis, half)
     other, tied = lax.optimization_barrier((other, tied))
-    pair = jnp.where(me < half, jnp.stack([block, other]), jnp.stack([other, block]))
+    wide = (half, 2) + block.shape
+    mine = jnp.broadcast_to(block[None, None], wide)
+    theirs = jnp.broadcast_to(other[None, None], wide)
+    slot = lax.broadcasted_iota(jnp.int32, wide, 1)
     groups = [list(range(half)), list(range(half, n_vis))]
     full = lax.all_to_all(
-        jnp.broadcast_to(pair[None], (half,) + pair.shape), "vis", 0, 0, axis_index_groups=groups
+        jnp.where((slot == 0) == (me < half), mine, theirs), "vis", 0, 0, axis_index_groups=groups
     )
     return full.reshape((n_vis * block.shape[0],) + block.shape[1:]), tied
 

time: 70.4 us -> 70.5 us (level)
  waiting for transfers between devices: 20.7 us -> 19.2 us
  other arithmetic: 14.7 us -> 15.9 us
    all_to_all x1, waiting for transfers between devices: 4.19 us -> 2.74 us  [gather_rows(): lax.all_to_all(jnp.where((slot == 0) == (me < half), mine, theirs), 'vis'...]
    broadcast_in_dim x1 -> x0, local copies, waits for them, and re-layouts: 1.12 us -> none  [gather_rows(): jnp.broadcast_to(pair[None], (half,) + pair.shape)]
    select_n x1, other arithmetic: 0.02 us -> 1.13 us  [gather_rows(): jnp.where((slot == 0) == (me < half), mine, theirs)]
    slice x1, local copies, waits for them, and re-layouts: 0.01 us -> 0.78 us  [local(): receiver_pairs[:, 1]]
    unnamed x23 -> x19, local copies, waits for them, and re-layouts: 3.45 us -> 3.44 us
  transfers between devices with their start and end apart: 6 -> 6, of which waited for: 3 -> 3; matrix products, arithmetic and copies ran while one was open for 22% -> 24% of each run, Pallas kernels for 0% -> 0%
where the time goes in v11:
time: 70.5 us; the launch traced here: 69.9 us
  waiting for transfers between devices  19.2 us (27%)
  starting transfers between devices  16 us (23%)
  other arithmetic  15.9 us (23%)
  local copies, waits for them, and re-layouts  10.5 us (15%)
  matrix products  6.72 us (10%)
  between operations  1.62 us (2%)
    all_to_all x1, waiting for transfers between devices, reduce_rows(): got = lax.all_to_all(slabs, 'vis', 0, 0, axis_index_groups=groups)  11.8 us
    ppermute x2, starting transfers between devices, exchange(): return lax.ppermute(x, 'vis', [(i, i ^ mask) for i in range(n_vis)])  5.09 us
    all_to_all x1, starting transfers between devices, gather_rows(): lax.all_to_all(jnp.where((slot == 0) == (me < half), mine, theirs), 'vis'...  4.74 us
    ppermute x2, waiting for transfers between devices, exchange(): return lax.ppermute(x, 'vis', [(i, i ^ mask) for i in range(n_vis)])  4.69 us
    dot_general x1, matrix products, local(): jnp.einsum('fij,fjk->fik', sky_rows, cols, preferred_element_type=jnp.flo...  4.05 us
    sin x2, other arithmetic, phase_factors(): jnp.sin(fine)  3.79 us
    all_to_all x1, starting transfers between devices, reduce_rows(): got = lax.all_to_all(slabs, 'vis', 0, 0, axis_index_groups=groups)  3.56 us
    unnamed x19, local copies, waits for them, and re-layouts  3.44 us
  transfers between devices with their start and end apart: 6, of which 3 were waited for; matrix products, arithmetic and copies ran while one was open for 24% of the time, Pallas kernels for 0%

profile of v11, /device:TPU:0, one launch (start us, length us, event | category | flops | bytes accessed | tf_op | source)
XLA Modules:
  0.0 69.9 jit_solution(2273912457544844459)
XLA Ops:
  0.6 0.9 %copy.42 = bf16[32,1,2,512]{3,0,2,1:T(8,128)(2,1)S(1)} copy(f32[32,1,2,512]{3,2,1,0:T(2,128)} %param.9) | data formatting | bytes 196608 | tf_op args[0]
  1.6 0.0 copy-start.3
  1.6 4.1 %collective-permute-start = (bf16[32,1,2,512]{3,0,2,1:T(8,128)(2,1)S(1)}, bf16[32,1,2,512]{3,0,2,1:T(8,128)(2,1)S(1)}, u32[]{:S(2)}, u32[]{:S(2)}) collective-permute-start(bf16[32,1,2,512]{3,0,2,1:T(8,128)(2,1)S(1)} %copy.42), channel_id=1, source_target_pairs={{0,16},{2,18},{4,20},{6,22},{8,24},{10,26},{12,28},{14,30},{16,0},... | collective-permute-start | bytes 196616 | tf_op jit(solution)/shard_map/ppermute | solution.py:95
  5.7 0.9 %copy.44 = bf16[32,1,2,512]{3,0,2,1:T(8,128)(2,1)S(1)} copy(f32[32,1,2,512]{3,2,1,0:T(2,128)} %param.9) | data formatting | bytes 196608 | tf_op args[0]
  6.6 0.8 %fusion.60 = (f32[1,512]{1,0:T(1,128)S(1)}, f32[1,512]{1,0:T(1,128)S(1)}) fusion(f32[2,512]{1,0:T(2,128)} %param.16), kind=kLoop, calls=%fused_computation.120 | loop fusion | bytes 8192 | tf_op jit(solution)/shard_map/slice | solution.py:154
  8.1 1.0 %add_reduce_fusion.1 = (s32[2]{0:T(128)S(1)}, s32[2]{0:T(128)S(1)}) fusion(s32[2,2]{1,0:T(2,128)} %param.17), kind=kLoop, calls=%fused_computation.106 | loop fusion | flops 8 | bytes 32 | tf_op jit(solution)/shard_map/sub | solution.py:171
  9.0 0.1 broadcast_add_fusion.1
  9.1 0.1 add.134
  9.2 0.1 broadcast_add_fusion
  9.3 0.1 add.144
  9.4 0.8 %fusion.57 = (f32[1,1,1024]{2,1,0:T(1,128)S(1)}, f32[1,1,1024]{2,1,0:T(1,128)S(1)}) fusion(f32[1,2,1024]{2,1,0:T(2,128)} %param.10), kind=kLoop, calls=%fused_computation.117 | loop fusion | bytes 16384 | tf_op jit(solution)/shard_map/slice | solution.py:193
  10.2 0.7 %select_reduce_fusion.4 = s32[1024]{0:T(1024)S(1)} fusion(s32[4]{0:T(128)} %param.12, s32[1024]{0:T(1024)S(1)} %add_select_fusion), kind=kLoop, calls=%fused_computation.76 | loop fusion | flops 11264 | bytes 8208 | tf_op jit(solution)/shard_map/reduce_sum | solution.py:165
  10.9 0.0 collective-permute-done
  10.9 1.1 %broadcast_select_fusion = bf16[8,2,32,1,2,512]{5,2,1,4,3,0:T(8,128)(2,1)} fusion(pred[2]{0:T(512)(128)(4,1)S(1)} %compare_compare_fusion, bf16[32,2,512]{2,0,1:T(8,128)(2,1)S(1)} %bitcast.168, bf16[32,2,512]{2,0,1:T(8,128)(2,1)S(1)} %bitcast.167), kind=kLoop, calls=%fused_computation.45 | loop fusion | flops 524288 | bytes 1179650 | tf_op jit(solution)/shard_map/jit(_where)/select_n | solution.py:109
  12.1 4.7 %all-to-all-start = ((bf16[8,2,32,1,2,512]{5,2,1,4,3,0:T(8,128)(2,1)}), bf16[8,2,32,1,2,512]{5,2,1,4,3,0:T(8,128)(2,1)S(1)}, u32[]{:S(2)}, u32[]{:S(2)}) async-start(bf16[8,2,32,1,2,512]{5,2,1,4,3,0:T(8,128)(2,1)} %broadcast_select_fusion), calls=%async_computation | async-start | bytes 2097152 | tf_op jit(solution)/shard_map/all_to_all | solution.py:108
  16.8 0.7 %fusion.59 = (f32[1024]{0:T(1024)S(1)}, f32[1024]{0:T(1024)S(1)}) fusion(f32[1024]{0:T(1024)} %param.14), kind=kLoop, calls=%fused_computation.119 | loop fusion | bytes 12288 | tf_op jit(solution)/shard_map/cos | solution.py:159
  17.5 0.8 %fusion.58 = (s32[1024,1]{0,1:T(1,128)S(1)}, s32[1024,1]{0,1:T(1,128)S(1)}) fusion(s32[1024,2]{0,1:T(2,128)} %param.13), kind=kLoop, calls=%fused_computation.118 | loop fusion | bytes 16384 | tf_op jit(solution)/shard_map/slice | solution.py:152
  18.3 1.7 %select_reduce_fusion.3 = (f32[1024]{0:T(1024)S(1)}, f32[1024]{0:T(1024)S(1)}, f32[1024]{0:T(1024)S(1)}, f32[1024]{0:T(1024)S(1)}) fusion(f32[512]{0:T(512)S(1)} %bitcast.176, s32[1024]{0:T(1024)S(1)} %bitcast.172, f32[512]{0:T(512)S(1)} %bitcast.175, s32[1024]{0:T(1024)S(1)} %bitcast.171), kind=kLoop, calls=%fused_computation.42 | loop fusion | flops 5238784 | bytes 28672 | tf_op jit(solution)/shard_map/reduce_sum | solution.py:38
  20.0 0.0 copy-done.3
  20.0 0.2 fusion.43
  20.2 2.0 %fusion.27 = (f32[128,1024]{1,0:T(8,128)S(1)}, f32[128,1024]{1,0:T(8,128)S(1)}) fusion(f32[128]{0:T(128)S(1)} %iota_convert_fusion.1, f32[1024]{0:T(1024)S(1)} %get-tuple-element.69, s32[1024]{0:T(1024)S(1)} %get-tuple-element.38), kind=kLoop, calls=%fused_computation.47 | loop fusion | flops 1048576 | bytes 1057280 | tf_op jit(solution)/shard_map/sin | solution.py:56
  22.2 0.6 broadcast_in_dim.188
  22.9 0.6 broadcast_in_dim.193
  23.5 0.0 copy-start.5
  23.5 1.8 %fusion.38 = (f32[32,1024]{1,0:T(8,128)S(1)}, f32[32,1024]{1,0:T(8,128)}, f32[32,1024]{1,0:T(8,128)S(1)}, f32[32,1024]{1,0:T(8,128)S(1)}) fusion(f32[32]{0:T(128)S(1)} %iota_convert_fusion, f32[1024]{0:T(1024)S(1)} %get-tuple-element.68, s32[1024]{0:T(1024)S(1)} %get-tuple-element.46, f32[32]{0:T(128)S(1)} %convert_element_type.120, s32[32]{0:T(128)S(1)} %add.144), kind=kLoop, calls=%fused_computation.64 | loop fusion | flops 524288 | bytes 532864 | tf_op jit(solution)/shard_map/sin | solution.py:56
  25.2 0.2 broadcast_in_dim.190
  25.5 0.2 broadcast_in_dim.195
  25.7 0.0 copy-done.5
  25.8 0.0 copy-done.6
  25.8 2.7 %fusion.1 = (bf16[2,512,1024]{2,1,0:T(8,128)(2,1)S(1)}, bf16[2,512,1024]{2,1,0:T(8,128)(2,1)}) fusion(f32[512,1024]{1,0:T(8,128)S(1)} %bitcast.156, f32[2,4,1024]{2,1,0:T(4,128)S(1)} %copy-done.6, f32[512,1024]{1,0:T(8,128)S(1)} %bitcast.155, f32[2,4,1024]{2,1,0:T(4,128)S(1)} %copy-done.5), kind=kLoop, calls=%fused_computation.13 | loop fusion | flops 8388608 | bytes 8454144 | tf_op jit(solution)/shard_map/convert
  28.4 2.7 %all-to-all-done = bf16[8,2,32,1,2,512]{5,2,1,4,3,0:T(8,128)(2,1)S(1)} async-done(((bf16[8,2,32,1,2,512]{5,2,1,4,3,0:T(8,128)(2,1)}), bf16[8,2,32,1,2,512]{5,2,1,4,3,0:T(8,128)(2,1)S(1)}, u32[]{:S(2)}, u32[]{:S(2)}) %all-to-all-start) | async-done | bytes 1048608 | tf_op jit(solution)/shard_map/all_to_all | solution.py:108
  31.2 0.1 copy.27
  31.3 0.0 copy-start.1
  31.3 4.0 %fusion.22 = f32[2,512,2048]{2,1,0:T(8,128)S(1)} fusion(bf16[2,512,512]{2,1,0:T(8,128)(2,1)S(1)} %bitcast.159, bf16[2,512,1024]{2,1,0:T(8,128)(2,1)} %get-tuple-element.43, bf16[2,512,1024]{2,1,0:T(8,128)(2,1)S(1)} %get-tuple-element.42), kind=kOutput, calls=%fused_computation.35 | convolution fusion | flops 2155872256 | bytes 13631488 | tf_op jit(solution)/shard_map/fij,fjk->fik/dot_general | solution.py:188
  35.3 0.0 copy-done.1
  35.3 0.2 broadcast_in_dim.202
  35.6 0.2 broadcast_in_dim.207
  35.8 0.0 copy-start.7
  35.9 2.0 %fusion.13 = (f32[1024]{0:T(1024)S(1)}, f32[1024]{0:T(1024)S(1)}) fusion(f32[2,512,2048]{2,1,0:T(8,128)S(1)} %fusion.22, f32[512,1024]{1,0:T(8,128)S(1)} %bitcast.158, f32[2,16,1024]{2,1,0:T(8,128)S(1)} %bitcast.163, f32[512,1024]{1,0:T(8,128)S(1)} %bitcast.157, f32[2,16,1024]{2,1,0:T(8,128)S(1)} %bitcast.160), kind=kLoop, calls=%fused_computation.25 | loop fusion | flops 14678016 | bytes 12853248 | tf_op jit(solution)/shard_map/reduce_sum | solution.py:191
  37.8 0.0 copy-done.7
  37.9 0.2 broadcast_in_dim.214
  38.1 0.2 broadcast_in_dim.217
  38.4 0.9 %fusion.7 = bf16[2,512,1024]{2,1,0:T(8,128)(2,1)S(1)} fusion(f32[512,1024]{1,0:T(8,128)S(1)} %bitcast.153, f32[512,1024]{1,0:T(8,128)S(1)} %bitcast.151, f32[2,16,1024]{2,1,0:T(8,128)S(1)} %bitcast.164, f32[2,16,1024]{2,1,0:T(8,128)S(1)} %bitcast.161), kind=kLoop, calls=%fused_computation.19 | loop fusion | flops 4194304 | bytes 6553600 | tf_op jit(solution)/shard_map/convert_element_type | solution.py:199
  39.3 0.0 copy-start
  39.3 0.8 %fusion.23 = bf16[2,512,1024]{2,1,0:T(8,128)(2,1)S(1)} fusion(f32[512,1024]{1,0:T(8,128)S(1)} %bitcast.154, f32[512,1024]{1,0:T(8,128)S(1)} %bitcast.152, f32[2,16,1024]{2,1,0:T(8,128)S(1)} %bitcast.165, f32[2,16,1024]{2,1,0:T(8,128)S(1)} %bitcast.162), kind=kLoop, calls=%fused_computation.36 | loop fusion | flops 5242880 | bytes 6553600 | tf_op jit(solution)/shard_map/neg | solution.py:201
  40.1 0.8 %copy-done = bf16[2,512,1024]{2,1,0:T(8,128)(2,1)S(1)} copy-done((bf16[2,512,1024]{2,1,0:T(8,128)(2,1)S(1)}, bf16[2,512,1024]{2,1,0:T(8,128)(2,1)}, u32[]{:S(2)}) %copy-start) | copy-done | bytes 2097176
  40.9 2.7 %fusion.24 = bf16[2,512,512]{1,2,0:T(8,128)(2,1)S(1)} fusion(bf16[2,512,1024]{2,1,0:T(8,128)(2,1)S(1)} %fusion.23, bf16[2,512,1024]{2,1,0:T(8,128)(2,1)S(1)} %fusion.7, bf16[2,512,1024]{2,1,0:T(8,128)(2,1)S(1)} %copy-done, bf16[2,512,1024]{2,1,0:T(8,128)(2,1)S(1)} %get-tuple-element.42), kind=kOutput, calls=%fused_computation.44 | convolution fusion | flops 2164785152 | bytes 9437184 | tf_op jit(solution)/shard_map/fik,fjk->ifj/dot_general | solution.py:202
  43.5 0.0 copy-start.4
  43.5 0.0 copy-start.2
  43.6 1.0 %copy.28 = bf16[8,2,32,1,2,512]{5,2,1,4,3,0:T(8,128)(2,1)} copy(bf16[8,2,32,1,2,512]{5,2,1,0,4,3:T(8,128)(2,1)S(1)} %bitcast.166) | data formatting | bytes 2097152 | tf_op jit(solution)/shard_map/reshape | solution.py:117
  44.6 3.6 %all-to-all-start.1 = ((bf16[8,2,32,1,2,512]{5,2,1,4,3,0:T(8,128)(2,1)}), bf16[8,2,32,1,2,512]{5,2,1,4,3,0:T(8,128)(2,1)S(1)}, u32[]{:S(2)}, u32[]{:S(2)}) async-start(bf16[8,2,32,1,2,512]{5,2,1,4,3,0:T(8,128)(2,1)} %copy.28), calls=%async_computation.1 | async-start | bytes 2097152 | tf_op jit(solution)/shard_map/all_to_all | solution.py:119
  48.2 0.0 copy-done.4
  48.2 1.3 %collective-permute-start.2 = (bf16[32,1,2,512]{3,0,2,1:T(8,128)(2,1)S(1)}, bf16[32,1,2,512]{3,0,2,1:T(8,128)(2,1)S(1)}, u32[]{:S(2)}, u32[]{:S(2)}) collective-permute-start(bf16[32,1,2,512]{3,0,2,1:T(8,128)(2,1)S(1)} %copy-done.4), channel_id=1, source_target_pairs={{0,1},{2,3},{4,5},{6,7},{8,9},{10,11},{12,13},{14,15},{16,17},{18,... | collective-permute-start | bytes 196616 | tf_op jit(solution)/shard_map/ppermute | solution.py:27
  49.5 1.3 %collective-permute-start.3 = (bf16[32,1,2,512]{3,0,2,1:T(8,128)(2,1)S(1)}, bf16[32,1,2,512]{3,0,2,1:T(8,128)(2,1)S(1)}, u32[]{:S(2)}, u32[]{:S(2)}) collective-permute-start(bf16[32,1,2,512]{3,0,2,1:T(8,128)(2,1)S(1)} %copy-done.4), channel_id=1, source_target_pairs={{1,0},{3,2},{5,4},{7,6},{9,8},{11,10},{13,12},{15,14},{17,16},{19,... | collective-permute-start | bytes 196616 | tf_op jit(solution)/shard_map/ppermute | solution.py:29
  50.8 11.8 %all-to-all-done.1 = bf16[8,2,32,1,2,512]{5,2,1,4,3,0:T(8,128)(2,1)S(1)} async-done(((bf16[8,2,32,1,2,512]{5,2,1,4,3,0:T(8,128)(2,1)}), bf16[8,2,32,1,2,512]{5,2,1,4,3,0:T(8,128)(2,1)S(1)}, u32[]{:S(2)}, u32[]{:S(2)}) %all-to-all-start.1) | async-done | bytes 1048608 | tf_op jit(solution)/shard_map/all_to_all | solution.py:119
  62.6 0.1 convert_reduce_fusion
  62.8 1.0 %collective-permute-start.1 = (bf16[32,1,2,512]{3,0,2,1:T(8,128)(2,1)S(1)}, bf16[32,1,2,512]{3,0,2,1:T(8,128)(2,1)S(1)}, u32[]{:S(2)}, u32[]{:S(2)}) collective-permute-start(bf16[32,1,2,512]{3,0,2,1:T(8,128)(2,1)S(1)} %fusion.42), channel_id=1, source_target_pairs={{0,16},{2,18},{4,20},{6,22},{8,24},{10,26},{12,28},{14,30},{16,0},... | collective-permute-start | bytes 196616 | tf_op jit(solution)/shard_map/ppermute | solution.py:95
  63.7 0.6 maximum_bitcast_fusion
  64.4 0.0 collective-permute-done.2
  64.4 0.0 collective-permute-done.3
  64.4 4.7 %collective-permute-done.1 = bf16[32,1,2,512]{3,0,2,1:T(8,128)(2,1)S(1)} collective-permute-done((bf16[32,1,2,512]{3,0,2,1:T(8,128)(2,1)S(1)}, bf16[32,1,2,512]{3,0,2,1:T(8,128)(2,1)S(1)}, u32[]{:S(2)}, u32[]{:S(2)}) %collective-permute-start.1) | collective-permute-done | bytes 65568 | tf_op jit(solution)/shard_map/ppermute | solution.py:95
  69.0 0.0 copy-done.2
  69.0 0.1 fusion.34
  69.1 0.8 %copy.37 = f32[32,1,2,512]{3,2,1,0:T(2,128)} copy(f32[32,1,2,512]{3,0,2,1:T(8,128)S(1)} %fusion.34) | data formatting | bytes 262144
  (14 shorter events, 0.1 us)
Async XLA Ops:
  1.6 18.4 %copy-start.3 = (bf16[32,1,2,512]{3,0,2,1:T(8,128)(2,1)}, bf16[32,1,2,512]{3,0,2,1:T(8,128)(2,1)S(1)}, u32[]{:S(2)}) copy-start(bf16[32,1,2,512]{3,0,2,1:T(8,128)(2,1)S(1)} %copy.42) | copy-start | bytes 196612
  1.6 9.3 %collective-permute-start = (bf16[32,1,2,512]{3,0,2,1:T(8,128)(2,1)S(1)}, bf16[32,1,2,512]{3,0,2,1:T(8,128)(2,1)S(1)}, u32[]{:S(2)}, u32[]{:S(2)}) collective-permute-start(bf16[32,1,2,512]{3,0,2,1:T(8,128)(2,1)S(1)} %copy.42), channel_id=1, source_target_pairs={{0,16},{2,18},{4,20},{6,22},{8,24},{10,26},{12,28},{14,30},{16,0},... | collective-permute-start | bytes 196616 | tf_op jit(solution)/shard_map/ppermute | solution.py:95
  12.1 19.1 %all-to-all-start = ((bf16[8,2,32,1,2,512]{5,2,1,4,3,0:T(8,128)(2,1)}), bf16[8,2,32,1,2,512]{5,2,1,4,3,0:T(8,128)(2,1)S(1)}, u32[]{:S(2)}, u32[]{:S(2)}) async-start(bf16[8,2,32,1,2,512]{5,2,1,4,3,0:T(8,128)(2,1)} %broadcast_select_fusion), calls=%async_computation | async-start | bytes 2097152 | tf_op jit(solution)/shard_map/all_to_all | solution.py:108
  23.5 2.3 %copy-start.5 = (f32[2,4,1024]{2,1,0:T(4,128)S(1)}, f32[2,4,1024]{2,1,0:T(4,128)}, u32[]{:S(2)}) copy-start(f32[2,4,1024]{2,1,0:T(4,128)} %broadcast_in_dim.188) | copy-start | bytes 98308
  23.5 2.3 %copy-start.6 = (f32[2,4,1024]{2,1,0:T(4,128)S(1)}, f32[2,4,1024]{2,1,0:T(4,128)}, u32[]{:S(2)}) copy-start(f32[2,4,1024]{2,1,0:T(4,128)} %broadcast_in_dim.193) | copy-start | bytes 98308
  31.3 4.1 %copy-start.1 = (f32[32,1024]{1,0:T(8,128)S(1)}, f32[32,1024]{1,0:T(8,128)}, u32[]{:S(2)}) copy-start(f32[32,1024]{1,0:T(8,128)} %get-tuple-element.20) | copy-start | bytes 393220
  35.8 2.0 %copy-start.7 = (f32[1024]{0:T(1024)S(1)}, f32[1024]{0:T(1024)}, u32[]{:S(2)}) copy-start(f32[1024]{0:T(1024)} %param.11) | copy-start | bytes 12292
  39.3 1.6 %copy-start = (bf16[2,512,1024]{2,1,0:T(8,128)(2,1)S(1)}, bf16[2,512,1024]{2,1,0:T(8,128)(2,1)}, u32[]{:S(2)}) copy-start(bf16[2,512,1024]{2,1,0:T(8,128)(2,1)} %get-tuple-element.43) | copy-start | bytes 6291460
  43.5 4.6 %copy-start.4 = (bf16[32,1,2,512]{3,0,2,1:T(8,128)(2,1)S(1)}, bf16[32,1,2,512]{3,0,2,1:T(8,128)(2,1)}, u32[]{:S(2)}) copy-start(bf16[32,1,2,512]{3,0,2,1:T(8,128)(2,1)} %copy-done.3) | copy-start | bytes 196612
  43.5 25.5 %copy-start.2 = (f32[32,1,2,512]{3,2,1,0:T(2,128)S(1)}, f32[32,1,2,512]{3,2,1,0:T(2,128)}, u32[]{:S(2)}) copy-start(f32[32,1,2,512]{3,2,1,0:T(2,128)} %param.9) | copy-start | bytes 393220
  44.6 18.0 %all-to-all-start.1 = ((bf16[8,2,32,1,2,512]{5,2,1,4,3,0:T(8,128)(2,1)}), bf16[8,2,32,1,2,512]{5,2,1,4,3,0:T(8,128)(2,1)S(1)}, u32[]{:S(2)}, u32[]{:S(2)}) async-start(bf16[8,2,32,1,2,512]{5,2,1,4,3,0:T(8,128)(2,1)} %copy.28), calls=%async_computation.1 | async-start | bytes 2097152 | tf_op jit(solution)/shard_map/all_to_all | solution.py:119
  48.2 16.2 %collective-permute-start.2 = (bf16[32,1,2,512]{3,0,2,1:T(8,128)(2,1)S(1)}, bf16[32,1,2,512]{3,0,2,1:T(8,128)(2,1)S(1)}, u32[]{:S(2)}, u32[]{:S(2)}) collective-permute-start(bf16[32,1,2,512]{3,0,2,1:T(8,128)(2,1)S(1)} %copy-done.4), channel_id=1, source_target_pairs={{0,1},{2,3},{4,5},{6,7},{8,9},{10,11},{12,13},{14,15},{16,17},{18,... | collective-permute-start | bytes 196616 | tf_op jit(solution)/shard_map/ppermute | solution.py:27
  49.5 14.9 %collective-permute-start.3 = (bf16[32,1,2,512]{3,0,2,1:T(8,128)(2,1)S(1)}, bf16[32,1,2,512]{3,0,2,1:T(8,128)(2,1)S(1)}, u32[]{:S(2)}, u32[]{:S(2)}) collective-permute-start(bf16[32,1,2,512]{3,0,2,1:T(8,128)(2,1)S(1)} %copy-done.4), channel_id=1, source_target_pairs={{1,0},{3,2},{5,4},{7,6},{9,8},{11,10},{13,12},{15,14},{17,16},{19,... | collective-permute-start | bytes 196616 | tf_op jit(solution)/shard_map/ppermute | solution.py:29
  62.8 6.3 %collective-permute-start.1 = (bf16[32,1,2,512]{3,0,2,1:T(8,128)(2,1)S(1)}, bf16[32,1,2,512]{3,0,2,1:T(8,128)(2,1)S(1)}, u32[]{:S(2)}, u32[]{:S(2)}) collective-permute-start(bf16[32,1,2,512]{3,0,2,1:T(8,128)(2,1)S(1)} %fusion.42), channel_id=1, source_target_pairs={{0,16},{2,18},{4,20},{6,22},{8,24},{10,26},{12,28},{14,30},{16,0},... | collective-permute-start | bytes 196616 | tf_op jit(solution)/shard_map/ppermute | solution.py:95

commit v12 on v11

--- a/solution.py
+++ b/solution.py
@@ -143,7 +143,7 @@
     image = GRID * facet
     norm_pred = 1.0 / math.sqrt(facets_here * facet * facet)
     norm_grad = 1.0 / math.sqrt(nvis * n_vis)
-    sky_half = patch_intensity.astype(jnp.bfloat16)
+    sky_half = lax.optimization_barrier(patch_intensity.astype(jnp.bfloat16))
     piece, (receiver_pairs, sample_rotation_phase) = gather_rows(
         sky_half, n_vis, (receiver_pairs, sample_rotation_phase)
     )
@@ -204,7 +204,7 @@
         residuals.append(jnp.stack([resid_real, resid_imag], axis=0))
     partial = jnp.stack(new_rows, axis=1)
     gradient = reduce_rows(partial, n_vis, rows_dev)
-    padded = extended(patch_intensity.astype(jnp.bfloat16), (("chan", 1),), 1).astype(
+    padded = extended(sky_half, (("chan", 1),), 1).astype(
         patch_intensity.dtype
     )
     left_side = padded[:, :-2]

time: 70.5 us -> 69.5 us (0.986)
  local copies, waits for them, and re-layouts: 10.5 us -> 9.56 us
  starting transfers between devices: 16 us -> 16.9 us
  waiting for transfers between devices: 19.2 us -> 18.3 us
    ppermute x2, waiting for transfers between devices: 4.69 us -> 3.73 us  [exchange(): return lax.ppermute(x, 'vis', [(i, i ^ mask) for i in range(n_vis)])]
    ppermute x2, starting transfers between devices: 5.09 us -> 6.03 us  [exchange(): return lax.ppermute(x, 'vis', [(i, i ^ mask) for i in range(n_vis)])]
    unnamed x19 -> x18, local copies, waits for them, and re-layouts: 3.44 us -> 2.51 us
  transfers between devices with their start and end apart: 6 -> 6, of which waited for: 3 -> 3; matrix products, arithmetic and copies ran while one was open for 24% -> 23% of each run, Pallas kernels for 0% -> 0%
where the time goes in v12:
time: 69.5 us; the launch traced here: 68.9 us
  waiting for transfers between devices  18.3 us (26%)
  starting transfers between devices  16.9 us (24%)
  other arithmetic  15.9 us (23%)
  local copies, waits for them, and re-layouts  9.56 us (14%)
  matrix products  6.72 us (10%)
  between operations  1.61 us (2%)
    all_to_all x1, waiting for transfers between devices, reduce_rows(): got = lax.all_to_all(slabs, 'vis', 0, 0, axis_index_groups=groups)  11.8 us
    ppermute x2, starting transfers between devices, exchange(): return lax.ppermute(x, 'vis', [(i, i ^ mask) for i in range(n_vis)])  6.03 us
    all_to_all x1, starting transfers between devices, gather_rows(): lax.all_to_all(jnp.where((slot == 0) == (me < half), mine, theirs), 'vis'...  4.74 us
    dot_general x1, matrix products, local(): jnp.einsum('fij,fjk->fik', sky_rows, cols, preferred_element_type=jnp.flo...  4.05 us
    sin x2, other arithmetic, phase_factors(): jnp.sin(fine)  3.79 us
    ppermute x2, waiting for transfers between devices, exchange(): return lax.ppermute(x, 'vis', [(i, i ^ mask) for i in range(n_vis)])  3.73 us
    all_to_all x1, starting transfers between devices, reduce_rows(): got = lax.all_to_all(slabs, 'vis', 0, 0, axis_index_groups=groups)  3.56 us
    all_to_all x1, waiting for transfers between devices, gather_rows(): lax.all_to_all(jnp.where((slot == 0) == (me < half), mine, theirs), 'vis'...  2.74 us
  transfers between devices with their start and end apart: 6, of which 3 were waited for; matrix products, arithmetic and copies ran while one was open for 23% of the time, Pallas kernels for 0%

profile of v12, /device:TPU:0, one launch (start us, length us, event | category | flops | bytes accessed | tf_op | source)
XLA Modules:
  0.0 68.9 jit_solution(11670279389980323180)
XLA Ops:
  0.6 0.9 %copy.42 = bf16[32,1,2,512]{3,0,2,1:T(8,128)(2,1)S(1)} copy(f32[32,1,2,512]{3,2,1,0:T(2,128)} %param.9) | data formatting | bytes 196608 | tf_op args[0]
  1.6 0.0 copy-start.2
  1.6 4.1 %collective-permute-start = (bf16[32,1,2,512]{3,0,2,1:T(8,128)(2,1)S(1)}, bf16[32,1,2,512]{3,0,2,1:T(8,128)(2,1)S(1)}, u32[]{:S(2)}, u32[]{:S(2)}) collective-permute-start(bf16[32,1,2,512]{3,0,2,1:T(8,128)(2,1)S(1)} %copy.42), channel_id=1, source_target_pairs={{0,16},{2,18},{4,20},{6,22},{8,24},{10,26},{12,28},{14,30},{16,0},... | collective-permute-start | bytes 196616 | tf_op jit(solution)/shard_map/ppermute | solution.py:95
  5.7 0.8 %fusion.60 = (f32[1,512]{1,0:T(1,128)S(1)}, f32[1,512]{1,0:T(1,128)S(1)}) fusion(f32[2,512]{1,0:T(2,128)} %param.16), kind=kLoop, calls=%fused_computation.120 | loop fusion | bytes 8192 | tf_op jit(solution)/shard_map/slice | solution.py:154
  7.1 1.0 %add_reduce_fusion.1 = (s32[2]{0:T(128)S(1)}, s32[2]{0:T(128)S(1)}) fusion(s32[2,2]{1,0:T(2,128)} %param.17), kind=kLoop, calls=%fused_computation.106 | loop fusion | flops 8 | bytes 32 | tf_op jit(solution)/shard_map/sub | solution.py:171
  8.1 0.1 broadcast_add_fusion.1
  8.2 0.1 add.134
  8.3 0.1 broadcast_add_fusion
  8.3 0.1 add.144
  8.4 0.8 %fusion.57 = (f32[1,1,1024]{2,1,0:T(1,128)S(1)}, f32[1,1,1024]{2,1,0:T(1,128)S(1)}) fusion(f32[1,2,1024]{2,1,0:T(2,128)} %param.10), kind=kLoop, calls=%fused_computation.117 | loop fusion | bytes 16384 | tf_op jit(solution)/shard_map/slice | solution.py:193
  9.2 0.7 %select_reduce_fusion.4 = s32[1024]{0:T(1024)S(1)} fusion(s32[4]{0:T(128)} %param.12, s32[1024]{0:T(1024)S(1)} %add_select_fusion), kind=kLoop, calls=%fused_computation.76 | loop fusion | flops 11264 | bytes 8208 | tf_op jit(solution)/shard_map/reduce_sum | solution.py:165
  10.0 0.0 collective-permute-done
  10.0 1.1 %broadcast_select_fusion = bf16[8,2,32,1,2,512]{5,2,1,4,3,0:T(8,128)(2,1)} fusion(pred[2]{0:T(512)(128)(4,1)S(1)} %compare_compare_fusion, bf16[32,2,512]{2,0,1:T(8,128)(2,1)S(1)} %bitcast.166, bf16[32,2,512]{2,0,1:T(8,128)(2,1)S(1)} %bitcast.165), kind=kLoop, calls=%fused_computation.45 | loop fusion | flops 524288 | bytes 1179650 | tf_op jit(solution)/shard_map/jit(_where)/select_n | solution.py:109
  11.1 4.7 %all-to-all-start = ((bf16[8,2,32,1,2,512]{5,2,1,4,3,0:T(8,128)(2,1)}), bf16[8,2,32,1,2,512]{5,2,1,4,3,0:T(8,128)(2,1)S(1)}, u32[]{:S(2)}, u32[]{:S(2)}) async-start(bf16[8,2,32,1,2,512]{5,2,1,4,3,0:T(8,128)(2,1)} %broadcast_select_fusion), calls=%async_computation | async-start | bytes 2097152 | tf_op jit(solution)/shard_map/all_to_all | solution.py:108
  15.9 0.7 %fusion.59 = (f32[1024]{0:T(1024)S(1)}, f32[1024]{0:T(1024)S(1)}) fusion(f32[1024]{0:T(1024)} %param.14), kind=kLoop, calls=%fused_computation.119 | loop fusion | bytes 12288 | tf_op jit(solution)/shard_map/cos | solution.py:159
  16.6 0.8 %fusion.58 = (s32[1024,1]{0,1:T(1,128)S(1)}, s32[1024,1]{0,1:T(1,128)S(1)}) fusion(s32[1024,2]{0,1:T(2,128)} %param.13), kind=kLoop, calls=%fused_computation.118 | loop fusion | bytes 16384 | tf_op jit(solution)/shard_map/slice | solution.py:152
  17.4 1.7 %select_reduce_fusion.3 = (f32[1024]{0:T(1024)S(1)}, f32[1024]{0:T(1024)S(1)}, f32[1024]{0:T(1024)S(1)}, f32[1024]{0:T(1024)S(1)}) fusion(f32[512]{0:T(512)S(1)} %bitcast.174, s32[1024]{0:T(1024)S(1)} %bitcast.170, f32[512]{0:T(512)S(1)} %bitcast.173, s32[1024]{0:T(1024)S(1)} %bitcast.169), kind=kLoop, calls=%fused_computation.42 | loop fusion | flops 5238784 | bytes 28672 | tf_op jit(solution)/shard_map/reduce_sum | solution.py:38
  19.1 0.0 copy-done.2
  19.1 0.2 fusion.43
  19.3 2.0 %fusion.27 = (f32[128,1024]{1,0:T(8,128)S(1)}, f32[128,1024]{1,0:T(8,128)S(1)}) fusion(f32[128]{0:T(128)S(1)} %iota_convert_fusion.1, f32[1024]{0:T(1024)S(1)} %get-tuple-element.69, s32[1024]{0:T(1024)S(1)} %get-tuple-element.38), kind=kLoop, calls=%fused_computation.47 | loop fusion | flops 1048576 | bytes 1057280 | tf_op jit(solution)/shard_map/sin | solution.py:56
  21.3 0.6 broadcast_in_dim.188
  21.9 0.6 broadcast_in_dim.193
  22.5 0.0 copy-start.5
  22.5 0.0 copy-start.6
  22.5 1.8 %fusion.38 = (f32[32,1024]{1,0:T(8,128)S(1)}, f32[32,1024]{1,0:T(8,128)}, f32[32,1024]{1,0:T(8,128)S(1)}, f32[32,1024]{1,0:T(8,128)S(1)}) fusion(f32[32]{0:T(128)S(1)} %iota_convert_fusion, f32[1024]{0:T(1024)S(1)} %get-tuple-element.68, s32[1024]{0:T(1024)S(1)} %get-tuple-element.46, f32[32]{0:T(128)S(1)} %convert_element_type.119, s32[32]{0:T(128)S(1)} %add.144), kind=kLoop, calls=%fused_computation.64 | loop fusion | flops 524288 | bytes 532864 | tf_op jit(solution)/shard_map/sin | solution.py:56
  24.3 0.2 broadcast_in_dim.190
  24.6 0.2 broadcast_in_dim.195
  24.8 0.0 copy-done.5
  24.8 0.0 copy-done.6
  24.8 2.7 %fusion.1 = (bf16[2,512,1024]{2,1,0:T(8,128)(2,1)S(1)}, bf16[2,512,1024]{2,1,0:T(8,128)(2,1)}) fusion(f32[512,1024]{1,0:T(8,128)S(1)} %bitcast.154, f32[2,4,1024]{2,1,0:T(4,128)S(1)} %copy-done.6, f32[512,1024]{1,0:T(8,128)S(1)} %bitcast.153, f32[2,4,1024]{2,1,0:T(4,128)S(1)} %copy-done.5), kind=kLoop, calls=%fused_computation.13 | loop fusion | flops 8388608 | bytes 8454144 | tf_op jit(solution)/shard_map/convert
  27.5 2.7 %all-to-all-done = bf16[8,2,32,1,2,512]{5,2,1,4,3,0:T(8,128)(2,1)S(1)} async-done(((bf16[8,2,32,1,2,512]{5,2,1,4,3,0:T(8,128)(2,1)}), bf16[8,2,32,1,2,512]{5,2,1,4,3,0:T(8,128)(2,1)S(1)}, u32[]{:S(2)}, u32[]{:S(2)}) %all-to-all-start) | async-done | bytes 1048608 | tf_op jit(solution)/shard_map/all_to_all | solution.py:108
  30.2 0.1 copy.27
  30.3 0.0 copy-start.1
  30.3 4.1 %fusion.22 = f32[2,512,2048]{2,1,0:T(8,128)S(1)} fusion(bf16[2,512,512]{2,1,0:T(8,128)(2,1)S(1)} %bitcast.157, bf16[2,512,1024]{2,1,0:T(8,128)(2,1)} %get-tuple-element.43, bf16[2,512,1024]{2,1,0:T(8,128)(2,1)S(1)} %get-tuple-element.42), kind=kOutput, calls=%fused_computation.35 | convolution fusion | flops 2155872256 | bytes 13631488 | tf_op jit(solution)/shard_map/fij,fjk->fik/dot_general | solution.py:188
  34.4 0.0 copy-done.1
  34.4 0.2 broadcast_in_dim.202
  34.7 0.2 broadcast_in_dim.207
  34.9 0.0 copy-start.7
  34.9 2.0 %fusion.13 = (f32[1024]{0:T(1024)S(1)}, f32[1024]{0:T(1024)S(1)}) fusion(f32[2,512,2048]{2,1,0:T(8,128)S(1)} %fusion.22, f32[512,1024]{1,0:T(8,128)S(1)} %bitcast.156, f32[2,16,1024]{2,1,0:T(8,128)S(1)} %bitcast.161, f32[512,1024]{1,0:T(8,128)S(1)} %bitcast.155, f32[2,16,1024]{2,1,0:T(8,128)S(1)} %bitcast.158), kind=kLoop, calls=%fused_computation.25 | loop fusion | flops 14678016 | bytes 12853248 | tf_op jit(solution)/shard_map/reduce_sum | solution.py:191
  36.9 0.0 copy-done.7
  37.0 0.2 broadcast_in_dim.214
  37.2 0.2 broadcast_in_dim.217
  37.5 0.9 %fusion.7 = bf16[2,512,1024]{2,1,0:T(8,128)(2,1)S(1)} fusion(f32[512,1024]{1,0:T(8,128)S(1)} %bitcast.151, f32[512,1024]{1,0:T(8,128)S(1)} %bitcast.149, f32[2,16,1024]{2,1,0:T(8,128)S(1)} %bitcast.162, f32[2,16,1024]{2,1,0:T(8,128)S(1)} %bitcast.159), kind=kLoop, calls=%fused_computation.19 | loop fusion | flops 4194304 | bytes 6553600 | tf_op jit(solution)/shard_map/convert_element_type | solution.py:199
  38.3 0.0 copy-start
  38.3 0.8 %fusion.23 = bf16[2,512,1024]{2,1,0:T(8,128)(2,1)S(1)} fusion(f32[512,1024]{1,0:T(8,128)S(1)} %bitcast.152, f32[512,1024]{1,0:T(8,128)S(1)} %bitcast.150, f32[2,16,1024]{2,1,0:T(8,128)S(1)} %bitcast.163, f32[2,16,1024]{2,1,0:T(8,128)S(1)} %bitcast.160), kind=kLoop, calls=%fused_computation.36 | loop fusion | flops 5242880 | bytes 6553600 | tf_op jit(solution)/shard_map/neg | solution.py:201
  39.1 0.8 %copy-done = bf16[2,512,1024]{2,1,0:T(8,128)(2,1)S(1)} copy-done((bf16[2,512,1024]{2,1,0:T(8,128)(2,1)S(1)}, bf16[2,512,1024]{2,1,0:T(8,128)(2,1)}, u32[]{:S(2)}) %copy-start) | copy-done | bytes 2097176
  39.9 2.7 %fusion.24 = bf16[2,512,512]{1,2,0:T(8,128)(2,1)S(1)} fusion(bf16[2,512,1024]{2,1,0:T(8,128)(2,1)S(1)} %fusion.23, bf16[2,512,1024]{2,1,0:T(8,128)(2,1)S(1)} %fusion.7, bf16[2,512,1024]{2,1,0:T(8,128)(2,1)S(1)} %copy-done, bf16[2,512,1024]{2,1,0:T(8,128)(2,1)S(1)} %get-tuple-element.42), kind=kOutput, calls=%fused_computation.44 | convolution fusion | flops 2164785152 | bytes 9437184 | tf_op jit(solution)/shard_map/fik,fjk->ifj/dot_general | solution.py:202
  42.6 0.0 copy-start.3
  42.6 0.0 copy-start.4
  42.6 1.0 %copy.28 = bf16[8,2,32,1,2,512]{5,2,1,4,3,0:T(8,128)(2,1)} copy(bf16[8,2,32,1,2,512]{5,2,1,0,4,3:T(8,128)(2,1)S(1)} %bitcast.164) | data formatting | bytes 2097152 | tf_op jit(solution)/shard_map/reshape | solution.py:117
  43.7 3.6 %all-to-all-start.1 = ((bf16[8,2,32,1,2,512]{5,2,1,4,3,0:T(8,128)(2,1)}), bf16[8,2,32,1,2,512]{5,2,1,4,3,0:T(8,128)(2,1)S(1)}, u32[]{:S(2)}, u32[]{:S(2)}) async-start(bf16[8,2,32,1,2,512]{5,2,1,4,3,0:T(8,128)(2,1)} %copy.28), calls=%async_computation.1 | async-start | bytes 2097152 | tf_op jit(solution)/shard_map/all_to_all | solution.py:119
  47.2 0.0 copy-done.3
  47.2 1.3 %collective-permute-start.2 = (bf16[32,1,2,512]{3,0,2,1:T(8,128)(2,1)S(1)}, bf16[32,1,2,512]{3,0,2,1:T(8,128)(2,1)S(1)}, u32[]{:S(2)}, u32[]{:S(2)}) collective-permute-start(bf16[32,1,2,512]{3,0,2,1:T(8,128)(2,1)S(1)} %copy-done.3), channel_id=1, source_target_pairs={{0,1},{2,3},{4,5},{6,7},{8,9},{10,11},{12,13},{14,15},{16,17},{18,... | collective-permute-start | bytes 196616 | tf_op jit(solution)/shard_map/ppermute | solution.py:27
  48.5 1.3 %collective-permute-start.3 = (bf16[32,1,2,512]{3,0,2,1:T(8,128)(2,1)S(1)}, bf16[32,1,2,512]{3,0,2,1:T(8,128)(2,1)S(1)}, u32[]{:S(2)}, u32[]{:S(2)}) collective-permute-start(bf16[32,1,2,512]{3,0,2,1:T(8,128)(2,1)S(1)} %copy-done.3), channel_id=1, source_target_pairs={{1,0},{3,2},{5,4},{7,6},{9,8},{11,10},{13,12},{15,14},{17,16},{19,... | collective-permute-start | bytes 196616 | tf_op jit(solution)/shard_map/ppermute | solution.py:29
  49.8 11.8 %all-to-all-done.1 = bf16[8,2,32,1,2,512]{5,2,1,4,3,0:T(8,128)(2,1)S(1)} async-done(((bf16[8,2,32,1,2,512]{5,2,1,4,3,0:T(8,128)(2,1)}), bf16[8,2,32,1,2,512]{5,2,1,4,3,0:T(8,128)(2,1)S(1)}, u32[]{:S(2)}, u32[]{:S(2)}) %all-to-all-start.1) | async-done | bytes 1048608 | tf_op jit(solution)/shard_map/all_to_all | solution.py:119
  61.6 0.1 convert_reduce_fusion
  61.8 1.9 %collective-permute-start.1 = (bf16[32,1,2,512]{3,0,2,1:T(8,128)(2,1)S(1)}, bf16[32,1,2,512]{3,0,2,1:T(8,128)(2,1)S(1)}, u32[]{:S(2)}, u32[]{:S(2)}) collective-permute-start(bf16[32,1,2,512]{3,0,2,1:T(8,128)(2,1)S(1)} %fusion.42), channel_id=1, source_target_pairs={{0,16},{2,18},{4,20},{6,22},{8,24},{10,26},{12,28},{14,30},{16,0},... | collective-permute-start | bytes 196616 | tf_op jit(solution)/shard_map/ppermute | solution.py:95
  63.7 0.6 maximum_bitcast_fusion
  64.4 0.0 collective-permute-done.2
  64.4 0.0 collective-permute-done.3
  64.4 3.7 %collective-permute-done.1 = bf16[32,1,2,512]{3,0,2,1:T(8,128)(2,1)S(1)} collective-permute-done((bf16[32,1,2,512]{3,0,2,1:T(8,128)(2,1)S(1)}, bf16[32,1,2,512]{3,0,2,1:T(8,128)(2,1)S(1)}, u32[]{:S(2)}, u32[]{:S(2)}) %collective-permute-start.1) | collective-permute-done | bytes 65568 | tf_op jit(solution)/shard_map/ppermute | solution.py:95
  68.1 0.0 copy-done.4
  68.1 0.1 fusion.34
  68.2 0.8 %copy.37 = f32[32,1,2,512]{3,2,1,0:T(2,128)} copy(f32[32,1,2,512]{3,0,2,1:T(8,128)S(1)} %fusion.34) | data formatting | bytes 262144
  (13 shorter events, 0.1 us)
Async XLA Ops:
  1.6 17.5 %copy-start.2 = (bf16[32,1,2,512]{3,0,2,1:T(8,128)(2,1)}, bf16[32,1,2,512]{3,0,2,1:T(8,128)(2,1)S(1)}, u32[]{:S(2)}) copy-start(bf16[32,1,2,512]{3,0,2,1:T(8,128)(2,1)S(1)} %copy.42) | copy-start | bytes 196612
  1.6 8.4 %collective-permute-start = (bf16[32,1,2,512]{3,0,2,1:T(8,128)(2,1)S(1)}, bf16[32,1,2,512]{3,0,2,1:T(8,128)(2,1)S(1)}, u32[]{:S(2)}, u32[]{:S(2)}) collective-permute-start(bf16[32,1,2,512]{3,0,2,1:T(8,128)(2,1)S(1)} %copy.42), channel_id=1, source_target_pairs={{0,16},{2,18},{4,20},{6,22},{8,24},{10,26},{12,28},{14,30},{16,0},... | collective-permute-start | bytes 196616 | tf_op jit(solution)/shard_map/ppermute | solution.py:95
  11.1 19.1 %all-to-all-start = ((bf16[8,2,32,1,2,512]{5,2,1,4,3,0:T(8,128)(2,1)}), bf16[8,2,32,1,2,512]{5,2,1,4,3,0:T(8,128)(2,1)S(1)}, u32[]{:S(2)}, u32[]{:S(2)}) async-start(bf16[8,2,32,1,2,512]{5,2,1,4,3,0:T(8,128)(2,1)} %broadcast_select_fusion), calls=%async_computation | async-start | bytes 2097152 | tf_op jit(solution)/shard_map/all_to_all | solution.py:108
  22.5 2.3 %copy-start.5 = (f32[2,4,1024]{2,1,0:T(4,128)S(1)}, f32[2,4,1024]{2,1,0:T(4,128)}, u32[]{:S(2)}) copy-start(f32[2,4,1024]{2,1,0:T(4,128)} %broadcast_in_dim.188) | copy-start | bytes 98308
  22.5 2.3 %copy-start.6 = (f32[2,4,1024]{2,1,0:T(4,128)S(1)}, f32[2,4,1024]{2,1,0:T(4,128)}, u32[]{:S(2)}) copy-start(f32[2,4,1024]{2,1,0:T(4,128)} %broadcast_in_dim.193) | copy-start | bytes 98308
  30.3 4.1 %copy-start.1 = (f32[32,1024]{1,0:T(8,128)S(1)}, f32[32,1024]{1,0:T(8,128)}, u32[]{:S(2)}) copy-start(f32[32,1024]{1,0:T(8,128)} %get-tuple-element.20) | copy-start | bytes 393220
  34.9 2.0 %copy-start.7 = (f32[1024]{0:T(1024)S(1)}, f32[1024]{0:T(1024)}, u32[]{:S(2)}) copy-start(f32[1024]{0:T(1024)} %param.11) | copy-start | bytes 12292
  38.3 1.6 %copy-start = (bf16[2,512,1024]{2,1,0:T(8,128)(2,1)S(1)}, bf16[2,512,1024]{2,1,0:T(8,128)(2,1)}, u32[]{:S(2)}) copy-start(bf16[2,512,1024]{2,1,0:T(8,128)(2,1)} %get-tuple-element.43) | copy-start | bytes 6291460
  42.6 4.6 %copy-start.3 = (bf16[32,1,2,512]{3,0,2,1:T(8,128)(2,1)S(1)}, bf16[32,1,2,512]{3,0,2,1:T(8,128)(2,1)}, u32[]{:S(2)}) copy-start(bf16[32,1,2,512]{3,0,2,1:T(8,128)(2,1)} %copy-done.2) | copy-start | bytes 196612
  42.6 25.5 %copy-start.4 = (f32[32,1,2,512]{3,2,1,0:T(2,128)S(1)}, f32[32,1,2,512]{3,2,1,0:T(2,128)}, u32[]{:S(2)}) copy-start(f32[32,1,2,512]{3,2,1,0:T(2,128)} %param.9) | copy-start | bytes 393220
  43.7 18.0 %all-to-all-start.1 = ((bf16[8,2,32,1,2,512]{5,2,1,4,3,0:T(8,128)(2,1)}), bf16[8,2,32,1,2,512]{5,2,1,4,3,0:T(8,128)(2,1)S(1)}, u32[]{:S(2)}, u32[]{:S(2)}) async-start(bf16[8,2,32,1,2,512]{5,2,1,4,3,0:T(8,128)(2,1)} %copy.28), calls=%async_computation.1 | async-start | bytes 2097152 | tf_op jit(solution)/shard_map/all_to_all | solution.py:119
  47.2 17.1 %collective-permute-start.2 = (bf16[32,1,2,512]{3,0,2,1:T(8,128)(2,1)S(1)}, bf16[32,1,2,512]{3,0,2,1:T(8,128)(2,1)S(1)}, u32[]{:S(2)}, u32[]{:S(2)}) collective-permute-start(bf16[32,1,2,512]{3,0,2,1:T(8,128)(2,1)S(1)} %copy-done.3), channel_id=1, source_target_pairs={{0,1},{2,3},{4,5},{6,7},{8,9},{10,11},{12,13},{14,15},{16,17},{18,... | collective-permute-start | bytes 196616 | tf_op jit(solution)/shard_map/ppermute | solution.py:27
  48.5 15.8 %collective-permute-start.3 = (bf16[32,1,2,512]{3,0,2,1:T(8,128)(2,1)S(1)}, bf16[32,1,2,512]{3,0,2,1:T(8,128)(2,1)S(1)}, u32[]{:S(2)}, u32[]{:S(2)}) collective-permute-start(bf16[32,1,2,512]{3,0,2,1:T(8,128)(2,1)S(1)} %copy-done.3), channel_id=1, source_target_pairs={{1,0},{3,2},{5,4},{7,6},{9,8},{11,10},{13,12},{15,14},{17,16},{19,... | collective-permute-start | bytes 196616 | tf_op jit(solution)/shard_map/ppermute | solution.py:29
  61.8 6.3 %collective-permute-start.1 = (bf16[32,1,2,512]{3,0,2,1:T(8,128)(2,1)S(1)}, bf16[32,1,2,512]{3,0,2,1:T(8,128)(2,1)S(1)}, u32[]{:S(2)}, u32[]{:S(2)}) collective-permute-start(bf16[32,1,2,512]{3,0,2,1:T(8,128)(2,1)S(1)} %fusion.42), channel_id=1, source_target_pairs={{0,16},{2,18},{4,20},{6,22},{8,24},{10,26},{12,28},{14,30},{16,0},... | collective-permute-start | bytes 196616 | tf_op jit(solution)/shard_map/ppermute | solution.py:95

commit v13 on v12

--- a/solution.py
+++ b/solution.py
@@ -2,6 +2,7 @@
 
 import jax
 import jax.numpy as jnp
+import numpy as np
 from jax import lax
 from jax.sharding import PartitionSpec as P
 
@@ -160,19 +161,17 @@
         sample_rotation_phase
     )
     slots = jnp.arange(nvis, dtype=jnp.int32)
-    block_of = slots // BLOCK
-    block_numbers = jnp.arange(block_populations.shape[0], dtype=jnp.int32)
-    block_count = jnp.sum(
-        jnp.where(block_of[:, None] == block_numbers[None, :], block_populations[None, :], 0),
-        axis=1,
-    )
+    block_count = jnp.broadcast_to(
+        block_populations[:, None], (block_populations.shape[0], BLOCK)
+    ).reshape(nvis)
     scale_vis = (slots % BLOCK < block_count).astype(jnp.float32) * sample_importance
     first_row = patch_layout_position[:, 0] * facet - image // 2
     first_col = patch_layout_position[:, 1] * facet - image // 2
-    chunk = jnp.arange(n_vis, dtype=jnp.int32)
+    chunk = np.arange(n_vis, dtype=np.int32)
     owner = (chunk % 2) * (n_vis // 2) + chunk // 2
-    row_starts = first_row[:, None] + rows_dev * owner[None, :]
-    col_starts = first_col[:, None] + LANE_BLOCK * jnp.arange(facet // LANE_BLOCK, dtype=jnp.int32)
+    row_starts = first_row[:, None] + jnp.asarray(rows_dev * owner, jnp.int32)[None, :]
+    col_offsets = LANE_BLOCK * np.arange(facet // LANE_BLOCK, dtype=np.int32)
+    col_starts = first_col[:, None] + jnp.asarray(col_offsets, jnp.int32)[None, :]
 
 
     new_rows = []

time: 69.5 us -> 69.5 us (level)
    reduce_sum x1 -> x0, other arithmetic: 0.74 us -> none  [local(): jnp.sum(jnp.where(block_of[:, None] == block_numbers[None, :], block_popu...]
    unnamed x18 -> x22, local copies, waits for them, and re-layouts: 2.51 us -> 2.6 us
    another operation x1 -> x2, other arithmetic: 2.68 us -> 2.68 us
where the time goes in v13:
time: 69.5 us; the launch traced here: 68.9 us
  waiting for transfers between devices  18.2 us (26%)
  starting transfers between devices  16.9 us (24%)
  other arithmetic  15.8 us (23%)
  local copies, waits for them, and re-layouts  9.64 us (14%)
  matrix products  6.68 us (10%)
  between operations  1.6 us (2%)
    all_to_all x1, waiting for transfers between devices, reduce_rows(): got = lax.all_to_all(slabs, 'vis', 0, 0, axis_index_groups=groups)  11.8 us
    ppermute x2, starting transfers between devices, exchange(): return lax.ppermute(x, 'vis', [(i, i ^ mask) for i in range(n_vis)])  6.07 us
    all_to_all x1, starting transfers between devices, gather_rows(): lax.all_to_all(jnp.where((slot == 0) == (me < half), mine, theirs), 'vis'...  4.74 us
    dot_general x1, matrix products, local(): jnp.einsum('fij,fjk->fik', sky_rows, cols, preferred_element_type=jnp.flo...  4.01 us
    sin x2, other arithmetic, phase_factors(): jnp.sin(fine)  3.79 us
    ppermute x2, waiting for transfers between devices, exchange(): return lax.ppermute(x, 'vis', [(i, i ^ mask) for i in range(n_vis)])  3.7 us
    all_to_all x1, starting transfers between devices, reduce_rows(): got = lax.all_to_all(slabs, 'vis', 0, 0, axis_index_groups=groups)  3.56 us
    all_to_all x1, waiting for transfers between devices, gather_rows(): lax.all_to_all(jnp.where((slot == 0) == (me < half), mine, theirs), 'vis'...  2.74 us
  transfers between devices with their start and end apart: 6, of which 3 were waited for; matrix products, arithmetic and copies ran while one was open for 23% of the time, Pallas kernels for 0%

profile of v13, /device:TPU:0, one launch (start us, length us, event | category | flops | bytes accessed | tf_op | source)
XLA Modules:
  0.0 68.9 jit_solution(147568093352487657)
XLA Ops:
  0.6 0.0 copy-start
  0.6 0.9 %copy.45 = bf16[32,1,2,512]{3,0,2,1:T(8,128)(2,1)S(1)} copy(f32[32,1,2,512]{3,2,1,0:T(2,128)} %param.11) | data formatting | bytes 196608 | tf_op args[0]
  1.6 0.0 copy-start.3
  1.6 4.1 %collective-permute-start = (bf16[32,1,2,512]{3,0,2,1:T(8,128)(2,1)S(1)}, bf16[32,1,2,512]{3,0,2,1:T(8,128)(2,1)S(1)}, u32[]{:S(2)}, u32[]{:S(2)}) collective-permute-start(bf16[32,1,2,512]{3,0,2,1:T(8,128)(2,1)S(1)} %copy.45), channel_id=1, source_target_pairs={{0,16},{2,18},{4,20},{6,22},{8,24},{10,26},{12,28},{14,30},{16,0},... | collective-permute-start | bytes 196616 | tf_op jit(solution)/shard_map/ppermute | solution.py:96
  5.7 0.8 %fusion.55 = (f32[1,512]{1,0:T(1,128)S(1)}, f32[1,512]{1,0:T(1,128)S(1)}) fusion(f32[2,512]{1,0:T(2,128)} %param.18), kind=kLoop, calls=%fused_computation.106 | loop fusion | bytes 8192 | tf_op jit(solution)/shard_map/slice | solution.py:155
  7.1 1.0 %add_reduce_fusion.1 = (s32[2]{0:T(128)S(1)}, s32[2]{0:T(128)S(1)}) fusion(s32[2,2]{1,0:T(2,128)} %param.19), kind=kLoop, calls=%fused_computation.95 | loop fusion | flops 8 | bytes 32 | tf_op jit(solution)/shard_map/sub | solution.py:169
  8.1 0.1 broadcast_add_fusion.1
  8.2 0.1 add.107
  8.3 0.7 %broadcast_add_fusion = s32[2,16]{1,0:T(2,128)S(1)} fusion(s32[16]{0:T(128)} %constant.81.clone, s32[2]{0:T(128)S(1)} %get-tuple-element.37), kind=kLoop, calls=%fused_computation.97 | loop fusion | flops 32 | bytes 200 | tf_op jit(solution)/shard_map/add | solution.py:172
  9.0 0.1 add.115
  9.1 0.8 %fusion.52 = (f32[1,1,1024]{2,1,0:T(1,128)S(1)}, f32[1,1,1024]{2,1,0:T(1,128)S(1)}) fusion(f32[1,2,1024]{2,1,0:T(2,128)} %param.12), kind=kLoop, calls=%fused_computation.103 | loop fusion | bytes 16384 | tf_op jit(solution)/shard_map/slice | solution.py:192
  9.9 0.0 copy-done
  9.9 0.1 broadcast_bitcast_fusion
  10.0 0.0 collective-permute-done
  10.0 1.1 %broadcast_select_fusion = bf16[8,2,32,1,2,512]{5,2,1,4,3,0:T(8,128)(2,1)} fusion(pred[2]{0:T(512)(128)(4,1)S(1)} %compare_compare_fusion, bf16[32,2,512]{2,0,1:T(8,128)(2,1)S(1)} %bitcast.169, bf16[32,2,512]{2,0,1:T(8,128)(2,1)S(1)} %bitcast.168), kind=kLoop, calls=%fused_computation.45 | loop fusion | flops 524288 | bytes 1179650 | tf_op jit(solution)/shard_map/jit(_where)/select_n | solution.py:110
  11.1 4.7 %all-to-all-start = ((bf16[8,2,32,1,2,512]{5,2,1,4,3,0:T(8,128)(2,1)}), bf16[8,2,32,1,2,512]{5,2,1,4,3,0:T(8,128)(2,1)S(1)}, u32[]{:S(2)}, u32[]{:S(2)}) async-start(bf16[8,2,32,1,2,512]{5,2,1,4,3,0:T(8,128)(2,1)} %broadcast_select_fusion), calls=%async_computation | async-start | bytes 2097152 | tf_op jit(solution)/shard_map/all_to_all | solution.py:109
  15.8 0.7 %fusion.54 = (f32[1024]{0:T(1024)S(1)}, f32[1024]{0:T(1024)S(1)}) fusion(f32[1024]{0:T(1024)} %param.16), kind=kLoop, calls=%fused_computation.105 | loop fusion | bytes 12288 | tf_op jit(solution)/shard_map/cos | solution.py:160
  16.6 0.8 %fusion.53 = (s32[1024,1]{0,1:T(1,128)S(1)}, s32[1024,1]{0,1:T(1,128)S(1)}) fusion(s32[1024,2]{0,1:T(2,128)} %param.15), kind=kLoop, calls=%fused_computation.104 | loop fusion | bytes 16384 | tf_op jit(solution)/shard_map/slice | solution.py:153
  17.3 1.7 %select_reduce_fusion.3 = (f32[1024]{0:T(1024)S(1)}, f32[1024]{0:T(1024)S(1)}, f32[1024]{0:T(1024)S(1)}, f32[1024]{0:T(1024)S(1)}) fusion(f32[512]{0:T(512)S(1)} %bitcast.178, s32[1024]{0:T(1024)S(1)} %bitcast.173, f32[512]{0:T(512)S(1)} %bitcast.177, s32[1024]{0:T(1024)S(1)} %bitcast.172), kind=kLoop, calls=%fused_computation.42 | loop fusion | flops 5238784 | bytes 28672 | tf_op jit(solution)/shard_map/reduce_sum | solution.py:39
  19.0 0.0 copy-done.3
  19.0 0.2 fusion.43
  19.3 2.0 %fusion.27 = (f32[128,1024]{1,0:T(8,128)S(1)}, f32[128,1024]{1,0:T(8,128)S(1)}) fusion(f32[128]{0:T(128)S(1)} %iota_convert_fusion.1, f32[1024]{0:T(1024)S(1)} %get-tuple-element.69, s32[1024]{0:T(1024)S(1)} %get-tuple-element.38), kind=kLoop, calls=%fused_computation.47 | loop fusion | flops 1048576 | bytes 1057280 | tf_op jit(solution)/shard_map/sin | solution.py:57
  21.3 0.6 broadcast_in_dim.179
  21.9 0.6 broadcast_in_dim.184
  22.5 1.8 %fusion.38 = (f32[32,1024]{1,0:T(8,128)S(1)}, f32[32,1024]{1,0:T(8,128)}, f32[32,1024]{1,0:T(8,128)S(1)}, f32[32,1024]{1,0:T(8,128)S(1)}) fusion(f32[32]{0:T(128)S(1)} %iota_convert_fusion, f32[1024]{0:T(1024)S(1)} %get-tuple-element.68, s32[1024]{0:T(1024)S(1)} %get-tuple-element.46, f32[32]{0:T(128)S(1)} %convert_element_type.119, s32[32]{0:T(128)S(1)} %add.115), kind=kLoop, calls=%fused_computation.64 | loop fusion | flops 524288 | bytes 532864 | tf_op jit(solution)/shard_map/sin | solution.py:57
  24.3 0.2 broadcast_in_dim.181
  24.5 0.2 broadcast_in_dim.186
  24.8 0.0 copy-done.6
  24.8 0.0 copy-done.7
  24.8 2.7 %fusion.1 = (bf16[2,512,1024]{2,1,0:T(8,128)(2,1)S(1)}, bf16[2,512,1024]{2,1,0:T(8,128)(2,1)}) fusion(f32[512,1024]{1,0:T(8,128)S(1)} %bitcast.157, f32[2,4,1024]{2,1,0:T(4,128)S(1)} %copy-done.7, f32[512,1024]{1,0:T(8,128)S(1)} %bitcast.156, f32[2,4,1024]{2,1,0:T(4,128)S(1)} %copy-done.6), kind=kLoop, calls=%fused_computation.13 | loop fusion | flops 8388608 | bytes 8454144 | tf_op jit(solution)/shard_map/convert
  27.5 2.7 %all-to-all-done = bf16[8,2,32,1,2,512]{5,2,1,4,3,0:T(8,128)(2,1)S(1)} async-done(((bf16[8,2,32,1,2,512]{5,2,1,4,3,0:T(8,128)(2,1)}), bf16[8,2,32,1,2,512]{5,2,1,4,3,0:T(8,128)(2,1)S(1)}, u32[]{:S(2)}, u32[]{:S(2)}) %all-to-all-start) | async-done | bytes 1048608 | tf_op jit(solution)/shard_map/all_to_all | solution.py:109
  30.2 0.1 copy.29
  30.3 0.0 copy-start.2
  30.3 4.0 %fusion.22 = f32[2,512,2048]{2,1,0:T(8,128)S(1)} fusion(bf16[2,512,512]{2,1,0:T(8,128)(2,1)S(1)} %bitcast.160, bf16[2,512,1024]{2,1,0:T(8,128)(2,1)} %get-tuple-element.43, bf16[2,512,1024]{2,1,0:T(8,128)(2,1)S(1)} %get-tuple-element.42), kind=kOutput, calls=%fused_computation.35 | convolution fusion | flops 2155872256 | bytes 13631488 | tf_op jit(solution)/shard_map/fij,fjk->fik/dot_general | solution.py:187
  34.3 0.0 copy-done.2
  34.3 0.2 broadcast_in_dim.192
  34.6 0.2 broadcast_in_dim.197
  34.8 0.0 copy-start.8
  34.9 2.0 %fusion.13 = (f32[1024]{0:T(1024)S(1)}, f32[1024]{0:T(1024)S(1)}) fusion(f32[2,512,2048]{2,1,0:T(8,128)S(1)} %fusion.22, f32[512,1024]{1,0:T(8,128)S(1)} %bitcast.159, f32[2,16,1024]{2,1,0:T(8,128)S(1)} %bitcast.164, f32[512,1024]{1,0:T(8,128)S(1)} %bitcast.158, f32[2,16,1024]{2,1,0:T(8,128)S(1)} %bitcast.161), kind=kLoop, calls=%fused_computation.25 | loop fusion | flops 14678016 | bytes 12853248 | tf_op jit(solution)/shard_map/reduce_sum | solution.py:190
  36.8 0.0 copy-done.8
  36.9 0.2 broadcast_in_dim.204
  37.1 0.2 broadcast_in_dim.207
  37.4 0.9 %fusion.7 = bf16[2,512,1024]{2,1,0:T(8,128)(2,1)S(1)} fusion(f32[512,1024]{1,0:T(8,128)S(1)} %bitcast.154, f32[512,1024]{1,0:T(8,128)S(1)} %bitcast.152, f32[2,16,1024]{2,1,0:T(8,128)S(1)} %bitcast.165, f32[2,16,1024]{2,1,0:T(8,128)S(1)} %bitcast.162), kind=kLoop, calls=%fused_computation.19 | loop fusion | flops 4194304 | bytes 6553600 | tf_op jit(solution)/shard_map/convert_element_type | solution.py:198
  38.3 0.0 copy-start.1
  38.3 0.8 %fusion.23 = bf16[2,512,1024]{2,1,0:T(8,128)(2,1)S(1)} fusion(f32[512,1024]{1,0:T(8,128)S(1)} %bitcast.155, f32[512,1024]{1,0:T(8,128)S(1)} %bitcast.153, f32[2,16,1024]{2,1,0:T(8,128)S(1)} %bitcast.166, f32[2,16,1024]{2,1,0:T(8,128)S(1)} %bitcast.163), kind=kLoop, calls=%fused_computation.36 | loop fusion | flops 5242880 | bytes 6553600 | tf_op jit(solution)/shard_map/neg | solution.py:200
  39.1 0.8 %copy-done.1 = bf16[2,512,1024]{2,1,0:T(8,128)(2,1)S(1)} copy-done((bf16[2,512,1024]{2,1,0:T(8,128)(2,1)S(1)}, bf16[2,512,1024]{2,1,0:T(8,128)(2,1)}, u32[]{:S(2)}) %copy-start.1) | copy-done | bytes 2097176
  39.9 2.7 %fusion.24 = bf16[2,512,512]{1,2,0:T(8,128)(2,1)S(1)} fusion(bf16[2,512,1024]{2,1,0:T(8,128)(2,1)S(1)} %fusion.23, bf16[2,512,1024]{2,1,0:T(8,128)(2,1)S(1)} %fusion.7, bf16[2,512,1024]{2,1,0:T(8,128)(2,1)S(1)} %copy-done.1, bf16[2,512,1024]{2,1,0:T(8,128)(2,1)S(1)} %get-tuple-element.42), kind=kOutput, calls=%fused_computation.44 | convolution fusion | flops 2164785152 | bytes 9437184 | tf_op jit(solution)/shard_map/fik,fjk->ifj/dot_general | solution.py:201
  42.6 0.0 copy-start.4
  42.6 0.0 copy-start.5
  42.6 1.0 %copy.30 = bf16[8,2,32,1,2,512]{5,2,1,4,3,0:T(8,128)(2,1)} copy(bf16[8,2,32,1,2,512]{5,2,1,0,4,3:T(8,128)(2,1)S(1)} %bitcast.167) | data formatting | bytes 2097152 | tf_op jit(solution)/shard_map/reshape | solution.py:118
  43.6 3.6 %all-to-all-start.1 = ((bf16[8,2,32,1,2,512]{5,2,1,4,3,0:T(8,128)(2,1)}), bf16[8,2,32,1,2,512]{5,2,1,4,3,0:T(8,128)(2,1)S(1)}, u32[]{:S(2)}, u32[]{:S(2)}) async-start(bf16[8,2,32,1,2,512]{5,2,1,4,3,0:T(8,128)(2,1)} %copy.30), calls=%async_computation.1 | async-start | bytes 2097152 | tf_op jit(solution)/shard_map/all_to_all | solution.py:120
  47.2 0.0 copy-done.4
  47.2 1.3 %collective-permute-start.2 = (bf16[32,1,2,512]{3,0,2,1:T(8,128)(2,1)S(1)}, bf16[32,1,2,512]{3,0,2,1:T(8,128)(2,1)S(1)}, u32[]{:S(2)}, u32[]{:S(2)}) collective-permute-start(bf16[32,1,2,512]{3,0,2,1:T(8,128)(2,1)S(1)} %copy-done.4), channel_id=1, source_target_pairs={{0,1},{2,3},{4,5},{6,7},{8,9},{10,11},{12,13},{14,15},{16,17},{18,... | collective-permute-start | bytes 196616 | tf_op jit(solution)/shard_map/ppermute | solution.py:28
  48.5 1.3 %collective-permute-start.3 = (bf16[32,1,2,512]{3,0,2,1:T(8,128)(2,1)S(1)}, bf16[32,1,2,512]{3,0,2,1:T(8,128)(2,1)S(1)}, u32[]{:S(2)}, u32[]{:S(2)}) collective-permute-start(bf16[32,1,2,512]{3,0,2,1:T(8,128)(2,1)S(1)} %copy-done.4), channel_id=1, source_target_pairs={{1,0},{3,2},{5,4},{7,6},{9,8},{11,10},{13,12},{15,14},{17,16},{19,... | collective-permute-start | bytes 196616 | tf_op jit(solution)/shard_map/ppermute | solution.py:30
  49.8 11.8 %all-to-all-done.1 = bf16[8,2,32,1,2,512]{5,2,1,4,3,0:T(8,128)(2,1)S(1)} async-done(((bf16[8,2,32,1,2,512]{5,2,1,4,3,0:T(8,128)(2,1)}), bf16[8,2,32,1,2,512]{5,2,1,4,3,0:T(8,128)(2,1)S(1)}, u32[]{:S(2)}, u32[]{:S(2)}) %all-to-all-start.1) | async-done | bytes 1048608 | tf_op jit(solution)/shard_map/all_to_all | solution.py:120
  61.6 0.1 convert_reduce_fusion
  61.8 2.0 %collective-permute-start.1 = (bf16[32,1,2,512]{3,0,2,1:T(8,128)(2,1)S(1)}, bf16[32,1,2,512]{3,0,2,1:T(8,128)(2,1)S(1)}, u32[]{:S(2)}, u32[]{:S(2)}) collective-permute-start(bf16[32,1,2,512]{3,0,2,1:T(8,128)(2,1)S(1)} %fusion.42), channel_id=1, source_target_pairs={{0,16},{2,18},{4,20},{6,22},{8,24},{10,26},{12,28},{14,30},{16,0},... | collective-permute-start | bytes 196616 | tf_op jit(solution)/shard_map/ppermute | solution.py:96
  63.8 0.6 maximum_bitcast_fusion
  64.4 0.0 collective-permute-done.2
  64.4 0.0 collective-permute-done.3
  64.4 3.7 %collective-permute-done.1 = bf16[32,1,2,512]{3,0,2,1:T(8,128)(2,1)S(1)} collective-permute-done((bf16[32,1,2,512]{3,0,2,1:T(8,128)(2,1)S(1)}, bf16[32,1,2,512]{3,0,2,1:T(8,128)(2,1)S(1)}, u32[]{:S(2)}, u32[]{:S(2)}) %collective-permute-start.1) | collective-permute-done | bytes 65568 | tf_op jit(solution)/shard_map/ppermute | solution.py:96
  68.1 0.0 copy-done.5
  68.1 0.1 fusion.34
  68.2 0.8 %copy.39 = f32[32,1,2,512]{3,2,1,0:T(2,128)} copy(f32[32,1,2,512]{3,0,2,1:T(8,128)S(1)} %fusion.34) | data formatting | bytes 262144
  (14 shorter events, 0.1 us)
Async XLA Ops:
  0.6 9.2 %copy-start = (s32[4]{0:T(128)S(1)}, s32[4]{0:T(128)}, u32[]{:S(2)}) copy-start(s32[4]{0:T(128)} %param.14) | copy-start | bytes 52
  1.6 17.5 %copy-start.3 = (bf16[32,1,2,512]{3,0,2,1:T(8,128)(2,1)}, bf16[32,1,2,512]{3,0,2,1:T(8,128)(2,1)S(1)}, u32[]{:S(2)}) copy-start(bf16[32,1,2,512]{3,0,2,1:T(8,128)(2,1)S(1)} %copy.45) | copy-start | bytes 196612
  1.6 8.4 %collective-permute-start = (bf16[32,1,2,512]{3,0,2,1:T(8,128)(2,1)S(1)}, bf16[32,1,2,512]{3,0,2,1:T(8,128)(2,1)S(1)}, u32[]{:S(2)}, u32[]{:S(2)}) collective-permute-start(bf16[32,1,2,512]{3,0,2,1:T(8,128)(2,1)S(1)} %copy.45), channel_id=1, source_target_pairs={{0,16},{2,18},{4,20},{6,22},{8,24},{10,26},{12,28},{14,30},{16,0},... | collective-permute-start | bytes 196616 | tf_op jit(solution)/shard_map/ppermute | solution.py:96
  11.1 19.1 %all-to-all-start = ((bf16[8,2,32,1,2,512]{5,2,1,4,3,0:T(8,128)(2,1)}), bf16[8,2,32,1,2,512]{5,2,1,4,3,0:T(8,128)(2,1)S(1)}, u32[]{:S(2)}, u32[]{:S(2)}) async-start(bf16[8,2,32,1,2,512]{5,2,1,4,3,0:T(8,128)(2,1)} %broadcast_select_fusion), calls=%async_computation | async-start | bytes 2097152 | tf_op jit(solution)/shard_map/all_to_all | solution.py:109
  22.5 2.3 %copy-start.6 = (f32[2,4,1024]{2,1,0:T(4,128)S(1)}, f32[2,4,1024]{2,1,0:T(4,128)}, u32[]{:S(2)}) copy-start(f32[2,4,1024]{2,1,0:T(4,128)} %broadcast_in_dim.179) | copy-start | bytes 98308
  22.5 2.3 %copy-start.7 = (f32[2,4,1024]{2,1,0:T(4,128)S(1)}, f32[2,4,1024]{2,1,0:T(4,128)}, u32[]{:S(2)}) copy-start(f32[2,4,1024]{2,1,0:T(4,128)} %broadcast_in_dim.184) | copy-start | bytes 98308
  30.3 4.0 %copy-start.2 = (f32[32,1024]{1,0:T(8,128)S(1)}, f32[32,1024]{1,0:T(8,128)}, u32[]{:S(2)}) copy-start(f32[32,1024]{1,0:T(8,128)} %get-tuple-element.20) | copy-start | bytes 393220
  34.8 2.0 %copy-start.8 = (f32[1024]{0:T(1024)S(1)}, f32[1024]{0:T(1024)}, u32[]{:S(2)}) copy-start(f32[1024]{0:T(1024)} %param.13) | copy-start | bytes 12292
  38.3 1.6 %copy-start.1 = (bf16[2,512,1024]{2,1,0:T(8,128)(2,1)S(1)}, bf16[2,512,1024]{2,1,0:T(8,128)(2,1)}, u32[]{:S(2)}) copy-start(bf16[2,512,1024]{2,1,0:T(8,128)(2,1)} %get-tuple-element.43) | copy-start | bytes 6291460
  42.6 4.6 %copy-start.4 = (bf16[32,1,2,512]{3,0,2,1:T(8,128)(2,1)S(1)}, bf16[32,1,2,512]{3,0,2,1:T(8,128)(2,1)}, u32[]{:S(2)}) copy-start(bf16[32,1,2,512]{3,0,2,1:T(8,128)(2,1)} %copy-done.3) | copy-start | bytes 196612
  42.6 25.5 %copy-start.5 = (f32[32,1,2,512]{3,2,1,0:T(2,128)S(1)}, f32[32,1,2,512]{3,2,1,0:T(2,128)}, u32[]{:S(2)}) copy-start(f32[32,1,2,512]{3,2,1,0:T(2,128)} %param.11) | copy-start | bytes 393220
  43.6 18.0 %all-to-all-start.1 = ((bf16[8,2,32,1,2,512]{5,2,1,4,3,0:T(8,128)(2,1)}), bf16[8,2,32,1,2,512]{5,2,1,4,3,0:T(8,128)(2,1)S(1)}, u32[]{:S(2)}, u32[]{:S(2)}) async-start(bf16[8,2,32,1,2,512]{5,2,1,4,3,0:T(8,128)(2,1)} %copy.30), calls=%async_computation.1 | async-start | bytes 2097152 | tf_op jit(solution)/shard_map/all_to_all | solution.py:120
  47.2 17.2 %collective-permute-start.2 = (bf16[32,1,2,512]{3,0,2,1:T(8,128)(2,1)S(1)}, bf16[32,1,2,512]{3,0,2,1:T(8,128)(2,1)S(1)}, u32[]{:S(2)}, u32[]{:S(2)}) collective-permute-start(bf16[32,1,2,512]{3,0,2,1:T(8,128)(2,1)S(1)} %copy-done.4), channel_id=1, source_target_pairs={{0,1},{2,3},{4,5},{6,7},{8,9},{10,11},{12,13},{14,15},{16,17},{18,... | collective-permute-start | bytes 196616 | tf_op jit(solution)/shard_map/ppermute | solution.py:28
  48.5 15.9 %collective-permute-start.3 = (bf16[32,1,2,512]{3,0,2,1:T(8,128)(2,1)S(1)}, bf16[32,1,2,512]{3,0,2,1:T(8,128)(2,1)S(1)}, u32[]{:S(2)}, u32[]{:S(2)}) collective-permute-start(bf16[32,1,2,512]{3,0,2,1:T(8,128)(2,1)S(1)} %copy-done.4), channel_id=1, source_target_pairs={{1,0},{3,2},{5,4},{7,6},{9,8},{11,10},{13,12},{15,14},{17,16},{19,... | collective-permute-start | bytes 196616 | tf_op jit(solution)/shard_map/ppermute | solution.py:30
  61.8 6.3 %collective-permute-start.1 = (bf16[32,1,2,512]{3,0,2,1:T(8,128)(2,1)S(1)}, bf16[32,1,2,512]{3,0,2,1:T(8,128)(2,1)S(1)}, u32[]{:S(2)}, u32[]{:S(2)}) collective-permute-start(bf16[32,1,2,512]{3,0,2,1:T(8,128)(2,1)S(1)} %fusion.42), channel_id=1, source_target_pairs={{0,16},{2,18},{4,20},{6,22},{8,24},{10,26},{12,28},{14,30},{16,0},... | collective-permute-start | bytes 196616 | tf_op jit(solution)/shard_map/ppermute | solution.py:96

commit v14 on v13

--- a/solution.py
+++ b/solution.py
@@ -180,15 +180,20 @@
         coord_u = spectral_scaling[c] * base_u
         coord_v = spectral_scaling[c] * base_v
         row_factors = phase_factors(coord_u, row_starts, rows_dev, image)
-        row_cos, row_sin = phase_table(row_factors)
         col_cos, col_sin = phase_table(phase_factors(coord_v, col_starts, LANE_BLOCK, image))
         cols = jnp.concatenate([col_cos, col_sin], axis=2).astype(jnp.bfloat16)
         sky_rows = jnp.transpose(piece[:, c], (1, 0, 2))
         waves = jnp.einsum("fij,fjk->fik", sky_rows, cols, preferred_element_type=jnp.float32)
         wave_c = waves[:, :, :nvis]
         wave_s = waves[:, :, nvis:]
-        sum_re = jnp.sum(row_cos * wave_c - row_sin * wave_s, axis=(0, 1))
-        sum_im = -jnp.sum(row_cos * wave_s + row_sin * wave_c, axis=(0, 1))
+        coarse_c, coarse_s, fine_c, fine_s = row_factors
+        faces, chunks, _ = coarse_c.shape
+        wave_c = wave_c.reshape(faces, chunks, rows_dev, nvis)
+        wave_s = wave_s.reshape(faces, chunks, rows_dev, nvis)
+        part_a = jnp.sum(fine_c * wave_c - fine_s * wave_s, axis=2)
+        part_b = jnp.sum(fine_s * wave_c + fine_c * wave_s, axis=2)
+        sum_re = jnp.sum(coarse_c * part_a - coarse_s * part_b, axis=(0, 1))
+        sum_im = -jnp.sum(coarse_c * part_b + coarse_s * part_a, axis=(0, 1))
         resid_real = scale_vis * (norm_pred * sum_re - recorded_samples[c, 0])
         resid_imag = scale_vis * (norm_pred * sum_im - recorded_samples[c, 1])
         fine_c, fine_s = row_factors[2], row_factors[3]

time: 69.5 us -> 68.9 us (level)
    broadcast_in_dim x6 -> x4, local copies, waits for them, and re-layouts: 1.47 us -> 0.98 us  [tile(): jnp.broadcast_to(a[None, None], (faces, chunks, span, count))]
    reduce_sum x1 -> x2, other arithmetic: 1.96 us -> 1.9 us  [the longest x1 1.84 us: local(): part_a = jnp.sum(fine_c * wave_c - fine_s * wave_s, axis=2)]
where the time goes in v14:
time: 68.9 us; the launch traced here: 68.4 us
  waiting for transfers between devices  18.2 us (26%)
  starting transfers between devices  16.9 us (25%)
  other arithmetic  15.8 us (23%)
  local copies, waits for them, and re-layouts  9.18 us (13%)
  matrix products  6.69 us (10%)
  between operations  1.59 us (2%)
    all_to_all x1, waiting for transfers between devices, reduce_rows(): got = lax.all_to_all(slabs, 'vis', 0, 0, axis_index_groups=groups)  11.8 us
    ppermute x2, starting transfers between devices, exchange(): return lax.ppermute(x, 'vis', [(i, i ^ mask) for i in range(n_vis)])  6.07 us
    all_to_all x1, starting transfers between devices, gather_rows(): lax.all_to_all(jnp.where((slot == 0) == (me < half), mine, theirs), 'vis'...  4.74 us
    dot_general x1, matrix products, local(): jnp.einsum('fij,fjk->fik', sky_rows, cols, preferred_element_type=jnp.flo...  4.02 us
    sin x2, other arithmetic, phase_factors(): jnp.sin(fine)  3.79 us
    ppermute x2, waiting for transfers between devices, exchange(): return lax.ppermute(x, 'vis', [(i, i ^ mask) for i in range(n_vis)])  3.69 us
    all_to_all x1, starting transfers between devices, reduce_rows(): got = lax.all_to_all(slabs, 'vis', 0, 0, axis_index_groups=groups)  3.56 us
    all_to_all x1, waiting for transfers between devices, gather_rows(): lax.all_to_all(jnp.where((slot == 0) == (me < half), mine, theirs), 'vis'...  2.71 us
  transfers between devices with their start and end apart: 6, of which 3 were waited for; matrix products, arithmetic and copies ran while one was open for 23% of the time, Pallas kernels for 0%

profile of v14, /device:TPU:0, one launch (start us, length us, event | category | flops | bytes accessed | tf_op | source)
XLA Modules:
  0.0 68.4 jit_solution(479066415641472882)
XLA Ops:
  0.6 0.0 copy-start
  0.6 0.9 %copy.45 = bf16[32,1,2,512]{3,0,2,1:T(8,128)(2,1)S(1)} copy(f32[32,1,2,512]{3,2,1,0:T(2,128)} %param.11) | data formatting | bytes 196608 | tf_op args[0]
  1.6 0.0 copy-start.3
  1.6 4.1 %collective-permute-start = (bf16[32,1,2,512]{3,0,2,1:T(8,128)(2,1)S(1)}, bf16[32,1,2,512]{3,0,2,1:T(8,128)(2,1)S(1)}, u32[]{:S(2)}, u32[]{:S(2)}) collective-permute-start(bf16[32,1,2,512]{3,0,2,1:T(8,128)(2,1)S(1)} %copy.45), channel_id=1, source_target_pairs={{0,16},{2,18},{4,20},{6,22},{8,24},{10,26},{12,28},{14,30},{16,0},... | collective-permute-start | bytes 196616 | tf_op jit(solution)/shard_map/ppermute | solution.py:96
  5.7 0.8 %fusion.49 = (f32[1,512]{1,0:T(1,128)S(1)}, f32[1,512]{1,0:T(1,128)S(1)}) fusion(f32[2,512]{1,0:T(2,128)} %param.18), kind=kLoop, calls=%fused_computation.102 | loop fusion | bytes 8192 | tf_op jit(solution)/shard_map/slice | solution.py:155
  7.1 1.0 %add_reduce_fusion.2 = (s32[2]{0:T(128)S(1)}, s32[2]{0:T(128)S(1)}) fusion(s32[2,2]{1,0:T(2,128)} %param.19), kind=kLoop, calls=%fused_computation.91 | loop fusion | flops 8 | bytes 32 | tf_op jit(solution)/shard_map/sub | solution.py:169
  8.1 0.1 broadcast_add_fusion.1
  8.2 0.1 add.108
  8.3 0.7 %broadcast_add_fusion = s32[2,16]{1,0:T(2,128)S(1)} fusion(s32[16]{0:T(128)} %constant.81.clone, s32[2]{0:T(128)S(1)} %get-tuple-element.39), kind=kLoop, calls=%fused_computation.93 | loop fusion | flops 32 | bytes 200 | tf_op jit(solution)/shard_map/add | solution.py:172
  9.0 0.1 add.116
  9.1 0.8 %fusion.46 = (f32[1,1,1024]{2,1,0:T(1,128)S(1)}, f32[1,1,1024]{2,1,0:T(1,128)S(1)}) fusion(f32[1,2,1024]{2,1,0:T(2,128)} %param.12), kind=kLoop, calls=%fused_computation.99 | loop fusion | bytes 16384 | tf_op jit(solution)/shard_map/slice | solution.py:197
  9.9 0.0 copy-done
  9.9 0.1 broadcast_bitcast_fusion
  10.0 0.0 collective-permute-done
  10.0 1.1 %broadcast_select_fusion = bf16[8,2,32,1,2,512]{5,2,1,4,3,0:T(8,128)(2,1)} fusion(pred[2]{0:T(512)(128)(4,1)S(1)} %compare_compare_fusion, bf16[32,2,512]{2,0,1:T(8,128)(2,1)S(1)} %bitcast.135, bf16[32,2,512]{2,0,1:T(8,128)(2,1)S(1)} %bitcast.134), kind=kLoop, calls=%fused_computation.33 | loop fusion | flops 524288 | bytes 1179650 | tf_op jit(solution)/shard_map/jit(_where)/select_n | solution.py:110
  11.1 4.7 %all-to-all-start = ((bf16[8,2,32,1,2,512]{5,2,1,4,3,0:T(8,128)(2,1)}), bf16[8,2,32,1,2,512]{5,2,1,4,3,0:T(8,128)(2,1)S(1)}, u32[]{:S(2)}, u32[]{:S(2)}) async-start(bf16[8,2,32,1,2,512]{5,2,1,4,3,0:T(8,128)(2,1)} %broadcast_select_fusion), calls=%async_computation | async-start | bytes 2097152 | tf_op jit(solution)/shard_map/all_to_all | solution.py:109
  15.8 0.7 %fusion.48 = (f32[1024]{0:T(1024)S(1)}, f32[1024]{0:T(1024)S(1)}) fusion(f32[1024]{0:T(1024)} %param.16), kind=kLoop, calls=%fused_computation.101 | loop fusion | bytes 12288 | tf_op jit(solution)/shard_map/cos | solution.py:160
  16.6 0.8 %fusion.47 = (s32[1024,1]{0,1:T(1,128)S(1)}, s32[1024,1]{0,1:T(1,128)S(1)}) fusion(s32[1024,2]{0,1:T(2,128)} %param.15), kind=kLoop, calls=%fused_computation.100 | loop fusion | bytes 16384 | tf_op jit(solution)/shard_map/slice | solution.py:153
  17.4 1.7 %select_reduce_fusion.3 = (f32[1024]{0:T(1024)S(1)}, f32[1024]{0:T(1024)S(1)}, f32[1024]{0:T(1024)S(1)}, f32[1024]{0:T(1024)S(1)}) fusion(f32[512]{0:T(512)S(1)} %bitcast.144, s32[1024]{0:T(1024)S(1)} %bitcast.139, f32[512]{0:T(512)S(1)} %bitcast.143, s32[1024]{0:T(1024)S(1)} %bitcast.138), kind=kLoop, calls=%fused_computation.30 | loop fusion | flops 5238784 | bytes 28672 | tf_op jit(solution)/shard_map/reduce_sum | solution.py:39
  19.1 0.0 copy-done.3
  19.1 0.2 fusion.37
  19.3 2.0 %fusion.17 = (f32[128,1024]{1,0:T(8,128)S(1)}, f32[128,1024]{1,0:T(8,128)S(1)}) fusion(f32[128]{0:T(128)S(1)} %iota_convert_fusion.1, f32[1024]{0:T(1024)S(1)} %get-tuple-element.71, s32[1024]{0:T(1024)S(1)} %get-tuple-element.40), kind=kLoop, calls=%fused_computation.35 | loop fusion | flops 1048576 | bytes 1057280 | tf_op jit(solution)/shard_map/sin | solution.py:57
  21.3 0.6 broadcast_in_dim.157
  21.9 0.6 broadcast_in_dim.162
  22.6 0.0 copy-start.6
  22.6 1.8 %fusion.32 = (f32[32,1024]{1,0:T(8,128)S(1)}, f32[32,1024]{1,0:T(8,128)}, f32[32,1024]{1,0:T(8,128)S(1)}, f32[32,1024]{1,0:T(8,128)S(1)}) fusion(f32[32]{0:T(128)S(1)} %iota_convert_fusion, f32[1024]{0:T(1024)S(1)} %get-tuple-element.70, s32[1024]{0:T(1024)S(1)} %get-tuple-element.48, f32[32]{0:T(128)S(1)} %convert_element_type.119, s32[32]{0:T(128)S(1)} %add.116), kind=kLoop, calls=%fused_computation.60 | loop fusion | flops 524288 | bytes 532864 | tf_op jit(solution)/shard_map/sin | solution.py:57
  24.3 0.2 broadcast_in_dim.159
  24.6 0.2 broadcast_in_dim.164
  24.8 0.0 copy-done.6
  24.8 0.0 copy-done.7
  24.8 2.7 %fusion.1 = (bf16[2,512,1024]{2,1,0:T(8,128)(2,1)S(1)}, bf16[2,512,1024]{2,1,0:T(8,128)(2,1)}) fusion(f32[512,1024]{1,0:T(8,128)S(1)} %bitcast.127, f32[2,4,1024]{2,1,0:T(4,128)S(1)} %copy-done.7, f32[512,1024]{1,0:T(8,128)S(1)} %bitcast.126, f32[2,4,1024]{2,1,0:T(4,128)S(1)} %copy-done.6), kind=kLoop, calls=%fused_computation.9 | loop fusion | flops 8388608 | bytes 8454144 | tf_op jit(solution)/shard_map/convert
  27.5 2.7 %all-to-all-done = bf16[8,2,32,1,2,512]{5,2,1,4,3,0:T(8,128)(2,1)S(1)} async-done(((bf16[8,2,32,1,2,512]{5,2,1,4,3,0:T(8,128)(2,1)}), bf16[8,2,32,1,2,512]{5,2,1,4,3,0:T(8,128)(2,1)S(1)}, u32[]{:S(2)}, u32[]{:S(2)}) %all-to-all-start) | async-done | bytes 1048608 | tf_op jit(solution)/shard_map/all_to_all | solution.py:109
  30.2 0.1 copy.29
  30.3 0.0 copy-start.2
  30.3 4.0 %fusion.12 = f32[2,512,2048]{2,1,0:T(8,128)S(1)} fusion(bf16[2,512,512]{2,1,0:T(8,128)(2,1)S(1)} %bitcast.128, bf16[2,512,1024]{2,1,0:T(8,128)(2,1)} %get-tuple-element.45, bf16[2,512,1024]{2,1,0:T(8,128)(2,1)S(1)} %get-tuple-element.44), kind=kOutput, calls=%fused_computation.23 | convolution fusion | flops 2155872256 | bytes 13631488 | tf_op jit(solution)/shard_map/fij,fjk->fik/dot_general | solution.py:186
  34.3 0.0 copy-done.2
  34.4 0.0 copy-start.8
  34.4 1.8 %subtract_reduce_fusion = (f32[2,16,1024]{2,1,0:T(8,128)S(1)}, f32[2,16,1024]{2,1,0:T(8,128)S(1)}) fusion(f32[32,1024]{1,0:T(8,128)S(1)} %get-tuple-element.22, f32[32,1024]{1,0:T(8,128)S(1)} %copy-done.2, f32[2,512,2048]{2,1,0:T(8,128)S(1)} %fusion.12), kind=kLoop, calls=%fused_computation.22 | loop fusion | flops 8323072 | bytes 8912896 | tf_op jit(solution)/shard_map/reduce_sum | solution.py:193
  36.2 0.1 fusion.29
  36.3 0.0 copy-done.8
  36.3 0.2 broadcast_in_dim.174
  36.6 0.2 broadcast_in_dim.179
  36.9 0.9 %fusion.5 = bf16[2,512,1024]{2,1,0:T(8,128)(2,1)S(1)} fusion(f32[512,1024]{1,0:T(8,128)S(1)} %bitcast.124, f32[2,16,1024]{2,1,0:T(8,128)S(1)} %bitcast.131, f32[512,1024]{1,0:T(8,128)S(1)} %bitcast.122, f32[2,16,1024]{2,1,0:T(8,128)S(1)} %bitcast.129), kind=kLoop, calls=%fused_computation.13 | loop fusion | flops 4194304 | bytes 6553600 | tf_op jit(solution)/shard_map/convert_element_type | solution.py:203
  37.7 0.0 copy-start.1
  37.8 0.8 %fusion.13 = bf16[2,512,1024]{2,1,0:T(8,128)(2,1)S(1)} fusion(f32[512,1024]{1,0:T(8,128)S(1)} %bitcast.125, f32[2,16,1024]{2,1,0:T(8,128)S(1)} %bitcast.132, f32[512,1024]{1,0:T(8,128)S(1)} %bitcast.123, f32[2,16,1024]{2,1,0:T(8,128)S(1)} %bitcast.130), kind=kLoop, calls=%fused_computation.24 | loop fusion | flops 5242880 | bytes 6553600 | tf_op jit(solution)/shard_map/neg | solution.py:205
  38.6 0.8 %copy-done.1 = bf16[2,512,1024]{2,1,0:T(8,128)(2,1)S(1)} copy-done((bf16[2,512,1024]{2,1,0:T(8,128)(2,1)S(1)}, bf16[2,512,1024]{2,1,0:T(8,128)(2,1)}, u32[]{:S(2)}) %copy-start.1) | copy-done | bytes 2097176
  39.3 2.7 %fusion.14 = bf16[2,512,512]{1,2,0:T(8,128)(2,1)S(1)} fusion(bf16[2,512,1024]{2,1,0:T(8,128)(2,1)S(1)} %fusion.13, bf16[2,512,1024]{2,1,0:T(8,128)(2,1)S(1)} %fusion.5, bf16[2,512,1024]{2,1,0:T(8,128)(2,1)S(1)} %copy-done.1, bf16[2,512,1024]{2,1,0:T(8,128)(2,1)S(1)} %get-tuple-element.44), kind=kOutput, calls=%fused_computation.32 | convolution fusion | flops 2164785152 | bytes 9437184 | tf_op jit(solution)/shard_map/fik,fjk->ifj/dot_general | solution.py:206
  42.0 0.0 copy-start.4
  42.0 0.0 copy-start.5
  42.0 1.1 %copy.30 = bf16[8,2,32,1,2,512]{5,2,1,4,3,0:T(8,128)(2,1)} copy(bf16[8,2,32,1,2,512]{5,2,1,0,4,3:T(8,128)(2,1)S(1)} %bitcast.133) | data formatting | bytes 2097152 | tf_op jit(solution)/shard_map/reshape | solution.py:118
  43.1 3.6 %all-to-all-start.1 = ((bf16[8,2,32,1,2,512]{5,2,1,4,3,0:T(8,128)(2,1)}), bf16[8,2,32,1,2,512]{5,2,1,4,3,0:T(8,128)(2,1)S(1)}, u32[]{:S(2)}, u32[]{:S(2)}) async-start(bf16[8,2,32,1,2,512]{5,2,1,4,3,0:T(8,128)(2,1)} %copy.30), calls=%async_computation.1 | async-start | bytes 2097152 | tf_op jit(solution)/shard_map/all_to_all | solution.py:120
  46.7 0.0 copy-done.4
  46.7 1.3 %collective-permute-start.2 = (bf16[32,1,2,512]{3,0,2,1:T(8,128)(2,1)S(1)}, bf16[32,1,2,512]{3,0,2,1:T(8,128)(2,1)S(1)}, u32[]{:S(2)}, u32[]{:S(2)}) collective-permute-start(bf16[32,1,2,512]{3,0,2,1:T(8,128)(2,1)S(1)} %copy-done.4), channel_id=1, source_target_pairs={{0,1},{2,3},{4,5},{6,7},{8,9},{10,11},{12,13},{14,15},{16,17},{18,... | collective-permute-start | bytes 196616 | tf_op jit(solution)/shard_map/ppermute | solution.py:28
  48.0 1.3 %collective-permute-start.3 = (bf16[32,1,2,512]{3,0,2,1:T(8,128)(2,1)S(1)}, bf16[32,1,2,512]{3,0,2,1:T(8,128)(2,1)S(1)}, u32[]{:S(2)}, u32[]{:S(2)}) collective-permute-start(bf16[32,1,2,512]{3,0,2,1:T(8,128)(2,1)S(1)} %copy-done.4), channel_id=1, source_target_pairs={{1,0},{3,2},{5,4},{7,6},{9,8},{11,10},{13,12},{15,14},{17,16},{19,... | collective-permute-start | bytes 196616 | tf_op jit(solution)/shard_map/ppermute | solution.py:30
  49.3 11.8 %all-to-all-done.1 = bf16[8,2,32,1,2,512]{5,2,1,4,3,0:T(8,128)(2,1)S(1)} async-done(((bf16[8,2,32,1,2,512]{5,2,1,4,3,0:T(8,128)(2,1)}), bf16[8,2,32,1,2,512]{5,2,1,4,3,0:T(8,128)(2,1)S(1)}, u32[]{:S(2)}, u32[]{:S(2)}) %all-to-all-start.1) | async-done | bytes 1048608 | tf_op jit(solution)/shard_map/all_to_all | solution.py:120
  61.1 0.1 convert_reduce_fusion
  61.2 2.0 %collective-permute-start.1 = (bf16[32,1,2,512]{3,0,2,1:T(8,128)(2,1)S(1)}, bf16[32,1,2,512]{3,0,2,1:T(8,128)(2,1)S(1)}, u32[]{:S(2)}, u32[]{:S(2)}) collective-permute-start(bf16[32,1,2,512]{3,0,2,1:T(8,128)(2,1)S(1)} %fusion.36), channel_id=1, source_target_pairs={{0,16},{2,18},{4,20},{6,22},{8,24},{10,26},{12,28},{14,30},{16,0},... | collective-permute-start | bytes 196616 | tf_op jit(solution)/shard_map/ppermute | solution.py:96
  63.2 0.6 maximum_bitcast_fusion
  63.8 0.0 collective-permute-done.2
  63.8 0.0 collective-permute-done.3
  63.8 3.7 %collective-permute-done.1 = bf16[32,1,2,512]{3,0,2,1:T(8,128)(2,1)S(1)} collective-permute-done((bf16[32,1,2,512]{3,0,2,1:T(8,128)(2,1)S(1)}, bf16[32,1,2,512]{3,0,2,1:T(8,128)(2,1)S(1)}, u32[]{:S(2)}, u32[]{:S(2)}) %collective-permute-start.1) | collective-permute-done | bytes 65568 | tf_op jit(solution)/shard_map/ppermute | solution.py:96
  67.5 0.0 copy-done.5
  67.5 0.1 fusion.24
  67.6 0.8 %copy.39 = f32[32,1,2,512]{3,2,1,0:T(2,128)} copy(f32[32,1,2,512]{3,0,2,1:T(8,128)S(1)} %fusion.24) | data formatting | bytes 262144
  (13 shorter events, 0.1 us)
Async XLA Ops:
  0.6 9.2 %copy-start = (s32[4]{0:T(128)S(1)}, s32[4]{0:T(128)}, u32[]{:S(2)}) copy-start(s32[4]{0:T(128)} %param.14) | copy-start | bytes 52
  1.6 17.5 %copy-start.3 = (bf16[32,1,2,512]{3,0,2,1:T(8,128)(2,1)}, bf16[32,1,2,512]{3,0,2,1:T(8,128)(2,1)S(1)}, u32[]{:S(2)}) copy-start(bf16[32,1,2,512]{3,0,2,1:T(8,128)(2,1)S(1)} %copy.45) | copy-start | bytes 196612
  1.6 8.4 %collective-permute-start = (bf16[32,1,2,512]{3,0,2,1:T(8,128)(2,1)S(1)}, bf16[32,1,2,512]{3,0,2,1:T(8,128)(2,1)S(1)}, u32[]{:S(2)}, u32[]{:S(2)}) collective-permute-start(bf16[32,1,2,512]{3,0,2,1:T(8,128)(2,1)S(1)} %copy.45), channel_id=1, source_target_pairs={{0,16},{2,18},{4,20},{6,22},{8,24},{10,26},{12,28},{14,30},{16,0},... | collective-permute-start | bytes 196616 | tf_op jit(solution)/shard_map/ppermute | solution.py:96
  11.1 19.1 %all-to-all-start = ((bf16[8,2,32,1,2,512]{5,2,1,4,3,0:T(8,128)(2,1)}), bf16[8,2,32,1,2,512]{5,2,1,4,3,0:T(8,128)(2,1)S(1)}, u32[]{:S(2)}, u32[]{:S(2)}) async-start(bf16[8,2,32,1,2,512]{5,2,1,4,3,0:T(8,128)(2,1)} %broadcast_select_fusion), calls=%async_computation | async-start | bytes 2097152 | tf_op jit(solution)/shard_map/all_to_all | solution.py:109
  22.6 2.3 %copy-start.6 = (f32[2,4,1024]{2,1,0:T(4,128)S(1)}, f32[2,4,1024]{2,1,0:T(4,128)}, u32[]{:S(2)}) copy-start(f32[2,4,1024]{2,1,0:T(4,128)} %broadcast_in_dim.157) | copy-start | bytes 98308
  22.6 2.3 %copy-start.7 = (f32[2,4,1024]{2,1,0:T(4,128)S(1)}, f32[2,4,1024]{2,1,0:T(4,128)}, u32[]{:S(2)}) copy-start(f32[2,4,1024]{2,1,0:T(4,128)} %broadcast_in_dim.162) | copy-start | bytes 98308
  30.3 4.0 %copy-start.2 = (f32[32,1024]{1,0:T(8,128)S(1)}, f32[32,1024]{1,0:T(8,128)}, u32[]{:S(2)}) copy-start(f32[32,1024]{1,0:T(8,128)} %get-tuple-element.20) | copy-start | bytes 393220
  34.4 1.9 %copy-start.8 = (f32[1024]{0:T(1024)S(1)}, f32[1024]{0:T(1024)}, u32[]{:S(2)}) copy-start(f32[1024]{0:T(1024)} %param.13) | copy-start | bytes 12292
  37.7 1.6 %copy-start.1 = (bf16[2,512,1024]{2,1,0:T(8,128)(2,1)S(1)}, bf16[2,512,1024]{2,1,0:T(8,128)(2,1)}, u32[]{:S(2)}) copy-start(bf16[2,512,1024]{2,1,0:T(8,128)(2,1)} %get-tuple-element.45) | copy-start | bytes 6291460
  42.0 4.6 %copy-start.4 = (bf16[32,1,2,512]{3,0,2,1:T(8,128)(2,1)S(1)}, bf16[32,1,2,512]{3,0,2,1:T(8,128)(2,1)}, u32[]{:S(2)}) copy-start(bf16[32,1,2,512]{3,0,2,1:T(8,128)(2,1)} %copy-done.3) | copy-start | bytes 196612
  42.0 25.5 %copy-start.5 = (f32[32,1,2,512]{3,2,1,0:T(2,128)S(1)}, f32[32,1,2,512]{3,2,1,0:T(2,128)}, u32[]{:S(2)}) copy-start(f32[32,1,2,512]{3,2,1,0:T(2,128)} %param.11) | copy-start | bytes 393220
  43.1 18.0 %all-to-all-start.1 = ((bf16[8,2,32,1,2,512]{5,2,1,4,3,0:T(8,128)(2,1)}), bf16[8,2,32,1,2,512]{5,2,1,4,3,0:T(8,128)(2,1)S(1)}, u32[]{:S(2)}, u32[]{:S(2)}) async-start(bf16[8,2,32,1,2,512]{5,2,1,4,3,0:T(8,128)(2,1)} %copy.30), calls=%async_computation.1 | async-start | bytes 2097152 | tf_op jit(solution)/shard_map/all_to_all | solution.py:120
  46.7 17.2 %collective-permute-start.2 = (bf16[32,1,2,512]{3,0,2,1:T(8,128)(2,1)S(1)}, bf16[32,1,2,512]{3,0,2,1:T(8,128)(2,1)S(1)}, u32[]{:S(2)}, u32[]{:S(2)}) collective-permute-start(bf16[32,1,2,512]{3,0,2,1:T(8,128)(2,1)S(1)} %copy-done.4), channel_id=1, source_target_pairs={{0,1},{2,3},{4,5},{6,7},{8,9},{10,11},{12,13},{14,15},{16,17},{18,... | collective-permute-start | bytes 196616 | tf_op jit(solution)/shard_map/ppermute | solution.py:28
  48.0 15.9 %collective-permute-start.3 = (bf16[32,1,2,512]{3,0,2,1:T(8,128)(2,1)S(1)}, bf16[32,1,2,512]{3,0,2,1:T(8,128)(2,1)S(1)}, u32[]{:S(2)}, u32[]{:S(2)}) collective-permute-start(bf16[32,1,2,512]{3,0,2,1:T(8,128)(2,1)S(1)} %copy-done.4), channel_id=1, source_target_pairs={{1,0},{3,2},{5,4},{7,6},{9,8},{11,10},{13,12},{15,14},{17,16},{19,... | collective-permute-start | bytes 196616 | tf_op jit(solution)/shard_map/ppermute | solution.py:30
  61.2 6.3 %collective-permute-start.1 = (bf16[32,1,2,512]{3,0,2,1:T(8,128)(2,1)S(1)}, bf16[32,1,2,512]{3,0,2,1:T(8,128)(2,1)S(1)}, u32[]{:S(2)}, u32[]{:S(2)}) collective-permute-start(bf16[32,1,2,512]{3,0,2,1:T(8,128)(2,1)S(1)} %fusion.36), channel_id=1, source_target_pairs={{0,16},{2,18},{4,20},{6,22},{8,24},{10,26},{12,28},{14,30},{16,0},... | collective-permute-start | bytes 196616 | tf_op jit(solution)/shard_map/ppermute | solution.py:96

commit v15 on v14

--- a/solution.py
+++ b/solution.py
@@ -4,6 +4,7 @@
 import jax.numpy as jnp
 import numpy as np
 from jax import lax
+from jax.experimental.layout import Layout, with_layout_constraint
 from jax.sharding import PartitionSpec as P
 
 GRID = 64
@@ -116,6 +117,7 @@
     half = n_vis // 2
     me = lax.axis_index("vis")
     slabs = partial.astype(jnp.bfloat16).reshape((half, 2, rows) + partial.shape[1:])
+    slabs = with_layout_constraint(slabs, Layout(tuple(range(slabs.ndim)), None))
     groups = [list(range(half)), list(range(half, n_vis))]
     got = lax.all_to_all(slabs, "vis", 0, 0, axis_index_groups=groups)
     acc = jnp.sum(got.astype(jnp.float32), axis=0)

time: 68.9 us -> 71 us (1.030)
  other arithmetic: 15.8 us -> 18.5 us
    convert_element_type x0 -> x1, local copies, waits for them, and re-layouts: none -> 2.07 us  [reduce_rows(): partial.astype(jnp.bfloat16).reshape((half, 2, rows) + partial.shape[1:])]
    unnamed x22 -> x20, local copies, waits for them, and re-layouts: 2.6 us -> 0.91 us
    reshape x1 -> x0, local copies, waits for them, and re-layouts: 1.06 us -> none  [reduce_rows(): partial.astype(jnp.bfloat16).reshape((half, 2, rows) + partial.shape[1:])]
    convert_element_type x0 -> x1, other arithmetic: none -> 0.96 us  [local(): sky_half = lax.optimization_barrier(patch_intensity.astype(jnp.bfloat16))]
    sub x1, other arithmetic: 0.08 us -> 0.95 us  [local(): patch_intensity - step_size * (norm_grad * gradient + smooth_weight * smo...]
    reduce_sum x1, other arithmetic: 0.15 us -> 0.96 us  [reduce_rows(): acc = jnp.sum(got.astype(jnp.float32), axis=0)]
  transfers between devices with their start and end apart: 6 -> 6, of which waited for: 3 -> 3; matrix products, arithmetic and copies ran while one was open for 23% -> 24% of each run, Pallas kernels for 0% -> 0%
where the time goes in v15:
time: 71 us; the launch traced here: 70.4 us
  other arithmetic  18.5 us (26%)
  waiting for transfers between devices  18.2 us (26%)
  starting transfers between devices  16.9 us (24%)
  local copies, waits for them, and re-layouts  8.53 us (12%)
  matrix products  6.69 us (9%)
  between operations  1.61 us (2%)
    all_to_all x1, waiting for transfers between devices, reduce_rows(): got = lax.all_to_all(slabs, 'vis', 0, 0, axis_index_groups=groups)  11.8 us
    ppermute x2, starting transfers between devices, exchange(): return lax.ppermute(x, 'vis', [(i, i ^ mask) for i in range(n_vis)])  6.05 us
    all_to_all x1, starting transfers between devices, gather_rows(): lax.all_to_all(jnp.where((slot == 0) == (me < half), mine, theirs), 'vis'...  4.74 us
    dot_general x1, matrix products, local(): jnp.einsum('fij,fjk->fik', sky_rows, cols, preferred_element_type=jnp.flo...  4.02 us
    sin x2, other arithmetic, phase_factors(): jnp.sin(fine)  3.79 us
    ppermute x2, waiting for transfers between devices, exchange(): return lax.ppermute(x, 'vis', [(i, i ^ mask) for i in range(n_vis)])  3.72 us
    all_to_all x1, starting transfers between devices, reduce_rows(): got = lax.all_to_all(slabs, 'vis', 0, 0, axis_index_groups=groups)  3.56 us
    all_to_all x1, waiting for transfers between devices, gather_rows(): lax.all_to_all(jnp.where((slot == 0) == (me < half), mine, theirs), 'vis'...  2.71 us
  transfers between devices with their start and end apart: 6, of which 3 were waited for; matrix products, arithmetic and copies ran while one was open for 24% of the time, Pallas kernels for 0%

profile of v15, /device:TPU:0, one launch (start us, length us, event | category | flops | bytes accessed | tf_op | source)
XLA Modules:
  0.0 70.4 jit_solution(17037252714955986834)
XLA Ops:
  0.6 0.0 copy-start
  0.6 1.0 %convert_element_type.109 = bf16[32,1,2,512]{3,2,1,0:T(2,128)(2,1)S(1)} convert(f32[32,1,2,512]{3,2,1,0:T(2,128)} %param.11) | non-fusion elementwise | flops 32768 | bytes 196608 | tf_op jit(solution)/shard_map/convert_element_type | solution.py:149
  1.6 0.0 copy-start.3
  1.6 4.1 %collective-permute-start = (bf16[32,1,2,512]{3,2,1,0:T(2,128)(2,1)S(1)}, bf16[32,1,2,512]{3,2,1,0:T(2,128)(2,1)S(1)}, u32[]{:S(2)}, u32[]{:S(2)}) collective-permute-start(bf16[32,1,2,512]{3,2,1,0:T(2,128)(2,1)S(1)} %convert_element_type.109), channel_id=1, source_target_pairs={{0,16},{2,18},{4,20},{6,22},{8,24},{10,26},{12,28},{14,30},{16,0},... | collective-permute-start | bytes 196616 | tf_op jit(solution)/shard_map/ppermute | solution.py:97
  5.7 0.8 %fusion.48 = (f32[1,512]{1,0:T(1,128)S(1)}, f32[1,512]{1,0:T(1,128)S(1)}) fusion(f32[2,512]{1,0:T(2,128)} %param.18), kind=kLoop, calls=%fused_computation.99 | loop fusion | bytes 8192 | tf_op jit(solution)/shard_map/slice | solution.py:157
  7.1 1.0 %add_reduce_fusion.2 = (s32[2]{0:T(128)S(1)}, s32[2]{0:T(128)S(1)}) fusion(s32[2,2]{1,0:T(2,128)} %param.19), kind=kLoop, calls=%fused_computation.88 | loop fusion | flops 8 | bytes 32 | tf_op jit(solution)/shard_map/sub | solution.py:171
  8.1 0.1 broadcast_add_fusion.1
  8.2 0.1 add.108
  8.3 0.7 %broadcast_add_fusion = s32[2,16]{1,0:T(2,128)S(1)} fusion(s32[16]{0:T(128)} %constant.81.clone, s32[2]{0:T(128)S(1)} %get-tuple-element.35), kind=kLoop, calls=%fused_computation.90 | loop fusion | flops 32 | bytes 200 | tf_op jit(solution)/shard_map/add | solution.py:174
  9.0 0.1 add.116
  9.1 0.8 %fusion.45 = (f32[1,1,1024]{2,1,0:T(1,128)S(1)}, f32[1,1,1024]{2,1,0:T(1,128)S(1)}) fusion(f32[1,2,1024]{2,1,0:T(2,128)} %param.12), kind=kLoop, calls=%fused_computation.96 | loop fusion | bytes 16384 | tf_op jit(solution)/shard_map/slice | solution.py:199
  9.9 0.0 copy-done
  9.9 0.1 broadcast_bitcast_fusion
  10.0 0.0 collective-permute-done
  10.0 1.1 %broadcast_select_fusion = bf16[8,2,32,1,2,512]{5,2,1,4,3,0:T(8,128)(2,1)} fusion(pred[2]{0:T(512)(128)(4,1)S(1)} %compare_compare_fusion, bf16[32,2,512]{2,0,1:T(8,128)(2,1)S(1)} %copy.23, bf16[32,2,512]{2,0,1:T(8,128)(2,1)S(1)} %copy.22), kind=kLoop, calls=%fused_computation.34 | loop fusion | flops 524288 | bytes 1179650 | tf_op jit(solution)/shard_map/jit(_where)/select_n | solution.py:111
  11.2 4.7 %all-to-all-start = ((bf16[8,2,32,1,2,512]{5,2,1,4,3,0:T(8,128)(2,1)}), bf16[8,2,32,1,2,512]{5,2,1,4,3,0:T(8,128)(2,1)S(1)}, u32[]{:S(2)}, u32[]{:S(2)}) async-start(bf16[8,2,32,1,2,512]{5,2,1,4,3,0:T(8,128)(2,1)} %broadcast_select_fusion), calls=%async_computation | async-start | bytes 2097152 | tf_op jit(solution)/shard_map/all_to_all | solution.py:110
  15.9 0.7 %fusion.47 = (f32[1024]{0:T(1024)S(1)}, f32[1024]{0:T(1024)S(1)}) fusion(f32[1024]{0:T(1024)} %param.16), kind=kLoop, calls=%fused_computation.98 | loop fusion | bytes 12288 | tf_op jit(solution)/shard_map/cos | solution.py:162
  16.6 0.8 %fusion.46 = (s32[1024,1]{0,1:T(1,128)S(1)}, s32[1024,1]{0,1:T(1,128)S(1)}) fusion(s32[1024,2]{0,1:T(2,128)} %param.15), kind=kLoop, calls=%fused_computation.97 | loop fusion | bytes 16384 | tf_op jit(solution)/shard_map/slice | solution.py:155
  17.4 1.7 %select_reduce_fusion.3 = (f32[1024]{0:T(1024)S(1)}, f32[1024]{0:T(1024)S(1)}, f32[1024]{0:T(1024)S(1)}, f32[1024]{0:T(1024)S(1)}) fusion(f32[512]{0:T(512)S(1)} %bitcast.127, s32[1024]{0:T(1024)S(1)} %bitcast.122, f32[512]{0:T(512)S(1)} %bitcast.126, s32[1024]{0:T(1024)S(1)} %bitcast.121), kind=kLoop, calls=%fused_computation.30 | loop fusion | flops 5238784 | bytes 28672 | tf_op jit(solution)/shard_map/reduce_sum | solution.py:40
  19.1 0.0 copy-done.3
  19.1 0.2 fusion.36
  19.3 2.0 %fusion.20 = (f32[128,1024]{1,0:T(8,128)S(1)}, f32[128,1024]{1,0:T(8,128)S(1)}) fusion(f32[128]{0:T(128)S(1)} %iota_convert_fusion.1, f32[1024]{0:T(1024)S(1)} %get-tuple-element.67, s32[1024]{0:T(1024)S(1)} %get-tuple-element.36), kind=kLoop, calls=%fused_computation.36 | loop fusion | flops 1048576 | bytes 1057280 | tf_op jit(solution)/shard_map/sin | solution.py:58
  21.4 0.6 broadcast_in_dim.157
  22.0 0.6 broadcast_in_dim.162
  22.6 0.0 copy-start.6
  22.6 1.8 %fusion.31 = (f32[32,1024]{1,0:T(8,128)S(1)}, f32[32,1024]{1,0:T(8,128)}, f32[32,1024]{1,0:T(8,128)S(1)}, f32[32,1024]{1,0:T(8,128)S(1)}) fusion(f32[32]{0:T(128)S(1)} %iota_convert_fusion, f32[1024]{0:T(1024)S(1)} %get-tuple-element.66, s32[1024]{0:T(1024)S(1)} %get-tuple-element.44, f32[32]{0:T(128)S(1)} %convert_element_type.119, s32[32]{0:T(128)S(1)} %add.116), kind=kLoop, calls=%fused_computation.58 | loop fusion | flops 524288 | bytes 532864 | tf_op jit(solution)/shard_map/sin | solution.py:58
  24.4 0.2 broadcast_in_dim.159
  24.6 0.2 broadcast_in_dim.164
  24.9 0.0 copy-done.6
  24.9 0.0 copy-done.7
  24.9 2.7 %fusion.1 = (bf16[2,512,1024]{2,1,0:T(8,128)(2,1)S(1)}, bf16[2,512,1024]{2,1,0:T(8,128)(2,1)}) fusion(f32[512,1024]{1,0:T(8,128)S(1)} %bitcast.111, f32[2,4,1024]{2,1,0:T(4,128)S(1)} %copy-done.7, f32[512,1024]{1,0:T(8,128)S(1)} %bitcast.110, f32[2,4,1024]{2,1,0:T(4,128)S(1)} %copy-done.6), kind=kLoop, calls=%fused_computation.9 | loop fusion | flops 8388608 | bytes 8454144 | tf_op jit(solution)/shard_map/convert
  27.6 2.7 %all-to-all-done = bf16[8,2,32,1,2,512]{5,2,1,4,3,0:T(8,128)(2,1)S(1)} async-done(((bf16[8,2,32,1,2,512]{5,2,1,4,3,0:T(8,128)(2,1)}), bf16[8,2,32,1,2,512]{5,2,1,4,3,0:T(8,128)(2,1)S(1)}, u32[]{:S(2)}, u32[]{:S(2)}) %all-to-all-start) | async-done | bytes 1048608 | tf_op jit(solution)/shard_map/all_to_all | solution.py:110
  30.3 0.1 copy.24
  30.4 0.0 copy-start.2
  30.4 4.0 %fusion.12 = f32[2,512,2048]{2,1,0:T(8,128)S(1)} fusion(bf16[2,512,512]{2,1,0:T(8,128)(2,1)S(1)} %bitcast.112, bf16[2,512,1024]{2,1,0:T(8,128)(2,1)} %get-tuple-element.41, bf16[2,512,1024]{2,1,0:T(8,128)(2,1)S(1)} %get-tuple-element.40), kind=kOutput, calls=%fused_computation.23 | convolution fusion | flops 2155872256 | bytes 13631488 | tf_op jit(solution)/shard_map/fij,fjk->fik/dot_general | solution.py:188
  34.4 0.0 copy-done.2
  34.4 0.0 copy-start.8
  34.4 1.8 %subtract_reduce_fusion = (f32[2,16,1024]{2,1,0:T(8,128)S(1)}, f32[2,16,1024]{2,1,0:T(8,128)S(1)}) fusion(f32[32,1024]{1,0:T(8,128)S(1)} %get-tuple-element.22, f32[32,1024]{1,0:T(8,128)S(1)} %copy-done.2, f32[2,512,2048]{2,1,0:T(8,128)S(1)} %fusion.12), kind=kLoop, calls=%fused_computation.22 | loop fusion | flops 8323072 | bytes 8912896 | tf_op jit(solution)/shard_map/reduce_sum | solution.py:195
  36.3 0.1 fusion.28
  36.3 0.0 copy-done.8
  36.4 0.2 broadcast_in_dim.174
  36.7 0.2 broadcast_in_dim.179
  36.9 0.9 %fusion.5 = bf16[2,512,1024]{2,1,0:T(8,128)(2,1)S(1)} fusion(f32[512,1024]{1,0:T(8,128)S(1)} %bitcast.108, f32[2,16,1024]{2,1,0:T(8,128)S(1)} %bitcast.115, f32[512,1024]{1,0:T(8,128)S(1)} %bitcast.106, f32[2,16,1024]{2,1,0:T(8,128)S(1)} %bitcast.113), kind=kLoop, calls=%fused_computation.13 | loop fusion | flops 4194304 | bytes 6553600 | tf_op jit(solution)/shard_map/convert_element_type | solution.py:205
  37.8 0.0 copy-start.1
  37.8 0.8 %fusion.13 = bf16[2,512,1024]{2,1,0:T(8,128)(2,1)S(1)} fusion(f32[512,1024]{1,0:T(8,128)S(1)} %bitcast.109, f32[2,16,1024]{2,1,0:T(8,128)S(1)} %bitcast.116, f32[512,1024]{1,0:T(8,128)S(1)} %bitcast.107, f32[2,16,1024]{2,1,0:T(8,128)S(1)} %bitcast.114), kind=kLoop, calls=%fused_computation.24 | loop fusion | flops 5242880 | bytes 6553600 | tf_op jit(solution)/shard_map/neg | solution.py:207
  38.6 0.8 %copy-done.1 = bf16[2,512,1024]{2,1,0:T(8,128)(2,1)S(1)} copy-done((bf16[2,512,1024]{2,1,0:T(8,128)(2,1)S(1)}, bf16[2,512,1024]{2,1,0:T(8,128)(2,1)}, u32[]{:S(2)}) %copy-start.1) | copy-done | bytes 2097176
  39.4 2.7 %fusion.17 = bf16[512,2,512]{2,0,1:T(8,128)(2,1)S(1)} fusion(bf16[2,512,1024]{2,1,0:T(8,128)(2,1)S(1)} %fusion.13, bf16[2,512,1024]{2,1,0:T(8,128)(2,1)S(1)} %fusion.5, bf16[2,512,1024]{2,1,0:T(8,128)(2,1)S(1)} %copy-done.1, bf16[2,512,1024]{2,1,0:T(8,128)(2,1)S(1)} %get-tuple-element.40), kind=kOutput, calls=%fused_computation.33 | convolution fusion | flops 2164785152 | bytes 9437184 | tf_op jit(solution)/shard_map/fik,fjk->ifj/dot_general | solution.py:208
  42.1 0.0 copy-start.4
  42.1 0.0 copy-start.5
  42.1 2.1 %copy.25 = bf16[512,2,512]{2,1,0:T(2,128)(2,1)} copy(bf16[512,2,512]{2,0,1:T(8,128)(2,1)S(1)} %fusion.17) | data formatting | bytes 2097152 | tf_op jit(solution)/shard_map/convert_element_type | solution.py:119
  44.2 3.6 %all-to-all-start.1 = ((bf16[8,2,32,1,2,512]{5,4,3,2,1,0:T(2,128)(2,1)}), bf16[8,2,32,1,2,512]{5,4,3,2,1,0:T(2,128)(2,1)S(1)}, u32[]{:S(2)}, u32[]{:S(2)}) async-start(bf16[8,2,32,1,2,512]{5,4,3,2,1,0:T(2,128)(2,1)} %bitcast.26), calls=%async_computation.1 | async-start | bytes 2097152 | tf_op jit(solution)/shard_map/all_to_all | solution.py:122
  47.7 0.0 copy-done.4
  47.7 1.3 %collective-permute-start.2 = (bf16[32,1,2,512]{3,2,1,0:T(2,128)(2,1)S(1)}, bf16[32,1,2,512]{3,2,1,0:T(2,128)(2,1)S(1)}, u32[]{:S(2)}, u32[]{:S(2)}) collective-permute-start(bf16[32,1,2,512]{3,2,1,0:T(2,128)(2,1)S(1)} %copy-done.4), channel_id=1, source_target_pairs={{0,1},{2,3},{4,5},{6,7},{8,9},{10,11},{12,13},{14,15},{16,17},{18,... | collective-permute-start | bytes 196616 | tf_op jit(solution)/shard_map/ppermute | solution.py:29
  49.0 1.3 %collective-permute-start.3 = (bf16[32,1,2,512]{3,2,1,0:T(2,128)(2,1)S(1)}, bf16[32,1,2,512]{3,2,1,0:T(2,128)(2,1)S(1)}, u32[]{:S(2)}, u32[]{:S(2)}) collective-permute-start(bf16[32,1,2,512]{3,2,1,0:T(2,128)(2,1)S(1)} %copy-done.4), channel_id=1, source_target_pairs={{1,0},{3,2},{5,4},{7,6},{9,8},{11,10},{13,12},{15,14},{17,16},{19,... | collective-permute-start | bytes 196616 | tf_op jit(solution)/shard_map/ppermute | solution.py:31
  50.4 11.8 %all-to-all-done.1 = bf16[8,2,32,1,2,512]{5,4,3,2,1,0:T(2,128)(2,1)S(1)} async-done(((bf16[8,2,32,1,2,512]{5,4,3,2,1,0:T(2,128)(2,1)}), bf16[8,2,32,1,2,512]{5,4,3,2,1,0:T(2,128)(2,1)S(1)}, u32[]{:S(2)}, u32[]{:S(2)}) %all-to-all-start.1) | async-done | bytes 1048608 | tf_op jit(solution)/shard_map/all_to_all | solution.py:122
  62.1 1.0 %convert_reduce_fusion = f32[2,32,2,512]{3,2,1,0:T(2,128)S(1)} fusion(bf16[8,2,32,1,2,512]{5,4,3,2,1,0:T(2,128)(2,1)S(1)} %all-to-all-done.1), kind=kLoop, calls=%fused_computation.25 | loop fusion | flops 983040 | bytes 1310720 | tf_op jit(solution)/shard_map/reduce_sum | solution.py:123
  63.1 0.1 fusion.35
  63.2 1.9 %collective-permute-start.1 = (bf16[32,1,2,512]{3,2,1,0:T(2,128)(2,1)S(1)}, bf16[32,1,2,512]{3,2,1,0:T(2,128)(2,1)S(1)}, u32[]{:S(2)}, u32[]{:S(2)}) collective-permute-start(bf16[32,1,2,512]{3,2,1,0:T(2,128)(2,1)S(1)} %fusion.35), channel_id=1, source_target_pairs={{0,16},{2,18},{4,20},{6,22},{8,24},{10,26},{12,28},{14,30},{16,0},... | collective-permute-start | bytes 196616 | tf_op jit(solution)/shard_map/ppermute | solution.py:97
  65.1 0.6 maximum_bitcast_fusion
  65.7 0.0 collective-permute-done.2
  65.8 0.0 collective-permute-done.3
  65.8 3.7 %collective-permute-done.1 = bf16[32,1,2,512]{3,2,1,0:T(2,128)(2,1)S(1)} collective-permute-done((bf16[32,1,2,512]{3,2,1,0:T(2,128)(2,1)S(1)}, bf16[32,1,2,512]{3,2,1,0:T(2,128)(2,1)S(1)}, u32[]{:S(2)}, u32[]{:S(2)}) %collective-permute-start.1) | collective-permute-done | bytes 65568 | tf_op jit(solution)/shard_map/ppermute | solution.py:97
  69.5 0.0 copy-done.5
  69.5 1.0 %multiply_subtract_fusion = f32[32,1,2,512]{3,2,1,0:T(2,128)} fusion(f32[32,1,2,512]{3,2,1,0:T(2,128)S(1)} %copy-done.5, bf16[32,1,2,512]{3,2,1,0:T(2,128)(2,1)S(1)} %collective-permute-done.1, pred[]{:T(512)S(6)} %lt.14, f32[2,32,2,512]{3,2,1,0:T(2,128)S(1)} %convert_reduce_fusion, bf16[32,1,2,512]{3,2,1,0:T(2,128)(2,1)S(1)} %collective-permute-done.3, ...), kind=kLoop, calls=%fused_computation.53 | loop fusion | flops 622592 | bytes 786441 | tf_op jit(solution)/shard_map/sub | solution.py:223
  (14 shorter events, 0.1 us)
Async XLA Ops:
  0.6 9.3 %copy-start = (s32[4]{0:T(128)S(1)}, s32[4]{0:T(128)}, u32[]{:S(2)}) copy-start(s32[4]{0:T(128)} %param.14) | copy-start | bytes 52
  1.6 17.5 %copy-start.3 = (bf16[32,1,2,512]{3,2,1,0:T(2,128)(2,1)}, bf16[32,1,2,512]{3,2,1,0:T(2,128)(2,1)S(1)}, u32[]{:S(2)}) copy-start(bf16[32,1,2,512]{3,2,1,0:T(2,128)(2,1)S(1)} %convert_element_type.109) | copy-start | bytes 196612
  1.6 8.4 %collective-permute-start = (bf16[32,1,2,512]{3,2,1,0:T(2,128)(2,1)S(1)}, bf16[32,1,2,512]{3,2,1,0:T(2,128)(2,1)S(1)}, u32[]{:S(2)}, u32[]{:S(2)}) collective-permute-start(bf16[32,1,2,512]{3,2,1,0:T(2,128)(2,1)S(1)} %convert_element_type.109), channel_id=1, source_target_pairs={{0,16},{2,18},{4,20},{6,22},{8,24},{10,26},{12,28},{14,30},{16,0},... | collective-permute-start | bytes 196616 | tf_op jit(solution)/shard_map/ppermute | solution.py:97
  11.2 19.1 %all-to-all-start = ((bf16[8,2,32,1,2,512]{5,2,1,4,3,0:T(8,128)(2,1)}), bf16[8,2,32,1,2,512]{5,2,1,4,3,0:T(8,128)(2,1)S(1)}, u32[]{:S(2)}, u32[]{:S(2)}) async-start(bf16[8,2,32,1,2,512]{5,2,1,4,3,0:T(8,128)(2,1)} %broadcast_select_fusion), calls=%async_computation | async-start | bytes 2097152 | tf_op jit(solution)/shard_map/all_to_all | solution.py:110
  22.6 2.3 %copy-start.6 = (f32[2,4,1024]{2,1,0:T(4,128)S(1)}, f32[2,4,1024]{2,1,0:T(4,128)}, u32[]{:S(2)}) copy-start(f32[2,4,1024]{2,1,0:T(4,128)} %broadcast_in_dim.157) | copy-start | bytes 98308
  22.6 2.3 %copy-start.7 = (f32[2,4,1024]{2,1,0:T(4,128)S(1)}, f32[2,4,1024]{2,1,0:T(4,128)}, u32[]{:S(2)}) copy-start(f32[2,4,1024]{2,1,0:T(4,128)} %broadcast_in_dim.162) | copy-start | bytes 98308
  30.4 4.0 %copy-start.2 = (f32[32,1024]{1,0:T(8,128)S(1)}, f32[32,1024]{1,0:T(8,128)}, u32[]{:S(2)}) copy-start(f32[32,1024]{1,0:T(8,128)} %get-tuple-element.20) | copy-start | bytes 393220
  34.4 1.9 %copy-start.8 = (f32[1024]{0:T(1024)S(1)}, f32[1024]{0:T(1024)}, u32[]{:S(2)}) copy-start(f32[1024]{0:T(1024)} %param.13) | copy-start | bytes 12292
  37.8 1.6 %copy-start.1 = (bf16[2,512,1024]{2,1,0:T(8,128)(2,1)S(1)}, bf16[2,512,1024]{2,1,0:T(8,128)(2,1)}, u32[]{:S(2)}) copy-start(bf16[2,512,1024]{2,1,0:T(8,128)(2,1)} %get-tuple-element.41) | copy-start | bytes 6291460
  42.1 5.7 %copy-start.4 = (bf16[32,1,2,512]{3,2,1,0:T(2,128)(2,1)S(1)}, bf16[32,1,2,512]{3,2,1,0:T(2,128)(2,1)}, u32[]{:S(2)}) copy-start(bf16[32,1,2,512]{3,2,1,0:T(2,128)(2,1)} %copy-done.3) | copy-start | bytes 196612
  42.1 27.4 %copy-start.5 = (f32[32,1,2,512]{3,2,1,0:T(2,128)S(1)}, f32[32,1,2,512]{3,2,1,0:T(2,128)}, u32[]{:S(2)}) copy-start(f32[32,1,2,512]{3,2,1,0:T(2,128)} %param.11) | copy-start | bytes 393220
  44.2 18.0 %all-to-all-start.1 = ((bf16[8,2,32,1,2,512]{5,4,3,2,1,0:T(2,128)(2,1)}), bf16[8,2,32,1,2,512]{5,4,3,2,1,0:T(2,128)(2,1)S(1)}, u32[]{:S(2)}, u32[]{:S(2)}) async-start(bf16[8,2,32,1,2,512]{5,4,3,2,1,0:T(2,128)(2,1)} %bitcast.26), calls=%async_computation.1 | async-start | bytes 2097152 | tf_op jit(solution)/shard_map/all_to_all | solution.py:122
  47.7 18.0 %collective-permute-start.2 = (bf16[32,1,2,512]{3,2,1,0:T(2,128)(2,1)S(1)}, bf16[32,1,2,512]{3,2,1,0:T(2,128)(2,1)S(1)}, u32[]{:S(2)}, u32[]{:S(2)}) collective-permute-start(bf16[32,1,2,512]{3,2,1,0:T(2,128)(2,1)S(1)} %copy-done.4), channel_id=1, source_target_pairs={{0,1},{2,3},{4,5},{6,7},{8,9},{10,11},{12,13},{14,15},{16,17},{18,... | collective-permute-start | bytes 196616 | tf_op jit(solution)/shard_map/ppermute | solution.py:29
  49.0 16.7 %collective-permute-start.3 = (bf16[32,1,2,512]{3,2,1,0:T(2,128)(2,1)S(1)}, bf16[32,1,2,512]{3,2,1,0:T(2,128)(2,1)S(1)}, u32[]{:S(2)}, u32[]{:S(2)}) collective-permute-start(bf16[32,1,2,512]{3,2,1,0:T(2,128)(2,1)S(1)} %copy-done.4), channel_id=1, source_target_pairs={{1,0},{3,2},{5,4},{7,6},{9,8},{11,10},{13,12},{15,14},{17,16},{19,... | collective-permute-start | bytes 196616 | tf_op jit(solution)/shard_map/ppermute | solution.py:31
  63.2 6.3 %collective-permute-start.1 = (bf16[32,1,2,512]{3,2,1,0:T(2,128)(2,1)S(1)}, bf16[32,1,2,512]{3,2,1,0:T(2,128)(2,1)S(1)}, u32[]{:S(2)}, u32[]{:S(2)}) collective-permute-start(bf16[32,1,2,512]{3,2,1,0:T(2,128)(2,1)S(1)} %fusion.35), channel_id=1, source_target_pairs={{0,16},{2,18},{4,20},{6,22},{8,24},{10,26},{12,28},{14,30},{16,0},... | collective-permute-start | bytes 196616 | tf_op jit(solution)/shard_map/ppermute | solution.py:97

commit v16 on v14

--- a/solution.py
+++ b/solution.py
@@ -197,9 +197,12 @@
         resid_real = scale_vis * (norm_pred * sum_re - recorded_samples[c, 0])
         resid_imag = scale_vis * (norm_pred * sum_im - recorded_samples[c, 1])
         fine_c, fine_s = row_factors[2], row_factors[3]
-        turned_c = fine_c * resid_real[None, :] - fine_s * resid_imag[None, :]
-        turned_s = fine_s * resid_real[None, :] + fine_c * resid_imag[None, :]
-        z_one, z_two = rotate(row_factors, turned_c, turned_s)
+        coarse_c, coarse_s = row_factors[0], row_factors[1]
+        turned = (
+            coarse_c * resid_real[None, None, :] - coarse_s * resid_imag[None, None, :],
+            coarse_s * resid_real[None, None, :] + coarse_c * resid_imag[None, None, :],
+        )
+        z_one, z_two = rotate(turned, fine_c, fine_s)
         z_one = z_one.astype(jnp.bfloat16)
         z_two = z_two.astype(jnp.bfloat16)
         zs = jnp.concatenate([z_one, -z_two], axis=2)

time: 68.9 us -> 68.9 us (level)
  no operation moved by 1% of the time
where the time goes in v16:
time: 68.9 us; the launch traced here: 68.3 us
  waiting for transfers between devices  18.2 us (26%)
  starting transfers between devices  16.9 us (25%)
  other arithmetic  15.8 us (23%)
  local copies, waits for them, and re-layouts  9.18 us (13%)
  matrix products  6.64 us (10%)
  between operations  1.59 us (2%)
    all_to_all x1, waiting for transfers between devices, reduce_rows(): got = lax.all_to_all(slabs, 'vis', 0, 0, axis_index_groups=groups)  11.8 us
    ppermute x2, starting transfers between devices, exchange(): return lax.ppermute(x, 'vis', [(i, i ^ mask) for i in range(n_vis)])  6.07 us
    all_to_all x1, starting transfers between devices, gather_rows(): lax.all_to_all(jnp.where((slot == 0) == (me < half), mine, theirs), 'vis'...  4.74 us
    dot_general x1, matrix products, local(): jnp.einsum('fij,fjk->fik', sky_rows, cols, preferred_element_type=jnp.flo...  3.98 us
    sin x2, other arithmetic, phase_factors(): jnp.sin(fine)  3.8 us
    ppermute x2, waiting for transfers between devices, exchange(): return lax.ppermute(x, 'vis', [(i, i ^ mask) for i in range(n_vis)])  3.71 us
    all_to_all x1, starting transfers between devices, reduce_rows(): got = lax.all_to_all(slabs, 'vis', 0, 0, axis_index_groups=groups)  3.56 us
    all_to_all x1, waiting for transfers between devices, gather_rows(): lax.all_to_all(jnp.where((slot == 0) == (me < half), mine, theirs), 'vis'...  2.7 us
  transfers between devices with their start and end apart: 6, of which 3 were waited for; matrix products, arithmetic and copies ran while one was open for 23% of the time, Pallas kernels for 0%

profile of v16, /device:TPU:0, one launch (start us, length us, event | category | flops | bytes accessed | tf_op | source)
XLA Modules:
  0.0 68.3 jit_solution(3116395053401989622)
XLA Ops:
  0.6 0.0 copy-start
  0.6 0.9 %copy.45 = bf16[32,1,2,512]{3,0,2,1:T(8,128)(2,1)S(1)} copy(f32[32,1,2,512]{3,2,1,0:T(2,128)} %param.11) | data formatting | bytes 196608 | tf_op args[0]
  1.6 0.0 copy-start.3
  1.6 4.1 %collective-permute-start = (bf16[32,1,2,512]{3,0,2,1:T(8,128)(2,1)S(1)}, bf16[32,1,2,512]{3,0,2,1:T(8,128)(2,1)S(1)}, u32[]{:S(2)}, u32[]{:S(2)}) collective-permute-start(bf16[32,1,2,512]{3,0,2,1:T(8,128)(2,1)S(1)} %copy.45), channel_id=1, source_target_pairs={{0,16},{2,18},{4,20},{6,22},{8,24},{10,26},{12,28},{14,30},{16,0},... | collective-permute-start | bytes 196616 | tf_op jit(solution)/shard_map/ppermute | solution.py:96
  5.7 0.8 %fusion.49 = (f32[1,512]{1,0:T(1,128)S(1)}, f32[1,512]{1,0:T(1,128)S(1)}) fusion(f32[2,512]{1,0:T(2,128)} %param.18), kind=kLoop, calls=%fused_computation.102 | loop fusion | bytes 8192 | tf_op jit(solution)/shard_map/slice | solution.py:155
  7.1 1.0 %add_reduce_fusion.2 = (s32[2]{0:T(128)S(1)}, s32[2]{0:T(128)S(1)}) fusion(s32[2,2]{1,0:T(2,128)} %param.19), kind=kLoop, calls=%fused_computation.91 | loop fusion | flops 8 | bytes 32 | tf_op jit(solution)/shard_map/sub | solution.py:169
  8.1 0.1 broadcast_add_fusion.1
  8.2 0.1 add.112
  8.3 0.7 %broadcast_add_fusion = s32[2,16]{1,0:T(2,128)S(1)} fusion(s32[16]{0:T(128)} %constant.81.clone, s32[2]{0:T(128)S(1)} %get-tuple-element.39), kind=kLoop, calls=%fused_computation.93 | loop fusion | flops 32 | bytes 200 | tf_op jit(solution)/shard_map/add | solution.py:172
  9.0 0.1 add.120
  9.1 0.8 %fusion.46 = (f32[1,1,1024]{2,1,0:T(1,128)S(1)}, f32[1,1,1024]{2,1,0:T(1,128)S(1)}) fusion(f32[1,2,1024]{2,1,0:T(2,128)} %param.12), kind=kLoop, calls=%fused_computation.99 | loop fusion | bytes 16384 | tf_op jit(solution)/shard_map/slice | solution.py:197
  9.9 0.0 copy-done
  9.9 0.1 broadcast_bitcast_fusion
  10.0 0.0 collective-permute-done
  10.0 1.1 %broadcast_select_fusion = bf16[8,2,32,1,2,512]{5,2,1,4,3,0:T(8,128)(2,1)} fusion(pred[2]{0:T(512)(128)(4,1)S(1)} %compare_compare_fusion, bf16[32,2,512]{2,0,1:T(8,128)(2,1)S(1)} %bitcast.133, bf16[32,2,512]{2,0,1:T(8,128)(2,1)S(1)} %bitcast.132), kind=kLoop, calls=%fused_computation.33 | loop fusion | flops 524288 | bytes 1179650 | tf_op jit(solution)/shard_map/jit(_where)/select_n | solution.py:110
  11.1 4.7 %all-to-all-start = ((bf16[8,2,32,1,2,512]{5,2,1,4,3,0:T(8,128)(2,1)}), bf16[8,2,32,1,2,512]{5,2,1,4,3,0:T(8,128)(2,1)S(1)}, u32[]{:S(2)}, u32[]{:S(2)}) async-start(bf16[8,2,32,1,2,512]{5,2,1,4,3,0:T(8,128)(2,1)} %broadcast_select_fusion), calls=%async_computation | async-start | bytes 2097152 | tf_op jit(solution)/shard_map/all_to_all | solution.py:109
  15.8 0.7 %fusion.48 = (f32[1024]{0:T(1024)S(1)}, f32[1024]{0:T(1024)S(1)}) fusion(f32[1024]{0:T(1024)} %param.16), kind=kLoop, calls=%fused_computation.101 | loop fusion | bytes 12288 | tf_op jit(solution)/shard_map/cos | solution.py:160
  16.6 0.8 %fusion.47 = (s32[1024,1]{0,1:T(1,128)S(1)}, s32[1024,1]{0,1:T(1,128)S(1)}) fusion(s32[1024,2]{0,1:T(2,128)} %param.15), kind=kLoop, calls=%fused_computation.100 | loop fusion | bytes 16384 | tf_op jit(solution)/shard_map/slice | solution.py:153
  17.4 1.7 %select_reduce_fusion.3 = (f32[1024]{0:T(1024)S(1)}, f32[1024]{0:T(1024)S(1)}, f32[1024]{0:T(1024)S(1)}, f32[1024]{0:T(1024)S(1)}) fusion(f32[512]{0:T(512)S(1)} %bitcast.142, s32[1024]{0:T(1024)S(1)} %bitcast.137, f32[512]{0:T(512)S(1)} %bitcast.141, s32[1024]{0:T(1024)S(1)} %bitcast.136), kind=kLoop, calls=%fused_computation.30 | loop fusion | flops 5238784 | bytes 28672 | tf_op jit(solution)/shard_map/reduce_sum | solution.py:39
  19.1 0.0 copy-done.3
  19.1 0.2 fusion.37
  19.3 2.0 %fusion.17 = (f32[128,1024]{1,0:T(8,128)S(1)}, f32[128,1024]{1,0:T(8,128)S(1)}) fusion(f32[128]{0:T(128)S(1)} %iota_convert_fusion.1, f32[1024]{0:T(1024)S(1)} %get-tuple-element.71, s32[1024]{0:T(1024)S(1)} %get-tuple-element.40), kind=kLoop, calls=%fused_computation.35 | loop fusion | flops 1048576 | bytes 1057280 | tf_op jit(solution)/shard_map/sin | solution.py:57
  21.3 0.6 broadcast_in_dim.69
  21.9 0.6 broadcast_in_dim.74
  22.6 0.0 copy-start.6
  22.6 1.8 %fusion.32 = (f32[32,1024]{1,0:T(8,128)S(1)}, f32[32,1024]{1,0:T(8,128)S(1)}, f32[32,1024]{1,0:T(8,128)S(1)}, f32[32,1024]{1,0:T(8,128)}) fusion(f32[32]{0:T(128)S(1)} %iota_convert_fusion, f32[1024]{0:T(1024)S(1)} %get-tuple-element.70, s32[1024]{0:T(1024)S(1)} %get-tuple-element.48, f32[32]{0:T(128)S(1)} %convert_element_type.119, s32[32]{0:T(128)S(1)} %add.120), kind=kLoop, calls=%fused_computation.60 | loop fusion | flops 524288 | bytes 532864 | tf_op jit(solution)/shard_map/sin | solution.py:57
  24.3 0.2 broadcast_in_dim.71
  24.6 0.2 broadcast_in_dim.76
  24.8 0.0 copy-done.6
  24.8 0.0 copy-done.7
  24.9 2.7 %fusion.1 = (bf16[2,512,1024]{2,1,0:T(8,128)(2,1)S(1)}, bf16[2,512,1024]{2,1,0:T(8,128)(2,1)}) fusion(f32[512,1024]{1,0:T(8,128)S(1)} %bitcast.127, f32[2,4,1024]{2,1,0:T(4,128)S(1)} %copy-done.7, f32[512,1024]{1,0:T(8,128)S(1)} %bitcast.126, f32[2,4,1024]{2,1,0:T(4,128)S(1)} %copy-done.6), kind=kLoop, calls=%fused_computation.9 | loop fusion | flops 8388608 | bytes 8454144 | tf_op jit(solution)/shard_map/convert
  27.5 2.7 %all-to-all-done = bf16[8,2,32,1,2,512]{5,2,1,4,3,0:T(8,128)(2,1)S(1)} async-done(((bf16[8,2,32,1,2,512]{5,2,1,4,3,0:T(8,128)(2,1)}), bf16[8,2,32,1,2,512]{5,2,1,4,3,0:T(8,128)(2,1)S(1)}, u32[]{:S(2)}, u32[]{:S(2)}) %all-to-all-start) | async-done | bytes 1048608 | tf_op jit(solution)/shard_map/all_to_all | solution.py:109
  30.2 0.1 copy.29
  30.3 4.0 %fusion.12 = f32[2,512,2048]{2,1,0:T(8,128)S(1)} fusion(bf16[2,512,512]{2,1,0:T(8,128)(2,1)S(1)} %bitcast.128, bf16[2,512,1024]{2,1,0:T(8,128)(2,1)} %get-tuple-element.45, bf16[2,512,1024]{2,1,0:T(8,128)(2,1)S(1)} %get-tuple-element.44), kind=kOutput, calls=%fused_computation.23 | convolution fusion | flops 2155872256 | bytes 13631488 | tf_op jit(solution)/shard_map/fij,fjk->fik/dot_general | solution.py:186
  34.3 0.0 copy-start.2
  34.3 0.0 copy-start.8
  34.3 1.8 %subtract_reduce_fusion = (f32[2,16,1024]{2,1,0:T(8,128)S(1)}, f32[2,16,1024]{2,1,0:T(8,128)S(1)}) fusion(f32[32,1024]{1,0:T(8,128)S(1)} %get-tuple-element.22, f32[32,1024]{1,0:T(8,128)S(1)} %get-tuple-element.20, f32[2,512,2048]{2,1,0:T(8,128)S(1)} %fusion.12), kind=kLoop, calls=%fused_computation.22 | loop fusion | flops 8323072 | bytes 8912896 | tf_op jit(solution)/shard_map/reduce_sum | solution.py:193
  36.2 0.0 copy-done.2
  36.2 0.1 fusion.29
  36.2 0.0 copy-done.8
  36.3 0.2 mul.385
  36.6 0.2 mul.391
  36.8 0.9 %fusion.5 = bf16[2,512,1024]{2,1,0:T(8,128)(2,1)S(1)} fusion(f32[512,1024]{1,0:T(8,128)S(1)} %bitcast.124, f32[2,16,1024]{2,1,0:T(8,128)S(1)} %get-tuple-element.47, f32[512,1024]{1,0:T(8,128)S(1)} %bitcast.122, f32[2,16,1024]{2,1,0:T(8,128)S(1)} %get-tuple-element.46), kind=kLoop, calls=%fused_computation.13 | loop fusion | flops 4194304 | bytes 6553600 | tf_op jit(solution)/shard_map/convert_element_type | solution.py:206
  37.7 0.0 copy-start.1
  37.7 0.8 %fusion.13 = bf16[2,512,1024]{2,1,0:T(8,128)(2,1)S(1)} fusion(f32[512,1024]{1,0:T(8,128)S(1)} %bitcast.125, f32[2,16,1024]{2,1,0:T(8,128)S(1)} %get-tuple-element.47, f32[512,1024]{1,0:T(8,128)S(1)} %bitcast.123, f32[2,16,1024]{2,1,0:T(8,128)S(1)} %get-tuple-element.46), kind=kLoop, calls=%fused_computation.24 | loop fusion | flops 5242880 | bytes 6553600 | tf_op jit(solution)/shard_map/neg | solution.py:208
  38.5 0.8 %copy-done.1 = bf16[2,512,1024]{2,1,0:T(8,128)(2,1)S(1)} copy-done((bf16[2,512,1024]{2,1,0:T(8,128)(2,1)S(1)}, bf16[2,512,1024]{2,1,0:T(8,128)(2,1)}, u32[]{:S(2)}) %copy-start.1) | copy-done | bytes 2097176
  39.3 2.7 %fusion.14 = bf16[2,512,512]{1,2,0:T(8,128)(2,1)S(1)} fusion(bf16[2,512,1024]{2,1,0:T(8,128)(2,1)S(1)} %fusion.13, bf16[2,512,1024]{2,1,0:T(8,128)(2,1)S(1)} %fusion.5, bf16[2,512,1024]{2,1,0:T(8,128)(2,1)S(1)} %copy-done.1, bf16[2,512,1024]{2,1,0:T(8,128)(2,1)S(1)} %get-tuple-element.44), kind=kOutput, calls=%fused_computation.32 | convolution fusion | flops 2164785152 | bytes 9437184 | tf_op jit(solution)/shard_map/fik,fjk->ifj/dot_general | solution.py:209
  42.0 0.0 copy-start.4
  42.0 0.0 copy-start.5
  42.0 1.1 %copy.30 = bf16[8,2,32,1,2,512]{5,2,1,4,3,0:T(8,128)(2,1)} copy(bf16[8,2,32,1,2,512]{5,2,1,0,4,3:T(8,128)(2,1)S(1)} %bitcast.131) | data formatting | bytes 2097152 | tf_op jit(solution)/shard_map/reshape | solution.py:118
  43.1 3.6 %all-to-all-start.1 = ((bf16[8,2,32,1,2,512]{5,2,1,4,3,0:T(8,128)(2,1)}), bf16[8,2,32,1,2,512]{5,2,1,4,3,0:T(8,128)(2,1)S(1)}, u32[]{:S(2)}, u32[]{:S(2)}) async-start(bf16[8,2,32,1,2,512]{5,2,1,4,3,0:T(8,128)(2,1)} %copy.30), calls=%async_computation.1 | async-start | bytes 2097152 | tf_op jit(solution)/shard_map/all_to_all | solution.py:120
  46.6 0.0 copy-done.4
  46.6 1.3 %collective-permute-start.2 = (bf16[32,1,2,512]{3,0,2,1:T(8,128)(2,1)S(1)}, bf16[32,1,2,512]{3,0,2,1:T(8,128)(2,1)S(1)}, u32[]{:S(2)}, u32[]{:S(2)}) collective-permute-start(bf16[32,1,2,512]{3,0,2,1:T(8,128)(2,1)S(1)} %copy-done.4), channel_id=1, source_target_pairs={{0,1},{2,3},{4,5},{6,7},{8,9},{10,11},{12,13},{14,15},{16,17},{18,... | collective-permute-start | bytes 196616 | tf_op jit(solution)/shard_map/ppermute | solution.py:28
  47.9 1.3 %collective-permute-start.3 = (bf16[32,1,2,512]{3,0,2,1:T(8,128)(2,1)S(1)}, bf16[32,1,2,512]{3,0,2,1:T(8,128)(2,1)S(1)}, u32[]{:S(2)}, u32[]{:S(2)}) collective-permute-start(bf16[32,1,2,512]{3,0,2,1:T(8,128)(2,1)S(1)} %copy-done.4), channel_id=1, source_target_pairs={{1,0},{3,2},{5,4},{7,6},{9,8},{11,10},{13,12},{15,14},{17,16},{19,... | collective-permute-start | bytes 196616 | tf_op jit(solution)/shard_map/ppermute | solution.py:30
  49.2 11.8 %all-to-all-done.1 = bf16[8,2,32,1,2,512]{5,2,1,4,3,0:T(8,128)(2,1)S(1)} async-done(((bf16[8,2,32,1,2,512]{5,2,1,4,3,0:T(8,128)(2,1)}), bf16[8,2,32,1,2,512]{5,2,1,4,3,0:T(8,128)(2,1)S(1)}, u32[]{:S(2)}, u32[]{:S(2)}) %all-to-all-start.1) | async-done | bytes 1048608 | tf_op jit(solution)/shard_map/all_to_all | solution.py:120
  61.0 0.1 convert_reduce_fusion
  61.2 2.0 %collective-permute-start.1 = (bf16[32,1,2,512]{3,0,2,1:T(8,128)(2,1)S(1)}, bf16[32,1,2,512]{3,0,2,1:T(8,128)(2,1)S(1)}, u32[]{:S(2)}, u32[]{:S(2)}) collective-permute-start(bf16[32,1,2,512]{3,0,2,1:T(8,128)(2,1)S(1)} %fusion.36), channel_id=1, source_target_pairs={{0,16},{2,18},{4,20},{6,22},{8,24},{10,26},{12,28},{14,30},{16,0},... | collective-permute-start | bytes 196616 | tf_op jit(solution)/shard_map/ppermute | solution.py:96
  63.2 0.6 maximum_bitcast_fusion
  63.8 0.0 collective-permute-done.2
  63.8 0.0 collective-permute-done.3
  63.8 3.7 %collective-permute-done.1 = bf16[32,1,2,512]{3,0,2,1:T(8,128)(2,1)S(1)} collective-permute-done((bf16[32,1,2,512]{3,0,2,1:T(8,128)(2,1)S(1)}, bf16[32,1,2,512]{3,0,2,1:T(8,128)(2,1)S(1)}, u32[]{:S(2)}, u32[]{:S(2)}) %collective-permute-start.1) | collective-permute-done | bytes 65568 | tf_op jit(solution)/shard_map/ppermute | solution.py:96
  67.5 0.0 copy-done.5
  67.5 0.1 fusion.24
  67.6 0.8 %copy.39 = f32[32,1,2,512]{3,2,1,0:T(2,128)} copy(f32[32,1,2,512]{3,0,2,1:T(8,128)S(1)} %fusion.24) | data formatting | bytes 262144
  (13 shorter events, 0.1 us)
Async XLA Ops:
  0.6 9.2 %copy-start = (s32[4]{0:T(128)S(1)}, s32[4]{0:T(128)}, u32[]{:S(2)}) copy-start(s32[4]{0:T(128)} %param.14) | copy-start | bytes 52
  1.6 17.5 %copy-start.3 = (bf16[32,1,2,512]{3,0,2,1:T(8,128)(2,1)}, bf16[32,1,2,512]{3,0,2,1:T(8,128)(2,1)S(1)}, u32[]{:S(2)}) copy-start(bf16[32,1,2,512]{3,0,2,1:T(8,128)(2,1)S(1)} %copy.45) | copy-start | bytes 196612
  1.6 8.4 %collective-permute-start = (bf16[32,1,2,512]{3,0,2,1:T(8,128)(2,1)S(1)}, bf16[32,1,2,512]{3,0,2,1:T(8,128)(2,1)S(1)}, u32[]{:S(2)}, u32[]{:S(2)}) collective-permute-start(bf16[32,1,2,512]{3,0,2,1:T(8,128)(2,1)S(1)} %copy.45), channel_id=1, source_target_pairs={{0,16},{2,18},{4,20},{6,22},{8,24},{10,26},{12,28},{14,30},{16,0},... | collective-permute-start | bytes 196616 | tf_op jit(solution)/shard_map/ppermute | solution.py:96
  11.1 19.1 %all-to-all-start = ((bf16[8,2,32,1,2,512]{5,2,1,4,3,0:T(8,128)(2,1)}), bf16[8,2,32,1,2,512]{5,2,1,4,3,0:T(8,128)(2,1)S(1)}, u32[]{:S(2)}, u32[]{:S(2)}) async-start(bf16[8,2,32,1,2,512]{5,2,1,4,3,0:T(8,128)(2,1)} %broadcast_select_fusion), calls=%async_computation | async-start | bytes 2097152 | tf_op jit(solution)/shard_map/all_to_all | solution.py:109
  22.6 2.3 %copy-start.6 = (f32[2,4,1024]{2,1,0:T(4,128)S(1)}, f32[2,4,1024]{2,1,0:T(4,128)}, u32[]{:S(2)}) copy-start(f32[2,4,1024]{2,1,0:T(4,128)} %broadcast_in_dim.69) | copy-start | bytes 98308
  22.6 2.3 %copy-start.7 = (f32[2,4,1024]{2,1,0:T(4,128)S(1)}, f32[2,4,1024]{2,1,0:T(4,128)}, u32[]{:S(2)}) copy-start(f32[2,4,1024]{2,1,0:T(4,128)} %broadcast_in_dim.74) | copy-start | bytes 98308
  34.3 1.9 %copy-start.2 = (f32[32,1024]{1,0:T(8,128)S(1)}, f32[32,1024]{1,0:T(8,128)}, u32[]{:S(2)}) copy-start(f32[32,1024]{1,0:T(8,128)} %get-tuple-element.23) | copy-start | bytes 393220
  34.3 1.9 %copy-start.8 = (f32[1024]{0:T(1024)S(1)}, f32[1024]{0:T(1024)}, u32[]{:S(2)}) copy-start(f32[1024]{0:T(1024)} %param.13) | copy-start | bytes 12292
  37.7 1.6 %copy-start.1 = (bf16[2,512,1024]{2,1,0:T(8,128)(2,1)S(1)}, bf16[2,512,1024]{2,1,0:T(8,128)(2,1)}, u32[]{:S(2)}) copy-start(bf16[2,512,1024]{2,1,0:T(8,128)(2,1)} %get-tuple-element.45) | copy-start | bytes 6291460
  42.0 4.6 %copy-start.4 = (bf16[32,1,2,512]{3,0,2,1:T(8,128)(2,1)S(1)}, bf16[32,1,2,512]{3,0,2,1:T(8,128)(2,1)}, u32[]{:S(2)}) copy-start(bf16[32,1,2,512]{3,0,2,1:T(8,128)(2,1)} %copy-done.3) | copy-start | bytes 196612
  42.0 25.5 %copy-start.5 = (f32[32,1,2,512]{3,2,1,0:T(2,128)S(1)}, f32[32,1,2,512]{3,2,1,0:T(2,128)}, u32[]{:S(2)}) copy-start(f32[32,1,2,512]{3,2,1,0:T(2,128)} %param.11) | copy-start | bytes 393220
  43.1 18.0 %all-to-all-start.1 = ((bf16[8,2,32,1,2,512]{5,2,1,4,3,0:T(8,128)(2,1)}), bf16[8,2,32,1,2,512]{5,2,1,4,3,0:T(8,128)(2,1)S(1)}, u32[]{:S(2)}, u32[]{:S(2)}) async-start(bf16[8,2,32,1,2,512]{5,2,1,4,3,0:T(8,128)(2,1)} %copy.30), calls=%async_computation.1 | async-start | bytes 2097152 | tf_op jit(solution)/shard_map/all_to_all | solution.py:120
  46.6 17.2 %collective-permute-start.2 = (bf16[32,1,2,512]{3,0,2,1:T(8,128)(2,1)S(1)}, bf16[32,1,2,512]{3,0,2,1:T(8,128)(2,1)S(1)}, u32[]{:S(2)}, u32[]{:S(2)}) collective-permute-start(bf16[32,1,2,512]{3,0,2,1:T(8,128)(2,1)S(1)} %copy-done.4), channel_id=1, source_target_pairs={{0,1},{2,3},{4,5},{6,7},{8,9},{10,11},{12,13},{14,15},{16,17},{18,... | collective-permute-start | bytes 196616 | tf_op jit(solution)/shard_map/ppermute | solution.py:28
  47.9 15.9 %collective-permute-start.3 = (bf16[32,1,2,512]{3,0,2,1:T(8,128)(2,1)S(1)}, bf16[32,1,2,512]{3,0,2,1:T(8,128)(2,1)S(1)}, u32[]{:S(2)}, u32[]{:S(2)}) collective-permute-start(bf16[32,1,2,512]{3,0,2,1:T(8,128)(2,1)S(1)} %copy-done.4), channel_id=1, source_target_pairs={{1,0},{3,2},{5,4},{7,6},{9,8},{11,10},{13,12},{15,14},{17,16},{19,... | collective-permute-start | bytes 196616 | tf_op jit(solution)/shard_map/ppermute | solution.py:30
  61.2 6.3 %collective-permute-start.1 = (bf16[32,1,2,512]{3,0,2,1:T(8,128)(2,1)S(1)}, bf16[32,1,2,512]{3,0,2,1:T(8,128)(2,1)S(1)}, u32[]{:S(2)}, u32[]{:S(2)}) collective-permute-start(bf16[32,1,2,512]{3,0,2,1:T(8,128)(2,1)S(1)} %fusion.36), channel_id=1, source_target_pairs={{0,16},{2,18},{4,20},{6,22},{8,24},{10,26},{12,28},{14,30},{16,0},... | collective-permute-start | bytes 196616 | tf_op jit(solution)/shard_map/ppermute | solution.py:96

commit v17 on v16

--- a/solution.py
+++ b/solution.py
@@ -202,10 +202,10 @@
             coarse_c * resid_real[None, None, :] - coarse_s * resid_imag[None, None, :],
             coarse_s * resid_real[None, None, :] + coarse_c * resid_imag[None, None, :],
         )
-        z_one, z_two = rotate(turned, fine_c, fine_s)
-        z_one = z_one.astype(jnp.bfloat16)
-        z_two = z_two.astype(jnp.bfloat16)
-        zs = jnp.concatenate([z_one, -z_two], axis=2)
+        first = (jnp.concatenate([turned[0], -turned[1]], axis=2), jnp.concatenate([turned[1], turned[0]], axis=2))
+        fine_cc = jnp.concatenate([fine_c, fine_c], axis=1)
+        fine_ss = jnp.concatenate([fine_s, fine_s], axis=1)
+        zs = rotate(first, fine_cc, fine_ss)[0].astype(jnp.bfloat16)
         grad = jnp.einsum("fik,fjk->ifj", zs, cols, preferred_element_type=jnp.float32)
         new_rows.append(grad)
         residuals.append(jnp.stack([resid_real, resid_imag], axis=0))

time: 68.9 us -> 69.8 us (1.013)
  other arithmetic: 15.8 us -> 17.6 us
    concatenate x0 -> x3, other arithmetic: none -> 1.47 us  [the longest x1 0.72 us: local(): fine_cc = jnp.concatenate([fine_c, fine_c], axis=1)]
    convert_element_type x1, other arithmetic: 0.88 us -> 2.02 us  [local(): zs = rotate(first, fine_cc, fine_ss)[0].astype(jnp.bfloat16)]
    broadcast_in_dim x2 -> x4, local copies, waits for them, and re-layouts: 0.49 us -> 1.48 us  [tile(): jnp.broadcast_to(a[None, None], (faces, chunks, span, count))]
    neg x1, other arithmetic: 0.79 us -> 0.04 us  [local(): -turned[1]]
    unnamed x22 -> x26, local copies, waits for them, and re-layouts: 2.6 us -> 2.05 us
  transfers between devices with their start and end apart: 6 -> 6, of which waited for: 3 -> 3; matrix products, arithmetic and copies ran while one was open for 23% -> 24% of each run, Pallas kernels for 0% -> 0%
where the time goes in v17:
time: 69.8 us; the launch traced here: 69.2 us
  other arithmetic  17.6 us (25%)
  waiting for transfers between devices  17.6 us (25%)
  starting transfers between devices  16.9 us (24%)
  local copies, waits for them, and re-layouts  9.1 us (13%)
  matrix products  6.35 us (9%)
  between operations  1.63 us (2%)
    all_to_all x1, waiting for transfers between devices, reduce_rows(): got = lax.all_to_all(slabs, 'vis', 0, 0, axis_index_groups=groups)  11.8 us
    ppermute x2, starting transfers between devices, exchange(): return lax.ppermute(x, 'vis', [(i, i ^ mask) for i in range(n_vis)])  6.07 us
    all_to_all x1, starting transfers between devices, gather_rows(): lax.all_to_all(jnp.where((slot == 0) == (me < half), mine, theirs), 'vis'...  4.74 us
    dot_general x1, matrix products, local(): jnp.einsum('fij,fjk->fik', sky_rows, cols, preferred_element_type=jnp.flo...  3.98 us
    sin x2, other arithmetic, phase_factors(): jnp.sin(fine)  3.8 us
    ppermute x2, waiting for transfers between devices, exchange(): return lax.ppermute(x, 'vis', [(i, i ^ mask) for i in range(n_vis)])  3.69 us
    all_to_all x1, starting transfers between devices, reduce_rows(): got = lax.all_to_all(slabs, 'vis', 0, 0, axis_index_groups=groups)  3.56 us
    another operation x2, other arithmetic  2.67 us
  transfers between devices with their start and end apart: 6, of which 3 were waited for; matrix products, arithmetic and copies ran while one was open for 24% of the time, Pallas kernels for 0%

profile of v17, /device:TPU:0, one launch (start us, length us, event | category | flops | bytes accessed | tf_op | source)
XLA Modules:
  0.0 69.2 jit_solution(11104973496300383211)
XLA Ops:
  0.6 0.0 copy-start
  0.6 0.9 %copy.45 = bf16[32,1,2,512]{3,0,2,1:T(8,128)(2,1)S(1)} copy(f32[32,1,2,512]{3,2,1,0:T(2,128)} %param.11) | data formatting | bytes 196608 | tf_op args[0]
  1.6 0.0 copy-start.5
  1.6 4.1 %collective-permute-start = (bf16[32,1,2,512]{3,0,2,1:T(8,128)(2,1)S(1)}, bf16[32,1,2,512]{3,0,2,1:T(8,128)(2,1)S(1)}, u32[]{:S(2)}, u32[]{:S(2)}) collective-permute-start(bf16[32,1,2,512]{3,0,2,1:T(8,128)(2,1)S(1)} %copy.45), channel_id=1, source_target_pairs={{0,16},{2,18},{4,20},{6,22},{8,24},{10,26},{12,28},{14,30},{16,0},... | collective-permute-start | bytes 196616 | tf_op jit(solution)/shard_map/ppermute | solution.py:96
  5.7 0.8 %fusion.42 = (f32[1,512]{1,0:T(1,128)S(1)}, f32[1,512]{1,0:T(1,128)S(1)}) fusion(f32[2,512]{1,0:T(2,128)} %param.18), kind=kLoop, calls=%fused_computation.99 | loop fusion | bytes 8192 | tf_op jit(solution)/shard_map/slice | solution.py:155
  7.1 1.0 %add_reduce_fusion.2 = (s32[2]{0:T(128)S(1)}, s32[2]{0:T(128)S(1)}) fusion(s32[2,2]{1,0:T(2,128)} %param.19), kind=kLoop, calls=%fused_computation.87 | loop fusion | flops 8 | bytes 32 | tf_op jit(solution)/shard_map/sub | solution.py:169
  8.1 0.1 broadcast_add_fusion.1
  8.2 0.1 add.105
  8.3 0.7 %broadcast_add_fusion = s32[2,16]{1,0:T(2,128)S(1)} fusion(s32[16]{0:T(128)} %constant.81.clone, s32[2]{0:T(128)S(1)} %get-tuple-element.39), kind=kLoop, calls=%fused_computation.89 | loop fusion | flops 32 | bytes 200 | tf_op jit(solution)/shard_map/add | solution.py:172
  9.0 0.1 add.113
  9.1 0.8 %fusion.39 = (f32[1,1,1024]{2,1,0:T(1,128)S(1)}, f32[1,1,1024]{2,1,0:T(1,128)S(1)}) fusion(f32[1,2,1024]{2,1,0:T(2,128)} %param.12), kind=kLoop, calls=%fused_computation.96 | loop fusion | bytes 16384 | tf_op jit(solution)/shard_map/slice | solution.py:197
  9.9 0.0 copy-done
  9.9 0.1 broadcast_bitcast_fusion
  10.0 0.0 collective-permute-done
  10.0 0.8 %fusion.40 = (s32[1024,1]{0,1:T(1,128)S(1)}, s32[1024,1]{0,1:T(1,128)S(1)}) fusion(s32[1024,2]{0,1:T(2,128)} %param.15), kind=kLoop, calls=%fused_computation.97 | loop fusion | bytes 16384 | tf_op jit(solution)/shard_map/slice | solution.py:153
  10.8 1.1 %broadcast_select_fusion = bf16[8,2,32,1,2,512]{5,2,1,4,3,0:T(8,128)(2,1)} fusion(pred[2]{0:T(512)(128)(4,1)S(1)} %compare_compare_fusion, bf16[32,2,512]{2,0,1:T(8,128)(2,1)S(1)} %bitcast.120, bf16[32,2,512]{2,0,1:T(8,128)(2,1)S(1)} %bitcast.119), kind=kLoop, calls=%fused_computation.25 | loop fusion | flops 524288 | bytes 1179650 | tf_op jit(solution)/shard_map/jit(_where)/select_n | solution.py:110
  11.9 4.7 %all-to-all-start = ((bf16[8,2,32,1,2,512]{5,2,1,4,3,0:T(8,128)(2,1)}), bf16[8,2,32,1,2,512]{5,2,1,4,3,0:T(8,128)(2,1)S(1)}, u32[]{:S(2)}, u32[]{:S(2)}) async-start(bf16[8,2,32,1,2,512]{5,2,1,4,3,0:T(8,128)(2,1)} %broadcast_select_fusion), calls=%async_computation | async-start | bytes 2097152 | tf_op jit(solution)/shard_map/all_to_all | solution.py:109
  16.6 1.6 %select_reduce_fusion.3 = (f32[1024]{0:T(1024)S(1)}, f32[1024]{0:T(1024)S(1)}, f32[1024]{0:T(1024)S(1)}, f32[1024]{0:T(1024)S(1)}) fusion(f32[512]{0:T(512)S(1)} %bitcast.129, s32[1024]{0:T(1024)S(1)} %bitcast.124, f32[512]{0:T(512)S(1)} %bitcast.128, s32[1024]{0:T(1024)S(1)} %bitcast.123), kind=kLoop, calls=%fused_computation.22 | loop fusion | flops 5238784 | bytes 28672 | tf_op jit(solution)/shard_map/reduce_sum | solution.py:39
  18.3 0.7 %fusion.41 = (f32[1024]{0:T(1024)S(1)}, f32[1024]{0:T(1024)S(1)}) fusion(f32[1024]{0:T(1024)} %param.16), kind=kLoop, calls=%fused_computation.98 | loop fusion | bytes 12288 | tf_op jit(solution)/shard_map/cos | solution.py:160
  19.0 0.0 copy-done.5
  19.1 0.2 fusion.29
  19.3 2.0 %fusion.9 = (f32[128,1024]{1,0:T(8,128)S(1)}, f32[128,1024]{1,0:T(8,128)S(1)}) fusion(f32[128]{0:T(128)S(1)} %iota_convert_fusion.1, f32[1024]{0:T(1024)S(1)} %get-tuple-element.74, s32[1024]{0:T(1024)S(1)} %get-tuple-element.42), kind=kLoop, calls=%fused_computation.27 | loop fusion | flops 1048576 | bytes 1057280 | tf_op jit(solution)/shard_map/sin | solution.py:57
  21.3 0.6 broadcast_in_dim.151
  21.9 0.6 broadcast_in_dim.156
  22.5 1.8 %fusion.24 = (f32[32,1024]{1,0:T(8,128)S(1)}, f32[32,1024]{1,0:T(8,128)S(1)}, f32[32,1024]{1,0:T(8,128)S(1)}, f32[32,1024]{1,0:T(8,128)}) fusion(f32[32]{0:T(128)S(1)} %iota_convert_fusion, f32[1024]{0:T(1024)S(1)} %get-tuple-element.73, s32[1024]{0:T(1024)S(1)} %get-tuple-element.51, f32[32]{0:T(128)S(1)} %convert_element_type.116, s32[32]{0:T(128)S(1)} %add.113), kind=kLoop, calls=%fused_computation.56 | loop fusion | flops 524288 | bytes 532864 | tf_op jit(solution)/shard_map/sin | solution.py:57
  24.3 0.2 broadcast_in_dim.153
  24.6 0.2 broadcast_in_dim.158
  24.8 0.0 copy-done.8
  24.8 0.0 copy-done.9
  24.8 2.7 %fusion.3 = (bf16[2,512,1024]{2,1,0:T(8,128)(2,1)S(1)}, bf16[2,512,1024]{2,1,0:T(8,128)(2,1)}) fusion(f32[512,1024]{1,0:T(8,128)S(1)} %bitcast.114, f32[2,4,1024]{2,1,0:T(4,128)S(1)} %copy-done.9, f32[512,1024]{1,0:T(8,128)S(1)} %bitcast.113, f32[2,4,1024]{2,1,0:T(4,128)S(1)} %copy-done.8), kind=kLoop, calls=%fused_computation.9 | loop fusion | flops 8388608 | bytes 8454144 | tf_op jit(solution)/shard_map/convert
  27.5 0.7 %pad_maximum_fusion.6 = f32[32,2048]{1,0:T(8,128)} fusion(f32[32,1024]{1,0:T(8,128)S(1)} %get-tuple-element.20), kind=kLoop, calls=%fused_computation.30 | loop fusion | flops 65536 | bytes 393216 | tf_op jit(solution)/shard_map/concatenate | solution.py:206
  28.2 0.7 %pad_maximum_fusion.8 = f32[32,2048]{1,0:T(8,128)} fusion(f32[32,1024]{1,0:T(8,128)S(1)} %get-tuple-element.22), kind=kLoop, calls=%fused_computation.32 | loop fusion | flops 65536 | bytes 393216 | tf_op jit(solution)/shard_map/concatenate | solution.py:207
  28.9 2.1 %all-to-all-done = bf16[8,2,32,1,2,512]{5,2,1,4,3,0:T(8,128)(2,1)S(1)} async-done(((bf16[8,2,32,1,2,512]{5,2,1,4,3,0:T(8,128)(2,1)}), bf16[8,2,32,1,2,512]{5,2,1,4,3,0:T(8,128)(2,1)S(1)}, u32[]{:S(2)}, u32[]{:S(2)}) %all-to-all-start) | async-done | bytes 1048608 | tf_op jit(solution)/shard_map/all_to_all | solution.py:109
  31.0 0.1 copy.29
  31.1 4.0 %fusion.7 = f32[2,512,2048]{2,1,0:T(8,128)S(1)} fusion(bf16[2,512,512]{2,1,0:T(8,128)(2,1)S(1)} %bitcast.115, bf16[2,512,1024]{2,1,0:T(8,128)(2,1)} %get-tuple-element.47, bf16[2,512,1024]{2,1,0:T(8,128)(2,1)S(1)} %get-tuple-element.46), kind=kOutput, calls=%fused_computation.16 | convolution fusion | flops 2155872256 | bytes 13631488 | tf_op jit(solution)/shard_map/fij,fjk->fik/dot_general | solution.py:186
  35.1 0.0 copy-start.2
  35.1 0.0 copy-start.10
  35.1 0.0 copy-start.4
  35.1 1.8 %subtract_reduce_fusion = (f32[2,16,1024]{2,1,0:T(8,128)S(1)}, f32[2,16,1024]{2,1,0:T(8,128)S(1)}) fusion(f32[32,1024]{1,0:T(8,128)S(1)} %get-tuple-element.22, f32[32,1024]{1,0:T(8,128)S(1)} %get-tuple-element.20, f32[2,512,2048]{2,1,0:T(8,128)S(1)} %fusion.7), kind=kLoop, calls=%fused_computation.14 | loop fusion | flops 8323072 | bytes 8912896 | tf_op jit(solution)/shard_map/reduce_sum | solution.py:193
  37.0 0.0 copy-start.3
  37.0 0.0 copy-done.2
  37.0 0.1 fusion.21
  37.2 0.0 copy-done.4
  37.2 0.5 broadcast_in_dim.167
  37.7 0.2 copy-done.3
  37.9 0.5 broadcast_in_dim.171
  38.4 2.0 %fusion.1 = bf16[2,512,2048]{2,1,0:T(8,128)(2,1)S(1)} fusion(f32[512,2048]{1,0:T(8,128)S(1)} %bitcast.112, f32[2,16,2048]{2,1,0:T(8,128)S(1)} %get-tuple-element.50, f32[512,2048]{1,0:T(8,128)S(1)} %bitcast.111, f32[2,16,2048]{2,1,0:T(8,128)S(1)} %get-tuple-element.49), kind=kLoop, calls=%fused_computation.2 | loop fusion | flops 8388608 | bytes 13107200 | tf_op jit(solution)/shard_map/convert_element_type | solution.py:208
  40.5 2.4 %fusion.8 = bf16[2,512,512]{1,2,0:T(8,128)(2,1)S(1)} fusion(bf16[2,512,2048]{2,1,0:T(8,128)(2,1)S(1)} %fusion.1, bf16[2,512,1024]{2,1,0:T(8,128)(2,1)S(1)} %copy-done.1, bf16[2,512,1024]{2,1,0:T(8,128)(2,1)S(1)} %get-tuple-element.46), kind=kOutput, calls=%fused_computation.24 | convolution fusion | flops 2156396544 | bytes 9437184 | tf_op jit(solution)/shard_map/fik,fjk->ifj/dot_general | solution.py:209
  42.9 0.0 copy-start.7
  42.9 1.0 %copy.30 = bf16[8,2,32,1,2,512]{5,2,1,4,3,0:T(8,128)(2,1)} copy(bf16[8,2,32,1,2,512]{5,2,1,0,4,3:T(8,128)(2,1)S(1)} %bitcast.118) | data formatting | bytes 2097152 | tf_op jit(solution)/shard_map/reshape | solution.py:118
  43.9 3.6 %all-to-all-start.1 = ((bf16[8,2,32,1,2,512]{5,2,1,4,3,0:T(8,128)(2,1)}), bf16[8,2,32,1,2,512]{5,2,1,4,3,0:T(8,128)(2,1)S(1)}, u32[]{:S(2)}, u32[]{:S(2)}) async-start(bf16[8,2,32,1,2,512]{5,2,1,4,3,0:T(8,128)(2,1)} %copy.30), calls=%async_computation.1 | async-start | bytes 2097152 | tf_op jit(solution)/shard_map/all_to_all | solution.py:120
  47.5 0.0 copy-done.6
  47.5 1.3 %collective-permute-start.2 = (bf16[32,1,2,512]{3,0,2,1:T(8,128)(2,1)S(1)}, bf16[32,1,2,512]{3,0,2,1:T(8,128)(2,1)S(1)}, u32[]{:S(2)}, u32[]{:S(2)}) collective-permute-start(bf16[32,1,2,512]{3,0,2,1:T(8,128)(2,1)S(1)} %copy-done.6), channel_id=1, source_target_pairs={{0,1},{2,3},{4,5},{6,7},{8,9},{10,11},{12,13},{14,15},{16,17},{18,... | collective-permute-start | bytes 196616 | tf_op jit(solution)/shard_map/ppermute | solution.py:28
  48.8 1.3 %collective-permute-start.3 = (bf16[32,1,2,512]{3,0,2,1:T(8,128)(2,1)S(1)}, bf16[32,1,2,512]{3,0,2,1:T(8,128)(2,1)S(1)}, u32[]{:S(2)}, u32[]{:S(2)}) collective-permute-start(bf16[32,1,2,512]{3,0,2,1:T(8,128)(2,1)S(1)} %copy-done.6), channel_id=1, source_target_pairs={{1,0},{3,2},{5,4},{7,6},{9,8},{11,10},{13,12},{15,14},{17,16},{19,... | collective-permute-start | bytes 196616 | tf_op jit(solution)/shard_map/ppermute | solution.py:30
  50.1 11.8 %all-to-all-done.1 = bf16[8,2,32,1,2,512]{5,2,1,4,3,0:T(8,128)(2,1)S(1)} async-done(((bf16[8,2,32,1,2,512]{5,2,1,4,3,0:T(8,128)(2,1)}), bf16[8,2,32,1,2,512]{5,2,1,4,3,0:T(8,128)(2,1)S(1)}, u32[]{:S(2)}, u32[]{:S(2)}) %all-to-all-start.1) | async-done | bytes 1048608 | tf_op jit(solution)/shard_map/all_to_all | solution.py:120
  61.9 0.1 convert_reduce_fusion
  62.1 2.0 %collective-permute-start.1 = (bf16[32,1,2,512]{3,0,2,1:T(8,128)(2,1)S(1)}, bf16[32,1,2,512]{3,0,2,1:T(8,128)(2,1)S(1)}, u32[]{:S(2)}, u32[]{:S(2)}) collective-permute-start(bf16[32,1,2,512]{3,0,2,1:T(8,128)(2,1)S(1)} %fusion.28), channel_id=1, source_target_pairs={{0,16},{2,18},{4,20},{6,22},{8,24},{10,26},{12,28},{14,30},{16,0},... | collective-permute-start | bytes 196616 | tf_op jit(solution)/shard_map/ppermute | solution.py:96
  64.0 0.6 maximum_bitcast_fusion
  64.6 0.0 collective-permute-done.2
  64.6 0.0 collective-permute-done.3
  64.6 3.7 %collective-permute-done.1 = bf16[32,1,2,512]{3,0,2,1:T(8,128)(2,1)S(1)} collective-permute-done((bf16[32,1,2,512]{3,0,2,1:T(8,128)(2,1)S(1)}, bf16[32,1,2,512]{3,0,2,1:T(8,128)(2,1)S(1)}, u32[]{:S(2)}, u32[]{:S(2)}) %collective-permute-start.1) | collective-permute-done | bytes 65568 | tf_op jit(solution)/shard_map/ppermute | solution.py:96
  68.3 0.0 copy-done.7
  68.3 0.1 fusion.16
  68.4 0.8 %copy.39 = f32[32,1,2,512]{3,2,1,0:T(2,128)} copy(f32[32,1,2,512]{3,0,2,1:T(8,128)S(1)} %fusion.16) | data formatting | bytes 262144
  (19 shorter events, 0.2 us)
Async XLA Ops:
  0.6 9.2 %copy-start = (s32[4]{0:T(128)S(1)}, s32[4]{0:T(128)}, u32[]{:S(2)}) copy-start(s32[4]{0:T(128)} %param.14) | copy-start | bytes 52
  1.6 17.5 %copy-start.5 = (bf16[32,1,2,512]{3,0,2,1:T(8,128)(2,1)}, bf16[32,1,2,512]{3,0,2,1:T(8,128)(2,1)S(1)}, u32[]{:S(2)}) copy-start(bf16[32,1,2,512]{3,0,2,1:T(8,128)(2,1)S(1)} %copy.45) | copy-start | bytes 196612
  1.6 8.4 %collective-permute-start = (bf16[32,1,2,512]{3,0,2,1:T(8,128)(2,1)S(1)}, bf16[32,1,2,512]{3,0,2,1:T(8,128)(2,1)S(1)}, u32[]{:S(2)}, u32[]{:S(2)}) collective-permute-start(bf16[32,1,2,512]{3,0,2,1:T(8,128)(2,1)S(1)} %copy.45), channel_id=1, source_target_pairs={{0,16},{2,18},{4,20},{6,22},{8,24},{10,26},{12,28},{14,30},{16,0},... | collective-permute-start | bytes 196616 | tf_op jit(solution)/shard_map/ppermute | solution.py:96
  11.9 19.1 %all-to-all-start = ((bf16[8,2,32,1,2,512]{5,2,1,4,3,0:T(8,128)(2,1)}), bf16[8,2,32,1,2,512]{5,2,1,4,3,0:T(8,128)(2,1)S(1)}, u32[]{:S(2)}, u32[]{:S(2)}) async-start(bf16[8,2,32,1,2,512]{5,2,1,4,3,0:T(8,128)(2,1)} %broadcast_select_fusion), calls=%async_computation | async-start | bytes 2097152 | tf_op jit(solution)/shard_map/all_to_all | solution.py:109
  22.5 2.3 %copy-start.8 = (f32[2,4,1024]{2,1,0:T(4,128)S(1)}, f32[2,4,1024]{2,1,0:T(4,128)}, u32[]{:S(2)}) copy-start(f32[2,4,1024]{2,1,0:T(4,128)} %broadcast_in_dim.151) | copy-start | bytes 98308
  22.5 2.3 %copy-start.9 = (f32[2,4,1024]{2,1,0:T(4,128)S(1)}, f32[2,4,1024]{2,1,0:T(4,128)}, u32[]{:S(2)}) copy-start(f32[2,4,1024]{2,1,0:T(4,128)} %broadcast_in_dim.156) | copy-start | bytes 98308
  35.1 1.9 %copy-start.2 = (f32[32,1024]{1,0:T(8,128)S(1)}, f32[32,1024]{1,0:T(8,128)}, u32[]{:S(2)}) copy-start(f32[32,1024]{1,0:T(8,128)} %get-tuple-element.23) | copy-start | bytes 393220
  35.1 2.0 %copy-start.10 = (f32[1024]{0:T(1024)S(1)}, f32[1024]{0:T(1024)}, u32[]{:S(2)}) copy-start(f32[1024]{0:T(1024)} %param.13) | copy-start | bytes 12292
  35.1 2.1 %copy-start.4 = (f32[32,2048]{1,0:T(8,128)S(1)}, f32[32,2048]{1,0:T(8,128)}, u32[]{:S(2)}) copy-start(f32[32,2048]{1,0:T(8,128)} %pad_maximum_fusion.6) | copy-start | bytes 786436
  37.0 1.0 %copy-start.3 = (f32[32,2048]{1,0:T(8,128)S(1)}, f32[32,2048]{1,0:T(8,128)}, u32[]{:S(2)}) copy-start(f32[32,2048]{1,0:T(8,128)} %pad_maximum_fusion.8) | copy-start | bytes 786436
  38.4 2.0 %copy-start.1 = (bf16[2,512,1024]{2,1,0:T(8,128)(2,1)S(1)}, bf16[2,512,1024]{2,1,0:T(8,128)(2,1)}, u32[]{:S(2)}) copy-start(bf16[2,512,1024]{2,1,0:T(8,128)(2,1)} %get-tuple-element.47) | copy-start | bytes 6291460
  42.8 4.6 %copy-start.6 = (bf16[32,1,2,512]{3,0,2,1:T(8,128)(2,1)S(1)}, bf16[32,1,2,512]{3,0,2,1:T(8,128)(2,1)}, u32[]{:S(2)}) copy-start(bf16[32,1,2,512]{3,0,2,1:T(8,128)(2,1)} %copy-done.5) | copy-start | bytes 196612
  42.9 25.5 %copy-start.7 = (f32[32,1,2,512]{3,2,1,0:T(2,128)S(1)}, f32[32,1,2,512]{3,2,1,0:T(2,128)}, u32[]{:S(2)}) copy-start(f32[32,1,2,512]{3,2,1,0:T(2,128)} %param.11) | copy-start | bytes 393220
  43.9 18.0 %all-to-all-start.1 = ((bf16[8,2,32,1,2,512]{5,2,1,4,3,0:T(8,128)(2,1)}), bf16[8,2,32,1,2,512]{5,2,1,4,3,0:T(8,128)(2,1)S(1)}, u32[]{:S(2)}, u32[]{:S(2)}) async-start(bf16[8,2,32,1,2,512]{5,2,1,4,3,0:T(8,128)(2,1)} %copy.30), calls=%async_computation.1 | async-start | bytes 2097152 | tf_op jit(solution)/shard_map/all_to_all | solution.py:120
  47.5 17.2 %collective-permute-start.2 = (bf16[32,1,2,512]{3,0,2,1:T(8,128)(2,1)S(1)}, bf16[32,1,2,512]{3,0,2,1:T(8,128)(2,1)S(1)}, u32[]{:S(2)}, u32[]{:S(2)}) collective-permute-start(bf16[32,1,2,512]{3,0,2,1:T(8,128)(2,1)S(1)} %copy-done.6), channel_id=1, source_target_pairs={{0,1},{2,3},{4,5},{6,7},{8,9},{10,11},{12,13},{14,15},{16,17},{18,... | collective-permute-start | bytes 196616 | tf_op jit(solution)/shard_map/ppermute | solution.py:28
  48.8 15.9 %collective-permute-start.3 = (bf16[32,1,2,512]{3,0,2,1:T(8,128)(2,1)S(1)}, bf16[32,1,2,512]{3,0,2,1:T(8,128)(2,1)S(1)}, u32[]{:S(2)}, u32[]{:S(2)}) collective-permute-start(bf16[32,1,2,512]{3,0,2,1:T(8,128)(2,1)S(1)} %copy-done.6), channel_id=1, source_target_pairs={{1,0},{3,2},{5,4},{7,6},{9,8},{11,10},{13,12},{15,14},{17,16},{19,... | collective-permute-start | bytes 196616 | tf_op jit(solution)/shard_map/ppermute | solution.py:30
  62.1 6.3 %collective-permute-start.1 = (bf16[32,1,2,512]{3,0,2,1:T(8,128)(2,1)S(1)}, bf16[32,1,2,512]{3,0,2,1:T(8,128)(2,1)S(1)}, u32[]{:S(2)}, u32[]{:S(2)}) collective-permute-start(bf16[32,1,2,512]{3,0,2,1:T(8,128)(2,1)S(1)} %fusion.28), channel_id=1, source_target_pairs={{0,16},{2,18},{4,20},{6,22},{8,24},{10,26},{12,28},{14,30},{16,0},... | collective-permute-start | bytes 196616 | tf_op jit(solution)/shard_map/ppermute | solution.py:96
